TPU v7x, 32 devices: a whole 2x2x4 slice. The times are simulated.
32 devices in a mesh: group: 2 (over x), dev: 16 (over z, y, core).
Axes of the slice: x: 2, y: 2, z: 4, core: 2. Of those that a mesh axis runs over, the one named last changes fastest.
Arguments:
- suffix_x: bfloat16 [2, 4096, 1600], P('group', 'dev'), may hold values from -6 to 6
- suffix_query: bfloat16 [2, 4096, 1024], P('group', 'dev'), may hold values from -128 to 128
- suffix_keyval: bfloat16 [2, 4096, 2048], P('group', 'dev'), may hold values from -6 to 6
- prefix_keyval: bfloat16 [2, 128, 2048], P('group', 'dev'), may hold values from -6 to 6
- prefix_hidden: bfloat16 [2, 128, 1600], P('group', 'dev'), may hold values from -6 to 6
- kv_weight: bfloat16 [1600, 2048], replicated, may hold values from -0.15625 to 0.15625
- out_weight: bfloat16 [1024, 1600], replicated, may hold values from -0.1875 to 0.1875
- fc_weight: bfloat16 [1600, 3840], P(None, ('group', 'dev')), may hold values from -0.15625 to 0.15625
- proj_weight: bfloat16 [3840, 1600], P(('group', 'dev')), may hold values from -0.09375 to 0.09375
- lengths: int32 [2, 16], P('group'), may hold values from 1 to 256, 2048 in all within a row
- placement: int32 [2, 16], P('group'), may hold values from 0 to 15, each once within a row
- owners: int32 [2, 16], P('group'), may hold values from 0 to 15, each once within a row
- recompute: int32 [2, 2], P('group'), may hold values from 0 to 15
Outputs:
- layer_out: bfloat16 [2, 4096, 1600], P('group', 'dev')
All inputs are finite; a program needn't handle non-finite values.
Results may differ from a plain program's by a relative error of at most 0.008.
Values may be sent and summed in bfloat16 or wider, within the bound.
No kernel may reach another device: no remote copies, remote signals or barrier semaphores. Data moves between devices by JAX's collectives and lax.ppermute only.
A program may use at most 128 MiB of HBM per device.

v0:
```python
import jax
import jax.numpy as jnp
from jax import lax
from jax.sharding import PartitionSpec as P

HEAD_DIM = 64


NEGATIVE = -1e30
EPSILON = 1e-05
SCORE_SCALE = 0.125


def normalize(values_in):
    values_in = values_in.astype(jnp.float32)
    average = jnp.mean(values_in, axis=-1, keepdims=True)
    centered = values_in - average
    variance = jnp.mean(centered * centered, axis=-1, keepdims=True)
    return centered / jnp.sqrt(variance + EPSILON)


def absorb(state, queries, keyval, allowed):
    running_top, running_total, accumulated = state
    head_count = queries.shape[1]
    head_size = queries.shape[2]
    row_count = keyval.shape[0]
    width_att = head_count * head_size
    key_rows = keyval[:, :width_att].reshape(row_count, head_count, head_size)
    val_rows = keyval[:, width_att:].reshape(row_count, head_count, head_size)
    scores = (
        jnp.einsum("qhd,khd->hqk", queries, key_rows, preferred_element_type=jnp.float32)
        * SCORE_SCALE
    )
    scores = jnp.where(allowed[None], scores, NEGATIVE)
    new_top = jnp.maximum(running_top, jnp.max(scores, axis=-1))
    factor = jnp.exp(running_top - new_top)
    weights = jnp.where(allowed[None], jnp.exp(scores - new_top[:, :, None]), 0.0)
    running_total = running_total * factor + jnp.sum(weights, axis=-1)
    weights_low = weights.astype(jnp.bfloat16)
    update = jnp.einsum("hqk,khd->qhd", weights_low, val_rows, preferred_element_type=jnp.float32)
    accumulated = accumulated * jnp.transpose(factor)[:, :, None] + update
    return (new_top, running_total, accumulated)


def per_device(
    suffix_x,
    suffix_query,
    suffix_keyval,
    prefix_keyval,
    prefix_hidden,
    kv_weight,
    out_weight,
    fc_weight,
    proj_weight,
    lengths,
    placement,
    owners,
    recompute,
):
    device_count = lax.axis_size("dev")
    my_device = lax.axis_index("dev")
    slots = suffix_x.shape[1]
    block_rows = prefix_keyval.shape[1]
    width_att = suffix_query.shape[2]
    head_count = width_att // HEAD_DIM
    device_ids = jnp.arange(device_count, dtype=jnp.int32)
    hits = placement[0][:, None] == device_ids[None, :]
    device_length = jnp.sum(jnp.where(hits, lengths[0][:, None], 0), axis=0)
    my_length = jnp.sum(jnp.where(device_ids == my_device, device_length, 0))
    block_ids = jnp.arange(owners.shape[1], dtype=jnp.int32)
    chosen = recompute[0]
    chosen_owner = jnp.sum(
        jnp.where(chosen[:, None] == block_ids[None, :], owners[0][None, :], 0), axis=1
    )
    stale_device = jnp.any(chosen_owner[:, None] == device_ids[None, :], axis=0)
    queries = suffix_query[0].reshape(slots, head_count, HEAD_DIM)
    normed_prefix = normalize(prefix_hidden[0]).astype(jnp.bfloat16)
    fresh = jnp.dot(normed_prefix, kv_weight, preferred_element_type=jnp.float32).astype(
        jnp.bfloat16
    )
    my_stale = jnp.any(chosen_owner == my_device)
    local_kv = jnp.where(my_stale, fresh, prefix_keyval[0])
    skip_device = jnp.zeros_like(stale_device)
    gathered = lax.all_gather(local_kv, "dev", axis=0, tiled=True)
    prefix_count = gathered.shape[0]
    row_device = jnp.arange(prefix_count, dtype=jnp.int32) // block_rows
    skipped = jnp.any((row_device[:, None] == device_ids[None, :]) & skip_device[None, :], axis=1)
    state = (
        jnp.full((head_count, slots), NEGATIVE, jnp.float32),
        jnp.zeros((head_count, slots), jnp.float32),
        jnp.zeros((slots, head_count, HEAD_DIM), jnp.float32),
    )
    key_block = 512 if prefix_count % 512 == 0 else prefix_count
    for block_start in range(0, prefix_count, key_block):
        kept = jnp.logical_not(skipped[block_start : block_start + key_block])
        allowed = jnp.broadcast_to(kept[None, :], (slots, key_block))
        state = absorb(state, queries, gathered[block_start : block_start + key_block], allowed)
    positions = jnp.arange(slots, dtype=jnp.int32)
    causal = (positions[None, :] <= positions[:, None]) & (positions[None, :] < my_length)
    state = absorb(state, queries, suffix_keyval[0], causal)
    final_top, final_total, accumulated = state
    attended = (
        (accumulated / jnp.transpose(final_total)[:, :, None])
        .reshape(slots, width_att)
        .astype(jnp.bfloat16)
    )
    projected = jnp.dot(attended, out_weight, preferred_element_type=jnp.float32)
    residual = suffix_x[0].astype(jnp.float32) + projected
    normed = normalize(residual).astype(jnp.bfloat16)
    fc_full, proj_full = (
        lax.all_gather(fc_weight, ("group", "dev"), axis=1, tiled=True),
        lax.all_gather(proj_weight, ("group", "dev"), axis=0, tiled=True),
    )
    inner = jnp.dot(normed, fc_full, preferred_element_type=jnp.float32)
    activated = jax.nn.gelu(inner, approximate=True).astype(jnp.bfloat16)
    feed_out = jnp.dot(activated, proj_full, preferred_element_type=jnp.float32)
    live = positions[:, None] < my_length
    return jnp.where(live, residual + feed_out, 0.0).astype(jnp.bfloat16)[None]


def solution(mesh):
    return jax.shard_map(
        per_device,
        mesh=mesh,
        in_specs=(
            P("group", "dev", None),
            P("group", "dev", None),
            P("group", "dev", None),
            P("group", "dev", None),
            P("group", "dev", None),
            P(),
            P(),
            P(None, ("group", "dev")),
            P(("group", "dev"), None),
            P("group", None),
            P("group", None),
            P("group", None),
            P("group", None),
        ),
        out_specs=P("group", "dev", None),
        check_vma=False,
    )
```

profile of v0, /device:TPU:0, one launch (start us, length us, event | category | flops | bytes accessed | tf_op | source)
XLA Modules:
  0.0 235.2 jit_solution(8602153443183435182)
XLA Ops:
  6.5 0.0 copy-start
  6.5 0.0 all-gather.3.cloned.1.call-start
  6.6 0.7 all-gather.3.cloned.1.call-update
  7.3 0.0 all-gather.5.cloned.1.call-start
  7.3 0.7 all-gather.5.cloned.1.call-update
  8.0 2.2 fusion.67
  10.3 2.0 copy.33
  12.3 2.1 copy.30
  14.4 0.0 copy-done.8
  14.4 0.0 copy-done.7
  14.4 0.2 fusion.55
  14.6 0.6 compare_reduce_fusion
  15.2 0.0 copy-done.4
  15.2 0.1 convert_reduce_fusion
  15.4 0.2 fusion.46
  15.6 0.0 copy-done.5
  15.6 0.0 copy-start.9
  15.6 0.0 copy-start.10
  15.6 4.5 %fusion.14 = bf16[8,2048]{1,0:T(8,128)(2,1)S(1)} fusion(bf16[1600,2048]{1,0:T(8,128)(2,1)} %param.18, bf16[1,8,2048]{2,1,0:T(8,128)(2,1)S(1)} %copy-done.5, pred[]{:T(512)} %compare_reduce_fusion, bf16[1,8,1600]{2,1,0:T(8,128)(2,1)S(1)} %copy-done.4, f32[8]{0:T(128)S(1)} %add_sqrt_fusion.1, f32[8]{0:T(128)S(1)} %broadcast_multiply_fusion.1), kind=kOutput, calls=%fused_computation.20 | convolution fusion | flops 52512768 | bytes 6644801 | tf_op jit(solution)/shard_map/dot_general | solution.py:78
  20.1 25.2 %all_gather.9 = bf16[128,2048]{1,0:T(8,128)(2,1)S(1)} all-gather(bf16[8,2048]{1,0:T(8,128)(2,1)S(1)} %fusion.14), channel_id=1, replica_groups=mesh['group'=2,'dev'=16] {'dev'}, dimensions={0}, use_global_device_ids=true | all-gather | bytes 557056 | tf_op jit(solution)/shard_map/all_gather | solution.py:84
  45.3 0.7 fusion.68
  46.1 1.8 copy.29
  47.9 2.0 copy.34
  49.9 0.8 copy.31
  50.7 0.0 copy-done.9
  50.8 0.0 copy-done.10
  50.8 0.1 select_reduce_fusion
  50.8 0.6 fusion.56
  51.5 0.6 iota_compare_fusion.2
  52.1 0.1 fusion.42
  52.2 1.6 bitcast_reduce_fusion
  53.9 2.0 fusion.8
  55.9 0.0 copy-start.2
  55.9 0.4 fusion.24
  56.3 1.0 fusion.9
  57.3 0.0 copy-done.2
  57.3 0.0 copy-start.3
  57.3 1.1 fusion.26
  58.5 0.0 copy-done.3
  58.5 0.6 fusion.33
  59.1 0.0 copy-done
  59.1 0.5 copy-done.6
  59.6 1.1 fusion.69
  60.7 1.2 copy-done.1
  61.9 0.2 multiply_reduce_fusion
  62.2 49.0 %all-gather.3.cloned.1.call-done = bf16[1600,3840]{0,1:T(8,128)(2,1)} async-done(((bf16[1600,120]{0,1:T(8,128)(2,1)}), bf16[1600,3840]{0,1:T(8,128)(2,1)}) %all-gather.3.cloned.1.call-update) | async-done | bytes 12288016 | tf_op jit(solution)/shard_map/all_gather | solution.py:111
  111.2 98.2 %all-gather.5.cloned.1.call-done = bf16[3840,1600]{1,0:T(8,128)(2,1)} async-done(((bf16[120,1600]{1,0:T(8,128)(2,1)}), bf16[3840,1600]{1,0:T(8,128)(2,1)}) %all-gather.5.cloned.1.call-update) | async-done | bytes 12288016 | tf_op jit(solution)/shard_map/all_gather | solution.py:112
  209.4 19.0 %fusion.13 = bf16[1,256,1600]{1,2,0:T(8,128)(2,1)} fusion(f32[256,1600]{0,1:T(8,128)} %copy-done.1, bf16[3840,1600]{1,0:T(8,128)(2,1)} %all-gather.5.cloned.1.call-done, bf16[1600,3840]{0,1:T(8,128)(2,1)} %all-gather.3.cloned.1.call-done, f32[256]{0:T(256)S(1)} %add_sqrt_fusion, f32[256]{0:T(256)S(1)} %broadcast_multiply_fusion, ...), kind=kOutput, calls=%fused_computation.18 | convolution fusion | flops 6302760960 | bytes 27035904 | tf_op jit(solution)/shard_map/dot_general | solution.py:116
  (12 shorter events, 0.1 us)
Async XLA Ops:
  6.5 52.6 %copy-start = (bf16[1024,1600]{0,1:T(8,128)(2,1)S(1)}, bf16[1024,1600]{0,1:T(8,128)(2,1)}, u32[]{:S(2)}) copy-start(bf16[1024,1600]{0,1:T(8,128)(2,1)} %param.19) | copy-start | bytes 9830404
  6.5 7.9 %copy-start.8 = (s32[1,2]{1,0:T(1,128)S(1)}, s32[1,2]{1,0:T(1,128)}, u32[]{:S(2)}) copy-start(s32[1,2]{1,0:T(1,128)} %param.25) | copy-start | bytes 28
  6.5 7.9 %copy-start.7 = (s32[1,16]{1,0:T(1,128)S(1)}, s32[1,16]{1,0:T(1,128)}, u32[]{:S(2)}) copy-start(s32[1,16]{1,0:T(1,128)} %param.24) | copy-start | bytes 196
  6.5 8.7 %copy-start.4 = (bf16[1,8,1600]{2,1,0:T(8,128)(2,1)S(1)}, bf16[1,8,1600]{2,1,0:T(8,128)(2,1)}, u32[]{:S(2)}) copy-start(bf16[1,8,1600]{2,1,0:T(8,128)(2,1)} %param.17) | copy-start | bytes 76804
  6.5 9.1 %copy-start.5 = (bf16[1,8,2048]{2,1,0:T(8,128)(2,1)S(1)}, bf16[1,8,2048]{2,1,0:T(8,128)(2,1)}, u32[]{:S(2)}) copy-start(bf16[1,8,2048]{2,1,0:T(8,128)(2,1)} %param.16) | copy-start | bytes 98308
  6.5 104.7 %all-gather.3.cloned.1.call-start = ((), (), s32[]{:S(2)}) async-start(), calls=%async_computation | async-start | bytes 13178880 | tf_op jit(solution)/shard_map/all_gather | solution.py:111
  7.3 202.1 %all-gather.5.cloned.1.call-start = ((), (), s32[]{:S(2)}) async-start(), calls=%async_computation.1 | async-start | bytes 13178880 | tf_op jit(solution)/shard_map/all_gather | solution.py:112
  15.6 35.2 %copy-start.9 = (s32[1,16]{1,0:T(1,128)S(1)}, s32[1,16]{1,0:T(1,128)}, u32[]{:S(2)}) copy-start(s32[1,16]{1,0:T(1,128)} %param.22) | copy-start | bytes 196
  15.6 35.1 %copy-start.10 = (s32[1,16]{1,0:T(1,128)S(1)}, s32[1,16]{1,0:T(1,128)}, u32[]{:S(2)}) copy-start(s32[1,16]{1,0:T(1,128)} %param.23) | copy-start | bytes 196
  55.9 1.4 copy-start.2
  57.3 1.1 copy-start.3
  58.5 1.2 copy-start.6
  60.7 1.2 copy-start.1
Sparse Core Ops, SparseCore 0:
  10.2 100.9 all-gather.2
  114.0 95.2 all-gather.4
where the time goes:
time: 236 us; the launch traced here: 235 us
  waiting for transfers between devices  149 us (63%)
  matrix products  29.9 us (13%)
  blocking collectives  25.2 us (11%)
  local copies, waits for them, and re-layouts  13.6 us (6%)
  between operations  13.6 us (6%)
  other arithmetic  4.28 us (2%)
    all_gather x1, waiting for transfers between devices, per_device(): lax.all_gather(proj_weight, ('group', 'dev'), axis=0, tiled=True)  98.2 us
    all_gather x1, waiting for transfers between devices, per_device(): lax.all_gather(fc_weight, ('group', 'dev'), axis=1, tiled=True)  49 us
    all_gather x1, blocking collectives, per_device(): gathered = lax.all_gather(local_kv, 'dev', axis=0, tiled=True)  25.2 us
    dot_general x1, matrix products, per_device(): feed_out = jnp.dot(activated, proj_full, preferred_element_type=jnp.float32)  19 us
    slice x3, local copies, waits for them, and re-layouts, absorb(): key_rows = keyval[:, :width_att].reshape(row_count, head_count, head_size)  6.07 us
  transfers between devices with their start and end apart: 2, of which 2 were waited for; matrix products, arithmetic and copies ran while one was open for 11% of the time, Pallas kernels for 0%

commit v1 on v0

--- a/solution.py
+++ b/solution.py
@@ -1,7 +1,7 @@
 import jax
 import jax.numpy as jnp
 from jax import lax
-from jax.sharding import PartitionSpec as P
+from jax.sharding import Mesh, PartitionSpec as P
 
 HEAD_DIM = 64
 
@@ -57,8 +57,8 @@
     owners,
     recompute,
 ):
-    device_count = lax.axis_size("dev")
-    my_device = lax.axis_index("dev")
+    device_count = lax.axis_size("chip") * lax.axis_size("core")
+    my_device = lax.axis_index("chip") * lax.axis_size("core") + lax.axis_index("core")
     slots = suffix_x.shape[1]
     block_rows = prefix_keyval.shape[1]
     width_att = suffix_query.shape[2]
@@ -81,7 +81,7 @@
     my_stale = jnp.any(chosen_owner == my_device)
     local_kv = jnp.where(my_stale, fresh, prefix_keyval[0])
     skip_device = jnp.zeros_like(stale_device)
-    gathered = lax.all_gather(local_kv, "dev", axis=0, tiled=True)
+    gathered = lax.all_gather(local_kv, ("chip", "core"), axis=0, tiled=True)
     prefix_count = gathered.shape[0]
     row_device = jnp.arange(prefix_count, dtype=jnp.int32) // block_rows
     skipped = jnp.any((row_device[:, None] == device_ids[None, :]) & skip_device[None, :], axis=1)
@@ -107,36 +107,43 @@
     projected = jnp.dot(attended, out_weight, preferred_element_type=jnp.float32)
     residual = suffix_x[0].astype(jnp.float32) + projected
     normed = normalize(residual).astype(jnp.bfloat16)
-    fc_full, proj_full = (
-        lax.all_gather(fc_weight, ("group", "dev"), axis=1, tiled=True),
-        lax.all_gather(proj_weight, ("group", "dev"), axis=0, tiled=True),
+    fc_part, proj_part = (
+        lax.all_gather(fc_weight, ("group", "chip"), axis=1, tiled=True),
+        lax.all_gather(proj_weight, ("group", "chip"), axis=0, tiled=True),
     )
-    inner = jnp.dot(normed, fc_full, preferred_element_type=jnp.float32)
+    normed_pair = lax.all_gather(normed, "core", axis=0, tiled=True)
+    inner = jnp.dot(normed_pair, fc_part, preferred_element_type=jnp.float32)
     activated = jax.nn.gelu(inner, approximate=True).astype(jnp.bfloat16)
-    feed_out = jnp.dot(activated, proj_full, preferred_element_type=jnp.float32)
+    feed_pair = jnp.dot(activated, proj_part, preferred_element_type=jnp.float32)
+    feed_out = lax.psum_scatter(feed_pair, "core", scatter_dimension=0, tiled=True)
     live = positions[:, None] < my_length
     return jnp.where(live, residual + feed_out, 0.0).astype(jnp.bfloat16)[None]
 
 
 def solution(mesh):
+    group_count, device_count = mesh.devices.shape
+    split = Mesh(
+        mesh.devices.reshape(group_count, device_count // 2, 2), ("group", "chip", "core")
+    )
+    rows = ("chip", "core")
     return jax.shard_map(
         per_device,
-        mesh=mesh,
+        mesh=split,
         in_specs=(
-            P("group", "dev", None),
-            P("group", "dev", None),
-            P("group", "dev", None),
-            P("group", "dev", None),
-            P("group", "dev", None),
+            P("group", rows, None),
+            P("group", rows, None),
+            P("group", rows, None),
+            P("group", rows, None),
+            P("group", rows, None),
             P(),
             P(),
-            P(None, ("group", "dev")),
-            P(("group", "dev"), None),
+            P(None, ("group", "chip", "core")),
+            P(("group", "chip", "core"), None),
             P("group", None),
             P("group", None),
             P("group", None),
             P("group", None),
         ),
-        out_specs=P("group", "dev", None),
+        out_specs=P("group", rows, None),
         check_vma=False,
     )

time: 236 us -> 307 us (1.30)
  waiting for transfers between devices: 149 us -> 212 us
  other arithmetic: 4.28 us -> 13.4 us
    all_gather x2 -> x3, waiting for transfers between devices: 147 us -> 201 us  [the longest x1 99.2 us: per_device(): lax.all_gather(fc_weight, ('group', 'chip'), axis=1, tiled=True)]
    reduce_scatter x0 -> x1, waiting for transfers between devices: none -> 9.49 us  [per_device(): lax.psum_scatter(feed_pair, 'core', scatter_dimension=0, tiled=True)]
    dot_general x1, matrix products: 19 us -> 14.3 us  [per_device(): jnp.dot(activated, proj_part, preferred_element_type=jnp.float32)]
  transfers between devices with their start and end apart: 2 -> 4, of which waited for: 2 -> 4; matrix products, arithmetic and copies ran while one was open for 11% -> 0% of each run, Pallas kernels for 0% -> 0%
where the time goes in v1:
time: 307 us
  waiting for transfers between devices  212 us (69%)
  matrix products  29.6 us (10%)
  blocking collectives  24.6 us (8%)
  local copies, waits for them, and re-layouts  13.8 us (4%)
  other arithmetic  13.4 us (4%)
  between operations  13.2 us (4%)
    all_gather x1, waiting for transfers between devices, per_device(): lax.all_gather(fc_weight, ('group', 'chip'), axis=1, tiled=True)  99.2 us
    all_gather x1, waiting for transfers between devices, per_device(): lax.all_gather(proj_weight, ('group', 'chip'), axis=0, tiled=True)  96.3 us
    all_gather x1, blocking collectives, per_device(): gathered = lax.all_gather(local_kv, ('chip', 'core'), axis=0, tiled=True)  24.6 us
    dot_general x1, matrix products, per_device(): jnp.dot(activated, proj_part, preferred_element_type=jnp.float32)  14.3 us
    reduce_scatter x1, waiting for transfers between devices, per_device(): lax.psum_scatter(feed_pair, 'core', scatter_dimension=0, tiled=True)  9.49 us
  transfers between devices with their start and end apart: 4, of which 4 were waited for; matrix products, arithmetic and copies ran while one was open for 0% of the time, Pallas kernels for 0%

profile of v1, /device:TPU:0, one launch (start us, length us, event | category | flops | bytes accessed | tf_op | source)
XLA Modules:
  0.0 306.9 jit_solution(11257704507788021502)
XLA Ops:
  6.5 0.0 copy-start
  6.5 0.0 all-gather.4.cloned.1.call-start
  6.6 0.9 select_reduce_fusion
  7.5 0.6 fusion.50
  8.1 0.6 iota_compare_fusion.2
  8.8 0.0 copy-start.7
  8.8 0.5 copy-done.7
  9.3 0.7 fusion.36
  10.0 2.2 fusion.61
  12.3 2.1 copy.33
  14.3 2.0 copy.30
  16.4 0.0 copy-done.11
  16.4 0.2 fusion.49
  16.6 0.6 compare_reduce_fusion
  17.2 0.1 convert_reduce_fusion
  17.3 0.2 fusion.40
  17.6 4.5 %fusion.11 = bf16[8,2048]{1,0:T(8,128)(2,1)S(1)} fusion(bf16[1600,2048]{1,0:T(8,128)(2,1)} %param.18, bf16[1,8,2048]{2,1,0:T(8,128)(2,1)S(1)} %copy-done.6, pred[]{:T(512)} %compare_reduce_fusion, bf16[1,8,1600]{2,1,0:T(8,128)(2,1)S(1)} %copy-done.4, f32[8]{0:T(128)S(1)} %add_sqrt_fusion.1, f32[8]{0:T(128)S(1)} %broadcast_multiply_fusion.1), kind=kOutput, calls=%fused_computation.16 | convolution fusion | flops 52512768 | bytes 6644801 | tf_op jit(solution)/shard_map/dot_general | solution.py:78
  22.1 24.6 %all_gather.12 = bf16[128,2048]{1,0:T(8,128)(2,1)S(1)} all-gather(bf16[8,2048]{1,0:T(8,128)(2,1)S(1)} %fusion.11), channel_id=1, replica_groups=mesh['group'=2,'chip'=8,'core'=2] {'chip','core'}, dimensions={0}, use_global_device_ids=true | all-gather | bytes 557056 | tf_op jit(solution)/shard_map/all_gather | solution.py:84
  46.6 0.7 fusion.62
  47.4 1.8 copy.29
  49.2 2.0 copy.34
  51.2 3.0 bitcast_reduce_fusion
  54.2 2.1 fusion.8
  56.3 0.6 copy-done.5
  56.9 0.6 broadcast_maximum_fusion
  57.5 1.6 fusion.9
  59.1 2.1 fusion.24
  61.2 0.8 copy.31
  62.1 2.0 fusion.22
  64.1 0.8 bitcast_add_fusion
  64.9 2.5 fusion.31
  67.4 1.1 fusion.63
  68.5 0.2 multiply_reduce_fusion
  68.8 0.9 copy-done.1
  69.6 1.1 divide_convert_fusion
  70.7 0.0 all-gather.4.cloned.1.call-update
  70.7 0.0 all-gather.6.cloned.1.call-start
  70.8 0.7 all-gather.6.cloned.1.call-update
  71.5 0.0 all-gather.8.cloned.1.call-start
  71.5 0.7 all-gather.8.cloned.1.call-update
  72.2 0.2 reduce-scatter.2.cloned.1.call-start
  72.5 5.5 %all-gather.4.cloned.1.call-done = bf16[512,1600]{0,1:T(8,128)(2,1)} async-done(((bf16[256,1600]{0,1:T(8,128)(2,1)}), bf16[512,1600]{0,1:T(8,128)(2,1)}) %all-gather.4.cloned.1.call-update) | async-done | bytes 1638416 | tf_op jit(solution)/shard_map/all_gather | solution.py:114
  77.9 99.2 %all-gather.6.cloned.1.call-done = bf16[1600,1920]{0,1:T(8,128)(2,1)} async-done(((bf16[1600,120]{0,1:T(8,128)(2,1)}), bf16[1600,1920]{0,1:T(8,128)(2,1)}) %all-gather.6.cloned.1.call-update) | async-done | bytes 6144016 | tf_op jit(solution)/shard_map/all_gather | solution.py:111
  177.2 96.3 %all-gather.8.cloned.1.call-done = bf16[1920,1600]{1,0:T(8,128)(2,1)} async-done(((bf16[120,1600]{1,0:T(8,128)(2,1)}), bf16[1920,1600]{1,0:T(8,128)(2,1)}) %all-gather.8.cloned.1.call-update) | async-done | bytes 6144016 | tf_op jit(solution)/shard_map/all_gather | solution.py:112
  273.5 14.3 %fusion.16 = f32[512,1600]{0,1:T(8,128)} fusion(bf16[1920,1600]{1,0:T(8,128)(2,1)} %all-gather.8.cloned.1.call-done, bf16[512,1600]{0,1:T(8,128)(2,1)} %all-gather.4.cloned.1.call-done, bf16[1600,1920]{0,1:T(8,128)(2,1)} %all-gather.6.cloned.1.call-done), kind=kOutput, calls=%fused_computation.22 | convolution fusion | flops 6300303360 | bytes 17203200 | tf_op jit(solution)/shard_map/dot_general | solution.py:117
  287.8 0.0 reduce-scatter.2.cloned.1.call-update
  287.8 9.5 %reduce-scatter.2.cloned.1.call-done = f32[256,1600]{0,1:T(8,128)} async-done(((f32[512,1600]{0,1:T(8,128)}), f32[256,1600]{0,1:T(8,128)}) %reduce-scatter.2.cloned.1.call-update) | async-done | bytes 1638416 | tf_op jit(solution)/shard_map/reduce_scatter | solution.py:118
  297.3 3.0 fusion.35
  (22 shorter events, 0.1 us)
Async XLA Ops:
  6.5 60.8 %copy-start = (bf16[1024,1600]{0,1:T(8,128)(2,1)S(1)}, bf16[1024,1600]{0,1:T(8,128)(2,1)}, u32[]{:S(2)}) copy-start(bf16[1024,1600]{0,1:T(8,128)(2,1)} %param.19) | copy-start | bytes 9830404
  6.5 9.8 %copy-start.11 = (s32[1,2]{1,0:T(1,128)S(1)}, s32[1,2]{1,0:T(1,128)}, u32[]{:S(2)}) copy-start(s32[1,2]{1,0:T(1,128)} %param.25) | copy-start | bytes 28
  6.5 9.8 %copy-start.10 = (s32[1,16]{1,0:T(1,128)S(1)}, s32[1,16]{1,0:T(1,128)}, u32[]{:S(2)}) copy-start(s32[1,16]{1,0:T(1,128)} %param.24) | copy-start | bytes 196
  6.5 10.7 %copy-start.4 = (bf16[1,8,1600]{2,1,0:T(8,128)(2,1)S(1)}, bf16[1,8,1600]{2,1,0:T(8,128)(2,1)}, u32[]{:S(2)}) copy-start(bf16[1,8,1600]{2,1,0:T(8,128)(2,1)} %param.17) | copy-start | bytes 76804
  6.5 11.0 %copy-start.6 = (bf16[1,8,2048]{2,1,0:T(8,128)(2,1)S(1)}, bf16[1,8,2048]{2,1,0:T(8,128)(2,1)}, u32[]{:S(2)}) copy-start(bf16[1,8,2048]{2,1,0:T(8,128)(2,1)} %param.16) | copy-start | bytes 98308
  6.5 71.4 %all-gather.4.cloned.1.call-start = ((), (), s32[]{:S(2)}) async-start(), calls=%async_computation.1 | async-start | bytes 2457600 | tf_op jit(solution)/shard_map/all_gather | solution.py:114
  8.8 0.5 copy-start.7
  51.2 6.3 %copy-start.2 = (pred[256,256]{0,1:T(8,128)(4,1)S(1)}, pred[256,256]{0,1:T(8,128)(4,1)}, u32[]{:S(2)}) copy-start(pred[256,256]{0,1:T(8,128)(4,1)} %fusion.36) | copy-start | bytes 196612
  54.2 4.9 %copy-start.3 = (bf16[256,1024]{0,1:T(8,128)(2,1)S(1)}, bf16[256,1024]{0,1:T(8,128)(2,1)}, u32[]{:S(2)}) copy-start(bf16[256,1024]{0,1:T(8,128)(2,1)} %copy.34) | copy-start | bytes 1572868
  56.3 0.6 copy-start.5
  62.0 5.3 %copy-start.9 = (bf16[1,256,1600]{1,2,0:T(8,128)(2,1)S(1)}, bf16[1,256,1600]{1,2,0:T(8,128)(2,1)}, u32[]{:S(2)}) copy-start(bf16[1,256,1600]{1,2,0:T(8,128)(2,1)} %param.13) | copy-start | bytes 2457604
  68.5 1.2 copy-start.1
  70.7 106.4 %all-gather.6.cloned.1.call-start = ((), (), s32[]{:S(2)}) async-start(), calls=%async_computation.2 | async-start | bytes 6789120 | tf_op jit(solution)/shard_map/all_gather | solution.py:111
  71.5 202.0 %all-gather.8.cloned.1.call-start = ((), (), s32[]{:S(2)}) async-start(), calls=%async_computation.3 | async-start | bytes 6789120 | tf_op jit(solution)/shard_map/all_gather | solution.py:112
  72.2 225.1 %copy-start.8 = (pred[256]{0:T(512)(128)(4,1)S(1)}, pred[256]{0:T(512)(128)(4,1)}, u32[]{:S(2)}) copy-start(pred[256]{0:T(512)(128)(4,1)} %copy-done.7) | copy-start | bytes 772
  72.2 225.1 %reduce-scatter.2.cloned.1.call-start = ((), (), s32[]{:S(2)}) async-start(), calls=%async_computation.4 | async-start | bytes 4915200 | tf_op jit(solution)/shard_map/reduce_scatter | solution.py:118
Sparse Core Ops, SparseCore 0:
  70.9 7.0 all-gather.3
  80.6 96.4 all-gather.5
  179.9 93.5 all-gather.7
  288.0 9.3 reduce-scatter.1

commit v2 on v0

--- a/solution.py
+++ b/solution.py
@@ -107,11 +107,14 @@
     projected = jnp.dot(attended, out_weight, preferred_element_type=jnp.float32)
     residual = suffix_x[0].astype(jnp.float32) + projected
     normed = normalize(residual).astype(jnp.bfloat16)
-    fc_full, proj_full = (
-        lax.all_gather(fc_weight, ("group", "dev"), axis=1, tiled=True),
-        lax.all_gather(proj_weight, ("group", "dev"), axis=0, tiled=True),
+    hidden_part = fc_weight.shape[1]
+    both = jnp.concatenate([fc_weight.T, proj_weight], axis=0)
+    both_full = lax.all_gather(both, ("group", "dev"), axis=0)
+    fc_rows = both_full[:, :hidden_part].reshape(-1, both.shape[1])
+    proj_full = both_full[:, hidden_part:].reshape(-1, both.shape[1])
+    inner = lax.dot_general(
+        normed, fc_rows, (((1,), (1,)), ((), ())), preferred_element_type=jnp.float32
     )
-    inner = jnp.dot(normed, fc_full, preferred_element_type=jnp.float32)
     activated = jax.nn.gelu(inner, approximate=True).astype(jnp.bfloat16)
     feed_out = jnp.dot(activated, proj_full, preferred_element_type=jnp.float32)
     live = positions[:, None] < my_length

time: 236 us -> 215 us (0.911)
  waiting for transfers between devices: 149 us -> 104 us
  local copies, waits for them, and re-layouts: 13.6 us -> 31.1 us
  other arithmetic: 4.28 us -> 8.57 us
    all_gather x2 -> x1, waiting for transfers between devices: 147 us -> 104 us  [per_device(): both_full = lax.all_gather(both, ('group', 'dev'), axis=0)]
    slice x0 -> x1, local copies, waits for them, and re-layouts: none -> 17.2 us  [per_device(): fc_rows = both_full[:, :hidden_part].reshape(-1, both.shape[1])]
  transfers between devices with their start and end apart: 2 -> 1, of which waited for: 2 -> 1; matrix products, arithmetic and copies ran while one was open for 11% -> 14% of each run, Pallas kernels for 0% -> 0%
where the time goes in v2:
time: 215 us
  waiting for transfers between devices  104 us (48%)
  local copies, waits for them, and re-layouts  31.1 us (14%)
  matrix products  30 us (14%)
  blocking collectives  27.4 us (13%)
  between operations  13.5 us (6%)
  other arithmetic  8.57 us (4%)
    all_gather x1, waiting for transfers between devices, per_device(): both_full = lax.all_gather(both, ('group', 'dev'), axis=0)  104 us
    all_gather x1, blocking collectives, per_device(): gathered = lax.all_gather(local_kv, 'dev', axis=0, tiled=True)  27.4 us
    dot_general x1, matrix products, per_device(): feed_out = jnp.dot(activated, proj_full, preferred_element_type=jnp.float32)  19.2 us
    slice x1, local copies, waits for them, and re-layouts, per_device(): fc_rows = both_full[:, :hidden_part].reshape(-1, both.shape[1])  17.2 us
    slice x3, local copies, waits for them, and re-layouts, absorb(): key_rows = keyval[:, :width_att].reshape(row_count, head_count, head_size)  5.46 us
    slice x3, local copies, waits for them, and re-layouts, absorb(): val_rows = keyval[:, width_att:].reshape(row_count, head_count, head_size)  4.57 us
    dot_general x1, matrix products, per_device(): jnp.dot(normed_prefix, kv_weight, preferred_element_type=jnp.float32)  4.43 us
  transfers between devices with their start and end apart: 1, of which 1 were waited for; matrix products, arithmetic and copies ran while one was open for 14% of the time, Pallas kernels for 0%

profile of v2, /device:TPU:0, one launch (start us, length us, event | category | flops | bytes accessed | tf_op | source)
XLA Modules:
  0.0 214.9 jit_solution(16076185544255898113)
XLA Ops:
  6.5 0.0 copy-start
  6.5 0.0 all-gather.3.cloned.1.call-start
  6.5 2.2 %pad_maximum_fusion = bf16[240,1600]{1,0:T(8,128)(2,1)} fusion(bf16[120,1600]{1,0:T(8,128)(2,1)} %param.21, bf16[120,1600]{1,0:T(8,128)(2,1)} %bitcast.100), kind=kLoop, calls=%fused_computation.46 | loop fusion | flops 1536000 | bytes 1536000 | tf_op jit(solution)/shard_map/concatenate | solution.py:111
  8.8 0.0 all-gather.3.cloned.1.call-update
  8.8 0.9 fusion.55
  9.6 0.6 compare_reduce_fusion
  10.3 0.9 convert_reduce_fusion
  11.1 0.9 fusion.46
  12.1 4.4 %fusion.14 = bf16[8,2048]{1,0:T(8,128)(2,1)S(1)} fusion(bf16[1600,2048]{1,0:T(8,128)(2,1)} %param.18, bf16[1,8,2048]{2,1,0:T(8,128)(2,1)} %param.16, pred[]{:T(512)} %compare_reduce_fusion, bf16[1,8,1600]{2,1,0:T(8,128)(2,1)} %param.17, f32[8]{0:T(128)S(1)} %add_sqrt_fusion.1, f32[8]{0:T(128)S(1)} %broadcast_multiply_fusion.1), kind=kOutput, calls=%fused_computation.20 | convolution fusion | flops 52512768 | bytes 6644801 | tf_op jit(solution)/shard_map/dot_general | solution.py:78
  16.5 0.0 copy-start.7
  16.5 27.4 %all_gather.9 = bf16[128,2048]{1,0:T(8,128)(2,1)S(1)} all-gather(bf16[8,2048]{1,0:T(8,128)(2,1)S(1)} %fusion.14), channel_id=1, replica_groups=mesh['group'=2,'dev'=16] {'dev'}, dimensions={0}, use_global_device_ids=true | all-gather | bytes 557056 | tf_op jit(solution)/shard_map/all_gather | solution.py:84
  44.0 0.7 fusion.69
  44.7 1.8 copy.31
  46.5 0.8 copy.29
  47.3 0.0 copy-start.3
  47.3 2.1 copy.30
  49.5 2.6 %fusion.68 = (bf16[256,1024]{1,0:T(8,128)(2,1)}, bf16[256,1024]{1,0:T(8,128)(2,1)}) fusion(bf16[256,2048]{1,0:T(8,128)(2,1)} %bitcast.97), kind=kLoop, calls=%fused_computation.89 | loop fusion | bytes 2097152 | tf_op jit(solution)/shard_map/slice | solution.py:28
  52.1 2.0 copy.33
  54.1 2.0 copy.34
  56.1 0.0 copy-done.7
  56.1 0.0 copy-done.8
  56.1 0.1 select_reduce_fusion
  56.2 0.6 fusion.56
  56.9 0.6 iota_compare_fusion.2
  57.4 0.1 fusion.42
  57.6 0.0 copy-done.3
  57.6 1.5 bitcast_reduce_fusion
  59.1 2.0 fusion.8
  61.2 0.0 copy-start.4
  61.2 0.4 fusion.24
  61.6 1.0 fusion.9
  62.6 0.0 copy-done.4
  62.6 0.0 copy-start.5
  62.6 1.1 fusion.26
  63.7 0.0 copy-start.6
  63.7 0.0 copy-done.5
  63.8 0.6 fusion.33
  64.4 0.0 copy-done
  64.4 0.5 copy-done.6
  64.9 1.1 fusion.70
  66.0 0.0 copy-start.2
  66.0 1.2 copy-done.2
  67.1 0.2 multiply_reduce_fusion
  67.4 104.2 %all-gather.3.cloned.1.call-done = bf16[7680,1600]{1,0:T(8,128)(2,1)} async-done(((bf16[240,1600]{1,0:T(8,128)(2,1)}), bf16[7680,1600]{1,0:T(8,128)(2,1)}) %all-gather.3.cloned.1.call-update) | async-done | bytes 24576016 | tf_op jit(solution)/shard_map/all_gather | solution.py:112
  171.6 17.2 %fusion.67 = (bf16[32,120,1600]{2,1,0:T(8,128)(2,1)}, bf16[32,120,1600]{2,1,0:T(8,128)(2,1)}) fusion(bf16[32,240,1600]{2,1,0:T(8,128)(2,1)} %bitcast.91), kind=kLoop, calls=%fused_computation.88 | loop fusion | bytes 49152000 | tf_op jit(solution)/shard_map/slice | solution.py:113
  188.8 0.0 copy-start.1
  188.8 19.2 %fusion.13 = bf16[1,256,1600]{1,2,0:T(8,128)(2,1)} fusion(f32[256,1600]{0,1:T(8,128)} %copy-done.2, bf16[3840,1600]{1,0:T(8,128)(2,1)} %bitcast.93, bf16[3840,1600]{1,0:T(8,128)(2,1)} %bitcast.92, f32[256]{0:T(256)S(1)} %add_sqrt_fusion, f32[256]{0:T(256)S(1)} %broadcast_multiply_fusion, pred[256]{0:T(512)(128)(4,1)S(1)} %iota_compare_fusion.2), kind=kOutput, calls=%fused_computation.18 | convolution fusion | flops 6302760960 | bytes 27035904 | tf_op jit(solution)/shard_map/dot_general | solution.py:119
  208.0 0.0 copy-done.1
  (7 shorter events, 0.1 us)
Async XLA Ops:
  6.5 57.8 %copy-start = (bf16[1024,1600]{0,1:T(8,128)(2,1)S(1)}, bf16[1024,1600]{0,1:T(8,128)(2,1)}, u32[]{:S(2)}) copy-start(bf16[1024,1600]{0,1:T(8,128)(2,1)} %param.19) | copy-start | bytes 9830404
  6.5 165.1 %all-gather.3.cloned.1.call-start = ((), (), s32[]{:S(2)}) async-start(), calls=%async_computation | async-start | bytes 26357760 | tf_op jit(solution)/shard_map/all_gather | solution.py:112
  16.5 39.6 %copy-start.7 = (s32[1,16]{1,0:T(1,128)S(1)}, s32[1,16]{1,0:T(1,128)}, u32[]{:S(2)}) copy-start(s32[1,16]{1,0:T(1,128)} %param.22) | copy-start | bytes 196
  16.5 39.6 %copy-start.8 = (s32[1,16]{1,0:T(1,128)S(1)}, s32[1,16]{1,0:T(1,128)}, u32[]{:S(2)}) copy-start(s32[1,16]{1,0:T(1,128)} %param.23) | copy-start | bytes 196
  47.3 10.2 %copy-start.3 = (bf16[128,1024]{0,1:T(8,128)(2,1)S(1)}, bf16[128,1024]{0,1:T(8,128)(2,1)}, u32[]{:S(2)}) copy-start(bf16[128,1024]{0,1:T(8,128)(2,1)} %copy.29) | copy-start | bytes 786436
  61.2 1.4 copy-start.4
  62.6 1.1 copy-start.5
  63.7 1.2 copy-start.6
  66.0 1.2 copy-start.2
  188.8 19.2 %copy-start.1 = (bf16[1024,1600]{0,1:T(8,128)(2,1)S(1)}, bf16[1024,1600]{0,1:T(8,128)(2,1)}, u32[]{:S(2)}) copy-start(bf16[1024,1600]{0,1:T(8,128)(2,1)} %param.19) | copy-start | bytes 9830404
Sparse Core Ops, SparseCore 0:
  10.3 161.3 all-gather.2

commit v3 on v2

--- a/solution.py
+++ b/solution.py
@@ -107,16 +107,30 @@
     projected = jnp.dot(attended, out_weight, preferred_element_type=jnp.float32)
     residual = suffix_x[0].astype(jnp.float32) + projected
     normed = normalize(residual).astype(jnp.bfloat16)
+    group_count = lax.axis_size("group")
     hidden_part = fc_weight.shape[1]
     both = jnp.concatenate([fc_weight.T, proj_weight], axis=0)
-    both_full = lax.all_gather(both, ("group", "dev"), axis=0)
-    fc_rows = both_full[:, :hidden_part].reshape(-1, both.shape[1])
-    proj_full = both_full[:, hidden_part:].reshape(-1, both.shape[1])
-    inner = lax.dot_general(
-        normed, fc_rows, (((1,), (1,)), ((), ())), preferred_element_type=jnp.float32
-    )
-    activated = jax.nn.gelu(inner, approximate=True).astype(jnp.bfloat16)
-    feed_out = jnp.dot(activated, proj_full, preferred_element_type=jnp.float32)
+    both_half = lax.all_gather(both, "dev", axis=0)
+    fc_rows = both_half[:, :hidden_part].reshape(-1, both.shape[1])
+    proj_rows = both_half[:, hidden_part:].reshape(-1, both.shape[1])
+
+    def feed(rows_in):
+        inner = lax.dot_general(
+            rows_in, fc_rows, (((1,), (1,)), ((), ())), preferred_element_type=jnp.float32
+        )
+        activated = jax.nn.gelu(inner, approximate=True).astype(jnp.bfloat16)
+        return jnp.dot(activated, proj_rows, preferred_element_type=jnp.float32)
+
+    returned = []
+    for shift in range(1, group_count):
+        there = [(g, (g + shift) % group_count) for g in range(group_count)]
+        back = [(g, (g - shift) % group_count) for g in range(group_count)]
+        partner_normed = lax.ppermute(normed, "group", there)
+        partner_feed = feed(partner_normed).astype(jnp.bfloat16)
+        returned.append(lax.ppermute(partner_feed, "group", back))
+    feed_out = lax.optimization_barrier(feed(normed))
+    for part in returned:
+        feed_out = feed_out + part.astype(jnp.float32)
     live = positions[:, None] < my_length
     return jnp.where(live, residual + feed_out, 0.0).astype(jnp.bfloat16)[None]
 

time: 215 us -> 168 us (0.78)
  waiting for transfers between devices: 104 us -> 58.9 us
  local copies, waits for them, and re-layouts: 31.1 us -> 23.7 us
  starting transfers between devices: 0.01 us -> 2.91 us
  other arithmetic: 8.57 us -> 11.1 us
    all_gather x1, waiting for transfers between devices: 104 us -> 50.1 us  [per_device(): both_half = lax.all_gather(both, 'dev', axis=0)]
    ppermute x0 -> x2, waiting for transfers between devices: none -> 8.76 us  [the longest x1 8.76 us: per_device(): returned.append(lax.ppermute(partner_feed, 'group', back))]
    slice x1, local copies, waits for them, and re-layouts: 17.2 us -> 10.3 us  [per_device(): fc_rows = both_half[:, :hidden_part].reshape(-1, both.shape[1])]
    broadcast_in_dim x0 -> x1, other arithmetic: none -> 3.31 us  [per_device(): return jnp.where(live, residual + feed_out, 0.0).astype(jnp.bfloat16)[None]]
    ppermute x0 -> x2, starting transfers between devices: none -> 2.87 us  [the longest x1 1.47 us: per_device(): returned.append(lax.ppermute(partner_feed, 'group', back))]
    dot_general x1 -> x2, matrix products: 19.2 us -> 20.7 us  [feed(): return jnp.dot(activated, proj_rows, preferred_element_type=jnp.float32)]
  transfers between devices with their start and end apart: 1 -> 3, of which waited for: 1 -> 2; matrix products, arithmetic and copies ran while one was open for 14% -> 28% of each run, Pallas kernels for 0% -> 0%
where the time goes in v3:
time: 168 us
  waiting for transfers between devices  58.9 us (35%)
  matrix products  30.4 us (18%)
  blocking collectives  27.3 us (16%)
  local copies, waits for them, and re-layouts  23.7 us (14%)
  between operations  13.6 us (8%)
  other arithmetic  11.1 us (7%)
  starting transfers between devices  2.91 us (2%)
    all_gather x1, waiting for transfers between devices, per_device(): both_half = lax.all_gather(both, 'dev', axis=0)  50.1 us
    all_gather x1, blocking collectives, per_device(): gathered = lax.all_gather(local_kv, 'dev', axis=0, tiled=True)  27.3 us
    dot_general x2, matrix products, feed(): return jnp.dot(activated, proj_rows, preferred_element_type=jnp.float32)  20.7 us
    slice x1, local copies, waits for them, and re-layouts, per_device(): fc_rows = both_half[:, :hidden_part].reshape(-1, both.shape[1])  10.3 us
    ppermute x1, waiting for transfers between devices, per_device(): returned.append(lax.ppermute(partner_feed, 'group', back))  8.76 us
    slice x3, local copies, waits for them, and re-layouts, absorb(): key_rows = keyval[:, :width_att].reshape(row_count, head_count, head_size)  5.19 us
    slice x3, local copies, waits for them, and re-layouts, absorb(): val_rows = keyval[:, width_att:].reshape(row_count, head_count, head_size)  4.57 us
    dot_general x1, matrix products, per_device(): jnp.dot(normed_prefix, kv_weight, preferred_element_type=jnp.float32)  4.51 us
  transfers between devices with their start and end apart: 3, of which 2 were waited for; matrix products, arithmetic and copies ran while one was open for 28% of the time, Pallas kernels for 0%

profile of v3, /device:TPU:0, one launch (start us, length us, event | category | flops | bytes accessed | tf_op | source)
XLA Modules:
  0.0 167.8 jit_solution(2028076263584685843)
XLA Ops:
  6.5 0.0 copy-start
  6.5 0.0 all-gather.3.cloned.1.call-start
  6.6 2.3 %pad_maximum_fusion = bf16[240,1600]{1,0:T(8,128)(2,1)} fusion(bf16[120,1600]{1,0:T(8,128)(2,1)} %param.21, bf16[120,1600]{1,0:T(8,128)(2,1)} %bitcast.106), kind=kLoop, calls=%fused_computation.56 | loop fusion | flops 1536000 | bytes 1536000 | tf_op jit(solution)/shard_map/concatenate | solution.py:112
  8.9 0.0 all-gather.3.cloned.1.call-update
  8.9 0.0 copy-done.11
  8.9 0.0 copy-done.10
  8.9 0.2 fusion.62
  9.1 0.6 compare_reduce_fusion
  9.8 0.0 copy-done.7
  9.8 0.1 convert_reduce_fusion
  9.9 0.2 fusion.53
  10.1 0.0 copy-done.8
  10.1 4.5 %fusion.3 = bf16[8,2048]{1,0:T(8,128)(2,1)S(1)} fusion(bf16[1600,2048]{1,0:T(8,128)(2,1)} %param.18, bf16[1,8,2048]{2,1,0:T(8,128)(2,1)S(1)} %copy-done.8, pred[]{:T(512)} %compare_reduce_fusion, bf16[1,8,1600]{2,1,0:T(8,128)(2,1)S(1)} %copy-done.7, f32[8]{0:T(128)S(1)} %add_sqrt_fusion.1, f32[8]{0:T(128)S(1)} %broadcast_multiply_fusion.1), kind=kOutput, calls=%fused_computation.10 | convolution fusion | flops 52512768 | bytes 6644801 | tf_op jit(solution)/shard_map/dot_general | solution.py:78
  14.6 27.3 %all_gather.9 = bf16[128,2048]{1,0:T(8,128)(2,1)S(1)} all-gather(bf16[8,2048]{1,0:T(8,128)(2,1)S(1)} %fusion.3), channel_id=1, replica_groups=mesh['group'=2,'dev'=16] {'dev'}, dimensions={0}, use_global_device_ids=true | all-gather | bytes 557056 | tf_op jit(solution)/shard_map/all_gather | solution.py:84
  41.9 0.7 fusion.80
  42.6 1.8 %copy.31 = bf16[128,1024]{0,1:T(8,128)(2,1)} copy(bf16[128,1024]{1,0:T(8,128)(2,1)} %get-tuple-element.11) | data formatting | bytes 524288 | tf_op jit(solution)/shard_map/slice | solution.py:29
  44.4 0.8 copy.29
  45.3 2.0 %copy.30 = bf16[1,256,1024]{1,2,0:T(8,128)(2,1)} copy(bf16[1,256,1024]{2,1,0:T(8,128)(2,1)} %param.14) | data formatting | bytes 1048576 | tf_op args[1]
  47.3 2.3 %fusion.79 = (bf16[256,1024]{1,0:T(8,128)(2,1)}, bf16[256,1024]{1,0:T(8,128)(2,1)}) fusion(bf16[256,2048]{1,0:T(8,128)(2,1)} %bitcast.103), kind=kLoop, calls=%fused_computation.103 | loop fusion | bytes 2097152 | tf_op jit(solution)/shard_map/slice | solution.py:28
  49.6 2.0 %copy.33 = bf16[256,1024]{0,1:T(8,128)(2,1)} copy(bf16[256,1024]{1,0:T(8,128)(2,1)} %get-tuple-element.9) | data formatting | bytes 1048576 | tf_op jit(solution)/shard_map/slice | solution.py:28
  51.7 2.0 %copy.34 = bf16[256,1024]{0,1:T(8,128)(2,1)} copy(bf16[256,1024]{1,0:T(8,128)(2,1)} %get-tuple-element.10) | data formatting | bytes 1048576 | tf_op jit(solution)/shard_map/slice | solution.py:29
  53.7 0.1 select_reduce_fusion
  53.8 0.7 fusion.63
  54.5 0.7 iota_compare_fusion.2
  55.2 0.1 fusion.49
  55.3 1.5 bitcast_reduce_fusion
  56.9 0.8 fusion
  57.8 0.4 fusion.24
  58.1 0.0 copy-start.5
  58.2 1.0 fusion.1
  59.2 0.1 copy-done.5
  59.2 1.1 fusion.26
  60.4 0.0 copy-start.9
  60.4 0.6 fusion.33
  61.0 0.5 copy-done.9
  61.5 1.1 fusion.81
  62.6 0.2 multiply_reduce_fusion
  62.9 0.9 copy-done.1
  63.8 1.1 divide_convert_fusion
  64.9 1.4 collective-permute-start
  66.3 50.1 %all-gather.3.cloned.1.call-done = bf16[3840,1600]{1,0:T(8,128)(2,1)} async-done(((bf16[240,1600]{1,0:T(8,128)(2,1)}), bf16[3840,1600]{1,0:T(8,128)(2,1)}) %all-gather.3.cloned.1.call-update) | async-done | bytes 12288016 | tf_op jit(solution)/shard_map/all_gather | solution.py:113
  116.4 10.3 %fusion.78 = (bf16[16,120,1600]{2,1,0:T(8,128)(2,1)}, bf16[16,120,1600]{2,1,0:T(8,128)(2,1)}) fusion(bf16[16,240,1600]{2,1,0:T(8,128)(2,1)} %bitcast.95), kind=kLoop, calls=%fused_computation.102 | loop fusion | bytes 24576000 | tf_op jit(solution)/shard_map/slice | solution.py:114
  126.7 0.0 collective-permute-done
  126.7 10.2 %convolution_convert_fusion = bf16[256,1600]{0,1:T(8,128)(2,1)} fusion(bf16[1920,1600]{1,0:T(8,128)(2,1)} %bitcast.98, bf16[256,1600]{0,1:T(8,128)(2,1)} %collective-permute-done, bf16[1920,1600]{1,0:T(8,128)(2,1)} %bitcast.96), kind=kOutput, calls=%fused_computation.8 | convolution fusion | flops 3150561280 | bytes 13926400 | tf_op jit(solution)/shard_map/dot_general | solution.py:122
  136.9 1.5 collective-permute-start.1
  138.4 10.5 %fusion.38 = f32[256,1600]{0,1:T(8,128)} fusion(bf16[1920,1600]{1,0:T(8,128)(2,1)} %bitcast.99, bf16[256,1600]{0,1:T(8,128)(2,1)} %divide_convert_fusion, bf16[1920,1600]{1,0:T(8,128)(2,1)} %bitcast.97), kind=kOutput, calls=%fused_computation.46 | convolution fusion | flops 3150151680 | bytes 14745600 | tf_op jit(solution)/shard_map/dot_general | solution.py:122
  148.9 8.8 %collective-permute-done.1 = bf16[256,1600]{0,1:T(8,128)(2,1)} collective-permute-done((bf16[256,1600]{0,1:T(8,128)(2,1)}, bf16[256,1600]{0,1:T(8,128)(2,1)}, u32[]{:S(2)}, u32[]{:S(2)}) %collective-permute-start.1) | collective-permute-done | bytes 819232 | tf_op jit(solution)/shard_map/ppermute | solution.py:130
  157.6 3.3 %fusion.48 = bf16[1,256,1600]{1,2,0:T(8,128)(2,1)} fusion(f32[256,1600]{0,1:T(8,128)} %copy-done.1, f32[256,1600]{0,1:T(8,128)} %fusion.38, bf16[256,1600]{0,1:T(8,128)(2,1)} %collective-permute-done.1, pred[256]{0:T(512)(128)(4,1)S(1)} %iota_compare_fusion.2), kind=kLoop, calls=%fused_computation.55 | loop fusion | flops 2048000 | bytes 4915456 | tf_op jit(solution)/shard_map/broadcast_in_dim | solution.py:135
  (24 shorter events, 0.1 us)
Async XLA Ops:
  6.5 54.5 %copy-start = (bf16[1024,1600]{0,1:T(8,128)(2,1)S(1)}, bf16[1024,1600]{0,1:T(8,128)(2,1)}, u32[]{:S(2)}) copy-start(bf16[1024,1600]{0,1:T(8,128)(2,1)} %param.19) | copy-start | bytes 9830404
  6.5 2.4 %copy-start.11 = (s32[1,2]{1,0:T(1,128)S(1)}, s32[1,2]{1,0:T(1,128)}, u32[]{:S(2)}) copy-start(s32[1,2]{1,0:T(1,128)} %param.25) | copy-start | bytes 28
  6.5 2.4 %copy-start.10 = (s32[1,16]{1,0:T(1,128)S(1)}, s32[1,16]{1,0:T(1,128)}, u32[]{:S(2)}) copy-start(s32[1,16]{1,0:T(1,128)} %param.24) | copy-start | bytes 196
  6.5 3.2 %copy-start.7 = (bf16[1,8,1600]{2,1,0:T(8,128)(2,1)S(1)}, bf16[1,8,1600]{2,1,0:T(8,128)(2,1)}, u32[]{:S(2)}) copy-start(bf16[1,8,1600]{2,1,0:T(8,128)(2,1)} %param.17) | copy-start | bytes 76804
  6.5 3.6 %copy-start.8 = (bf16[1,8,2048]{2,1,0:T(8,128)(2,1)S(1)}, bf16[1,8,2048]{2,1,0:T(8,128)(2,1)}, u32[]{:S(2)}) copy-start(bf16[1,8,2048]{2,1,0:T(8,128)(2,1)} %param.16) | copy-start | bytes 98308
  6.5 109.8 %all-gather.3.cloned.1.call-start = ((), (), s32[]{:S(2)}) async-start(), calls=%async_computation | async-start | bytes 13578240 | tf_op jit(solution)/shard_map/all_gather | solution.py:113
  47.3 6.4 %copy-start.12 = (s32[1,16]{1,0:T(1,128)S(1)}, s32[1,16]{1,0:T(1,128)}, u32[]{:S(2)}) copy-start(s32[1,16]{1,0:T(1,128)} %param.22) | copy-start | bytes 196
  47.3 6.4 %copy-start.13 = (s32[1,16]{1,0:T(1,128)S(1)}, s32[1,16]{1,0:T(1,128)}, u32[]{:S(2)}) copy-start(s32[1,16]{1,0:T(1,128)} %param.23) | copy-start | bytes 196
  47.3 8.0 %copy-start.4 = (bf16[128,1024]{0,1:T(8,128)(2,1)S(1)}, bf16[128,1024]{0,1:T(8,128)(2,1)}, u32[]{:S(2)}) copy-start(bf16[128,1024]{0,1:T(8,128)(2,1)} %copy.29) | copy-start | bytes 786436
  53.7 3.2 %copy-start.2 = (bf16[1,256,1024]{1,2,0:T(8,128)(2,1)S(1)}, bf16[1,256,1024]{1,2,0:T(8,128)(2,1)}, u32[]{:S(2)}) copy-start(bf16[1,256,1024]{1,2,0:T(8,128)(2,1)} %copy.30) | copy-start | bytes 1572868
  53.7 3.2 %copy-start.3 = (bf16[256,1024]{0,1:T(8,128)(2,1)S(1)}, bf16[256,1024]{0,1:T(8,128)(2,1)}, u32[]{:S(2)}) copy-start(bf16[256,1024]{0,1:T(8,128)(2,1)} %copy.33) | copy-start | bytes 1572868
  58.1 1.1 copy-start.5
  59.2 1.1 copy-start.6
  60.4 1.1 copy-start.9
  62.6 1.2 copy-start.1
  64.9 61.8 %collective-permute-start = (bf16[256,1600]{0,1:T(8,128)(2,1)}, bf16[256,1600]{0,1:T(8,128)(2,1)}, u32[]{:S(2)}, u32[]{:S(2)}) collective-permute-start(bf16[256,1600]{0,1:T(8,128)(2,1)} %divide_convert_fusion), channel_id=1, source_target_pairs={{0,16},{16,0},{1,17},{17,1},{2,18},{18,2},{3,19},{19,3},{4,20},{20... | collective-permute-start | bytes 2457608 | tf_op jit(solution)/shard_map/ppermute | solution.py:128
  136.9 20.7 %collective-permute-start.1 = (bf16[256,1600]{0,1:T(8,128)(2,1)}, bf16[256,1600]{0,1:T(8,128)(2,1)}, u32[]{:S(2)}, u32[]{:S(2)}) collective-permute-start(bf16[256,1600]{0,1:T(8,128)(2,1)} %convolution_convert_fusion), channel_id=1, source_target_pairs={{0,16},{16,0},{1,17},{17,1},{2,18},{18,2},{3,19},{19,3},{4,20},{20... | collective-permute-start | bytes 2457608 | tf_op jit(solution)/shard_map/ppermute | solution.py:130
Sparse Core Ops, SparseCore 0:
  9.6 106.7 all-gather.2

commit v4 on v3

--- a/solution.py
+++ b/solution.py
@@ -109,10 +109,10 @@
     normed = normalize(residual).astype(jnp.bfloat16)
     group_count = lax.axis_size("group")
     hidden_part = fc_weight.shape[1]
-    both = jnp.concatenate([fc_weight.T, proj_weight], axis=0)
-    both_half = lax.all_gather(both, "dev", axis=0)
-    fc_rows = both_half[:, :hidden_part].reshape(-1, both.shape[1])
-    proj_rows = both_half[:, hidden_part:].reshape(-1, both.shape[1])
+    both = jnp.stack([fc_weight.T, proj_weight])
+    both_half = lax.all_gather(both, "dev", axis=1)
+    fc_rows = both_half[0].reshape(-1, both.shape[2])
+    proj_rows = both_half[1].reshape(-1, both.shape[2])
 
     def feed(rows_in):
         inner = lax.dot_general(

time: 168 us -> 159 us (0.946)
  local copies, waits for them, and re-layouts: 23.7 us -> 14.2 us
    all_gather x1, waiting for transfers between devices: 50.1 us -> 30.9 us  [per_device(): both_half = lax.all_gather(both, 'dev', axis=1)]
    ppermute x1, waiting for transfers between devices: 0.01 us -> 19.1 us  [per_device(): partner_normed = lax.ppermute(normed, 'group', there)]
    slice x1 -> x0, local copies, waits for them, and re-layouts: 10.3 us -> none  [per_device(): fc_rows = both_half[:, :hidden_part].reshape(-1, both.shape[1])]
    concatenate x1 -> x0, other arithmetic: 2.29 us -> none  [per_device(): both = jnp.concatenate([fc_weight.T, proj_weight], axis=0)]
    another operation x0 -> x1, other arithmetic: none -> 2.27 us  [per_device(): both = jnp.stack([fc_weight.T, proj_weight])]
  transfers between devices with their start and end apart: 3 -> 3, of which waited for: 2 -> 3; matrix products, arithmetic and copies ran while one was open for 28% -> 23% of each run, Pallas kernels for 0% -> 0%
where the time goes in v4:
time: 159 us; the launch traced here: 158 us
  waiting for transfers between devices  58.6 us (37%)
  matrix products  30.8 us (19%)
  blocking collectives  27.9 us (18%)
  local copies, waits for them, and re-layouts  14.2 us (9%)
  between operations  13.6 us (9%)
  other arithmetic  10.1 us (6%)
  starting transfers between devices  2.94 us (2%)
    all_gather x1, waiting for transfers between devices, per_device(): both_half = lax.all_gather(both, 'dev', axis=1)  30.9 us
    all_gather x1, blocking collectives, per_device(): gathered = lax.all_gather(local_kv, 'dev', axis=0, tiled=True)  27.9 us
    dot_general x2, matrix products, feed(): return jnp.dot(activated, proj_rows, preferred_element_type=jnp.float32)  20.9 us
    ppermute x1, waiting for transfers between devices, per_device(): partner_normed = lax.ppermute(normed, 'group', there)  19.1 us
    ppermute x1, waiting for transfers between devices, per_device(): returned.append(lax.ppermute(partner_feed, 'group', back))  8.57 us
    slice x3, local copies, waits for them, and re-layouts, absorb(): key_rows = keyval[:, :width_att].reshape(row_count, head_count, head_size)  6.11 us
    dot_general x1, matrix products, per_device(): jnp.dot(normed_prefix, kv_weight, preferred_element_type=jnp.float32)  4.71 us
    unnamed x29, local copies, waits for them, and re-layouts  4.5 us
  transfers between devices with their start and end apart: 3, of which 3 were waited for; matrix products, arithmetic and copies ran while one was open for 23% of the time, Pallas kernels for 0%

profile of v4, /device:TPU:0, one launch (start us, length us, event | category | flops | bytes accessed | tf_op | source)
XLA Modules:
  0.0 158.2 jit_solution(2306186666512414033)
XLA Ops:
  6.5 2.3 %pad_maximum_fusion = bf16[2,120,1600]{2,1,0:T(8,128)(2,1)} fusion(bf16[1,120,1600]{2,1,0:T(8,128)(2,1)} %bitcast.119, bf16[1,120,1600]{2,1,0:T(8,128)(2,1)} %bitcast.120), kind=kLoop, calls=%fused_computation.61 | loop fusion | flops 384000 | bytes 1536000 | tf_op jit(solution)/shard_map/stack | solution.py:112
  8.8 0.0 all-gather.3.cloned.1.call-update
  8.8 0.0 copy-start.10
  8.8 0.0 copy-start.11
  8.9 0.0 copy-start.7
  8.9 0.0 copy-start.8
  8.9 2.3 %fusion.80 = (bf16[256,1024]{1,0:T(8,128)(2,1)}, bf16[256,1024]{1,0:T(8,128)(2,1)}) fusion(bf16[256,2048]{1,0:T(8,128)(2,1)} %bitcast.116), kind=kLoop, calls=%fused_computation.107 | loop fusion | bytes 2097152 | tf_op jit(solution)/shard_map/slice | solution.py:28
  11.1 2.1 %copy.33 = bf16[256,1024]{0,1:T(8,128)(2,1)} copy(bf16[256,1024]{1,0:T(8,128)(2,1)} %get-tuple-element.7) | data formatting | bytes 1048576 | tf_op jit(solution)/shard_map/slice | solution.py:28
  13.2 2.1 %copy.30 = bf16[1,256,1024]{1,2,0:T(8,128)(2,1)} copy(bf16[1,256,1024]{2,1,0:T(8,128)(2,1)} %param.14) | data formatting | bytes 1048576 | tf_op args[1]
  15.3 0.0 copy-done.10
  15.3 0.2 fusion.64
  15.5 0.6 compare_reduce_fusion
  16.1 0.1 convert_reduce_fusion
  16.2 0.2 fusion.55
  16.4 4.7 %fusion.8 = bf16[8,2048]{1,0:T(8,128)(2,1)S(1)} fusion(bf16[1600,2048]{1,0:T(8,128)(2,1)} %param.18, bf16[1,8,2048]{2,1,0:T(8,128)(2,1)S(1)} %copy-done.8, pred[]{:T(512)} %compare_reduce_fusion, bf16[1,8,1600]{2,1,0:T(8,128)(2,1)S(1)} %copy-done.7, f32[8]{0:T(128)S(1)} %add_sqrt_fusion.1, f32[8]{0:T(128)S(1)} %broadcast_multiply_fusion.1), kind=kOutput, calls=%fused_computation.16 | convolution fusion | flops 52512768 | bytes 6644801 | tf_op jit(solution)/shard_map/dot_general | solution.py:78
  21.2 27.9 %all_gather.9 = bf16[128,2048]{1,0:T(8,128)(2,1)S(1)} all-gather(bf16[8,2048]{1,0:T(8,128)(2,1)S(1)} %fusion.8), channel_id=1, replica_groups=mesh['group'=2,'dev'=16] {'dev'}, dimensions={0}, use_global_device_ids=true | all-gather | bytes 557056 | tf_op jit(solution)/shard_map/all_gather | solution.py:84
  49.1 0.7 fusion.81
  49.8 1.8 %copy.29 = bf16[128,1024]{0,1:T(8,128)(2,1)} copy(bf16[128,1024]{1,0:T(8,128)(2,1)} %get-tuple-element.10) | data formatting | bytes 524288 | tf_op jit(solution)/shard_map/slice | solution.py:28
  51.6 2.0 %copy.34 = bf16[256,1024]{0,1:T(8,128)(2,1)} copy(bf16[256,1024]{1,0:T(8,128)(2,1)} %get-tuple-element.8) | data formatting | bytes 1048576 | tf_op jit(solution)/shard_map/slice | solution.py:29
  53.6 0.8 copy.31
  54.5 0.1 select_reduce_fusion
  54.5 0.7 fusion.65
  55.2 0.6 iota_compare_fusion.2
  55.9 0.1 fusion.51
  56.0 1.6 %bitcast_reduce_fusion = (f32[16,256]{1,0:T(8,128)S(1)}, f32[16,128,256]{2,1,0:T(8,128)S(1)}) fusion(bf16[128,16,64]{0,2,1:T(8,128)(2,1)} %bitcast.117, bf16[256,16,64]{0,2,1:T(8,128)(2,1)} %bitcast.113), kind=kOutput, calls=%fused_computation.18 | convolution fusion | flops 68153344 | bytes 2899968 | tf_op jit(solution)/shard_map/qhd,khd->hqk/dot_general | solution.py:31
  57.6 0.8 fusion.4
  58.5 0.4 fusion.29
  58.9 0.0 copy-start.5
  58.9 1.0 fusion.5
  59.9 0.1 copy-done.5
  60.0 1.1 fusion.31
  61.1 0.0 copy-start.9
  61.1 0.6 fusion.38
  61.7 0.5 copy-done.9
  62.2 1.1 fusion.82
  63.3 0.2 multiply_reduce_fusion
  63.6 0.9 copy-done.1
  64.5 0.2 divide_convert_fusion
  64.7 0.0 copy-start.4
  64.7 0.9 copy-done.4
  65.6 1.5 collective-permute-start
  67.1 19.1 %collective-permute-done = bf16[256,1600]{0,1:T(8,128)(2,1)} collective-permute-done((bf16[256,1600]{0,1:T(8,128)(2,1)S(1)}, bf16[256,1600]{0,1:T(8,128)(2,1)}, u32[]{:S(2)}, u32[]{:S(2)}) %collective-permute-start) | collective-permute-done | bytes 819232 | tf_op jit(solution)/shard_map/ppermute | solution.py:128
  86.2 30.9 %all-gather.3.cloned.1.call-done = bf16[2,1920,1600]{2,1,0:T(8,128)(2,1)} async-done(((bf16[2,120,1600]{2,1,0:T(8,128)(2,1)}), bf16[2,1920,1600]{2,1,0:T(8,128)(2,1)}) %all-gather.3.cloned.1.call-update) | async-done | bytes 12288016 | tf_op jit(solution)/shard_map/all_gather | solution.py:113
  117.1 10.2 %fusion.7 = bf16[256,1600]{0,1:T(8,128)(2,1)} fusion(bf16[2,1920,1600]{2,1,0:T(8,128)(2,1)} %all-gather.3.cloned.1.call-done, bf16[256,1600]{0,1:T(8,128)(2,1)} %collective-permute-done), kind=kOutput, calls=%fused_computation.14 | convolution fusion | flops 3150561280 | bytes 13926400 | tf_op jit(solution)/shard_map/dot_general | solution.py:122
  127.3 1.5 collective-permute-start.1
  128.8 10.7 %fusion.3 = f32[256,1600]{0,1:T(8,128)} fusion(bf16[2,1920,1600]{2,1,0:T(8,128)(2,1)} %all-gather.3.cloned.1.call-done, bf16[256,1600]{0,1:T(8,128)(2,1)} %copy-done.4), kind=kOutput, calls=%fused_computation.5 | convolution fusion | flops 3150151680 | bytes 14745600 | tf_op jit(solution)/shard_map/dot_general | solution.py:122
  139.5 8.6 %collective-permute-done.1 = bf16[256,1600]{0,1:T(8,128)(2,1)} collective-permute-done((bf16[256,1600]{0,1:T(8,128)(2,1)}, bf16[256,1600]{0,1:T(8,128)(2,1)}, u32[]{:S(2)}, u32[]{:S(2)}) %collective-permute-start.1) | collective-permute-done | bytes 819232 | tf_op jit(solution)/shard_map/ppermute | solution.py:130
  148.0 3.3 %fusion.50 = bf16[1,256,1600]{1,2,0:T(8,128)(2,1)} fusion(f32[256,1600]{0,1:T(8,128)} %copy-done.1, f32[256,1600]{0,1:T(8,128)} %fusion.3, bf16[256,1600]{0,1:T(8,128)(2,1)} %collective-permute-done.1, pred[256]{0:T(512)(128)(4,1)S(1)} %iota_compare_fusion.2), kind=kLoop, calls=%fused_computation.60 | loop fusion | flops 2048000 | bytes 4915456 | tf_op jit(solution)/shard_map/broadcast_in_dim | solution.py:135
  (23 shorter events, 0.1 us)
Async XLA Ops:
  6.5 55.2 %copy-start = (bf16[1024,1600]{0,1:T(8,128)(2,1)S(1)}, bf16[1024,1600]{0,1:T(8,128)(2,1)}, u32[]{:S(2)}) copy-start(bf16[1024,1600]{0,1:T(8,128)(2,1)} %param.19) | copy-start | bytes 9830404
  6.5 110.5 %all-gather.3.cloned.1.call-start = ((), (), s32[]{:S(2)}) async-start(), calls=%async_computation | async-start | bytes 13578240 | tf_op jit(solution)/shard_map/all_gather | solution.py:113
  8.8 6.4 %copy-start.10 = (s32[1,16]{1,0:T(1,128)S(1)}, s32[1,16]{1,0:T(1,128)}, u32[]{:S(2)}) copy-start(s32[1,16]{1,0:T(1,128)} %param.24) | copy-start | bytes 196
  8.8 6.4 %copy-start.11 = (s32[1,2]{1,0:T(1,128)S(1)}, s32[1,2]{1,0:T(1,128)}, u32[]{:S(2)}) copy-start(s32[1,2]{1,0:T(1,128)} %param.25) | copy-start | bytes 28
  8.9 7.2 %copy-start.7 = (bf16[1,8,1600]{2,1,0:T(8,128)(2,1)S(1)}, bf16[1,8,1600]{2,1,0:T(8,128)(2,1)}, u32[]{:S(2)}) copy-start(bf16[1,8,1600]{2,1,0:T(8,128)(2,1)} %param.17) | copy-start | bytes 76804
  8.9 7.6 %copy-start.8 = (bf16[1,8,2048]{2,1,0:T(8,128)(2,1)S(1)}, bf16[1,8,2048]{2,1,0:T(8,128)(2,1)}, u32[]{:S(2)}) copy-start(bf16[1,8,2048]{2,1,0:T(8,128)(2,1)} %param.16) | copy-start | bytes 98308
  21.2 33.3 %copy-start.12 = (s32[1,16]{1,0:T(1,128)S(1)}, s32[1,16]{1,0:T(1,128)}, u32[]{:S(2)}) copy-start(s32[1,16]{1,0:T(1,128)} %param.22) | copy-start | bytes 196
  21.2 33.3 %copy-start.13 = (s32[1,16]{1,0:T(1,128)S(1)}, s32[1,16]{1,0:T(1,128)}, u32[]{:S(2)}) copy-start(s32[1,16]{1,0:T(1,128)} %param.23) | copy-start | bytes 196
  54.4 3.2 %copy-start.2 = (bf16[1,256,1024]{1,2,0:T(8,128)(2,1)S(1)}, bf16[1,256,1024]{1,2,0:T(8,128)(2,1)}, u32[]{:S(2)}) copy-start(bf16[1,256,1024]{1,2,0:T(8,128)(2,1)} %copy.30) | copy-start | bytes 1572868
  54.4 3.2 %copy-start.3 = (bf16[256,1024]{0,1:T(8,128)(2,1)S(1)}, bf16[256,1024]{0,1:T(8,128)(2,1)}, u32[]{:S(2)}) copy-start(bf16[256,1024]{0,1:T(8,128)(2,1)} %copy.33) | copy-start | bytes 1572868
  58.9 1.1 copy-start.5
  60.0 1.1 copy-start.6
  61.1 1.1 copy-start.9
  63.3 1.2 copy-start.1
  64.7 0.9 copy-start.4
  65.6 20.6 %collective-permute-start = (bf16[256,1600]{0,1:T(8,128)(2,1)S(1)}, bf16[256,1600]{0,1:T(8,128)(2,1)}, u32[]{:S(2)}, u32[]{:S(2)}) collective-permute-start(bf16[256,1600]{0,1:T(8,128)(2,1)S(1)} %divide_convert_fusion), channel_id=1, source_target_pairs={{0,16},{16,0},{1,17},{17,1},{2,18},{18,2},{3,19},{19,3},{4,20},{20... | collective-permute-start | bytes 2457608 | tf_op jit(solution)/shard_map/ppermute | solution.py:128
  127.3 20.7 %collective-permute-start.1 = (bf16[256,1600]{0,1:T(8,128)(2,1)}, bf16[256,1600]{0,1:T(8,128)(2,1)}, u32[]{:S(2)}, u32[]{:S(2)}) collective-permute-start(bf16[256,1600]{0,1:T(8,128)(2,1)} %fusion.7), channel_id=1, source_target_pairs={{0,16},{16,0},{1,17},{17,1},{2,18},{18,2},{3,19},{19,3},{4,20},{20... | collective-permute-start | bytes 2457608 | tf_op jit(solution)/shard_map/ppermute | solution.py:130
Sparse Core Ops, SparseCore 0:
  9.5 107.4 all-gather.2

commit v5 on v4

--- a/solution.py
+++ b/solution.py
@@ -121,13 +121,17 @@
         activated = jax.nn.gelu(inner, approximate=True).astype(jnp.bfloat16)
         return jnp.dot(activated, proj_rows, preferred_element_type=jnp.float32)
 
+    chunk = slots // 2 if slots % 32 == 0 else slots
     returned = []
     for shift in range(1, group_count):
         there = [(g, (g + shift) % group_count) for g in range(group_count)]
         back = [(g, (g - shift) % group_count) for g in range(group_count)]
         partner_normed = lax.ppermute(normed, "group", there)
-        partner_feed = feed(partner_normed).astype(jnp.bfloat16)
-        returned.append(lax.ppermute(partner_feed, "group", back))
+        pieces = []
+        for start in range(0, slots, chunk):
+            piece = feed(partner_normed[start : start + chunk]).astype(jnp.bfloat16)
+            pieces.append(lax.ppermute(piece, "group", back))
+        returned.append(jnp.concatenate(pieces, axis=0))
     feed_out = lax.optimization_barrier(feed(normed))
     for part in returned:
         feed_out = feed_out + part.astype(jnp.float32)

time: 159 us -> 159 us (level)
  matrix products: 30.8 us -> 38.9 us
  waiting for transfers between devices: 58.6 us -> 50.7 us
    dot_general x2 -> x3, matrix products: 20.9 us -> 29 us  [feed(): return jnp.dot(activated, proj_rows, preferred_element_type=jnp.float32)]
    ppermute x1 -> x2, waiting for transfers between devices: 8.57 us -> 0.63 us  [per_device(): pieces.append(lax.ppermute(piece, 'group', back))]
  transfers between devices with their start and end apart: 3 -> 4, of which waited for: 3 -> 3; matrix products, arithmetic and copies ran while one was open for 23% -> 29% of each run, Pallas kernels for 0% -> 0%
where the time goes in v5:
time: 159 us
  waiting for transfers between devices  50.7 us (32%)
  matrix products  38.9 us (24%)
  blocking collectives  27.9 us (18%)
  local copies, waits for them, and re-layouts  14.1 us (9%)
  between operations  13.6 us (9%)
  other arithmetic  10.1 us (6%)
  starting transfers between devices  3.49 us (2%)
    all_gather x1, waiting for transfers between devices, per_device(): both_half = lax.all_gather(both, 'dev', axis=1)  30.9 us
    dot_general x3, matrix products, feed(): return jnp.dot(activated, proj_rows, preferred_element_type=jnp.float32)  29 us
    all_gather x1, blocking collectives, per_device(): gathered = lax.all_gather(local_kv, 'dev', axis=0, tiled=True)  27.9 us
    ppermute x1, waiting for transfers between devices, per_device(): partner_normed = lax.ppermute(normed, 'group', there)  19.1 us
    slice x3, local copies, waits for them, and re-layouts, absorb(): key_rows = keyval[:, :width_att].reshape(row_count, head_count, head_size)  6.1 us
    dot_general x1, matrix products, per_device(): jnp.dot(normed_prefix, kv_weight, preferred_element_type=jnp.float32)  4.7 us
    unnamed x29, local copies, waits for them, and re-layouts  4.43 us
    slice x3, local copies, waits for them, and re-layouts, absorb(): val_rows = keyval[:, width_att:].reshape(row_count, head_count, head_size)  3.61 us
  transfers between devices with their start and end apart: 4, of which 3 were waited for; matrix products, arithmetic and copies ran while one was open for 29% of the time, Pallas kernels for 0%

profile of v5, /device:TPU:0, one launch (start us, length us, event | category | flops | bytes accessed | tf_op | source)
XLA Modules:
  0.0 158.9 jit_solution(4210390987935389169)
XLA Ops:
  6.5 0.0 all-gather.3.cloned.1.call-start
  6.6 2.3 %pad_maximum_fusion = bf16[2,120,1600]{2,1,0:T(8,128)(2,1)} fusion(bf16[1,120,1600]{2,1,0:T(8,128)(2,1)} %bitcast.128, bf16[1,120,1600]{2,1,0:T(8,128)(2,1)} %bitcast.129), kind=kLoop, calls=%fused_computation.69 | loop fusion | flops 384000 | bytes 1536000 | tf_op jit(solution)/shard_map/stack | solution.py:112
  8.8 0.0 all-gather.3.cloned.1.call-update
  8.9 2.3 %fusion.103 = (bf16[256,1024]{1,0:T(8,128)(2,1)}, bf16[256,1024]{1,0:T(8,128)(2,1)}) fusion(bf16[256,2048]{1,0:T(8,128)(2,1)} %bitcast.125), kind=kLoop, calls=%fused_computation.129 | loop fusion | bytes 2097152 | tf_op jit(solution)/shard_map/slice | solution.py:28
  11.1 2.1 %copy.33 = bf16[256,1024]{0,1:T(8,128)(2,1)} copy(bf16[256,1024]{1,0:T(8,128)(2,1)} %get-tuple-element.7) | data formatting | bytes 1048576 | tf_op jit(solution)/shard_map/slice | solution.py:28
  13.2 2.1 %copy.30 = bf16[1,256,1024]{1,2,0:T(8,128)(2,1)} copy(bf16[1,256,1024]{2,1,0:T(8,128)(2,1)} %param.14) | data formatting | bytes 1048576 | tf_op args[1]
  15.2 0.0 copy-done.10
  15.2 0.2 fusion.83
  15.4 0.6 compare_reduce_fusion
  16.1 0.1 convert_reduce_fusion
  16.2 0.2 fusion.74
  16.4 0.0 copy-done.8
  16.4 4.7 %fusion.11 = bf16[8,2048]{1,0:T(8,128)(2,1)S(1)} fusion(bf16[1600,2048]{1,0:T(8,128)(2,1)} %param.18, bf16[1,8,2048]{2,1,0:T(8,128)(2,1)S(1)} %copy-done.8, pred[]{:T(512)} %compare_reduce_fusion, bf16[1,8,1600]{2,1,0:T(8,128)(2,1)S(1)} %copy-done.7, f32[8]{0:T(128)S(1)} %add_sqrt_fusion.1, f32[8]{0:T(128)S(1)} %broadcast_multiply_fusion.1), kind=kOutput, calls=%fused_computation.18 | convolution fusion | flops 52512768 | bytes 6644801 | tf_op jit(solution)/shard_map/dot_general | solution.py:78
  21.1 27.9 %all_gather.9 = bf16[128,2048]{1,0:T(8,128)(2,1)S(1)} all-gather(bf16[8,2048]{1,0:T(8,128)(2,1)S(1)} %fusion.11), channel_id=1, replica_groups=mesh['group'=2,'dev'=16] {'dev'}, dimensions={0}, use_global_device_ids=true | all-gather | bytes 557056 | tf_op jit(solution)/shard_map/all_gather | solution.py:84
  49.0 0.7 fusion.104
  49.8 1.8 %copy.29 = bf16[128,1024]{0,1:T(8,128)(2,1)} copy(bf16[128,1024]{1,0:T(8,128)(2,1)} %get-tuple-element.10) | data formatting | bytes 524288 | tf_op jit(solution)/shard_map/slice | solution.py:28
  51.6 2.0 %copy.34 = bf16[256,1024]{0,1:T(8,128)(2,1)} copy(bf16[256,1024]{1,0:T(8,128)(2,1)} %get-tuple-element.8) | data formatting | bytes 1048576 | tf_op jit(solution)/shard_map/slice | solution.py:29
  53.6 0.8 copy.31
  54.4 0.0 copy-done.13
  54.5 0.1 select_reduce_fusion
  54.5 0.7 fusion.84
  55.2 0.6 iota_compare_fusion.2
  55.9 0.1 fusion.70
  56.0 1.6 %bitcast_reduce_fusion = (f32[16,256]{1,0:T(8,128)S(1)}, f32[16,128,256]{2,1,0:T(8,128)S(1)}) fusion(bf16[128,16,64]{0,2,1:T(8,128)(2,1)} %bitcast.126, bf16[256,16,64]{0,2,1:T(8,128)(2,1)} %bitcast.122), kind=kOutput, calls=%fused_computation.20 | convolution fusion | flops 68153344 | bytes 2899968 | tf_op jit(solution)/shard_map/qhd,khd->hqk/dot_general | solution.py:31
  57.6 0.8 fusion.6
  58.5 0.0 copy-start.5
  58.5 0.4 fusion.24
  58.9 1.0 fusion.7
  59.9 1.1 fusion.26
  61.1 0.6 fusion.33
  61.7 0.5 copy-done.9
  62.2 1.1 fusion.105
  63.3 0.2 multiply_reduce_fusion
  63.5 0.9 copy-done.1
  64.5 0.2 divide_convert_fusion
  64.6 0.0 copy-start.4
  64.7 0.9 copy-done.4
  65.5 1.5 collective-permute-start
  67.0 19.1 %collective-permute-done = bf16[256,1600]{0,1:T(8,128)(2,1)} collective-permute-done((bf16[256,1600]{0,1:T(8,128)(2,1)S(1)}, bf16[256,1600]{0,1:T(8,128)(2,1)}, u32[]{:S(2)}, u32[]{:S(2)}) %collective-permute-start) | collective-permute-done | bytes 819232 | tf_op jit(solution)/shard_map/ppermute | solution.py:129
  86.1 30.9 %all-gather.3.cloned.1.call-done = bf16[2,1920,1600]{2,1,0:T(8,128)(2,1)} async-done(((bf16[2,120,1600]{2,1,0:T(8,128)(2,1)}), bf16[2,1920,1600]{2,1,0:T(8,128)(2,1)}) %all-gather.3.cloned.1.call-update) | async-done | bytes 12288016 | tf_op jit(solution)/shard_map/all_gather | solution.py:113
  117.1 9.2 %fusion.9 = bf16[128,1600]{0,1:T(8,128)(2,1)} fusion(bf16[2,1920,1600]{2,1,0:T(8,128)(2,1)} %all-gather.3.cloned.1.call-done, bf16[256,1600]{0,1:T(8,128)(2,1)} %collective-permute-done), kind=kOutput, calls=%fused_computation.15 | convolution fusion | flops 1575280640 | bytes 13598720 | tf_op jit(solution)/shard_map/dot_general | solution.py:122
  126.2 1.5 collective-permute-start.1
  127.7 9.4 %fusion.10 = bf16[128,1600]{0,1:T(8,128)(2,1)} fusion(bf16[2,1920,1600]{2,1,0:T(8,128)(2,1)} %all-gather.3.cloned.1.call-done, bf16[256,1600]{0,1:T(8,128)(2,1)} %collective-permute-done), kind=kOutput, calls=%fused_computation.16 | convolution fusion | flops 1575280640 | bytes 13598720 | tf_op jit(solution)/shard_map/dot_general | solution.py:122
  137.1 0.6 collective-permute-start.2
  137.6 10.5 %fusion.5 = f32[256,1600]{0,1:T(8,128)} fusion(bf16[2,1920,1600]{2,1,0:T(8,128)(2,1)} %all-gather.3.cloned.1.call-done, bf16[256,1600]{0,1:T(8,128)(2,1)} %copy-done.4), kind=kOutput, calls=%fused_computation.7 | convolution fusion | flops 3150151680 | bytes 14745600 | tf_op jit(solution)/shard_map/dot_general | solution.py:122
  148.1 0.0 collective-permute-done.1
  148.1 0.6 collective-permute-done.2
  148.7 3.3 %fusion.57 = bf16[1,256,1600]{1,2,0:T(8,128)(2,1)} fusion(f32[256,1600]{0,1:T(8,128)} %copy-done.1, f32[256,1600]{0,1:T(8,128)} %fusion.5, bf16[128,1600]{0,1:T(8,128)(2,1)} %collective-permute-done.2, bf16[128,1600]{0,1:T(8,128)(2,1)} %collective-permute-done.1, pred[256]{0:T(512)(128)(4,1)S(1)} %iota_compare_fusion.2), kind=kLoop, calls=%fused_computation.68 | loop fusion | flops 3276800 | bytes 4915456 | tf_op jit(solution)/shard_map/broadcast_in_dim | solution.py:139
  (26 shorter events, 0.1 us)
Async XLA Ops:
  6.5 55.1 %copy-start = (bf16[1024,1600]{0,1:T(8,128)(2,1)S(1)}, bf16[1024,1600]{0,1:T(8,128)(2,1)}, u32[]{:S(2)}) copy-start(bf16[1024,1600]{0,1:T(8,128)(2,1)} %param.19) | copy-start | bytes 9830404
  6.5 110.5 %all-gather.3.cloned.1.call-start = ((), (), s32[]{:S(2)}) async-start(), calls=%async_computation | async-start | bytes 13578240 | tf_op jit(solution)/shard_map/all_gather | solution.py:113
  6.5 8.7 %copy-start.10 = (s32[1,16]{1,0:T(1,128)S(1)}, s32[1,16]{1,0:T(1,128)}, u32[]{:S(2)}) copy-start(s32[1,16]{1,0:T(1,128)} %param.24) | copy-start | bytes 196
  6.5 8.7 %copy-start.11 = (s32[1,2]{1,0:T(1,128)S(1)}, s32[1,2]{1,0:T(1,128)}, u32[]{:S(2)}) copy-start(s32[1,2]{1,0:T(1,128)} %param.25) | copy-start | bytes 28
  6.5 9.5 %copy-start.7 = (bf16[1,8,1600]{2,1,0:T(8,128)(2,1)S(1)}, bf16[1,8,1600]{2,1,0:T(8,128)(2,1)}, u32[]{:S(2)}) copy-start(bf16[1,8,1600]{2,1,0:T(8,128)(2,1)} %param.17) | copy-start | bytes 76804
  6.6 9.9 %copy-start.8 = (bf16[1,8,2048]{2,1,0:T(8,128)(2,1)S(1)}, bf16[1,8,2048]{2,1,0:T(8,128)(2,1)}, u32[]{:S(2)}) copy-start(bf16[1,8,2048]{2,1,0:T(8,128)(2,1)} %param.16) | copy-start | bytes 98308
  21.1 33.3 %copy-start.12 = (s32[1,16]{1,0:T(1,128)S(1)}, s32[1,16]{1,0:T(1,128)}, u32[]{:S(2)}) copy-start(s32[1,16]{1,0:T(1,128)} %param.22) | copy-start | bytes 196
  21.1 33.3 %copy-start.13 = (s32[1,16]{1,0:T(1,128)S(1)}, s32[1,16]{1,0:T(1,128)}, u32[]{:S(2)}) copy-start(s32[1,16]{1,0:T(1,128)} %param.23) | copy-start | bytes 196
  54.4 3.2 %copy-start.2 = (bf16[1,256,1024]{1,2,0:T(8,128)(2,1)S(1)}, bf16[1,256,1024]{1,2,0:T(8,128)(2,1)}, u32[]{:S(2)}) copy-start(bf16[1,256,1024]{1,2,0:T(8,128)(2,1)} %copy.30) | copy-start | bytes 1572868
  54.4 3.2 %copy-start.3 = (bf16[256,1024]{0,1:T(8,128)(2,1)S(1)}, bf16[256,1024]{0,1:T(8,128)(2,1)}, u32[]{:S(2)}) copy-start(bf16[256,1024]{0,1:T(8,128)(2,1)} %copy.33) | copy-start | bytes 1572868
  58.5 1.4 copy-start.5
  59.9 1.1 copy-start.6
  61.0 1.2 copy-start.9
  63.3 1.2 copy-start.1
  64.6 0.9 copy-start.4
  65.5 20.6 %collective-permute-start = (bf16[256,1600]{0,1:T(8,128)(2,1)S(1)}, bf16[256,1600]{0,1:T(8,128)(2,1)}, u32[]{:S(2)}, u32[]{:S(2)}) collective-permute-start(bf16[256,1600]{0,1:T(8,128)(2,1)S(1)} %divide_convert_fusion), channel_id=1, source_target_pairs={{0,16},{16,0},{1,17},{17,1},{2,18},{18,2},{3,19},{19,3},{4,20},{20... | collective-permute-start | bytes 2457608 | tf_op jit(solution)/shard_map/ppermute | solution.py:129
  126.2 21.9 %collective-permute-start.1 = (bf16[128,1600]{0,1:T(8,128)(2,1)}, bf16[128,1600]{0,1:T(8,128)(2,1)}, u32[]{:S(2)}, u32[]{:S(2)}) collective-permute-start(bf16[128,1600]{0,1:T(8,128)(2,1)} %fusion.9), channel_id=1, source_target_pairs={{0,16},{16,0},{1,17},{17,1},{2,18},{18,2},{3,19},{19,3},{4,20},{20... | collective-permute-start | bytes 1228808 | tf_op jit(solution)/shard_map/ppermute | solution.py:133
  137.1 11.7 %collective-permute-start.2 = (bf16[128,1600]{0,1:T(8,128)(2,1)}, bf16[128,1600]{0,1:T(8,128)(2,1)}, u32[]{:S(2)}, u32[]{:S(2)}) collective-permute-start(bf16[128,1600]{0,1:T(8,128)(2,1)} %fusion.10), channel_id=1, source_target_pairs={{0,16},{16,0},{1,17},{17,1},{2,18},{18,2},{3,19},{19,3},{4,20},{20... | collective-permute-start | bytes 1228808 | tf_op jit(solution)/shard_map/ppermute | solution.py:133
Sparse Core Ops, SparseCore 0:
  9.5 107.4 all-gather.2

commit v6 on v4

--- a/solution.py
+++ b/solution.py
@@ -128,11 +128,11 @@
         partner_normed = lax.ppermute(normed, "group", there)
         partner_feed = feed(partner_normed).astype(jnp.bfloat16)
         returned.append(lax.ppermute(partner_feed, "group", back))
-    feed_out = lax.optimization_barrier(feed(normed))
+    summed = lax.optimization_barrier(residual + feed(normed))
     for part in returned:
-        feed_out = feed_out + part.astype(jnp.float32)
+        summed = summed + part.astype(jnp.float32)
     live = positions[:, None] < my_length
-    return jnp.where(live, residual + feed_out, 0.0).astype(jnp.bfloat16)[None]
+    return jnp.where(live, summed, 0.0).astype(jnp.bfloat16)[None]
 
 
 def solution(mesh):

time: 159 us -> 158 us (level)
    unnamed x29 -> x27, local copies, waits for them, and re-layouts: 4.5 us -> 3.61 us
  transfers between devices with their start and end apart: 3 -> 3, of which waited for: 3 -> 3; matrix products, arithmetic and copies ran while one was open for 23% -> 24% of each run, Pallas kernels for 0% -> 0%
where the time goes in v6:
time: 158 us
  waiting for transfers between devices  58.9 us (37%)
  matrix products  31.4 us (20%)
  blocking collectives  27.9 us (18%)
  between operations  13.6 us (9%)
  local copies, waits for them, and re-layouts  13.3 us (8%)
  other arithmetic  9.5 us (6%)
  starting transfers between devices  2.98 us (2%)
    all_gather x1, waiting for transfers between devices, per_device(): both_half = lax.all_gather(both, 'dev', axis=1)  31.8 us
    all_gather x1, blocking collectives, per_device(): gathered = lax.all_gather(local_kv, 'dev', axis=0, tiled=True)  27.9 us
    dot_general x2, matrix products, feed(): return jnp.dot(activated, proj_rows, preferred_element_type=jnp.float32)  21.6 us
    ppermute x1, waiting for transfers between devices, per_device(): partner_normed = lax.ppermute(normed, 'group', there)  19.2 us
    ppermute x1, waiting for transfers between devices, per_device(): returned.append(lax.ppermute(partner_feed, 'group', back))  7.89 us
    slice x3, local copies, waits for them, and re-layouts, absorb(): key_rows = keyval[:, :width_att].reshape(row_count, head_count, head_size)  6.11 us
    dot_general x1, matrix products, per_device(): jnp.dot(normed_prefix, kv_weight, preferred_element_type=jnp.float32)  4.6 us
    unnamed x27, local copies, waits for them, and re-layouts  3.61 us
  transfers between devices with their start and end apart: 3, of which 3 were waited for; matrix products, arithmetic and copies ran while one was open for 24% of the time, Pallas kernels for 0%

profile of v6, /device:TPU:0, one launch (start us, length us, event | category | flops | bytes accessed | tf_op | source)
XLA Modules:
  0.0 157.6 jit_solution(7749705926982210608)
XLA Ops:
  6.5 0.0 all-gather.3.cloned.1.call-start
  6.5 2.2 %pad_maximum_fusion = bf16[2,120,1600]{2,1,0:T(8,128)(2,1)} fusion(bf16[1,120,1600]{2,1,0:T(8,128)(2,1)} %bitcast.120, bf16[1,120,1600]{2,1,0:T(8,128)(2,1)} %bitcast.121), kind=kLoop, calls=%fused_computation.62 | loop fusion | flops 384000 | bytes 1536000 | tf_op jit(solution)/shard_map/stack | solution.py:112
  8.8 0.0 all-gather.3.cloned.1.call-update
  8.8 0.0 copy-start.9
  8.8 0.0 copy-start.10
  8.8 0.0 copy-start.6
  8.8 0.0 copy-start.7
  8.9 2.3 %fusion.81 = (bf16[256,1024]{1,0:T(8,128)(2,1)}, bf16[256,1024]{1,0:T(8,128)(2,1)}) fusion(bf16[256,2048]{1,0:T(8,128)(2,1)} %bitcast.117), kind=kLoop, calls=%fused_computation.108 | loop fusion | bytes 2097152 | tf_op jit(solution)/shard_map/slice | solution.py:28
  11.1 2.1 %copy.33 = bf16[256,1024]{0,1:T(8,128)(2,1)} copy(bf16[256,1024]{1,0:T(8,128)(2,1)} %get-tuple-element.7) | data formatting | bytes 1048576 | tf_op jit(solution)/shard_map/slice | solution.py:28
  13.2 2.1 %copy.30 = bf16[1,256,1024]{1,2,0:T(8,128)(2,1)} copy(bf16[1,256,1024]{2,1,0:T(8,128)(2,1)} %param.14) | data formatting | bytes 1048576 | tf_op args[1]
  15.2 0.0 copy-done.10
  15.2 0.2 fusion.65
  15.4 0.6 compare_reduce_fusion
  16.1 0.1 convert_reduce_fusion
  16.2 0.2 fusion.56
  16.4 4.6 %fusion.9 = bf16[8,2048]{1,0:T(8,128)(2,1)S(1)} fusion(bf16[1600,2048]{1,0:T(8,128)(2,1)} %param.18, bf16[1,8,2048]{2,1,0:T(8,128)(2,1)S(1)} %copy-done.7, pred[]{:T(512)} %compare_reduce_fusion, bf16[1,8,1600]{2,1,0:T(8,128)(2,1)S(1)} %copy-done.6, f32[8]{0:T(128)S(1)} %add_sqrt_fusion.1, f32[8]{0:T(128)S(1)} %broadcast_multiply_fusion.1), kind=kOutput, calls=%fused_computation.17 | convolution fusion | flops 52512768 | bytes 6644801 | tf_op jit(solution)/shard_map/dot_general | solution.py:78
  21.0 27.9 %all_gather.9 = bf16[128,2048]{1,0:T(8,128)(2,1)S(1)} all-gather(bf16[8,2048]{1,0:T(8,128)(2,1)S(1)} %fusion.9), channel_id=1, replica_groups=mesh['group'=2,'dev'=16] {'dev'}, dimensions={0}, use_global_device_ids=true | all-gather | bytes 557056 | tf_op jit(solution)/shard_map/all_gather | solution.py:84
  49.0 0.7 fusion.82
  49.7 1.8 %copy.29 = bf16[128,1024]{0,1:T(8,128)(2,1)} copy(bf16[128,1024]{1,0:T(8,128)(2,1)} %get-tuple-element.10) | data formatting | bytes 524288 | tf_op jit(solution)/shard_map/slice | solution.py:28
  51.5 2.0 %copy.34 = bf16[256,1024]{0,1:T(8,128)(2,1)} copy(bf16[256,1024]{1,0:T(8,128)(2,1)} %get-tuple-element.8) | data formatting | bytes 1048576 | tf_op jit(solution)/shard_map/slice | solution.py:29
  53.5 0.8 copy.31
  54.4 0.1 select_reduce_fusion
  54.5 0.7 fusion.66
  55.2 0.6 iota_compare_fusion.2
  55.8 0.1 fusion.52
  55.9 1.6 %bitcast_reduce_fusion = (f32[16,256]{1,0:T(8,128)S(1)}, f32[16,128,256]{2,1,0:T(8,128)S(1)}) fusion(bf16[128,16,64]{0,2,1:T(8,128)(2,1)} %bitcast.118, bf16[256,16,64]{0,2,1:T(8,128)(2,1)} %bitcast.114), kind=kOutput, calls=%fused_computation.19 | convolution fusion | flops 68153344 | bytes 2899968 | tf_op jit(solution)/shard_map/qhd,khd->hqk/dot_general | solution.py:31
  57.5 0.0 copy-done.2
  57.5 0.0 copy-done.3
  57.6 0.8 fusion.4
  58.4 0.4 fusion.30
  58.8 1.0 fusion.5
  59.8 0.1 copy-done.4
  59.9 1.1 fusion.32
  61.0 0.0 copy-start.8
  61.0 0.6 fusion.39
  61.6 0.5 copy-done.8
  62.2 1.1 fusion.83
  63.3 0.3 multiply_reduce_fusion
  63.5 0.9 copy-done.1
  64.4 0.2 divide_convert_fusion
  64.6 1.5 collective-permute-start
  66.1 19.2 %collective-permute-done = bf16[256,1600]{0,1:T(8,128)(2,1)} collective-permute-done((bf16[256,1600]{0,1:T(8,128)(2,1)S(1)}, bf16[256,1600]{0,1:T(8,128)(2,1)}, u32[]{:S(2)}, u32[]{:S(2)}) %collective-permute-start) | collective-permute-done | bytes 819232 | tf_op jit(solution)/shard_map/ppermute | solution.py:128
  85.3 31.8 %all-gather.3.cloned.1.call-done = bf16[2,1920,1600]{2,1,0:T(8,128)(2,1)} async-done(((bf16[2,120,1600]{2,1,0:T(8,128)(2,1)}), bf16[2,1920,1600]{2,1,0:T(8,128)(2,1)}) %all-gather.3.cloned.1.call-update) | async-done | bytes 12288016 | tf_op jit(solution)/shard_map/all_gather | solution.py:113
  117.1 10.2 %fusion.8 = bf16[256,1600]{0,1:T(8,128)(2,1)} fusion(bf16[2,1920,1600]{2,1,0:T(8,128)(2,1)} %all-gather.3.cloned.1.call-done, bf16[256,1600]{0,1:T(8,128)(2,1)} %collective-permute-done), kind=kOutput, calls=%fused_computation.15 | convolution fusion | flops 3150561280 | bytes 13926400 | tf_op jit(solution)/shard_map/dot_general | solution.py:122
  127.3 1.5 collective-permute-start.1
  128.8 11.4 %fusion.7 = f32[256,1600]{0,1:T(8,128)} fusion(f32[256,1600]{0,1:T(8,128)} %copy-done.1, bf16[2,1920,1600]{2,1,0:T(8,128)(2,1)} %all-gather.3.cloned.1.call-done, f32[256]{0:T(256)S(1)} %add_sqrt_fusion, f32[256]{0:T(256)S(1)} %broadcast_multiply_fusion), kind=kOutput, calls=%fused_computation.14 | convolution fusion | flops 3151790080 | bytes 17696768 | tf_op jit(solution)/shard_map/dot_general | solution.py:122
  140.1 7.9 %collective-permute-done.1 = bf16[256,1600]{0,1:T(8,128)(2,1)} collective-permute-done((bf16[256,1600]{0,1:T(8,128)(2,1)}, bf16[256,1600]{0,1:T(8,128)(2,1)}, u32[]{:S(2)}, u32[]{:S(2)}) %collective-permute-start.1) | collective-permute-done | bytes 819232 | tf_op jit(solution)/shard_map/ppermute | solution.py:130
  148.0 2.7 %fusion.51 = bf16[1,256,1600]{1,2,0:T(8,128)(2,1)} fusion(f32[256,1600]{0,1:T(8,128)} %fusion.7, bf16[256,1600]{0,1:T(8,128)(2,1)} %collective-permute-done.1, pred[256]{0:T(512)(128)(4,1)S(1)} %iota_compare_fusion.2), kind=kLoop, calls=%fused_computation.61 | loop fusion | flops 1638400 | bytes 3277056 | tf_op jit(solution)/shard_map/broadcast_in_dim | solution.py:135
  (21 shorter events, 0.1 us)
Async XLA Ops:
  6.5 55.1 %copy-start = (bf16[1024,1600]{0,1:T(8,128)(2,1)S(1)}, bf16[1024,1600]{0,1:T(8,128)(2,1)}, u32[]{:S(2)}) copy-start(bf16[1024,1600]{0,1:T(8,128)(2,1)} %param.19) | copy-start | bytes 9830404
  6.5 110.5 %all-gather.3.cloned.1.call-start = ((), (), s32[]{:S(2)}) async-start(), calls=%async_computation | async-start | bytes 13578240 | tf_op jit(solution)/shard_map/all_gather | solution.py:113
  8.8 6.4 %copy-start.9 = (s32[1,16]{1,0:T(1,128)S(1)}, s32[1,16]{1,0:T(1,128)}, u32[]{:S(2)}) copy-start(s32[1,16]{1,0:T(1,128)} %param.24) | copy-start | bytes 196
  8.8 6.4 %copy-start.10 = (s32[1,2]{1,0:T(1,128)S(1)}, s32[1,2]{1,0:T(1,128)}, u32[]{:S(2)}) copy-start(s32[1,2]{1,0:T(1,128)} %param.25) | copy-start | bytes 28
  8.8 7.2 %copy-start.6 = (bf16[1,8,1600]{2,1,0:T(8,128)(2,1)S(1)}, bf16[1,8,1600]{2,1,0:T(8,128)(2,1)}, u32[]{:S(2)}) copy-start(bf16[1,8,1600]{2,1,0:T(8,128)(2,1)} %param.17) | copy-start | bytes 76804
  8.8 7.6 %copy-start.7 = (bf16[1,8,2048]{2,1,0:T(8,128)(2,1)S(1)}, bf16[1,8,2048]{2,1,0:T(8,128)(2,1)}, u32[]{:S(2)}) copy-start(bf16[1,8,2048]{2,1,0:T(8,128)(2,1)} %param.16) | copy-start | bytes 98308
  21.0 33.4 %copy-start.11 = (s32[1,16]{1,0:T(1,128)S(1)}, s32[1,16]{1,0:T(1,128)}, u32[]{:S(2)}) copy-start(s32[1,16]{1,0:T(1,128)} %param.22) | copy-start | bytes 196
  21.0 33.4 %copy-start.12 = (s32[1,16]{1,0:T(1,128)S(1)}, s32[1,16]{1,0:T(1,128)}, u32[]{:S(2)}) copy-start(s32[1,16]{1,0:T(1,128)} %param.23) | copy-start | bytes 196
  54.4 3.2 %copy-start.2 = (bf16[1,256,1024]{1,2,0:T(8,128)(2,1)S(1)}, bf16[1,256,1024]{1,2,0:T(8,128)(2,1)}, u32[]{:S(2)}) copy-start(bf16[1,256,1024]{1,2,0:T(8,128)(2,1)} %copy.30) | copy-start | bytes 1572868
  54.4 3.2 %copy-start.3 = (bf16[256,1024]{0,1:T(8,128)(2,1)S(1)}, bf16[256,1024]{0,1:T(8,128)(2,1)}, u32[]{:S(2)}) copy-start(bf16[256,1024]{0,1:T(8,128)(2,1)} %copy.33) | copy-start | bytes 1572868
  58.8 1.1 copy-start.4
  59.9 1.1 copy-start.5
  61.0 1.1 copy-start.8
  63.2 1.2 copy-start.1
  64.6 20.7 %collective-permute-start = (bf16[256,1600]{0,1:T(8,128)(2,1)S(1)}, bf16[256,1600]{0,1:T(8,128)(2,1)}, u32[]{:S(2)}, u32[]{:S(2)}) collective-permute-start(bf16[256,1600]{0,1:T(8,128)(2,1)S(1)} %divide_convert_fusion), channel_id=1, source_target_pairs={{0,16},{16,0},{1,17},{17,1},{2,18},{18,2},{3,19},{19,3},{4,20},{20... | collective-permute-start | bytes 2457608 | tf_op jit(solution)/shard_map/ppermute | solution.py:128
  127.3 20.7 %collective-permute-start.1 = (bf16[256,1600]{0,1:T(8,128)(2,1)}, bf16[256,1600]{0,1:T(8,128)(2,1)}, u32[]{:S(2)}, u32[]{:S(2)}) collective-permute-start(bf16[256,1600]{0,1:T(8,128)(2,1)} %fusion.8), channel_id=1, source_target_pairs={{0,16},{16,0},{1,17},{17,1},{2,18},{18,2},{3,19},{19,3},{4,20},{20... | collective-permute-start | bytes 2457608 | tf_op jit(solution)/shard_map/ppermute | solution.py:130
Sparse Core Ops, SparseCore 0:
  9.5 107.4 all-gather.2

commit v7 on v6

--- a/solution.py
+++ b/solution.py
@@ -1,3 +1,5 @@
+import functools
+
 import jax
 import jax.numpy as jnp
 from jax import lax
@@ -42,7 +44,67 @@
     return (new_top, running_total, accumulated)
 
 
+def ring_gather(shard, forward, backward, swap, steps_forward, steps_backward):
+    pieces = [shard]
+    ahead = shard
+    behind = shard
+    for step in range(steps_forward):
+        ahead = lax.ppermute(ahead, "dev", forward)
+        pieces.append(ahead)
+        if step < steps_backward:
+            behind = lax.ppermute(behind, "dev", backward)
+            pieces.append(behind)
+    pieces = pieces + [lax.ppermute(piece, "dev", swap) for piece in pieces]
+    return jnp.concatenate(pieces, axis=1)
+
+
+def plan_ring(mesh):
+    devices = mesh.devices
+    device_count = devices.shape[1]
+    if device_count % 2 or device_count < 4:
+        return None
+    chip_count = device_count // 2
+    try:
+        grids = []
+        for row in devices:
+            coords = [tuple(row[2 * k].coords) for k in range(chip_count)]
+            if any(tuple(row[2 * k + 1].coords) != coords[k] for k in range(chip_count)):
+                return None
+            grids.append(coords)
+    except AttributeError:
+        return None
+    coords = grids[0]
+    varying = [axis for axis in range(len(coords[0])) if len({c[axis] for c in coords}) > 1]
+    if len(varying) != 2:
+        return None
+    long_axis, short_axis = varying
+    if len({c[short_axis] for c in coords}) != 2:
+        long_axis, short_axis = short_axis, long_axis
+    if len({c[short_axis] for c in coords}) != 2:
+        return None
+    low, high = sorted({c[short_axis] for c in coords})
+    along = sorted({c[long_axis] for c in coords})
+    place = {(c[short_axis], c[long_axis]): k for k, c in enumerate(coords)}
+    if len(place) != chip_count:
+        return None
+    cycle = [place[(low, a)] for a in along] + [place[(high, a)] for a in reversed(along)]
+    for coords_g in grids:
+        for i in range(chip_count):
+            first = coords_g[cycle[i]]
+            second = coords_g[cycle[(i + 1) % chip_count]]
+            if sum(abs(p - q) for p, q in zip(first, second)) != 1:
+                return None
+    after = {cycle[i]: cycle[(i + 1) % chip_count] for i in range(chip_count)}
+    before = {cycle[i]: cycle[(i - 1) % chip_count] for i in range(chip_count)}
+    forward = [(2 * k + c, 2 * after[k] + c) for k in range(chip_count) for c in range(2)]
+    backward = [(2 * k + c, 2 * before[k] + c) for k in range(chip_count) for c in range(2)]
+    swap = [(2 * k + c, 2 * k + 1 - c) for k in range(chip_count) for c in range(2)]
+    steps_forward = chip_count // 2
+    return forward, backward, swap, steps_forward, chip_count - 1 - steps_forward
+
+
 def per_device(
+    ring_plan,
     suffix_x,
     suffix_query,
     suffix_keyval,
@@ -110,7 +172,10 @@
     group_count = lax.axis_size("group")
     hidden_part = fc_weight.shape[1]
     both = jnp.stack([fc_weight.T, proj_weight])
-    both_half = lax.all_gather(both, "dev", axis=1)
+    if ring_plan is None:
+        both_half = lax.all_gather(both, "dev", axis=1)
+    else:
+        both_half = ring_gather(both, *ring_plan)
     fc_rows = both_half[0].reshape(-1, both.shape[2])
     proj_rows = both_half[1].reshape(-1, both.shape[2])
 
@@ -137,7 +202,7 @@
 
 def solution(mesh):
     return jax.shard_map(
-        per_device,
+        functools.partial(per_device, plan_ring(mesh)),
         mesh=mesh,
         in_specs=(
             P("group", "dev", None),

time: 158 us -> 159 us (level)
  between operations: 13.6 us -> 0.39 us
  local copies, waits for them, and re-layouts: 13.3 us -> 22 us
  starting transfers between devices: 2.98 us -> 11.4 us
  blocking collectives: 27.9 us -> 23.6 us
    ppermute x0 -> x15, waiting for transfers between devices: none -> 50.8 us  [the longest x4 43.8 us: ring_gather(): ahead = lax.ppermute(ahead, 'dev', forward)]
    all_gather x1 -> x0, waiting for transfers between devices: 31.8 us -> none  [per_device(): both_half = lax.all_gather(both, 'dev', axis=1)]
    ppermute x1, waiting for transfers between devices: 19.2 us -> 0.01 us  [per_device(): partner_normed = lax.ppermute(normed, 'group', there)]
    unnamed x27 -> x49, local copies, waits for them, and re-layouts: 3.61 us -> 12.2 us
    ppermute x0 -> x15, starting transfers between devices: none -> 8.34 us  [the longest x4 3.89 us: ring_gather(): ahead = lax.ppermute(ahead, 'dev', forward)]
    all_gather x1, blocking collectives: 27.9 us -> 23.6 us  [per_device(): gathered = lax.all_gather(local_kv, 'dev', axis=0, tiled=True)]
  transfers between devices with their start and end apart: 3 -> 17, of which waited for: 3 -> 9; matrix products, arithmetic and copies ran while one was open for 24% -> 28% of each run, Pallas kernels for 0% -> 0%
where the time goes in v7:
time: 159 us
  waiting for transfers between devices  58.8 us (37%)
  matrix products  32.4 us (20%)
  blocking collectives  23.6 us (15%)
  local copies, waits for them, and re-layouts  22 us (14%)
  starting transfers between devices  11.4 us (7%)
  other arithmetic  10.3 us (6%)
    ppermute x4, waiting for transfers between devices, ring_gather(): ahead = lax.ppermute(ahead, 'dev', forward)  43.8 us
    all_gather x1, blocking collectives, per_device(): gathered = lax.all_gather(local_kv, 'dev', axis=0, tiled=True)  23.6 us
    dot_general x2, matrix products, feed(): return jnp.dot(activated, proj_rows, preferred_element_type=jnp.float32)  21.4 us
    unnamed x49, local copies, waits for them, and re-layouts  12.2 us
    ppermute x1, waiting for transfers between devices, per_device(): returned.append(lax.ppermute(partner_feed, 'group', back))  7.94 us
    slice x3, local copies, waits for them, and re-layouts, absorb(): key_rows = keyval[:, :width_att].reshape(row_count, head_count, head_size)  6.1 us
    dot_general x1, matrix products, per_device(): jnp.dot(normed_prefix, kv_weight, preferred_element_type=jnp.float32)  4.49 us
    ppermute x4, starting transfers between devices, ring_gather(): ahead = lax.ppermute(ahead, 'dev', forward)  3.89 us
  transfers between devices with their start and end apart: 17, of which 9 were waited for; matrix products, arithmetic and copies ran while one was open for 28% of the time, Pallas kernels for 0%

profile of v7, /device:TPU:0, one launch (start us, length us, event | category | flops | bytes accessed | tf_op | source)
XLA Modules:
  0.0 158.8 jit_solution(13525674185456450260)
XLA Ops:
  0.0 2.5 %pad_maximum_fusion = (bf16[2,120,1600]{2,1,0:T(8,128)(2,1)}, bf16[2,1920,1600]{2,1,0:T(8,128)(2,1)}) fusion(bf16[1,120,1600]{2,1,0:T(8,128)(2,1)} %bitcast.120, bf16[1,120,1600]{2,1,0:T(8,128)(2,1)} %bitcast.121), kind=kLoop, calls=%fused_computation.62 | loop fusion | flops 1535999 | bytes 2365440 | tf_op jit(solution)/shard_map/stack | solution.py:174
  2.6 3.0 %collective-permute-start = (bf16[2,120,1600]{2,1,0:T(8,128)(2,1)}, bf16[2,120,1600]{2,1,0:T(8,128)(2,1)}, u32[]{:S(2)}, u32[]{:S(2)}) collective-permute-start(bf16[2,120,1600]{2,1,0:T(8,128)(2,1)} %get-tuple-element.9), channel_id=1, source_target_pairs={{0,4},{1,5},{2,0},{3,1},{4,8},{5,9},{6,2},{7,3},{8,12},{9,13},{10,... | collective-permute-start | bytes 2304008 | tf_op jit(solution)/shard_map/ppermute | solution.py:52
  5.6 2.2 %fusion.81 = (bf16[256,1024]{1,0:T(8,128)(2,1)}, bf16[256,1024]{1,0:T(8,128)(2,1)}) fusion(bf16[256,2048]{1,0:T(8,128)(2,1)} %bitcast.117), kind=kLoop, calls=%fused_computation.124 | loop fusion | bytes 2097152 | tf_op jit(solution)/shard_map/slice | solution.py:30
  7.9 2.1 %copy.34 = bf16[256,1024]{0,1:T(8,128)(2,1)} copy(bf16[256,1024]{1,0:T(8,128)(2,1)} %get-tuple-element.8) | data formatting | bytes 1048576 | tf_op jit(solution)/shard_map/slice | solution.py:31
  10.1 0.6 fusion.66
  10.7 0.6 iota_compare_fusion.2
  11.3 0.7 fusion.52
  12.0 2.0 %copy.30 = bf16[1,256,1024]{1,2,0:T(8,128)(2,1)} copy(bf16[1,256,1024]{2,1,0:T(8,128)(2,1)} %param.14) | data formatting | bytes 1048576 | tf_op args[1]
  14.0 2.0 %copy.33 = bf16[256,1024]{0,1:T(8,128)(2,1)} copy(bf16[256,1024]{1,0:T(8,128)(2,1)} %get-tuple-element.7) | data formatting | bytes 1048576 | tf_op jit(solution)/shard_map/slice | solution.py:30
  16.3 0.7 compare_reduce_fusion
  17.3 4.5 %fusion.9 = bf16[8,2048]{1,0:T(8,128)(2,1)S(1)} fusion(bf16[1600,2048]{1,0:T(8,128)(2,1)} %param.18, bf16[1,8,2048]{2,1,0:T(8,128)(2,1)S(1)} %copy-done.7, pred[]{:T(512)} %compare_reduce_fusion, bf16[1,8,1600]{2,1,0:T(8,128)(2,1)S(1)} %copy-done.5, f32[8]{0:T(128)S(1)} %add_sqrt_fusion.1, f32[8]{0:T(128)S(1)} %broadcast_multiply_fusion.1), kind=kOutput, calls=%fused_computation.17 | convolution fusion | flops 52512768 | bytes 6644801 | tf_op jit(solution)/shard_map/dot_general | solution.py:140
  21.8 23.6 %all_gather.3 = bf16[128,2048]{1,0:T(8,128)(2,1)S(1)} all-gather(bf16[8,2048]{1,0:T(8,128)(2,1)S(1)} %fusion.9), channel_id=1, replica_groups=mesh['group'=2,'dev'=16] {'dev'}, dimensions={0}, use_global_device_ids=true | all-gather | bytes 557056 | tf_op jit(solution)/shard_map/all_gather | solution.py:146
  45.4 0.7 fusion.82
  46.1 1.8 %copy.29 = bf16[128,1024]{0,1:T(8,128)(2,1)} copy(bf16[128,1024]{1,0:T(8,128)(2,1)} %get-tuple-element.12) | data formatting | bytes 524288 | tf_op jit(solution)/shard_map/slice | solution.py:30
  47.9 0.8 copy.31
  48.7 1.6 %bitcast_reduce_fusion = (f32[16,256]{1,0:T(8,128)S(1)}, f32[16,128,256]{2,1,0:T(8,128)S(1)}) fusion(bf16[128,16,64]{0,2,1:T(8,128)(2,1)} %bitcast.118, bf16[256,16,64]{0,2,1:T(8,128)(2,1)} %bitcast.114), kind=kOutput, calls=%fused_computation.19 | convolution fusion | flops 68153344 | bytes 2899968 | tf_op jit(solution)/shard_map/qhd,khd->hqk/dot_general | solution.py:33
  50.4 2.0 %fusion.4 = (f32[16,256]{1,0:T(8,128)S(1)}, f32[16,256,256]{1,2,0:T(8,128)S(1)}) fusion(pred[256,256]{0,1:T(8,128)(4,1)} %fusion.52, bf16[256,16,64]{0,2,1:T(8,128)(2,1)} %bitcast.115, bf16[256,16,64]{0,2,1:T(8,128)(2,1)} %bitcast.116), kind=kOutput, calls=%fused_computation.8 | convolution fusion | flops 137359360 | bytes 5324800 | tf_op jit(solution)/shard_map/qhd,khd->hqk/dot_general | solution.py:33
  52.5 1.0 fusion.5
  53.5 0.4 fusion.30
  53.9 1.1 fusion.32
  55.1 0.6 fusion.39
  55.8 0.7 copy-done.8
  56.5 1.1 fusion.83
  57.6 0.3 multiply_reduce_fusion
  57.8 1.4 collective-permute-start.3
  59.2 16.8 %collective-permute-done.2 = bf16[2,120,1600]{2,1,0:T(8,128)(2,1)S(1)} collective-permute-done((bf16[2,120,1600]{2,1,0:T(8,128)(2,1)}, bf16[2,120,1600]{2,1,0:T(8,128)(2,1)S(1)}, u32[]{:S(2)}, u32[]{:S(2)}) %collective-permute-start.2) | collective-permute-done | bytes 768032 | tf_op jit(solution)/shard_map/ppermute | solution.py:52
  76.0 0.3 collective-permute-start.4
  76.5 1.6 collective-permute-start.15
  78.1 1.2 constant_dynamic-update-slice_fusion.14
  79.3 1.8 %collective-permute-start.5 = (bf16[2,120,1600]{2,1,0:T(8,128)(2,1)S(1)}, bf16[2,120,1600]{2,1,0:T(8,128)(2,1)S(1)}, u32[]{:S(2)}, u32[]{:S(2)}) collective-permute-start(bf16[2,120,1600]{2,1,0:T(8,128)(2,1)S(1)} %collective-permute-done.3), channel_id=1, source_target_pairs={{0,2},{1,3},{2,6},{3,7},{4,0},{5,1},{6,10},{7,11},{8,4},{9,5},{10,... | collective-permute-start | bytes 2304008 | tf_op jit(solution)/shard_map/ppermute | solution.py:55
  81.1 1.2 constant_dynamic-update-slice_fusion.13
  82.3 12.9 %collective-permute-done.4 = bf16[2,120,1600]{2,1,0:T(8,128)(2,1)S(1)} collective-permute-done((bf16[2,120,1600]{2,1,0:T(8,128)(2,1)S(1)}, bf16[2,120,1600]{2,1,0:T(8,128)(2,1)S(1)}, u32[]{:S(2)}, u32[]{:S(2)}) %collective-permute-start.4) | collective-permute-done | bytes 768032 | tf_op jit(solution)/shard_map/ppermute | solution.py:52
  95.3 0.5 collective-permute-start.6
  96.1 3.5 %collective-permute-done.5 = bf16[2,120,1600]{2,1,0:T(8,128)(2,1)S(1)} collective-permute-done((bf16[2,120,1600]{2,1,0:T(8,128)(2,1)S(1)}, bf16[2,120,1600]{2,1,0:T(8,128)(2,1)S(1)}, u32[]{:S(2)}, u32[]{:S(2)}) %collective-permute-start.5) | collective-permute-done | bytes 768032 | tf_op jit(solution)/shard_map/ppermute | solution.py:55
  99.7 14.0 %collective-permute-done.6 = bf16[2,120,1600]{2,1,0:T(8,128)(2,1)S(1)} collective-permute-done((bf16[2,120,1600]{2,1,0:T(8,128)(2,1)S(1)}, bf16[2,120,1600]{2,1,0:T(8,128)(2,1)S(1)}, u32[]{:S(2)}, u32[]{:S(2)}) %collective-permute-start.6) | collective-permute-done | bytes 768032 | tf_op jit(solution)/shard_map/ppermute | solution.py:52
  113.8 0.6 collective-permute-start.11
  114.4 1.2 constant_dynamic-update-slice_fusion.7
  115.8 0.6 collective-permute-start.13
  116.7 0.5 collective-permute-done.11
  117.3 1.0 collective-permute-done.12
  118.4 1.0 collective-permute-done.13
  119.5 1.0 collective-permute-done.14
  120.7 4.6 %copy-done.6 = bf16[2,1920,1600]{2,1,0:T(8,128)(2,1)} copy-done((bf16[2,1920,1600]{2,1,0:T(8,128)(2,1)}, bf16[2,1920,1600]{2,1,0:T(8,128)(2,1)S(1)}, u32[]{:S(2)}) %copy-start.6) | copy-done | bytes 12288024
  125.3 10.2 %fusion.8 = bf16[256,1600]{0,1:T(8,128)(2,1)} fusion(bf16[2,1920,1600]{2,1,0:T(8,128)(2,1)} %copy-done.6, bf16[256,1600]{0,1:T(8,128)(2,1)} %collective-permute-done.15), kind=kOutput, calls=%fused_computation.15 | convolution fusion | flops 3150561280 | bytes 13926400 | tf_op jit(solution)/shard_map/dot_general | solution.py:187
  135.5 1.5 collective-permute-start.16
  137.0 11.2 %fusion.7 = f32[256,1600]{0,1:T(8,128)} fusion(f32[256,1600]{0,1:T(8,128)} %copy-done.1, bf16[2,1920,1600]{2,1,0:T(8,128)(2,1)} %copy-done.6, f32[256]{0:T(256)S(1)} %add_sqrt_fusion, f32[256]{0:T(256)S(1)} %broadcast_multiply_fusion), kind=kOutput, calls=%fused_computation.14 | convolution fusion | flops 3151790080 | bytes 17696768 | tf_op jit(solution)/shard_map/dot_general | solution.py:187
  148.1 7.9 %collective-permute-done.16 = bf16[256,1600]{0,1:T(8,128)(2,1)} collective-permute-done((bf16[256,1600]{0,1:T(8,128)(2,1)}, bf16[256,1600]{0,1:T(8,128)(2,1)}, u32[]{:S(2)}, u32[]{:S(2)}) %collective-permute-start.16) | collective-permute-done | bytes 819232 | tf_op jit(solution)/shard_map/ppermute | solution.py:195
  156.1 2.7 %fusion.51 = bf16[1,256,1600]{1,2,0:T(8,128)(2,1)} fusion(f32[256,1600]{0,1:T(8,128)} %fusion.7, bf16[256,1600]{0,1:T(8,128)(2,1)} %collective-permute-done.16, pred[256]{0:T(512)(128)(4,1)S(1)} %iota_compare_fusion.2), kind=kLoop, calls=%fused_computation.61 | loop fusion | flops 1638400 | bytes 3277056 | tf_op jit(solution)/shard_map/broadcast_in_dim | solution.py:200
  (72 shorter events, 2.3 us)
Async XLA Ops:
  0.0 55.7 %copy-start = (bf16[1024,1600]{0,1:T(8,128)(2,1)S(1)}, bf16[1024,1600]{0,1:T(8,128)(2,1)}, u32[]{:S(2)}) copy-start(bf16[1024,1600]{0,1:T(8,128)(2,1)} %param.19) | copy-start | bytes 9830404
  0.0 10.0 %copy-start.9 = (s32[1,16]{1,0:T(1,128)S(1)}, s32[1,16]{1,0:T(1,128)}, u32[]{:S(2)}) copy-start(s32[1,16]{1,0:T(1,128)} %param.22) | copy-start | bytes 196
  0.0 10.0 %copy-start.10 = (s32[1,16]{1,0:T(1,128)S(1)}, s32[1,16]{1,0:T(1,128)}, u32[]{:S(2)}) copy-start(s32[1,16]{1,0:T(1,128)} %param.23) | copy-start | bytes 196
  0.0 16.1 %copy-start.11 = (s32[1,16]{1,0:T(1,128)S(1)}, s32[1,16]{1,0:T(1,128)}, u32[]{:S(2)}) copy-start(s32[1,16]{1,0:T(1,128)} %param.24) | copy-start | bytes 196
  0.0 16.1 %copy-start.12 = (s32[1,2]{1,0:T(1,128)S(1)}, s32[1,2]{1,0:T(1,128)}, u32[]{:S(2)}) copy-start(s32[1,2]{1,0:T(1,128)} %param.25) | copy-start | bytes 28
  0.0 16.9 %copy-start.5 = (bf16[1,8,1600]{2,1,0:T(8,128)(2,1)S(1)}, bf16[1,8,1600]{2,1,0:T(8,128)(2,1)}, u32[]{:S(2)}) copy-start(bf16[1,8,1600]{2,1,0:T(8,128)(2,1)} %param.17) | copy-start | bytes 76804
  0.0 17.3 %copy-start.7 = (bf16[1,8,2048]{2,1,0:T(8,128)(2,1)S(1)}, bf16[1,8,2048]{2,1,0:T(8,128)(2,1)}, u32[]{:S(2)}) copy-start(bf16[1,8,2048]{2,1,0:T(8,128)(2,1)} %param.16) | copy-start | bytes 98308
  2.6 53.1 %collective-permute-start = (bf16[2,120,1600]{2,1,0:T(8,128)(2,1)}, bf16[2,120,1600]{2,1,0:T(8,128)(2,1)}, u32[]{:S(2)}, u32[]{:S(2)}) collective-permute-start(bf16[2,120,1600]{2,1,0:T(8,128)(2,1)} %get-tuple-element.9), channel_id=1, source_target_pairs={{0,4},{1,5},{2,0},{3,1},{4,8},{5,9},{6,2},{7,3},{8,12},{9,13},{10,... | collective-permute-start | bytes 2304008 | tf_op jit(solution)/shard_map/ppermute | solution.py:52
  5.6 52.2 %collective-permute-start.1 = (bf16[2,120,1600]{2,1,0:T(8,128)(2,1)}, bf16[2,120,1600]{2,1,0:T(8,128)(2,1)}, u32[]{:S(2)}, u32[]{:S(2)}) collective-permute-start(bf16[2,120,1600]{2,1,0:T(8,128)(2,1)} %get-tuple-element.9), channel_id=1, source_target_pairs={{0,2},{1,3},{2,6},{3,7},{4,0},{5,1},{6,10},{7,11},{8,4},{9,5},{10,... | collective-permute-start | bytes 2304008 | tf_op jit(solution)/shard_map/ppermute | solution.py:55
  5.6 108.2 %collective-permute-start.7 = (bf16[2,120,1600]{2,1,0:T(8,128)(2,1)}, bf16[2,120,1600]{2,1,0:T(8,128)(2,1)}, u32[]{:S(2)}, u32[]{:S(2)}) collective-permute-start(bf16[2,120,1600]{2,1,0:T(8,128)(2,1)} %get-tuple-element.9), channel_id=1, source_target_pairs={{0,1},{1,0},{2,3},{3,2},{4,5},{5,4},{6,7},{7,6},{8,9},{9,8},{10,11... | collective-permute-start | bytes 2304008 | tf_op jit(solution)/shard_map/ppermute | solution.py:57
  48.7 3.7 %copy-start.2 = (pred[256,256]{0,1:T(8,128)(4,1)S(1)}, pred[256,256]{0,1:T(8,128)(4,1)}, u32[]{:S(2)}) copy-start(pred[256,256]{0,1:T(8,128)(4,1)} %fusion.52) | copy-start | bytes 196612
  52.4 1.5 copy-start.3
  53.8 1.2 copy-start.4
  53.9 24.1 %slice-start = ((s8[12779520]{0:T(1024)(128)(4,1)}), s8[196608]{0:T(1024)(128)(4,1)S(1)}, s32[]{:S(2)}) async-start(s8[12779520]{0:T(1024)(128)(4,1)} %bitcast.123), calls=%async_computation | async-start | bytes 393216
  53.9 24.1 %slice-start.1 = ((s8[12779520]{0:T(1024)(128)(4,1)}), s8[4194304]{0:T(1024)(128)(4,1)S(1)}, s32[]{:S(2)}) async-start(s8[12779520]{0:T(1024)(128)(4,1)} %bitcast.123), calls=%async_computation.1 | async-start | bytes 8388608
  55.0 1.4 copy-start.8
  55.1 23.0 %slice-start.2 = ((s8[12779520]{0:T(1024)(128)(4,1)}), s8[4194304]{0:T(1024)(128)(4,1)S(1)}, s32[]{:S(2)}) async-start(s8[12779520]{0:T(1024)(128)(4,1)} %bitcast.123), calls=%async_computation.2 | async-start | bytes 8388608
  55.7 20.3 %collective-permute-start.2 = (bf16[2,120,1600]{2,1,0:T(8,128)(2,1)}, bf16[2,120,1600]{2,1,0:T(8,128)(2,1)S(1)}, u32[]{:S(2)}, u32[]{:S(2)}) collective-permute-start(bf16[2,120,1600]{2,1,0:T(8,128)(2,1)} %collective-permute-done), channel_id=1, source_target_pairs={{0,4},{1,5},{2,0},{3,1},{4,8},{5,9},{6,2},{7,3},{8,12},{9,13},{10,... | collective-permute-start | bytes 2304008 | tf_op jit(solution)/shard_map/ppermute | solution.py:52
  56.5 21.6 %slice-start.3 = ((s8[12779520]{0:T(1024)(128)(4,1)}), s8[4194304]{0:T(1024)(128)(4,1)S(1)}, s32[]{:S(2)}) async-start(s8[12779520]{0:T(1024)(128)(4,1)} %bitcast.123), calls=%async_computation.3 | async-start | bytes 8388608
  57.5 38.3 %copy-start.1 = (f32[256,1600]{0,1:T(8,128)}, f32[256,1600]{0,1:T(8,128)S(1)}, u32[]{:S(2)}) copy-start(f32[256,1600]{0,1:T(8,128)S(1)} %get-tuple-element.21) | copy-start | bytes 4915204
  57.8 21.5 %collective-permute-start.3 = (bf16[2,120,1600]{2,1,0:T(8,128)(2,1)}, bf16[2,120,1600]{2,1,0:T(8,128)(2,1)S(1)}, u32[]{:S(2)}, u32[]{:S(2)}) collective-permute-start(bf16[2,120,1600]{2,1,0:T(8,128)(2,1)} %collective-permute-done.1), channel_id=1, source_target_pairs={{0,2},{1,3},{2,6},{3,7},{4,0},{5,1},{6,10},{7,11},{8,4},{9,5},{10,... | collective-permute-start | bytes 2304008 | tf_op jit(solution)/shard_map/ppermute | solution.py:55
  76.0 19.3 %collective-permute-start.4 = (bf16[2,120,1600]{2,1,0:T(8,128)(2,1)S(1)}, bf16[2,120,1600]{2,1,0:T(8,128)(2,1)S(1)}, u32[]{:S(2)}, u32[]{:S(2)}) collective-permute-start(bf16[2,120,1600]{2,1,0:T(8,128)(2,1)S(1)} %collective-permute-done.2), channel_id=1, source_target_pairs={{0,4},{1,5},{2,0},{3,1},{4,8},{5,9},{6,2},{7,3},{8,12},{9,13},{10,... | collective-permute-start | bytes 2304008 | tf_op jit(solution)/shard_map/ppermute | solution.py:52
  76.5 48.8 %collective-permute-start.15 = (bf16[256,1600]{0,1:T(8,128)(2,1)S(1)}, bf16[256,1600]{0,1:T(8,128)(2,1)}, u32[]{:S(2)}, u32[]{:S(2)}) collective-permute-start(bf16[256,1600]{0,1:T(8,128)(2,1)S(1)} %divide_convert_fusion), channel_id=1, source_target_pairs={{0,16},{16,0},{1,17},{17,1},{2,18},{18,2},{3,19},{19,3},{4,20},{20... | collective-permute-start | bytes 2457608 | tf_op jit(solution)/shard_map/ppermute | solution.py:193
  78.0 37.6 %collective-permute-start.8 = (bf16[2,120,1600]{2,1,0:T(8,128)(2,1)}, bf16[2,120,1600]{2,1,0:T(8,128)(2,1)S(1)}, u32[]{:S(2)}, u32[]{:S(2)}) collective-permute-start(bf16[2,120,1600]{2,1,0:T(8,128)(2,1)} %collective-permute-done), channel_id=1, source_target_pairs={{0,1},{1,0},{2,3},{3,2},{4,5},{5,4},{6,7},{7,6},{8,9},{9,8},{10,11... | collective-permute-start | bytes 2304008 | tf_op jit(solution)/shard_map/ppermute | solution.py:57
  79.3 20.3 %collective-permute-start.5 = (bf16[2,120,1600]{2,1,0:T(8,128)(2,1)S(1)}, bf16[2,120,1600]{2,1,0:T(8,128)(2,1)S(1)}, u32[]{:S(2)}, u32[]{:S(2)}) collective-permute-start(bf16[2,120,1600]{2,1,0:T(8,128)(2,1)S(1)} %collective-permute-done.3), channel_id=1, source_target_pairs={{0,2},{1,3},{2,6},{3,7},{4,0},{5,1},{6,10},{7,11},{8,4},{9,5},{10,... | collective-permute-start | bytes 2304008 | tf_op jit(solution)/shard_map/ppermute | solution.py:55
  95.3 18.4 %collective-permute-start.6 = (bf16[2,120,1600]{2,1,0:T(8,128)(2,1)S(1)}, bf16[2,120,1600]{2,1,0:T(8,128)(2,1)S(1)}, u32[]{:S(2)}, u32[]{:S(2)}) collective-permute-start(bf16[2,120,1600]{2,1,0:T(8,128)(2,1)S(1)} %collective-permute-done.4), channel_id=1, source_target_pairs={{0,4},{1,5},{2,0},{3,1},{4,8},{5,9},{6,2},{7,3},{8,12},{9,13},{10,... | collective-permute-start | bytes 2304008 | tf_op jit(solution)/shard_map/ppermute | solution.py:52
  99.6 16.3 %collective-permute-start.9 = (bf16[2,120,1600]{2,1,0:T(8,128)(2,1)}, bf16[2,120,1600]{2,1,0:T(8,128)(2,1)S(1)}, u32[]{:S(2)}, u32[]{:S(2)}) collective-permute-start(bf16[2,120,1600]{2,1,0:T(8,128)(2,1)} %collective-permute-done.1), channel_id=1, source_target_pairs={{0,1},{1,0},{2,3},{3,2},{4,5},{5,4},{6,7},{7,6},{8,9},{9,8},{10,11... | collective-permute-start | bytes 2304008 | tf_op jit(solution)/shard_map/ppermute | solution.py:57
  113.7 2.8 %collective-permute-start.10 = (bf16[2,120,1600]{2,1,0:T(8,128)(2,1)S(1)}, bf16[2,120,1600]{2,1,0:T(8,128)(2,1)S(1)}, u32[]{:S(2)}, u32[]{:S(2)}) collective-permute-start(bf16[2,120,1600]{2,1,0:T(8,128)(2,1)S(1)} %collective-permute-done.2), channel_id=1, source_target_pairs={{0,1},{1,0},{2,3},{3,2},{4,5},{5,4},{6,7},{7,6},{8,9},{9,8},{10,11... | collective-permute-start | bytes 2304008 | tf_op jit(solution)/shard_map/ppermute | solution.py:57
  113.8 3.3 %collective-permute-start.11 = (bf16[2,120,1600]{2,1,0:T(8,128)(2,1)S(1)}, bf16[2,120,1600]{2,1,0:T(8,128)(2,1)S(1)}, u32[]{:S(2)}, u32[]{:S(2)}) collective-permute-start(bf16[2,120,1600]{2,1,0:T(8,128)(2,1)S(1)} %collective-permute-done.3), channel_id=1, source_target_pairs={{0,1},{1,0},{2,3},{3,2},{4,5},{5,4},{6,7},{7,6},{8,9},{9,8},{10,11... | collective-permute-start | bytes 2304008 | tf_op jit(solution)/shard_map/ppermute | solution.py:57
  115.6 2.7 %collective-permute-start.12 = (bf16[2,120,1600]{2,1,0:T(8,128)(2,1)S(1)}, bf16[2,120,1600]{2,1,0:T(8,128)(2,1)S(1)}, u32[]{:S(2)}, u32[]{:S(2)}) collective-permute-start(bf16[2,120,1600]{2,1,0:T(8,128)(2,1)S(1)} %collective-permute-done.4), channel_id=1, source_target_pairs={{0,1},{1,0},{2,3},{3,2},{4,5},{5,4},{6,7},{7,6},{8,9},{9,8},{10,11... | collective-permute-start | bytes 2304008 | tf_op jit(solution)/shard_map/ppermute | solution.py:57
  115.8 3.6 %collective-permute-start.13 = (bf16[2,120,1600]{2,1,0:T(8,128)(2,1)S(1)}, bf16[2,120,1600]{2,1,0:T(8,128)(2,1)S(1)}, u32[]{:S(2)}, u32[]{:S(2)}) collective-permute-start(bf16[2,120,1600]{2,1,0:T(8,128)(2,1)S(1)} %collective-permute-done.5), channel_id=1, source_target_pairs={{0,1},{1,0},{2,3},{3,2},{4,5},{5,4},{6,7},{7,6},{8,9},{9,8},{10,11... | collective-permute-start | bytes 2304008 | tf_op jit(solution)/shard_map/ppermute | solution.py:57
  116.5 4.1 %collective-permute-start.14 = (bf16[2,120,1600]{2,1,0:T(8,128)(2,1)S(1)}, bf16[2,120,1600]{2,1,0:T(8,128)(2,1)S(1)}, u32[]{:S(2)}, u32[]{:S(2)}) collective-permute-start(bf16[2,120,1600]{2,1,0:T(8,128)(2,1)S(1)} %collective-permute-done.6), channel_id=1, source_target_pairs={{0,1},{1,0},{2,3},{3,2},{4,5},{5,4},{6,7},{7,6},{8,9},{9,8},{10,11... | collective-permute-start | bytes 2304008 | tf_op jit(solution)/shard_map/ppermute | solution.py:57
  120.7 4.6 %copy-start.6 = (bf16[2,1920,1600]{2,1,0:T(8,128)(2,1)}, bf16[2,1920,1600]{2,1,0:T(8,128)(2,1)S(1)}, u32[]{:S(2)}) copy-start(bf16[2,1920,1600]{2,1,0:T(8,128)(2,1)S(1)} %constant_dynamic-update-slice_fusion) | copy-start | bytes 36864004
  135.5 20.6 %collective-permute-start.16 = (bf16[256,1600]{0,1:T(8,128)(2,1)}, bf16[256,1600]{0,1:T(8,128)(2,1)}, u32[]{:S(2)}, u32[]{:S(2)}) collective-permute-start(bf16[256,1600]{0,1:T(8,128)(2,1)} %fusion.8), channel_id=1, source_target_pairs={{0,16},{16,0},{1,17},{17,1},{2,18},{18,2},{3,19},{19,3},{4,20},{20... | collective-permute-start | bytes 2457608 | tf_op jit(solution)/shard_map/ppermute | solution.py:195

commit v8 on v7

--- a/solution.py
+++ b/solution.py
@@ -44,11 +44,15 @@
     return (new_top, running_total, accumulated)
 
 
-def ring_gather(shard, forward, backward, swap, steps_forward, steps_backward):
-    pieces = [shard]
-    ahead = shard
-    behind = shard
-    for step in range(steps_forward):
+def ring_first(shard, forward, backward, swap, steps_forward, steps_backward):
+    ahead = lax.ppermute(shard, "dev", forward)
+    behind = lax.ppermute(shard, "dev", backward) if steps_backward else shard
+    return ahead, behind
+
+
+def ring_rest(shard, ahead, behind, forward, backward, swap, steps_forward, steps_backward):
+    pieces = [shard, ahead] + ([behind] if steps_backward else [])
+    for step in range(1, steps_forward):
         ahead = lax.ppermute(ahead, "dev", forward)
         pieces.append(ahead)
         if step < steps_backward:
@@ -143,7 +147,12 @@
     my_stale = jnp.any(chosen_owner == my_device)
     local_kv = jnp.where(my_stale, fresh, prefix_keyval[0])
     skip_device = jnp.zeros_like(stale_device)
+    both = jnp.stack([fc_weight.T, proj_weight])
+    if ring_plan is not None:
+        ahead, behind = ring_first(both, *ring_plan)
     gathered = lax.all_gather(local_kv, "dev", axis=0, tiled=True)
+    if ring_plan is not None:
+        gathered, ahead, behind = lax.optimization_barrier((gathered, ahead, behind))
     prefix_count = gathered.shape[0]
     row_device = jnp.arange(prefix_count, dtype=jnp.int32) // block_rows
     skipped = jnp.any((row_device[:, None] == device_ids[None, :]) & skip_device[None, :], axis=1)
@@ -171,11 +180,10 @@
     normed = normalize(residual).astype(jnp.bfloat16)
     group_count = lax.axis_size("group")
     hidden_part = fc_weight.shape[1]
-    both = jnp.stack([fc_weight.T, proj_weight])
     if ring_plan is None:
         both_half = lax.all_gather(both, "dev", axis=1)
     else:
-        both_half = ring_gather(both, *ring_plan)
+        both_half = ring_rest(both, ahead, behind, *ring_plan)
     fc_rows = both_half[0].reshape(-1, both.shape[2])
     proj_rows = both_half[1].reshape(-1, both.shape[2])
 

time: 159 us -> 163 us (1.025)
  waiting for transfers between devices: 58.8 us -> 35.3 us
  local copies, waits for them, and re-layouts: 22 us -> 35.3 us
  other arithmetic: 10.3 us -> 18.4 us
  matrix products: 32.4 us -> 37.5 us
    ppermute x15, waiting for transfers between devices: 50.8 us -> 27 us  [the longest x3 27 us: ring_rest(): ahead = lax.ppermute(ahead, 'dev', forward)]
    unnamed x49 -> x43, local copies, waits for them, and re-layouts: 12.2 us -> 24.6 us
    reduce_sum x2, other arithmetic: 1.37 us -> 5.82 us  [absorb(): running_total = running_total * factor + jnp.sum(weights, axis=-1)]
    dot_general x2, matrix products: 1.72 us -> 4.68 us  [absorb(): jnp.einsum('hqk,khd->qhd', weights_low, val_rows, preferred_element_type=...]
    another operation x1 -> x0, other arithmetic: 2.55 us -> none  [per_device(): both = jnp.stack([fc_weight.T, proj_weight])]
    unnamed x1, other arithmetic: 0.01 us -> 2.54 us
    dot_general x2, matrix products: 3.69 us -> 5.85 us  [absorb(): jnp.einsum('qhd,khd->hqk', queries, key_rows, preferred_element_type=jnp....]
  transfers between devices with their start and end apart: 17 -> 17, of which waited for: 9 -> 3; matrix products, arithmetic and copies ran while one was open for 28% -> 46% of each run, Pallas kernels for 0% -> 0%
where the time goes in v8:
time: 163 us; the launch traced here: 162 us
  matrix products  37.5 us (23%)
  local copies, waits for them, and re-layouts  35.3 us (22%)
  waiting for transfers between devices  35.3 us (22%)
  blocking collectives  23.6 us (14%)
  other arithmetic  18.4 us (11%)
  starting transfers between devices  11.8 us (7%)
    ppermute x3, waiting for transfers between devices, ring_rest(): ahead = lax.ppermute(ahead, 'dev', forward)  27 us
    unnamed x43, local copies, waits for them, and re-layouts  24.6 us
    all_gather x1, blocking collectives, per_device(): gathered = lax.all_gather(local_kv, 'dev', axis=0, tiled=True)  23.6 us
    dot_general x2, matrix products, feed(): return jnp.dot(activated, proj_rows, preferred_element_type=jnp.float32)  21.4 us
    ppermute x1, waiting for transfers between devices, per_device(): returned.append(lax.ppermute(partner_feed, 'group', back))  8.29 us
    slice x3, local copies, waits for them, and re-layouts, absorb(): key_rows = keyval[:, :width_att].reshape(row_count, head_count, head_size)  6.14 us
    dot_general x2, matrix products, absorb(): jnp.einsum('qhd,khd->hqk', queries, key_rows, preferred_element_type=jnp....  5.85 us
    reduce_sum x2, other arithmetic, absorb(): running_total = running_total * factor + jnp.sum(weights, axis=-1)  5.82 us
  transfers between devices with their start and end apart: 17, of which 3 were waited for; matrix products, arithmetic and copies ran while one was open for 46% of the time, Pallas kernels for 0%

profile of v8, /device:TPU:0, one launch (start us, length us, event | category | flops | bytes accessed | tf_op | source)
XLA Modules:
  0.0 162.0 jit_solution(4984123573397474138)
XLA Ops:
  0.0 2.5 %constant_dynamic-update-slice_fusion.15 = (bf16[2,1920,1600]{2,1,0:T(8,128)(2,1)}, bf16[2,120,1600]{2,1,0:T(8,128)(2,1)}) fusion(bf16[1,120,1600]{2,1,0:T(8,128)(2,1)} %bitcast.120, bf16[1,120,1600]{2,1,0:T(8,128)(2,1)} %bitcast.121), kind=kLoop, calls=%fused_computation.87 | loop fusion | flops 1535999 | bytes 2365440
  2.6 3.0 %collective-permute-start = (bf16[2,120,1600]{2,1,0:T(8,128)(2,1)}, bf16[2,120,1600]{2,1,0:T(8,128)(2,1)}, u32[]{:S(2)}, u32[]{:S(2)}) collective-permute-start(bf16[2,120,1600]{2,1,0:T(8,128)(2,1)} %get-tuple-element.16), channel_id=1, source_target_pairs={{0,4},{1,5},{2,0},{3,1},{4,8},{5,9},{6,2},{7,3},{8,12},{9,13},{10,... | collective-permute-start | bytes 2304008 | tf_op jit(solution)/shard_map/ppermute | solution.py:48
  5.6 0.9 convert_reduce_fusion
  6.5 0.9 fusion.56
  7.4 2.1 %copy.30 = bf16[1,256,1024]{1,2,0:T(8,128)(2,1)} copy(bf16[1,256,1024]{2,1,0:T(8,128)(2,1)} %param.14) | data formatting | bytes 1048576 | tf_op args[1]
  9.5 0.9 fusion.65
  11.0 0.8 select_reduce_fusion
  13.1 2.3 %fusion.81 = (bf16[256,1024]{1,0:T(8,128)(2,1)}, bf16[256,1024]{1,0:T(8,128)(2,1)}) fusion(bf16[256,2048]{1,0:T(8,128)(2,1)} %bitcast.117), kind=kLoop, calls=%fused_computation.124 | loop fusion | bytes 2097152 | tf_op jit(solution)/shard_map/slice | solution.py:30
  15.3 2.1 %copy.33 = bf16[256,1024]{0,1:T(8,128)(2,1)} copy(bf16[256,1024]{1,0:T(8,128)(2,1)} %get-tuple-element.13) | data formatting | bytes 1048576 | tf_op jit(solution)/shard_map/slice | solution.py:30
  17.4 2.1 %copy.34 = bf16[256,1024]{0,1:T(8,128)(2,1)} copy(bf16[256,1024]{1,0:T(8,128)(2,1)} %get-tuple-element.14) | data formatting | bytes 1048576 | tf_op jit(solution)/shard_map/slice | solution.py:31
  19.5 4.5 %fusion.9 = bf16[8,2048]{1,0:T(8,128)(2,1)S(1)} fusion(bf16[1600,2048]{1,0:T(8,128)(2,1)} %param.18, bf16[1,8,2048]{2,1,0:T(8,128)(2,1)S(1)} %copy-done.10, pred[]{:T(512)} %compare_reduce_fusion, bf16[1,8,1600]{2,1,0:T(8,128)(2,1)S(1)} %copy-done.8, f32[8]{0:T(128)S(1)} %add_sqrt_fusion.1, f32[8]{0:T(128)S(1)} %broadcast_multiply_fusion.1), kind=kOutput, calls=%fused_computation.17 | convolution fusion | flops 52512768 | bytes 6644801 | tf_op jit(solution)/shard_map/dot_general | solution.py:144
  24.1 23.6 %all_gather.3 = bf16[128,2048]{1,0:T(8,128)(2,1)S(1)} all-gather(bf16[8,2048]{1,0:T(8,128)(2,1)S(1)} %fusion.9), channel_id=1, replica_groups=mesh['group'=2,'dev'=16] {'dev'}, dimensions={0}, use_global_device_ids=true | all-gather | bytes 557056 | tf_op jit(solution)/shard_map/all_gather | solution.py:153
  47.7 2.8 %fusion.4 = (f32[16,256]{1,0:T(8,128)S(1)}, f32[16,256,256]{1,2,0:T(8,128)}) fusion(pred[256,256]{0,1:T(8,128)(4,1)S(1)} %fusion.52, bf16[256,16,64]{0,2,1:T(8,128)(2,1)S(1)} %bitcast.115, bf16[256,16,64]{0,2,1:T(8,128)(2,1)S(1)} %bitcast.116), kind=kOutput, calls=%fused_computation.8 | convolution fusion | flops 137359360 | bytes 5324800 | tf_op jit(solution)/shard_map/qhd,khd->hqk/dot_general | solution.py:33
  50.9 1.7 %collective-permute-start.3 = (bf16[2,120,1600]{2,1,0:T(8,128)(2,1)}, bf16[2,120,1600]{2,1,0:T(8,128)(2,1)}, u32[]{:S(2)}, u32[]{:S(2)}) collective-permute-start(bf16[2,120,1600]{2,1,0:T(8,128)(2,1)} %collective-permute-done.1), channel_id=1, source_target_pairs={{0,2},{1,3},{2,6},{3,7},{4,0},{5,1},{6,10},{7,11},{8,4},{9,5},{10,... | collective-permute-start | bytes 2304008 | tf_op jit(solution)/shard_map/ppermute | solution.py:59
  52.7 0.7 fusion.82
  53.5 1.8 %copy.29 = bf16[128,1024]{0,1:T(8,128)(2,1)} copy(bf16[128,1024]{1,0:T(8,128)(2,1)} %get-tuple-element.18) | data formatting | bytes 524288 | tf_op jit(solution)/shard_map/slice | solution.py:30
  55.3 3.1 %bitcast_reduce_fusion = (f32[16,256]{1,0:T(8,128)S(1)}, f32[16,128,256]{2,1,0:T(8,128)}) fusion(bf16[128,16,64]{0,2,1:T(8,128)(2,1)} %bitcast.118, bf16[256,16,64]{0,2,1:T(8,128)(2,1)} %bitcast.114), kind=kOutput, calls=%fused_computation.19 | convolution fusion | flops 68153344 | bytes 2899968 | tf_op jit(solution)/shard_map/qhd,khd->hqk/dot_general | solution.py:33
  59.6 3.8 %fusion.5 = f32[16,256]{1,0:T(8,128)} fusion(f32[16,256,256]{1,2,0:T(8,128)} %get-tuple-element.25, f32[16,256]{1,0:T(8,128)S(1)} %get-tuple-element.21, pred[256,256]{0,1:T(8,128)(4,1)} %copy-done.5), kind=kLoop, calls=%fused_computation.9 | loop fusion | flops 5238784 | bytes 4292608 | tf_op jit(solution)/shard_map/reduce_sum | solution.py:40
  63.4 2.2 %fusion.32 = f32[256,16,64]{0,2,1:T(8,128)} fusion(bf16[256,16,64]{0,2,1:T(8,128)(2,1)S(1)} %bitcast.119, f32[16,256,256]{1,2,0:T(8,128)S(1)} %copy-done.1, f32[16,256]{1,0:T(8,128)S(1)} %get-tuple-element.21, pred[256,256]{0,1:T(8,128)(4,1)S(1)} %copy-done.6), kind=kOutput, calls=%fused_computation.44 | convolution fusion | flops 139460608 | bytes 5849088 | tf_op jit(solution)/shard_map/hqk,khd->qhd/dot_general | solution.py:42
  65.5 0.8 copy.31
  66.4 2.0 %fusion.30 = f32[16,256]{1,0:T(8,128)S(1)} fusion(f32[16,128,256]{2,1,0:T(8,128)} %get-tuple-element.23, f32[16,256]{1,0:T(8,128)} %get-tuple-element.20), kind=kLoop, calls=%fused_computation.39 | loop fusion | flops 1568768 | bytes 2129920 | tf_op jit(solution)/shard_map/reduce_sum | solution.py:40
  68.4 0.8 bitcast_add_fusion
  69.2 2.5 %fusion.39 = bf16[256,16,64]{0,2,1:T(8,128)(2,1)S(1)} fusion(f32[256,16,64]{0,2,1:T(8,128)} %fusion.32, bf16[128,16,64]{0,2,1:T(8,128)(2,1)} %bitcast.122, f32[16,128,256]{2,1,0:T(8,128)} %get-tuple-element.23, f32[16,256]{1,0:T(8,128)} %get-tuple-element.20, f32[256,16]{0,1:T(8,128)S(1)} %get-tuple-element.11, f32[256,16]{0,1:T(8,128)S(1)} %get-tuple-element.12, ...), kind=kOutput, calls=%fused_computation.50 | convolution fusion | flops 69992448 | bytes 3997696 | tf_op jit(solution)/shard_map/hqk,khd->qhd/dot_general | solution.py:42
  71.7 1.1 fusion.83
  73.1 2.4 %constant_dynamic-update-slice_fusion.14 = bf16[2,1920,1600]{2,1,0:T(8,128)(2,1)} fusion(bf16[2,1920,1600]{2,1,0:T(8,128)(2,1)} %get-tuple-element.15, bf16[2,120,1600]{2,1,0:T(8,128)(2,1)} %collective-permute-done), kind=kLoop, calls=%fused_computation.86 | loop fusion | bytes 1597440
  75.8 1.9 %collective-permute-start.5 = (bf16[2,120,1600]{2,1,0:T(8,128)(2,1)}, bf16[2,120,1600]{2,1,0:T(8,128)(2,1)S(1)}, u32[]{:S(2)}, u32[]{:S(2)}) collective-permute-start(bf16[2,120,1600]{2,1,0:T(8,128)(2,1)} %collective-permute-done.3), channel_id=1, source_target_pairs={{0,2},{1,3},{2,6},{3,7},{4,0},{5,1},{6,10},{7,11},{8,4},{9,5},{10,... | collective-permute-start | bytes 2304008 | tf_op jit(solution)/shard_map/ppermute | solution.py:59
  77.7 2.1 %constant_dynamic-update-slice_fusion.13 = bf16[2,1920,1600]{2,1,0:T(8,128)(2,1)} fusion(bf16[2,1920,1600]{2,1,0:T(8,128)(2,1)} %constant_dynamic-update-slice_fusion.14, bf16[2,120,1600]{2,1,0:T(8,128)(2,1)} %collective-permute-done.1), kind=kLoop, calls=%fused_computation.85 | loop fusion | bytes 1597440
  79.8 15.9 %collective-permute-done.4 = bf16[2,120,1600]{2,1,0:T(8,128)(2,1)S(1)} collective-permute-done((bf16[2,120,1600]{2,1,0:T(8,128)(2,1)}, bf16[2,120,1600]{2,1,0:T(8,128)(2,1)S(1)}, u32[]{:S(2)}, u32[]{:S(2)}) %collective-permute-start.4) | collective-permute-done | bytes 768032 | tf_op jit(solution)/shard_map/ppermute | solution.py:56
  96.1 2.1 %constant_dynamic-update-slice_fusion.12 = bf16[2,1920,1600]{2,1,0:T(8,128)(2,1)} fusion(bf16[2,1920,1600]{2,1,0:T(8,128)(2,1)} %constant_dynamic-update-slice_fusion.13, bf16[2,120,1600]{2,1,0:T(8,128)(2,1)} %collective-permute-done.2), kind=kLoop, calls=%fused_computation.84 | loop fusion | bytes 1597440
  98.2 2.1 %constant_dynamic-update-slice_fusion.11 = bf16[2,1920,1600]{2,1,0:T(8,128)(2,1)} fusion(bf16[2,1920,1600]{2,1,0:T(8,128)(2,1)} %constant_dynamic-update-slice_fusion.12, bf16[2,120,1600]{2,1,0:T(8,128)(2,1)} %collective-permute-done.3), kind=kLoop, calls=%fused_computation.83 | loop fusion | bytes 1597440
  100.4 1.0 constant_dynamic-update-slice_fusion.10
  101.3 1.5 collective-permute-start.15
  102.8 1.0 constant_dynamic-update-slice_fusion.9
  103.8 11.1 %collective-permute-done.6 = bf16[2,120,1600]{2,1,0:T(8,128)(2,1)S(1)} collective-permute-done((bf16[2,120,1600]{2,1,0:T(8,128)(2,1)S(1)}, bf16[2,120,1600]{2,1,0:T(8,128)(2,1)S(1)}, u32[]{:S(2)}, u32[]{:S(2)}) %collective-permute-start.6) | collective-permute-done | bytes 768032 | tf_op jit(solution)/shard_map/ppermute | solution.py:56
  115.0 1.0 constant_dynamic-update-slice_fusion.8
  116.5 2.1 %constant_dynamic-update-slice_fusion.7 = bf16[2,1920,1600]{2,1,0:T(8,128)(2,1)} fusion(bf16[2,1920,1600]{2,1,0:T(8,128)(2,1)} %constant_dynamic-update-slice_fusion.8, bf16[2,120,1600]{2,1,0:T(8,128)(2,1)} %collective-permute-done.7), kind=kLoop, calls=%fused_computation.79 | loop fusion | bytes 1597440
  118.6 2.1 %constant_dynamic-update-slice_fusion.6 = bf16[2,1920,1600]{2,1,0:T(8,128)(2,1)} fusion(bf16[2,1920,1600]{2,1,0:T(8,128)(2,1)} %constant_dynamic-update-slice_fusion.7, bf16[2,120,1600]{2,1,0:T(8,128)(2,1)} %collective-permute-done.8), kind=kLoop, calls=%fused_computation.78 | loop fusion | bytes 1597440
  121.2 2.1 %constant_dynamic-update-slice_fusion.5 = bf16[2,1920,1600]{2,1,0:T(8,128)(2,1)} fusion(bf16[2,1920,1600]{2,1,0:T(8,128)(2,1)} %constant_dynamic-update-slice_fusion.6, bf16[2,120,1600]{2,1,0:T(8,128)(2,1)} %collective-permute-done.9), kind=kLoop, calls=%fused_computation.77 | loop fusion | bytes 1597440
  123.3 0.9 constant_dynamic-update-slice_fusion.4
  124.2 1.0 constant_dynamic-update-slice_fusion.3
  125.2 0.9 constant_dynamic-update-slice_fusion.2
  126.2 1.0 constant_dynamic-update-slice_fusion.1
  127.1 0.9 constant_dynamic-update-slice_fusion
  128.1 10.2 %fusion.8 = bf16[256,1600]{0,1:T(8,128)(2,1)} fusion(bf16[2,1920,1600]{2,1,0:T(8,128)(2,1)} %constant_dynamic-update-slice_fusion, bf16[256,1600]{0,1:T(8,128)(2,1)} %collective-permute-done.15), kind=kOutput, calls=%fused_computation.15 | convolution fusion | flops 3150561280 | bytes 13926400 | tf_op jit(solution)/shard_map/dot_general | solution.py:195
  138.3 1.5 collective-permute-start.16
  139.8 11.2 %fusion.7 = f32[256,1600]{0,1:T(8,128)} fusion(f32[256,1600]{0,1:T(8,128)} %copy-done.2, bf16[2,1920,1600]{2,1,0:T(8,128)(2,1)} %constant_dynamic-update-slice_fusion, f32[256]{0:T(256)S(1)} %add_sqrt_fusion, f32[256]{0:T(256)S(1)} %broadcast_multiply_fusion), kind=kOutput, calls=%fused_computation.14 | convolution fusion | flops 3151790080 | bytes 17696768 | tf_op jit(solution)/shard_map/dot_general | solution.py:195
  151.0 8.3 %collective-permute-done.16 = bf16[256,1600]{0,1:T(8,128)(2,1)} collective-permute-done((bf16[256,1600]{0,1:T(8,128)(2,1)}, bf16[256,1600]{0,1:T(8,128)(2,1)}, u32[]{:S(2)}, u32[]{:S(2)}) %collective-permute-start.16) | collective-permute-done | bytes 819232 | tf_op jit(solution)/shard_map/ppermute | solution.py:203
  159.2 2.7 %fusion.51 = bf16[1,256,1600]{1,2,0:T(8,128)(2,1)} fusion(f32[256,1600]{0,1:T(8,128)} %fusion.7, bf16[256,1600]{0,1:T(8,128)(2,1)} %collective-permute-done.16, pred[256]{0:T(512)(128)(4,1)S(1)} %copy-done.12), kind=kLoop, calls=%fused_computation.61 | loop fusion | flops 1638400 | bytes 3277056 | tf_op jit(solution)/shard_map/broadcast_in_dim | solution.py:208
  (65 shorter events, 5.9 us)
Async XLA Ops:
  0.0 71.7 %copy-start = (bf16[1024,1600]{0,1:T(8,128)(2,1)S(1)}, bf16[1024,1600]{0,1:T(8,128)(2,1)}, u32[]{:S(2)}) copy-start(bf16[1024,1600]{0,1:T(8,128)(2,1)} %param.19) | copy-start | bytes 9830404
  0.0 19.5 %copy-start.8 = (bf16[1,8,1600]{2,1,0:T(8,128)(2,1)S(1)}, bf16[1,8,1600]{2,1,0:T(8,128)(2,1)}, u32[]{:S(2)}) copy-start(bf16[1,8,1600]{2,1,0:T(8,128)(2,1)} %param.17) | copy-start | bytes 76804
  0.0 19.5 %copy-start.10 = (bf16[1,8,2048]{2,1,0:T(8,128)(2,1)S(1)}, bf16[1,8,2048]{2,1,0:T(8,128)(2,1)}, u32[]{:S(2)}) copy-start(bf16[1,8,2048]{2,1,0:T(8,128)(2,1)} %param.16) | copy-start | bytes 98308
  2.6 47.9 %collective-permute-start = (bf16[2,120,1600]{2,1,0:T(8,128)(2,1)}, bf16[2,120,1600]{2,1,0:T(8,128)(2,1)}, u32[]{:S(2)}, u32[]{:S(2)}) collective-permute-start(bf16[2,120,1600]{2,1,0:T(8,128)(2,1)} %get-tuple-element.16), channel_id=1, source_target_pairs={{0,4},{1,5},{2,0},{3,1},{4,8},{5,9},{6,2},{7,3},{8,12},{9,13},{10,... | collective-permute-start | bytes 2304008 | tf_op jit(solution)/shard_map/ppermute | solution.py:48
  5.6 44.9 %collective-permute-start.1 = (bf16[2,120,1600]{2,1,0:T(8,128)(2,1)}, bf16[2,120,1600]{2,1,0:T(8,128)(2,1)}, u32[]{:S(2)}, u32[]{:S(2)}) collective-permute-start(bf16[2,120,1600]{2,1,0:T(8,128)(2,1)} %get-tuple-element.16), channel_id=1, source_target_pairs={{0,2},{1,3},{2,6},{3,7},{4,0},{5,1},{6,10},{7,11},{8,4},{9,5},{10,... | collective-permute-start | bytes 2304008 | tf_op jit(solution)/shard_map/ppermute | solution.py:49
  5.6 110.4 %collective-permute-start.7 = (bf16[2,120,1600]{2,1,0:T(8,128)(2,1)}, bf16[2,120,1600]{2,1,0:T(8,128)(2,1)}, u32[]{:S(2)}, u32[]{:S(2)}) collective-permute-start(bf16[2,120,1600]{2,1,0:T(8,128)(2,1)} %get-tuple-element.16), channel_id=1, source_target_pairs={{0,1},{1,0},{2,3},{3,2},{4,5},{5,4},{6,7},{7,6},{8,9},{9,8},{10,11... | collective-permute-start | bytes 2304008 | tf_op jit(solution)/shard_map/ppermute | solution.py:61
  13.1 10.9 %copy-start.11 = (pred[256]{0:T(512)(128)(4,1)}, pred[256]{0:T(512)(128)(4,1)S(1)}, u32[]{:S(2)}) copy-start(pred[256]{0:T(512)(128)(4,1)S(1)} %iota_compare_fusion.2) | copy-start | bytes 772
  19.5 28.2 %copy-start.3 = (bf16[1,256,1024]{1,2,0:T(8,128)(2,1)S(1)}, bf16[1,256,1024]{1,2,0:T(8,128)(2,1)}, u32[]{:S(2)}) copy-start(bf16[1,256,1024]{1,2,0:T(8,128)(2,1)} %copy.30) | copy-start | bytes 1572868
  19.5 28.2 %copy-start.4 = (bf16[256,1024]{0,1:T(8,128)(2,1)S(1)}, bf16[256,1024]{0,1:T(8,128)(2,1)}, u32[]{:S(2)}) copy-start(bf16[256,1024]{0,1:T(8,128)(2,1)} %copy.33) | copy-start | bytes 1572868
  24.1 29.4 %copy-start.5 = (pred[256,256]{0,1:T(8,128)(4,1)}, pred[256,256]{0,1:T(8,128)(4,1)S(1)}, u32[]{:S(2)}) copy-start(pred[256,256]{0,1:T(8,128)(4,1)S(1)} %fusion.52) | copy-start | bytes 196612
  50.5 25.0 %collective-permute-start.2 = (bf16[2,120,1600]{2,1,0:T(8,128)(2,1)}, bf16[2,120,1600]{2,1,0:T(8,128)(2,1)}, u32[]{:S(2)}, u32[]{:S(2)}) collective-permute-start(bf16[2,120,1600]{2,1,0:T(8,128)(2,1)} %collective-permute-done), channel_id=1, source_target_pairs={{0,4},{1,5},{2,0},{3,1},{4,8},{5,9},{6,2},{7,3},{8,12},{9,13},{10,... | collective-permute-start | bytes 2304008 | tf_op jit(solution)/shard_map/ppermute | solution.py:56
  50.5 68.1 %collective-permute-start.8 = (bf16[2,120,1600]{2,1,0:T(8,128)(2,1)}, bf16[2,120,1600]{2,1,0:T(8,128)(2,1)}, u32[]{:S(2)}, u32[]{:S(2)}) collective-permute-start(bf16[2,120,1600]{2,1,0:T(8,128)(2,1)} %collective-permute-done), channel_id=1, source_target_pairs={{0,1},{1,0},{2,3},{3,2},{4,5},{5,4},{6,7},{7,6},{8,9},{9,8},{10,11... | collective-permute-start | bytes 2304008 | tf_op jit(solution)/shard_map/ppermute | solution.py:61
  50.9 24.9 %collective-permute-start.3 = (bf16[2,120,1600]{2,1,0:T(8,128)(2,1)}, bf16[2,120,1600]{2,1,0:T(8,128)(2,1)}, u32[]{:S(2)}, u32[]{:S(2)}) collective-permute-start(bf16[2,120,1600]{2,1,0:T(8,128)(2,1)} %collective-permute-done.1), channel_id=1, source_target_pairs={{0,2},{1,3},{2,6},{3,7},{4,0},{5,1},{6,10},{7,11},{8,4},{9,5},{10,... | collective-permute-start | bytes 2304008 | tf_op jit(solution)/shard_map/ppermute | solution.py:59
  52.6 68.1 %collective-permute-start.9 = (bf16[2,120,1600]{2,1,0:T(8,128)(2,1)}, bf16[2,120,1600]{2,1,0:T(8,128)(2,1)}, u32[]{:S(2)}, u32[]{:S(2)}) collective-permute-start(bf16[2,120,1600]{2,1,0:T(8,128)(2,1)} %collective-permute-done.1), channel_id=1, source_target_pairs={{0,1},{1,0},{2,3},{3,2},{4,5},{5,4},{6,7},{7,6},{8,9},{9,8},{10,11... | collective-permute-start | bytes 2304008 | tf_op jit(solution)/shard_map/ppermute | solution.py:61
  55.3 8.1 %copy-start.1 = (f32[16,256,256]{1,2,0:T(8,128)S(1)}, f32[16,256,256]{1,2,0:T(8,128)}, u32[]{:S(2)}) copy-start(f32[16,256,256]{1,2,0:T(8,128)} %get-tuple-element.25) | copy-start | bytes 12582916
  55.3 8.1 %copy-start.6 = (pred[256,256]{0,1:T(8,128)(4,1)S(1)}, pred[256,256]{0,1:T(8,128)(4,1)}, u32[]{:S(2)}) copy-start(pred[256,256]{0,1:T(8,128)(4,1)} %copy-done.5) | copy-start | bytes 196612
  55.3 8.1 %copy-start.7 = (bf16[256,1024]{0,1:T(8,128)(2,1)S(1)}, bf16[256,1024]{0,1:T(8,128)(2,1)}, u32[]{:S(2)}) copy-start(bf16[256,1024]{0,1:T(8,128)(2,1)} %copy.34) | copy-start | bytes 1572868
  58.4 0.6 copy-start.9
  66.4 5.3 %copy-start.13 = (bf16[1,256,1600]{1,2,0:T(8,128)(2,1)S(1)}, bf16[1,256,1600]{1,2,0:T(8,128)(2,1)}, u32[]{:S(2)}) copy-start(bf16[1,256,1600]{1,2,0:T(8,128)(2,1)} %param.13) | copy-start | bytes 2457604
  72.8 25.4 %copy-start.2 = (f32[256,1600]{0,1:T(8,128)}, f32[256,1600]{0,1:T(8,128)S(1)}, u32[]{:S(2)}) copy-start(f32[256,1600]{0,1:T(8,128)S(1)} %get-tuple-element.27) | copy-start | bytes 4915204
  75.5 20.3 %collective-permute-start.4 = (bf16[2,120,1600]{2,1,0:T(8,128)(2,1)}, bf16[2,120,1600]{2,1,0:T(8,128)(2,1)S(1)}, u32[]{:S(2)}, u32[]{:S(2)}) collective-permute-start(bf16[2,120,1600]{2,1,0:T(8,128)(2,1)} %collective-permute-done.2), channel_id=1, source_target_pairs={{0,4},{1,5},{2,0},{3,1},{4,8},{5,9},{6,2},{7,3},{8,12},{9,13},{10,... | collective-permute-start | bytes 2304008 | tf_op jit(solution)/shard_map/ppermute | solution.py:56
  75.8 25.5 %collective-permute-start.5 = (bf16[2,120,1600]{2,1,0:T(8,128)(2,1)}, bf16[2,120,1600]{2,1,0:T(8,128)(2,1)S(1)}, u32[]{:S(2)}, u32[]{:S(2)}) collective-permute-start(bf16[2,120,1600]{2,1,0:T(8,128)(2,1)} %collective-permute-done.3), channel_id=1, source_target_pairs={{0,2},{1,3},{2,6},{3,7},{4,0},{5,1},{6,10},{7,11},{8,4},{9,5},{10,... | collective-permute-start | bytes 2304008 | tf_op jit(solution)/shard_map/ppermute | solution.py:59
  95.7 19.2 %collective-permute-start.6 = (bf16[2,120,1600]{2,1,0:T(8,128)(2,1)S(1)}, bf16[2,120,1600]{2,1,0:T(8,128)(2,1)S(1)}, u32[]{:S(2)}, u32[]{:S(2)}) collective-permute-start(bf16[2,120,1600]{2,1,0:T(8,128)(2,1)S(1)} %collective-permute-done.4), channel_id=1, source_target_pairs={{0,4},{1,5},{2,0},{3,1},{4,8},{5,9},{6,2},{7,3},{8,12},{9,13},{10,... | collective-permute-start | bytes 2304008 | tf_op jit(solution)/shard_map/ppermute | solution.py:56
  101.3 26.7 %collective-permute-start.15 = (bf16[256,1600]{0,1:T(8,128)(2,1)S(1)}, bf16[256,1600]{0,1:T(8,128)(2,1)}, u32[]{:S(2)}, u32[]{:S(2)}) collective-permute-start(bf16[256,1600]{0,1:T(8,128)(2,1)S(1)} %divide_convert_fusion), channel_id=1, source_target_pairs={{0,16},{16,0},{1,17},{17,1},{2,18},{18,2},{3,19},{19,3},{4,20},{20... | collective-permute-start | bytes 2457608 | tf_op jit(solution)/shard_map/ppermute | solution.py:201
  115.0 8.3 %collective-permute-start.10 = (bf16[2,120,1600]{2,1,0:T(8,128)(2,1)}, bf16[2,120,1600]{2,1,0:T(8,128)(2,1)S(1)}, u32[]{:S(2)}, u32[]{:S(2)}) collective-permute-start(bf16[2,120,1600]{2,1,0:T(8,128)(2,1)} %collective-permute-done.2), channel_id=1, source_target_pairs={{0,1},{1,0},{2,3},{3,2},{4,5},{5,4},{6,7},{7,6},{8,9},{9,8},{10,11... | collective-permute-start | bytes 2304008 | tf_op jit(solution)/shard_map/ppermute | solution.py:61
  116.0 8.2 %collective-permute-start.11 = (bf16[2,120,1600]{2,1,0:T(8,128)(2,1)}, bf16[2,120,1600]{2,1,0:T(8,128)(2,1)S(1)}, u32[]{:S(2)}, u32[]{:S(2)}) collective-permute-start(bf16[2,120,1600]{2,1,0:T(8,128)(2,1)} %collective-permute-done.3), channel_id=1, source_target_pairs={{0,1},{1,0},{2,3},{3,2},{4,5},{5,4},{6,7},{7,6},{8,9},{9,8},{10,11... | collective-permute-start | bytes 2304008 | tf_op jit(solution)/shard_map/ppermute | solution.py:61
  118.6 6.6 %collective-permute-start.12 = (bf16[2,120,1600]{2,1,0:T(8,128)(2,1)S(1)}, bf16[2,120,1600]{2,1,0:T(8,128)(2,1)S(1)}, u32[]{:S(2)}, u32[]{:S(2)}) collective-permute-start(bf16[2,120,1600]{2,1,0:T(8,128)(2,1)S(1)} %collective-permute-done.4), channel_id=1, source_target_pairs={{0,1},{1,0},{2,3},{3,2},{4,5},{5,4},{6,7},{7,6},{8,9},{9,8},{10,11... | collective-permute-start | bytes 2304008 | tf_op jit(solution)/shard_map/ppermute | solution.py:61
  120.7 5.5 %collective-permute-start.13 = (bf16[2,120,1600]{2,1,0:T(8,128)(2,1)S(1)}, bf16[2,120,1600]{2,1,0:T(8,128)(2,1)S(1)}, u32[]{:S(2)}, u32[]{:S(2)}) collective-permute-start(bf16[2,120,1600]{2,1,0:T(8,128)(2,1)S(1)} %collective-permute-done.5), channel_id=1, source_target_pairs={{0,1},{1,0},{2,3},{3,2},{4,5},{5,4},{6,7},{7,6},{8,9},{9,8},{10,11... | collective-permute-start | bytes 2304008 | tf_op jit(solution)/shard_map/ppermute | solution.py:61
  123.3 3.8 %collective-permute-start.14 = (bf16[2,120,1600]{2,1,0:T(8,128)(2,1)S(1)}, bf16[2,120,1600]{2,1,0:T(8,128)(2,1)S(1)}, u32[]{:S(2)}, u32[]{:S(2)}) collective-permute-start(bf16[2,120,1600]{2,1,0:T(8,128)(2,1)S(1)} %collective-permute-done.6), channel_id=1, source_target_pairs={{0,1},{1,0},{2,3},{3,2},{4,5},{5,4},{6,7},{7,6},{8,9},{9,8},{10,11... | collective-permute-start | bytes 2304008 | tf_op jit(solution)/shard_map/ppermute | solution.py:61
  138.3 21.0 %copy-start.12 = (pred[256]{0:T(512)(128)(4,1)S(1)}, pred[256]{0:T(512)(128)(4,1)}, u32[]{:S(2)}) copy-start(pred[256]{0:T(512)(128)(4,1)} %copy-done.11) | copy-start | bytes 772
  138.3 21.0 %collective-permute-start.16 = (bf16[256,1600]{0,1:T(8,128)(2,1)}, bf16[256,1600]{0,1:T(8,128)(2,1)}, u32[]{:S(2)}, u32[]{:S(2)}) collective-permute-start(bf16[256,1600]{0,1:T(8,128)(2,1)} %fusion.8), channel_id=1, source_target_pairs={{0,16},{16,0},{1,17},{17,1},{2,18},{18,2},{3,19},{19,3},{4,20},{20... | collective-permute-start | bytes 2457608 | tf_op jit(solution)/shard_map/ppermute | solution.py:203

commit v9 on v8

--- a/solution.py
+++ b/solution.py
@@ -44,22 +44,48 @@
     return (new_top, running_total, accumulated)
 
 
-def ring_first(shard, forward, backward, swap, steps_forward, steps_backward):
-    ahead = lax.ppermute(shard, "dev", forward)
-    behind = lax.ppermute(shard, "dev", backward) if steps_backward else shard
-    return ahead, behind
-
-
-def ring_rest(shard, ahead, behind, forward, backward, swap, steps_forward, steps_backward):
-    pieces = [shard, ahead] + ([behind] if steps_backward else [])
-    for step in range(1, steps_forward):
-        ahead = lax.ppermute(ahead, "dev", forward)
-        pieces.append(ahead)
-        if step < steps_backward:
-            behind = lax.ppermute(behind, "dev", backward)
-            pieces.append(behind)
+def ring_issue(state, plan):
+    forward, backward, full_steps, split = plan[0], plan[1], plan[3], plan[4]
+    ahead, behind, pieces, done = state
+    if done < full_steps:
+        return lax.ppermute(ahead, "dev", forward), lax.ppermute(behind, "dev", backward)
+    if done == full_steps and split:
+        cut = ahead.shape[1] // 2
+        return (
+            lax.ppermute(ahead[:, :cut], "dev", forward),
+            lax.ppermute(behind[:, cut:], "dev", backward),
+        )
+    return None
+
+
+def ring_land(state, plan, sent, tie):
+    ahead, behind, pieces, done = state
+    if sent is None:
+        return state, tie
+    first, second = sent
+    tie, first, second = lax.optimization_barrier((tie, first, second))
+    if done < plan[3]:
+        return (first, second, pieces + [first, second], done + 1), tie
+    return (ahead, behind, pieces + [first, second], done + 1), tie
+
+
+def ring_step(state, plan, tie):
+    return ring_land(state, plan, ring_issue(state, plan), tie)
+
+
+def ring_finish(state, plan):
+    swap = plan[2]
+    while state[3] <= plan[3]:
+        state, _ = ring_step(state, plan, jnp.zeros((), jnp.float32))
+    pieces = state[2]
     pieces = pieces + [lax.ppermute(piece, "dev", swap) for piece in pieces]
-    return jnp.concatenate(pieces, axis=1)
+    rows = sum(piece.shape[1] for piece in pieces)
+    full = jnp.zeros((pieces[0].shape[0], rows, pieces[0].shape[2]), pieces[0].dtype)
+    offset = 0
+    for piece in pieces:
+        full = lax.dynamic_update_slice(full, piece, (0, offset, 0))
+        offset += piece.shape[1]
+    return full
 
 
 def plan_ring(mesh):
@@ -103,8 +129,8 @@
     forward = [(2 * k + c, 2 * after[k] + c) for k in range(chip_count) for c in range(2)]
     backward = [(2 * k + c, 2 * before[k] + c) for k in range(chip_count) for c in range(2)]
     swap = [(2 * k + c, 2 * k + 1 - c) for k in range(chip_count) for c in range(2)]
-    steps_forward = chip_count // 2
-    return forward, backward, swap, steps_forward, chip_count - 1 - steps_forward
+    full_steps = (chip_count - 1) // 2
+    return forward, backward, swap, full_steps, chip_count % 2 == 0
 
 
 def per_device(
@@ -149,10 +175,12 @@
     skip_device = jnp.zeros_like(stale_device)
     both = jnp.stack([fc_weight.T, proj_weight])
     if ring_plan is not None:
-        ahead, behind = ring_first(both, *ring_plan)
+        ring = (both, both, [both], 0)
+        ring, local_kv = ring_step(ring, ring_plan, local_kv)
+        sent = ring_issue(ring, ring_plan)
     gathered = lax.all_gather(local_kv, "dev", axis=0, tiled=True)
     if ring_plan is not None:
-        gathered, ahead, behind = lax.optimization_barrier((gathered, ahead, behind))
+        ring, gathered = ring_land(ring, ring_plan, sent, gathered)
     prefix_count = gathered.shape[0]
     row_device = jnp.arange(prefix_count, dtype=jnp.int32) // block_rows
     skipped = jnp.any((row_device[:, None] == device_ids[None, :]) & skip_device[None, :], axis=1)
@@ -178,12 +206,14 @@
     projected = jnp.dot(attended, out_weight, preferred_element_type=jnp.float32)
     residual = suffix_x[0].astype(jnp.float32) + projected
     normed = normalize(residual).astype(jnp.bfloat16)
+    if ring_plan is not None:
+        ring, normed = ring_step(ring, ring_plan, normed)
     group_count = lax.axis_size("group")
     hidden_part = fc_weight.shape[1]
     if ring_plan is None:
         both_half = lax.all_gather(both, "dev", axis=1)
     else:
-        both_half = ring_rest(both, ahead, behind, *ring_plan)
+        both_half = ring_finish(ring, ring_plan)
     fc_rows = both_half[0].reshape(-1, both.shape[2])
     proj_rows = both_half[1].reshape(-1, both.shape[2])
 

time: 163 us -> 187 us (1.15)
  local copies, waits for them, and re-layouts: 35.3 us -> 56.9 us
  starting transfers between devices: 11.8 us -> 13.9 us
    dynamic_update_slice x0 -> x18, local copies, waits for them, and re-layouts: none -> 43.7 us  [ring_finish(): full = lax.dynamic_update_slice(full, piece, (0, offset, 0))]
    unnamed x43 -> x37, local copies, waits for them, and re-layouts: 24.6 us -> 3.36 us
    ppermute x1, waiting for transfers between devices: 0.01 us -> 3.77 us  [per_device(): partner_normed = lax.ppermute(normed, 'group', there)]
    unnamed x1 -> x0, other arithmetic: 2.54 us -> none
    another operation x0 -> x1, other arithmetic: none -> 2.28 us  [per_device(): both = jnp.stack([fc_weight.T, proj_weight])]
    ppermute x15 -> x17, starting transfers between devices: 8.74 us -> 10.9 us  [the longest x3 4.66 us: ring_issue(): lax.ppermute(ahead, 'dev', forward)]
    ppermute x15 -> x17, waiting for transfers between devices: 27 us -> 25.2 us  [the longest x3 16 us: ring_issue(): lax.ppermute(ahead, 'dev', forward)]
  transfers between devices with their start and end apart: 17 -> 19, of which waited for: 3 -> 8; matrix products, arithmetic and copies ran while one was open for 46% -> 52% of each run, Pallas kernels for 0% -> 0%
where the time goes in v9:
time: 187 us; the launch traced here: 186 us
  local copies, waits for them, and re-layouts  56.9 us (30%)
  matrix products  37.2 us (20%)
  waiting for transfers between devices  36.7 us (20%)
  blocking collectives  21.9 us (12%)
  other arithmetic  19.1 us (10%)
  starting transfers between devices  13.9 us (7%)
    dynamic_update_slice x18, local copies, waits for them, and re-layouts, ring_finish(): full = lax.dynamic_update_slice(full, piece, (0, offset, 0))  43.7 us
    all_gather x1, blocking collectives, per_device(): gathered = lax.all_gather(local_kv, 'dev', axis=0, tiled=True)  21.9 us
    dot_general x2, matrix products, feed(): return jnp.dot(activated, proj_rows, preferred_element_type=jnp.float32)  21.2 us
    ppermute x3, waiting for transfers between devices, ring_issue(): lax.ppermute(ahead, 'dev', forward)  16 us
    ppermute x1, waiting for transfers between devices, per_device(): returned.append(lax.ppermute(partner_feed, 'group', back))  7.68 us
    slice x3, local copies, waits for them, and re-layouts, absorb(): key_rows = keyval[:, :width_att].reshape(row_count, head_count, head_size)  6.08 us
    dot_general x2, matrix products, absorb(): jnp.einsum('qhd,khd->hqk', queries, key_rows, preferred_element_type=jnp....  5.86 us
    reduce_sum x2, other arithmetic, absorb(): running_total = running_total * factor + jnp.sum(weights, axis=-1)  5.82 us
  transfers between devices with their start and end apart: 19, of which 8 were waited for; matrix products, arithmetic and copies ran while one was open for 52% of the time, Pallas kernels for 0%

profile of v9, /device:TPU:0, one launch (start us, length us, event | category | flops | bytes accessed | tf_op | source)
XLA Modules:
  0.0 185.9 jit_solution(17783551608477027402)
XLA Ops:
  0.0 2.3 %pad_maximum_fusion = bf16[2,120,1600]{2,1,0:T(8,128)(2,1)} fusion(bf16[1,120,1600]{2,1,0:T(8,128)(2,1)} %bitcast.121, bf16[1,120,1600]{2,1,0:T(8,128)(2,1)} %bitcast.122), kind=kLoop, calls=%fused_computation.62 | loop fusion | flops 384000 | bytes 1536000 | tf_op jit(solution)/shard_map/stack | solution.py:176
  2.3 3.0 %collective-permute-start = (bf16[2,120,1600]{2,1,0:T(8,128)(2,1)}, bf16[2,120,1600]{2,1,0:T(8,128)(2,1)}, u32[]{:S(2)}, u32[]{:S(2)}) collective-permute-start(bf16[2,120,1600]{2,1,0:T(8,128)(2,1)} %pad_maximum_fusion), channel_id=1, source_target_pairs={{0,4},{1,5},{2,0},{3,1},{4,8},{5,9},{6,2},{7,3},{8,12},{9,13},{10,... | collective-permute-start | bytes 2304008 | tf_op jit(solution)/shard_map/ppermute | solution.py:51
  7.2 2.1 %copy.30 = bf16[1,256,1024]{1,2,0:T(8,128)(2,1)} copy(bf16[1,256,1024]{2,1,0:T(8,128)(2,1)} %param.14) | data formatting | bytes 1048576 | tf_op args[1]
  12.2 2.2 %fusion.81 = (bf16[256,1024]{1,0:T(8,128)(2,1)}, bf16[256,1024]{1,0:T(8,128)(2,1)}) fusion(bf16[256,2048]{1,0:T(8,128)(2,1)} %bitcast.118), kind=kLoop, calls=%fused_computation.121 | loop fusion | bytes 2097152 | tf_op jit(solution)/shard_map/slice | solution.py:30
  14.5 2.0 %copy.33 = bf16[256,1024]{0,1:T(8,128)(2,1)} copy(bf16[256,1024]{1,0:T(8,128)(2,1)} %get-tuple-element.29) | data formatting | bytes 1048576 | tf_op jit(solution)/shard_map/slice | solution.py:30
  18.0 4.5 %fusion.9 = bf16[8,2048]{1,0:T(8,128)(2,1)S(1)} fusion(bf16[1600,2048]{1,0:T(8,128)(2,1)} %param.18, bf16[1,8,2048]{2,1,0:T(8,128)(2,1)S(1)} %copy-done.14, pred[]{:T(512)} %compare_reduce_fusion, bf16[1,8,1600]{2,1,0:T(8,128)(2,1)S(1)} %copy-done.12, f32[8]{0:T(128)S(1)} %add_sqrt_fusion.1, f32[8]{0:T(128)S(1)} %broadcast_multiply_fusion.1), kind=kOutput, calls=%fused_computation.17 | convolution fusion | flops 52512768 | bytes 6644801 | tf_op jit(solution)/shard_map/dot_general | solution.py:170
  22.4 1.0 collective-permute-done
  23.4 1.5 collective-permute-done.1
  24.9 1.6 collective-permute-start.2
  26.9 2.8 %fusion.4 = (f32[16,256]{1,0:T(8,128)S(1)}, f32[16,256,256]{1,2,0:T(8,128)}) fusion(pred[256,256]{0,1:T(8,128)(4,1)S(1)} %fusion.52, bf16[256,16,64]{0,2,1:T(8,128)(2,1)S(1)} %bitcast.116, bf16[256,16,64]{0,2,1:T(8,128)(2,1)S(1)} %bitcast.117), kind=kOutput, calls=%fused_computation.8 | convolution fusion | flops 137359360 | bytes 5324800 | tf_op jit(solution)/shard_map/qhd,khd->hqk/dot_general | solution.py:33
  29.7 2.0 %copy.34 = bf16[256,1024]{0,1:T(8,128)(2,1)} copy(bf16[256,1024]{1,0:T(8,128)(2,1)} %get-tuple-element.30) | data formatting | bytes 1048576 | tf_op jit(solution)/shard_map/slice | solution.py:31
  31.7 6.6 %dynamic_update_slice.54 = bf16[2,1920,1600]{2,1,0:T(8,128)(2,1)} pad(bf16[2,120,1600]{2,1,0:T(8,128)(2,1)} %pad_maximum_fusion, bf16[]{:T(256)} %constant.40.clone.1), padding=0_0x0_1800x0_0 | pad | bytes 13056002 | tf_op jit(solution)/shard_map/dynamic_update_slice | solution.py:86
  38.9 21.9 %all_gather.3 = bf16[128,2048]{1,0:T(8,128)(2,1)S(1)} all-gather(bf16[8,2048]{1,0:T(8,128)(2,1)S(1)} %fusion.9), channel_id=1, replica_groups=mesh['group'=2,'dev'=16] {'dev'}, dimensions={0}, use_global_device_ids=true | all-gather | bytes 557056 | tf_op jit(solution)/shard_map/all_gather | solution.py:181
  60.8 2.1 %constant_dynamic-update-slice_fusion.12 = bf16[2,1920,1600]{2,1,0:T(8,128)(2,1)} fusion(bf16[2,1920,1600]{2,1,0:T(8,128)(2,1)} %dynamic_update_slice.54, bf16[2,120,1600]{2,1,0:T(8,128)(2,1)} %collective-permute-done), kind=kLoop, calls=%fused_computation.97 | loop fusion | bytes 1597440 | tf_op jit(solution)/shard_map/dynamic_update_slice | solution.py:86
  62.9 2.1 %constant_dynamic-update-slice_fusion.11 = bf16[2,1920,1600]{2,1,0:T(8,128)(2,1)} fusion(bf16[2,1920,1600]{2,1,0:T(8,128)(2,1)} %constant_dynamic-update-slice_fusion.12, bf16[2,120,1600]{2,1,0:T(8,128)(2,1)} %collective-permute-done.1), kind=kLoop, calls=%fused_computation.96 | loop fusion | bytes 1597440 | tf_op jit(solution)/shard_map/dynamic_update_slice | solution.py:86
  65.8 1.8 copy.29
  67.6 3.1 %bitcast_reduce_fusion = (f32[16,256]{1,0:T(8,128)S(1)}, f32[16,128,256]{2,1,0:T(8,128)}) fusion(bf16[128,16,64]{0,2,1:T(8,128)(2,1)} %bitcast.119, bf16[256,16,64]{0,2,1:T(8,128)(2,1)} %bitcast.115), kind=kOutput, calls=%fused_computation.19 | convolution fusion | flops 68153344 | bytes 2899968 | tf_op jit(solution)/shard_map/qhd,khd->hqk/dot_general | solution.py:33
  71.9 3.8 %fusion.5 = f32[16,256]{1,0:T(8,128)} fusion(f32[16,256,256]{1,2,0:T(8,128)} %get-tuple-element.39, f32[16,256]{1,0:T(8,128)S(1)} %get-tuple-element.35, pred[256,256]{0,1:T(8,128)(4,1)} %copy-done.7), kind=kLoop, calls=%fused_computation.9 | loop fusion | flops 5238784 | bytes 4292608 | tf_op jit(solution)/shard_map/reduce_sum | solution.py:40
  75.7 2.1 %fusion.32 = f32[256,16,64]{0,2,1:T(8,128)} fusion(bf16[256,16,64]{0,2,1:T(8,128)(2,1)S(1)} %bitcast.120, f32[16,256,256]{1,2,0:T(8,128)S(1)} %copy-done.1, f32[16,256]{1,0:T(8,128)S(1)} %get-tuple-element.35, pred[256,256]{0,1:T(8,128)(4,1)S(1)} %copy-done.8), kind=kOutput, calls=%fused_computation.44 | convolution fusion | flops 139460608 | bytes 5849088 | tf_op jit(solution)/shard_map/hqk,khd->qhd/dot_general | solution.py:42
  78.6 2.0 %fusion.30 = f32[16,256]{1,0:T(8,128)S(1)} fusion(f32[16,128,256]{2,1,0:T(8,128)} %get-tuple-element.37, f32[16,256]{1,0:T(8,128)} %get-tuple-element.34), kind=kLoop, calls=%fused_computation.39 | loop fusion | flops 1568768 | bytes 2129920 | tf_op jit(solution)/shard_map/reduce_sum | solution.py:40
  81.4 2.5 %fusion.39 = bf16[256,16,64]{0,2,1:T(8,128)(2,1)S(1)} fusion(f32[256,16,64]{0,2,1:T(8,128)} %fusion.32, bf16[128,16,64]{0,2,1:T(8,128)(2,1)} %bitcast.123, f32[16,128,256]{2,1,0:T(8,128)} %get-tuple-element.37, f32[16,256]{1,0:T(8,128)} %get-tuple-element.34, f32[256,16]{0,1:T(8,128)S(1)} %get-tuple-element.27, f32[256,16]{0,1:T(8,128)S(1)} %get-tuple-element.28, ...), kind=kOutput, calls=%fused_computation.50 | convolution fusion | flops 69992448 | bytes 3997696 | tf_op jit(solution)/shard_map/hqk,khd->qhd/dot_general | solution.py:42
  84.0 1.1 fusion.83
  85.4 2.0 %collective-permute-start.5 = (bf16[2,120,1600]{2,1,0:T(8,128)(2,1)}, bf16[2,120,1600]{2,1,0:T(8,128)(2,1)S(1)}, u32[]{:S(2)}, u32[]{:S(2)}) collective-permute-start(bf16[2,120,1600]{2,1,0:T(8,128)(2,1)} %collective-permute-done.3), channel_id=1, source_target_pairs={{0,2},{1,3},{2,6},{3,7},{4,0},{5,1},{6,10},{7,11},{8,4},{9,5},{10,... | collective-permute-start | bytes 2304008 | tf_op jit(solution)/shard_map/ppermute | solution.py:51
  87.4 1.1 divide_convert_fusion
  88.5 2.1 %constant_dynamic-update-slice_fusion.10 = bf16[2,1920,1600]{2,1,0:T(8,128)(2,1)} fusion(bf16[2,1920,1600]{2,1,0:T(8,128)(2,1)} %constant_dynamic-update-slice_fusion.11, bf16[2,120,1600]{2,1,0:T(8,128)(2,1)} %collective-permute-done.2), kind=kLoop, calls=%fused_computation.95 | loop fusion | bytes 1597440 | tf_op jit(solution)/shard_map/dynamic_update_slice | solution.py:86
  90.6 15.0 %collective-permute-done.4 = bf16[2,120,1600]{2,1,0:T(8,128)(2,1)S(1)} collective-permute-done((bf16[2,120,1600]{2,1,0:T(8,128)(2,1)}, bf16[2,120,1600]{2,1,0:T(8,128)(2,1)S(1)}, u32[]{:S(2)}, u32[]{:S(2)}) %collective-permute-start.4) | collective-permute-done | bytes 768032 | tf_op jit(solution)/shard_map/ppermute | solution.py:51
  106.0 2.3 %constant_dynamic-update-slice_fusion.9 = bf16[2,1920,1600]{2,1,0:T(8,128)(2,1)} fusion(bf16[2,1920,1600]{2,1,0:T(8,128)(2,1)} %constant_dynamic-update-slice_fusion.10, bf16[2,120,1600]{2,1,0:T(8,128)(2,1)} %collective-permute-done.3), kind=kLoop, calls=%fused_computation.94 | loop fusion | bytes 1597440 | tf_op jit(solution)/shard_map/dynamic_update_slice | solution.py:86
  108.4 1.8 collective-permute-start.7
  110.3 1.0 constant_dynamic-update-slice_fusion.8
  111.3 5.8 %collective-permute-done.6 = bf16[2,60,1600]{2,1,0:T(8,128)(2,1)S(1)} collective-permute-done((bf16[2,60,1600]{2,1,0:T(8,128)(2,1)S(1)}, bf16[2,60,1600]{2,1,0:T(8,128)(2,1)S(1)}, u32[]{:S(2)}, u32[]{:S(2)}) %collective-permute-start.6) | collective-permute-done | bytes 384032 | tf_op jit(solution)/shard_map/ppermute | solution.py:55
  117.1 1.1 constant_dynamic-update-slice_fusion.7
  118.2 1.8 collective-permute-done.7
  120.0 3.5 %dynamic_update_slice.61 = bf16[2,1920,1600]{2,1,0:T(8,128)(2,1)} dynamic-update-slice(bf16[2,1920,1600]{2,1,0:T(8,128)(2,1)} %constant_dynamic-update-slice_fusion.7, bf16[2,60,1600]{2,1,0:T(8,128)(2,1)} %copy-done.10, s32[]{:T(128)} %constant.32.clone.1, s32[]{:T(128)} %constant.10.clone.1, s32[]{:T(128)} %constant.32.clone.1) | dynamic-update-slice | bytes 768004 | tf_op jit(solution)/shard_map/dynamic_update_slice | solution.py:86
  123.5 3.5 %dynamic_update_slice.62 = bf16[2,1920,1600]{2,1,0:T(8,128)(2,1)} dynamic-update-slice(bf16[2,1920,1600]{2,1,0:T(8,128)(2,1)} %dynamic_update_slice.61, bf16[2,60,1600]{2,1,0:T(8,128)(2,1)} %collective-permute-done.7, s32[]{:T(128)} %constant.32.clone.1, s32[]{:T(128)} %constant.11.clone.1, s32[]{:T(128)} %constant.32.clone.1) | dynamic-update-slice | bytes 768004 | tf_op jit(solution)/shard_map/dynamic_update_slice | solution.py:86
  127.6 2.1 %constant_dynamic-update-slice_fusion.6 = bf16[2,1920,1600]{2,1,0:T(8,128)(2,1)} fusion(bf16[2,1920,1600]{2,1,0:T(8,128)(2,1)} %dynamic_update_slice.62, bf16[2,120,1600]{2,1,0:T(8,128)(2,1)} %collective-permute-done.8), kind=kLoop, calls=%fused_computation.91 | loop fusion | bytes 1597440 | tf_op jit(solution)/shard_map/dynamic_update_slice | solution.py:86
  129.8 2.1 %constant_dynamic-update-slice_fusion.5 = bf16[2,1920,1600]{2,1,0:T(8,128)(2,1)} fusion(bf16[2,1920,1600]{2,1,0:T(8,128)(2,1)} %constant_dynamic-update-slice_fusion.6, bf16[2,120,1600]{2,1,0:T(8,128)(2,1)} %collective-permute-done.9), kind=kLoop, calls=%fused_computation.90 | loop fusion | bytes 1597440 | tf_op jit(solution)/shard_map/dynamic_update_slice | solution.py:86
  131.9 1.5 collective-permute-start.17
  133.4 2.1 %constant_dynamic-update-slice_fusion.4 = bf16[2,1920,1600]{2,1,0:T(8,128)(2,1)} fusion(bf16[2,1920,1600]{2,1,0:T(8,128)(2,1)} %constant_dynamic-update-slice_fusion.5, bf16[2,120,1600]{2,1,0:T(8,128)(2,1)} %collective-permute-done.10), kind=kLoop, calls=%fused_computation.89 | loop fusion | bytes 1597440 | tf_op jit(solution)/shard_map/dynamic_update_slice | solution.py:86
  135.7 2.1 %constant_dynamic-update-slice_fusion.3 = bf16[2,1920,1600]{2,1,0:T(8,128)(2,1)} fusion(bf16[2,1920,1600]{2,1,0:T(8,128)(2,1)} %constant_dynamic-update-slice_fusion.4, bf16[2,120,1600]{2,1,0:T(8,128)(2,1)} %collective-permute-done.11), kind=kLoop, calls=%fused_computation.88 | loop fusion | bytes 1597440 | tf_op jit(solution)/shard_map/dynamic_update_slice | solution.py:86
  138.1 2.1 %constant_dynamic-update-slice_fusion.2 = bf16[2,1920,1600]{2,1,0:T(8,128)(2,1)} fusion(bf16[2,1920,1600]{2,1,0:T(8,128)(2,1)} %constant_dynamic-update-slice_fusion.3, bf16[2,120,1600]{2,1,0:T(8,128)(2,1)} %collective-permute-done.12), kind=kLoop, calls=%fused_computation.87 | loop fusion | bytes 1597440 | tf_op jit(solution)/shard_map/dynamic_update_slice | solution.py:86
  142.1 3.5 %dynamic_update_slice.70 = bf16[2,1920,1600]{2,1,0:T(8,128)(2,1)} dynamic-update-slice(bf16[2,1920,1600]{2,1,0:T(8,128)(2,1)} %constant_dynamic-update-slice_fusion, bf16[2,60,1600]{2,1,0:T(8,128)(2,1)} %collective-permute-done.15, s32[]{:T(128)} %constant.32.clone.1, s32[]{:T(128)} %constant.19.clone.1, s32[]{:T(128)} %constant.32.clone.1) | dynamic-update-slice | bytes 768004 | tf_op jit(solution)/shard_map/dynamic_update_slice | solution.py:86
  145.6 3.4 %dynamic_update_slice.71 = bf16[2,1920,1600]{2,1,0:T(8,128)(2,1)} dynamic-update-slice(bf16[2,1920,1600]{2,1,0:T(8,128)(2,1)} %dynamic_update_slice.70, bf16[2,60,1600]{2,1,0:T(8,128)(2,1)} %collective-permute-done.16, s32[]{:T(128)} %constant.32.clone.1, s32[]{:T(128)} %constant.20.clone.1, s32[]{:T(128)} %constant.32.clone.1) | dynamic-update-slice | bytes 768004 | tf_op jit(solution)/shard_map/dynamic_update_slice | solution.py:86
  149.0 3.8 %collective-permute-done.17 = bf16[256,1600]{0,1:T(8,128)(2,1)} collective-permute-done((bf16[256,1600]{0,1:T(8,128)(2,1)}, bf16[256,1600]{0,1:T(8,128)(2,1)}, u32[]{:S(2)}, u32[]{:S(2)}) %collective-permute-start.17) | collective-permute-done | bytes 819232 | tf_op jit(solution)/shard_map/ppermute | solution.py:231
  152.8 10.2 %fusion.8 = bf16[256,1600]{0,1:T(8,128)(2,1)} fusion(bf16[2,1920,1600]{2,1,0:T(8,128)(2,1)} %dynamic_update_slice.71, bf16[256,1600]{0,1:T(8,128)(2,1)} %collective-permute-done.17), kind=kOutput, calls=%fused_computation.15 | convolution fusion | flops 3150561280 | bytes 13926400 | tf_op jit(solution)/shard_map/dot_general | solution.py:225
  163.0 1.5 collective-permute-start.18
  164.5 10.9 %fusion.7 = f32[256,1600]{0,1:T(8,128)} fusion(f32[256,1600]{0,1:T(8,128)} %copy-done.2, bf16[2,1920,1600]{2,1,0:T(8,128)(2,1)} %dynamic_update_slice.71, bf16[256,1600]{0,1:T(8,128)(2,1)} %divide_convert_fusion), kind=kOutput, calls=%fused_computation.14 | convolution fusion | flops 3150561280 | bytes 16384000 | tf_op jit(solution)/shard_map/dot_general | solution.py:225
  175.5 7.7 %collective-permute-done.18 = bf16[256,1600]{0,1:T(8,128)(2,1)} collective-permute-done((bf16[256,1600]{0,1:T(8,128)(2,1)}, bf16[256,1600]{0,1:T(8,128)(2,1)}, u32[]{:S(2)}, u32[]{:S(2)}) %collective-permute-start.18) | collective-permute-done | bytes 819232 | tf_op jit(solution)/shard_map/ppermute | solution.py:233
  183.1 2.7 %fusion.51 = bf16[1,256,1600]{1,2,0:T(8,128)(2,1)} fusion(f32[256,1600]{0,1:T(8,128)} %fusion.7, bf16[256,1600]{0,1:T(8,128)(2,1)} %collective-permute-done.18, pred[256]{0:T(512)(128)(4,1)S(1)} %copy-done.16), kind=kLoop, calls=%fused_computation.61 | loop fusion | flops 1638400 | bytes 3277056 | tf_op jit(solution)/shard_map/broadcast_in_dim | solution.py:238
  (82 shorter events, 14.6 us)
Async XLA Ops:
  0.0 84.0 %copy-start = (bf16[1024,1600]{0,1:T(8,128)(2,1)S(1)}, bf16[1024,1600]{0,1:T(8,128)(2,1)}, u32[]{:S(2)}) copy-start(bf16[1024,1600]{0,1:T(8,128)(2,1)} %param.19) | copy-start | bytes 9830404
  0.0 17.9 %copy-start.12 = (bf16[1,8,1600]{2,1,0:T(8,128)(2,1)S(1)}, bf16[1,8,1600]{2,1,0:T(8,128)(2,1)}, u32[]{:S(2)}) copy-start(bf16[1,8,1600]{2,1,0:T(8,128)(2,1)} %param.17) | copy-start | bytes 76804
  0.0 17.9 %copy-start.14 = (bf16[1,8,2048]{2,1,0:T(8,128)(2,1)S(1)}, bf16[1,8,2048]{2,1,0:T(8,128)(2,1)}, u32[]{:S(2)}) copy-start(bf16[1,8,2048]{2,1,0:T(8,128)(2,1)} %param.16) | copy-start | bytes 98308
  2.3 21.1 %collective-permute-start = (bf16[2,120,1600]{2,1,0:T(8,128)(2,1)}, bf16[2,120,1600]{2,1,0:T(8,128)(2,1)}, u32[]{:S(2)}, u32[]{:S(2)}) collective-permute-start(bf16[2,120,1600]{2,1,0:T(8,128)(2,1)} %pad_maximum_fusion), channel_id=1, source_target_pairs={{0,4},{1,5},{2,0},{3,1},{4,8},{5,9},{6,2},{7,3},{8,12},{9,13},{10,... | collective-permute-start | bytes 2304008 | tf_op jit(solution)/shard_map/ppermute | solution.py:51
  5.3 19.6 %collective-permute-start.1 = (bf16[2,120,1600]{2,1,0:T(8,128)(2,1)}, bf16[2,120,1600]{2,1,0:T(8,128)(2,1)}, u32[]{:S(2)}, u32[]{:S(2)}) collective-permute-start(bf16[2,120,1600]{2,1,0:T(8,128)(2,1)} %pad_maximum_fusion), channel_id=1, source_target_pairs={{0,2},{1,3},{2,6},{3,7},{4,0},{5,1},{6,10},{7,11},{8,4},{9,5},{10,... | collective-permute-start | bytes 2304008 | tf_op jit(solution)/shard_map/ppermute | solution.py:51
  5.3 121.7 %collective-permute-start.8 = (bf16[2,120,1600]{2,1,0:T(8,128)(2,1)}, bf16[2,120,1600]{2,1,0:T(8,128)(2,1)}, u32[]{:S(2)}, u32[]{:S(2)}) collective-permute-start(bf16[2,120,1600]{2,1,0:T(8,128)(2,1)} %pad_maximum_fusion), channel_id=1, source_target_pairs={{0,1},{1,0},{2,3},{3,2},{4,5},{5,4},{6,7},{7,6},{8,9},{9,8},{10,11... | collective-permute-start | bytes 2304008 | tf_op jit(solution)/shard_map/ppermute | solution.py:81
  16.5 10.4 %copy-start.3 = (bf16[1,256,1024]{1,2,0:T(8,128)(2,1)S(1)}, bf16[1,256,1024]{1,2,0:T(8,128)(2,1)}, u32[]{:S(2)}) copy-start(bf16[1,256,1024]{1,2,0:T(8,128)(2,1)} %copy.30) | copy-start | bytes 1572868
  16.5 10.4 %copy-start.4 = (bf16[256,1024]{0,1:T(8,128)(2,1)S(1)}, bf16[256,1024]{0,1:T(8,128)(2,1)}, u32[]{:S(2)}) copy-start(bf16[256,1024]{0,1:T(8,128)(2,1)} %copy.33) | copy-start | bytes 1572868
  17.2 0.6 copy-start.15
  17.9 11.8 %copy-start.7 = (pred[256,256]{0,1:T(8,128)(4,1)}, pred[256,256]{0,1:T(8,128)(4,1)S(1)}, u32[]{:S(2)}) copy-start(pred[256,256]{0,1:T(8,128)(4,1)S(1)} %fusion.52) | copy-start | bytes 196612
  24.9 40.1 %collective-permute-start.2 = (bf16[2,120,1600]{2,1,0:T(8,128)(2,1)}, bf16[2,120,1600]{2,1,0:T(8,128)(2,1)}, u32[]{:S(2)}, u32[]{:S(2)}) collective-permute-start(bf16[2,120,1600]{2,1,0:T(8,128)(2,1)} %collective-permute-done), channel_id=1, source_target_pairs={{0,4},{1,5},{2,0},{3,1},{4,8},{5,9},{6,2},{7,3},{8,12},{9,13},{10,... | collective-permute-start | bytes 2304008 | tf_op jit(solution)/shard_map/ppermute | solution.py:51
  26.5 38.5 %collective-permute-start.3 = (bf16[2,120,1600]{2,1,0:T(8,128)(2,1)}, bf16[2,120,1600]{2,1,0:T(8,128)(2,1)}, u32[]{:S(2)}, u32[]{:S(2)}) collective-permute-start(bf16[2,120,1600]{2,1,0:T(8,128)(2,1)} %collective-permute-done.1), channel_id=1, source_target_pairs={{0,2},{1,3},{2,6},{3,7},{4,0},{5,1},{6,10},{7,11},{8,4},{9,5},{10,... | collective-permute-start | bytes 2304008 | tf_op jit(solution)/shard_map/ppermute | solution.py:51
  38.4 91.3 %collective-permute-start.9 = (bf16[2,120,1600]{2,1,0:T(8,128)(2,1)}, bf16[2,120,1600]{2,1,0:T(8,128)(2,1)}, u32[]{:S(2)}, u32[]{:S(2)}) collective-permute-start(bf16[2,120,1600]{2,1,0:T(8,128)(2,1)} %collective-permute-done), channel_id=1, source_target_pairs={{0,1},{1,0},{2,3},{3,2},{4,5},{5,4},{6,7},{7,6},{8,9},{9,8},{10,11... | collective-permute-start | bytes 2304008 | tf_op jit(solution)/shard_map/ppermute | solution.py:81
  38.4 93.5 %collective-permute-start.10 = (bf16[2,120,1600]{2,1,0:T(8,128)(2,1)}, bf16[2,120,1600]{2,1,0:T(8,128)(2,1)}, u32[]{:S(2)}, u32[]{:S(2)}) collective-permute-start(bf16[2,120,1600]{2,1,0:T(8,128)(2,1)} %collective-permute-done.1), channel_id=1, source_target_pairs={{0,1},{1,0},{2,3},{3,2},{4,5},{5,4},{6,7},{7,6},{8,9},{9,8},{10,11... | collective-permute-start | bytes 2304008 | tf_op jit(solution)/shard_map/ppermute | solution.py:81
  67.6 8.1 %copy-start.1 = (f32[16,256,256]{1,2,0:T(8,128)S(1)}, f32[16,256,256]{1,2,0:T(8,128)}, u32[]{:S(2)}) copy-start(f32[16,256,256]{1,2,0:T(8,128)} %get-tuple-element.39) | copy-start | bytes 12582916
  67.6 8.1 %copy-start.8 = (pred[256,256]{0,1:T(8,128)(4,1)S(1)}, pred[256,256]{0,1:T(8,128)(4,1)}, u32[]{:S(2)}) copy-start(pred[256,256]{0,1:T(8,128)(4,1)} %copy-done.7) | copy-start | bytes 196612
  67.6 8.1 %copy-start.9 = (bf16[256,1024]{0,1:T(8,128)(2,1)S(1)}, bf16[256,1024]{0,1:T(8,128)(2,1)}, u32[]{:S(2)}) copy-start(bf16[256,1024]{0,1:T(8,128)(2,1)} %copy.34) | copy-start | bytes 1572868
  70.7 0.6 copy-start.13
  78.6 5.3 %copy-start.17 = (bf16[1,256,1600]{1,2,0:T(8,128)(2,1)S(1)}, bf16[1,256,1600]{1,2,0:T(8,128)(2,1)}, u32[]{:S(2)}) copy-start(bf16[1,256,1600]{1,2,0:T(8,128)(2,1)} %param.13) | copy-start | bytes 2457604
  85.0 23.4 %copy-start.2 = (f32[256,1600]{0,1:T(8,128)}, f32[256,1600]{0,1:T(8,128)S(1)}, u32[]{:S(2)}) copy-start(f32[256,1600]{0,1:T(8,128)S(1)} %get-tuple-element.41) | copy-start | bytes 4915204
  85.3 20.3 %collective-permute-start.4 = (bf16[2,120,1600]{2,1,0:T(8,128)(2,1)}, bf16[2,120,1600]{2,1,0:T(8,128)(2,1)S(1)}, u32[]{:S(2)}, u32[]{:S(2)}) collective-permute-start(bf16[2,120,1600]{2,1,0:T(8,128)(2,1)} %collective-permute-done.2), channel_id=1, source_target_pairs={{0,4},{1,5},{2,0},{3,1},{4,8},{5,9},{6,2},{7,3},{8,12},{9,13},{10,... | collective-permute-start | bytes 2304008 | tf_op jit(solution)/shard_map/ppermute | solution.py:51
  85.4 20.3 %collective-permute-start.5 = (bf16[2,120,1600]{2,1,0:T(8,128)(2,1)}, bf16[2,120,1600]{2,1,0:T(8,128)(2,1)S(1)}, u32[]{:S(2)}, u32[]{:S(2)}) collective-permute-start(bf16[2,120,1600]{2,1,0:T(8,128)(2,1)} %collective-permute-done.3), channel_id=1, source_target_pairs={{0,2},{1,3},{2,6},{3,7},{4,0},{5,1},{6,10},{7,11},{8,4},{9,5},{10,... | collective-permute-start | bytes 2304008 | tf_op jit(solution)/shard_map/ppermute | solution.py:51
  105.6 12.6 %copy-start.6 = (bf16[2,120,1600]{2,1,0:T(8,128)(2,1)}, bf16[2,120,1600]{2,1,0:T(8,128)(2,1)S(1)}, u32[]{:S(2)}) copy-start(bf16[2,120,1600]{2,1,0:T(8,128)(2,1)S(1)} %collective-permute-done.4) | copy-start | bytes 2304004
  105.7 11.4 %copy-start.5 = (bf16[2,120,1600]{2,1,0:T(8,128)(2,1)}, bf16[2,120,1600]{2,1,0:T(8,128)(2,1)S(1)}, u32[]{:S(2)}) copy-start(bf16[2,120,1600]{2,1,0:T(8,128)(2,1)S(1)} %collective-permute-done.5) | copy-start | bytes 2304004
  105.7 11.3 %collective-permute-start.6 = (bf16[2,60,1600]{2,1,0:T(8,128)(2,1)S(1)}, bf16[2,60,1600]{2,1,0:T(8,128)(2,1)S(1)}, u32[]{:S(2)}, u32[]{:S(2)}) collective-permute-start(bf16[2,60,1600]{2,1,0:T(8,128)(2,1)S(1)} %slice.28), channel_id=1, source_target_pairs={{0,4},{1,5},{2,0},{3,1},{4,8},{5,9},{6,2},{7,3},{8,12},{9,13},{10,... | collective-permute-start | bytes 1152008 | tf_op jit(solution)/shard_map/ppermute | solution.py:55
  108.4 11.6 %collective-permute-start.7 = (bf16[2,60,1600]{2,1,0:T(8,128)(2,1)S(1)}, bf16[2,60,1600]{2,1,0:T(8,128)(2,1)}, u32[]{:S(2)}, u32[]{:S(2)}) collective-permute-start(bf16[2,60,1600]{2,1,0:T(8,128)(2,1)S(1)} %slice.29), channel_id=1, source_target_pairs={{0,2},{1,3},{2,6},{3,7},{4,0},{5,1},{6,10},{7,11},{8,4},{9,5},{10,... | collective-permute-start | bytes 1152008 | tf_op jit(solution)/shard_map/ppermute | solution.py:56
  117.1 3.0 %copy-start.10 = (bf16[2,60,1600]{2,1,0:T(8,128)(2,1)}, bf16[2,60,1600]{2,1,0:T(8,128)(2,1)S(1)}, u32[]{:S(2)}) copy-start(bf16[2,60,1600]{2,1,0:T(8,128)(2,1)S(1)} %collective-permute-done.6) | copy-start | bytes 1152004
  117.1 18.4 %collective-permute-start.11 = (bf16[2,120,1600]{2,1,0:T(8,128)(2,1)}, bf16[2,120,1600]{2,1,0:T(8,128)(2,1)}, u32[]{:S(2)}, u32[]{:S(2)}) collective-permute-start(bf16[2,120,1600]{2,1,0:T(8,128)(2,1)} %collective-permute-done.2), channel_id=1, source_target_pairs={{0,1},{1,0},{2,3},{3,2},{4,5},{5,4},{6,7},{7,6},{8,9},{9,8},{10,11... | collective-permute-start | bytes 2304008 | tf_op jit(solution)/shard_map/ppermute | solution.py:81
  120.0 17.7 %collective-permute-start.12 = (bf16[2,120,1600]{2,1,0:T(8,128)(2,1)}, bf16[2,120,1600]{2,1,0:T(8,128)(2,1)}, u32[]{:S(2)}, u32[]{:S(2)}) collective-permute-start(bf16[2,120,1600]{2,1,0:T(8,128)(2,1)} %collective-permute-done.3), channel_id=1, source_target_pairs={{0,1},{1,0},{2,3},{3,2},{4,5},{5,4},{6,7},{7,6},{8,9},{9,8},{10,11... | collective-permute-start | bytes 2304008 | tf_op jit(solution)/shard_map/ppermute | solution.py:81
  127.0 8.5 %copy-start.11 = (bf16[2,60,1600]{2,1,0:T(8,128)(2,1)S(1)}, bf16[2,60,1600]{2,1,0:T(8,128)(2,1)}, u32[]{:S(2)}) copy-start(bf16[2,60,1600]{2,1,0:T(8,128)(2,1)} %copy-done.10) | copy-start | bytes 1152004
  127.0 13.2 %collective-permute-start.13 = (bf16[2,120,1600]{2,1,0:T(8,128)(2,1)}, bf16[2,120,1600]{2,1,0:T(8,128)(2,1)S(1)}, u32[]{:S(2)}, u32[]{:S(2)}) collective-permute-start(bf16[2,120,1600]{2,1,0:T(8,128)(2,1)} %copy-done.6), channel_id=1, source_target_pairs={{0,1},{1,0},{2,3},{3,2},{4,5},{5,4},{6,7},{7,6},{8,9},{9,8},{10,11... | collective-permute-start | bytes 2304008 | tf_op jit(solution)/shard_map/ppermute | solution.py:81
  129.7 11.4 %collective-permute-start.14 = (bf16[2,120,1600]{2,1,0:T(8,128)(2,1)}, bf16[2,120,1600]{2,1,0:T(8,128)(2,1)S(1)}, u32[]{:S(2)}, u32[]{:S(2)}) collective-permute-start(bf16[2,120,1600]{2,1,0:T(8,128)(2,1)} %copy-done.5), channel_id=1, source_target_pairs={{0,1},{1,0},{2,3},{3,2},{4,5},{5,4},{6,7},{7,6},{8,9},{9,8},{10,11... | collective-permute-start | bytes 2304008 | tf_op jit(solution)/shard_map/ppermute | solution.py:81
  131.9 20.9 %collective-permute-start.17 = (bf16[256,1600]{0,1:T(8,128)(2,1)}, bf16[256,1600]{0,1:T(8,128)(2,1)}, u32[]{:S(2)}, u32[]{:S(2)}) collective-permute-start(bf16[256,1600]{0,1:T(8,128)(2,1)} %divide_convert_fusion), channel_id=1, source_target_pairs={{0,16},{16,0},{1,17},{17,1},{2,18},{18,2},{3,19},{19,3},{4,20},{20... | collective-permute-start | bytes 2457608 | tf_op jit(solution)/shard_map/ppermute | solution.py:231
  135.5 6.6 %collective-permute-start.15 = (bf16[2,60,1600]{2,1,0:T(8,128)(2,1)S(1)}, bf16[2,60,1600]{2,1,0:T(8,128)(2,1)}, u32[]{:S(2)}, u32[]{:S(2)}) collective-permute-start(bf16[2,60,1600]{2,1,0:T(8,128)(2,1)S(1)} %copy-done.11), channel_id=1, source_target_pairs={{0,1},{1,0},{2,3},{3,2},{4,5},{5,4},{6,7},{7,6},{8,9},{9,8},{10,11... | collective-permute-start | bytes 1152008 | tf_op jit(solution)/shard_map/ppermute | solution.py:81
  137.8 7.8 %collective-permute-start.16 = (bf16[2,60,1600]{2,1,0:T(8,128)(2,1)}, bf16[2,60,1600]{2,1,0:T(8,128)(2,1)}, u32[]{:S(2)}, u32[]{:S(2)}) collective-permute-start(bf16[2,60,1600]{2,1,0:T(8,128)(2,1)} %collective-permute-done.7), channel_id=1, source_target_pairs={{0,1},{1,0},{2,3},{3,2},{4,5},{5,4},{6,7},{7,6},{8,9},{9,8},{10,11... | collective-permute-start | bytes 1152008 | tf_op jit(solution)/shard_map/ppermute | solution.py:81
  163.0 20.1 %copy-start.16 = (pred[256]{0:T(512)(128)(4,1)S(1)}, pred[256]{0:T(512)(128)(4,1)}, u32[]{:S(2)}) copy-start(pred[256]{0:T(512)(128)(4,1)} %copy-done.15) | copy-start | bytes 772
  163.0 20.1 %collective-permute-start.18 = (bf16[256,1600]{0,1:T(8,128)(2,1)}, bf16[256,1600]{0,1:T(8,128)(2,1)}, u32[]{:S(2)}, u32[]{:S(2)}) collective-permute-start(bf16[256,1600]{0,1:T(8,128)(2,1)} %fusion.8), channel_id=1, source_target_pairs={{0,16},{16,0},{1,17},{17,1},{2,18},{18,2},{3,19},{19,3},{4,20},{20... | collective-permute-start | bytes 2457608 | tf_op jit(solution)/shard_map/ppermute | solution.py:233

commit v10 on v7

--- a/solution.py
+++ b/solution.py
@@ -172,19 +172,27 @@
     group_count = lax.axis_size("group")
     hidden_part = fc_weight.shape[1]
     both = jnp.stack([fc_weight.T, proj_weight])
-    if ring_plan is None:
-        both_half = lax.all_gather(both, "dev", axis=1)
+    keep = hidden_part * 3 // 4
+    if ring_plan is None or keep == 0:
+        banks = [lax.all_gather(both, "dev", axis=1)]
     else:
-        both_half = ring_gather(both, *ring_plan)
-    fc_rows = both_half[0].reshape(-1, both.shape[2])
-    proj_rows = both_half[1].reshape(-1, both.shape[2])
+        banks = [
+            ring_gather(both[:, keep:], *ring_plan),
+            lax.all_gather(both[:, :keep], "dev", axis=1),
+        ]
 
     def feed(rows_in):
-        inner = lax.dot_general(
-            rows_in, fc_rows, (((1,), (1,)), ((), ())), preferred_element_type=jnp.float32
-        )
-        activated = jax.nn.gelu(inner, approximate=True).astype(jnp.bfloat16)
-        return jnp.dot(activated, proj_rows, preferred_element_type=jnp.float32)
+        total = None
+        for bank in banks:
+            fc_rows = bank[0].reshape(-1, both.shape[2])
+            proj_rows = bank[1].reshape(-1, both.shape[2])
+            inner = lax.dot_general(
+                rows_in, fc_rows, (((1,), (1,)), ((), ())), preferred_element_type=jnp.float32
+            )
+            activated = jax.nn.gelu(inner, approximate=True).astype(jnp.bfloat16)
+            part = jnp.dot(activated, proj_rows, preferred_element_type=jnp.float32)
+            total = part if total is None else total + part
+        return total
 
     returned = []
     for shift in range(1, group_count):

time: 159 us -> 205 us (1.29)
  local copies, waits for them, and re-layouts: 22 us -> 61.7 us
  waiting for transfers between devices: 58.8 us -> 27.3 us
  matrix products: 32.4 us -> 47.3 us
  between operations: 0.39 us -> 13.7 us
  starting transfers between devices: 11.4 us -> 16.4 us
    concatenate x1, local copies, waits for them, and re-layouts: 0.1 us -> 26.3 us  [ring_gather(): return jnp.concatenate(pieces, axis=1)]
    ppermute x4, waiting for transfers between devices: 43.8 us -> 18 us  [ring_gather(): ahead = lax.ppermute(ahead, 'dev', forward)]
    slice x0 -> x2, local copies, waits for them, and re-layouts: none -> 21.6 us  [the longest x1 20.3 us: feed(): fc_rows = bank[0].reshape(-1, both.shape[2])]
    dot_general x2 -> x4, matrix products: 21.4 us -> 37.5 us  [feed(): part = jnp.dot(activated, proj_rows, preferred_element_type=jnp.float32)]
    unnamed x49 -> x51, local copies, waits for them, and re-layouts: 12.2 us -> 4 us
    ppermute x4, starting transfers between devices: 3.89 us -> 11.4 us  [ring_gather(): ahead = lax.ppermute(ahead, 'dev', forward)]
    ppermute x1, waiting for transfers between devices: 7.94 us -> 0.9 us  [per_device(): returned.append(lax.ppermute(partner_feed, 'group', back))]
    ppermute x3, waiting for transfers between devices: 3.48 us -> 8.38 us  [ring_gather(): behind = lax.ppermute(behind, 'dev', backward)]
  transfers between devices with their start and end apart: 17 -> 18, of which waited for: 9 -> 6; matrix products, arithmetic and copies ran while one was open for 28% -> 47% of each run, Pallas kernels for 0% -> 0%
where the time goes in v10:
time: 205 us; the launch traced here: 203 us
  local copies, waits for them, and re-layouts  61.7 us (30%)
  matrix products  47.3 us (23%)
  waiting for transfers between devices  27.3 us (13%)
  blocking collectives  25.4 us (12%)
  starting transfers between devices  16.4 us (8%)
  between operations  13.7 us (7%)
  other arithmetic  11.2 us (5%)
    dot_general x4, matrix products, feed(): part = jnp.dot(activated, proj_rows, preferred_element_type=jnp.float32)  37.5 us
    concatenate x1, local copies, waits for them, and re-layouts, ring_gather(): return jnp.concatenate(pieces, axis=1)  26.3 us
    all_gather x1, blocking collectives, per_device(): gathered = lax.all_gather(local_kv, 'dev', axis=0, tiled=True)  25.4 us
    slice x1, local copies, waits for them, and re-layouts, feed(): fc_rows = bank[0].reshape(-1, both.shape[2])  20.3 us
    ppermute x4, waiting for transfers between devices, ring_gather(): ahead = lax.ppermute(ahead, 'dev', forward)  18 us
    ppermute x4, starting transfers between devices, ring_gather(): ahead = lax.ppermute(ahead, 'dev', forward)  11.4 us
    ppermute x3, waiting for transfers between devices, ring_gather(): behind = lax.ppermute(behind, 'dev', backward)  8.38 us
    slice x3, local copies, waits for them, and re-layouts, absorb(): key_rows = keyval[:, :width_att].reshape(row_count, head_count, head_size)  6.1 us
  transfers between devices with their start and end apart: 18, of which 6 were waited for; matrix products, arithmetic and copies ran while one was open for 47% of the time, Pallas kernels for 0%

profile of v10, /device:TPU:0, one launch (start us, length us, event | category | flops | bytes accessed | tf_op | source)
XLA Modules:
  0.0 203.0 jit_solution(8560090368053501264)
XLA Ops:
  6.5 1.3 pad_maximum_fusion
  7.8 1.3 copy.53
  9.1 1.7 pad_maximum_fusion.1
  10.8 3.0 %collective-permute-start = (bf16[2,30,1600]{2,1,0:T(8,128)(2,1)}, bf16[2,30,1600]{2,1,0:T(8,128)(2,1)}, u32[]{:S(2)}, u32[]{:S(2)}) collective-permute-start(bf16[2,30,1600]{2,1,0:T(8,128)(2,1)} %pad_maximum_fusion.1), channel_id=1, source_target_pairs={{0,4},{1,5},{2,0},{3,1},{4,8},{5,9},{6,2},{7,3},{8,12},{9,13},{10,... | collective-permute-start | bytes 576008 | tf_op jit(solution)/shard_map/ppermute | solution.py:52
  13.8 2.3 %fusion.108 = (bf16[256,1024]{1,0:T(8,128)(2,1)}, bf16[256,1024]{1,0:T(8,128)(2,1)}) fusion(bf16[256,2048]{1,0:T(8,128)(2,1)} %bitcast.140), kind=kLoop, calls=%fused_computation.142 | loop fusion | bytes 2097152 | tf_op jit(solution)/shard_map/slice | solution.py:30
  16.1 2.1 %copy.51 = bf16[256,1024]{0,1:T(8,128)(2,1)} copy(bf16[256,1024]{1,0:T(8,128)(2,1)} %get-tuple-element.10) | data formatting | bytes 1048576 | tf_op jit(solution)/shard_map/slice | solution.py:31
  18.2 2.1 %copy.47 = bf16[1,256,1024]{1,2,0:T(8,128)(2,1)} copy(bf16[1,256,1024]{2,1,0:T(8,128)(2,1)} %param.14) | data formatting | bytes 1048576 | tf_op args[1]
  20.3 2.1 %copy.50 = bf16[256,1024]{0,1:T(8,128)(2,1)} copy(bf16[256,1024]{1,0:T(8,128)(2,1)} %get-tuple-element.9) | data formatting | bytes 1048576 | tf_op jit(solution)/shard_map/slice | solution.py:30
  22.4 0.2 fusion.83
  22.5 0.6 compare_reduce_fusion
  23.3 0.2 fusion.74
  23.5 4.5 %fusion.5 = bf16[8,2048]{1,0:T(8,128)(2,1)S(1)} fusion(bf16[1600,2048]{1,0:T(8,128)(2,1)} %param.18, bf16[1,8,2048]{2,1,0:T(8,128)(2,1)S(1)} %copy-done.19, pred[]{:T(512)} %compare_reduce_fusion, bf16[1,8,1600]{2,1,0:T(8,128)(2,1)S(1)} %copy-done.8, f32[8]{0:T(128)S(1)} %add_sqrt_fusion.1, f32[8]{0:T(128)S(1)} %broadcast_multiply_fusion.1), kind=kOutput, calls=%fused_computation.13 | convolution fusion | flops 52512768 | bytes 6644801 | tf_op jit(solution)/shard_map/dot_general | solution.py:140
  28.1 25.4 %all_gather.9 = bf16[128,2048]{1,0:T(8,128)(2,1)S(1)} all-gather(bf16[8,2048]{1,0:T(8,128)(2,1)S(1)} %fusion.5), channel_id=1, replica_groups=mesh['group'=2,'dev'=16] {'dev'}, dimensions={0}, use_global_device_ids=true | all-gather | bytes 557056 | tf_op jit(solution)/shard_map/all_gather | solution.py:146
  53.5 0.7 fusion.109
  54.2 1.8 copy.46
  56.0 0.8 copy.48
  56.9 0.7 fusion.84
  57.7 0.7 iota_compare_fusion.2
  58.5 1.6 bitcast_reduce_fusion
  60.1 0.8 fusion
  61.0 0.4 fusion.14
  61.4 1.0 fusion.1
  62.4 1.1 fusion.34
  63.6 0.6 fusion.41
  64.2 0.5 copy-done.20
  64.7 1.1 fusion.110
  65.8 1.6 collective-permute-start.3
  67.4 9.5 %collective-permute-done.2 = bf16[2,30,1600]{2,1,0:T(8,128)(2,1)S(1)} collective-permute-done((bf16[2,30,1600]{2,1,0:T(8,128)(2,1)}, bf16[2,30,1600]{2,1,0:T(8,128)(2,1)S(1)}, u32[]{:S(2)}, u32[]{:S(2)}) %collective-permute-start.2) | collective-permute-done | bytes 192032 | tf_op jit(solution)/shard_map/ppermute | solution.py:52
  77.0 0.3 multiply_reduce_fusion
  77.3 0.5 collective-permute-start.9
  77.8 5.2 %collective-permute-done.3 = bf16[2,30,1600]{2,1,0:T(8,128)(2,1)S(1)} collective-permute-done((bf16[2,30,1600]{2,1,0:T(8,128)(2,1)}, bf16[2,30,1600]{2,1,0:T(8,128)(2,1)S(1)}, u32[]{:S(2)}, u32[]{:S(2)}) %collective-permute-start.3) | collective-permute-done | bytes 192032 | tf_op jit(solution)/shard_map/ppermute | solution.py:55
  83.0 4.5 %collective-permute-done.4 = bf16[2,30,1600]{2,1,0:T(8,128)(2,1)S(1)} collective-permute-done((bf16[2,30,1600]{2,1,0:T(8,128)(2,1)S(1)}, bf16[2,30,1600]{2,1,0:T(8,128)(2,1)S(1)}, u32[]{:S(2)}, u32[]{:S(2)}) %collective-permute-start.4) | collective-permute-done | bytes 192032 | tf_op jit(solution)/shard_map/ppermute | solution.py:52
  87.4 8.2 %collective-permute-start.6 = (bf16[2,30,1600]{2,1,0:T(8,128)(2,1)S(1)}, bf16[2,30,1600]{2,1,0:T(8,128)(2,1)S(1)}, u32[]{:S(2)}, u32[]{:S(2)}) collective-permute-start(bf16[2,30,1600]{2,1,0:T(8,128)(2,1)S(1)} %collective-permute-done.4), channel_id=1, source_target_pairs={{0,4},{1,5},{2,0},{3,1},{4,8},{5,9},{6,2},{7,3},{8,12},{9,13},{10,... | collective-permute-start | bytes 576008 | tf_op jit(solution)/shard_map/ppermute | solution.py:52
  95.8 0.5 collective-permute-start.11
  96.3 3.2 %collective-permute-done.5 = bf16[2,30,1600]{2,1,0:T(8,128)(2,1)S(1)} collective-permute-done((bf16[2,30,1600]{2,1,0:T(8,128)(2,1)S(1)}, bf16[2,30,1600]{2,1,0:T(8,128)(2,1)S(1)}, u32[]{:S(2)}, u32[]{:S(2)}) %collective-permute-start.5) | collective-permute-done | bytes 192032 | tf_op jit(solution)/shard_map/ppermute | solution.py:55
  99.6 4.0 %collective-permute-done.6 = bf16[2,30,1600]{2,1,0:T(8,128)(2,1)S(1)} collective-permute-done((bf16[2,30,1600]{2,1,0:T(8,128)(2,1)S(1)}, bf16[2,30,1600]{2,1,0:T(8,128)(2,1)S(1)}, u32[]{:S(2)}, u32[]{:S(2)}) %collective-permute-start.6) | collective-permute-done | bytes 192032 | tf_op jit(solution)/shard_map/ppermute | solution.py:52
  103.6 1.1 divide_convert_fusion
  104.7 2.1 %collective-permute-start.15 = (bf16[256,1600]{0,1:T(8,128)(2,1)}, bf16[256,1600]{0,1:T(8,128)(2,1)}, u32[]{:S(2)}, u32[]{:S(2)}) collective-permute-start(bf16[256,1600]{0,1:T(8,128)(2,1)} %divide_convert_fusion), channel_id=1, source_target_pairs={{0,16},{16,0},{1,17},{17,1},{2,18},{18,2},{3,19},{19,3},{4,20},{20... | collective-permute-start | bytes 2457608 | tf_op jit(solution)/shard_map/ppermute | solution.py:201
  106.9 0.6 copy-done.16
  107.6 0.7 copy-done.18
  108.3 26.3 %concatenate.3 = bf16[2,480,1600]{2,1,0:T(8,128)(2,1)S(1)} concatenate(bf16[2,30,1600]{2,1,0:T(8,128)(2,1)} %pad_maximum_fusion.1, bf16[2,30,1600]{2,1,0:T(8,128)(2,1)} %collective-permute-done, bf16[2,30,1600]{2,1,0:T(8,128)(2,1)} %collective-permute-done.1, bf16[2,30,1600]{2,1,0:T(8,128)(2,1)S(1)} %collective-permute-done.2, bf16[2,30,1600]{2,1,0:T(8,128)(2,1)} %copy-done.9, ...), dimensions={1} | concatenate | bytes 6144000 | tf_op jit(solution)/shard_map/concatenate | solution.py:58
  134.6 20.3 %fusion.107 = (bf16[1,1440,1600]{2,0,1:T(2,128)(2,1)}, bf16[1,1440,1600]{2,0,1:T(2,128)(2,1)}) fusion(bf16[2,1440,1600]{2,0,1:T(2,128)(2,1)} %all-gather.3.cloned.1.call-done), kind=kLoop, calls=%fused_computation.141 | loop fusion | bytes 18432000 | tf_op jit(solution)/shard_map/slice | solution.py:187
  154.9 13.3 %fusion.12 = f32[256,1600]{0,1:T(8,128)} fusion(bf16[1,1440,1600]{2,0,1:T(2,128)(2,1)} %get-tuple-element.8, bf16[256,1600]{0,1:T(8,128)(2,1)} %collective-permute-done.15, bf16[1,1440,1600]{2,0,1:T(2,128)(2,1)} %get-tuple-element.7), kind=kOutput, calls=%fused_computation.23 | convolution fusion | flops 2362613760 | bytes 11673600 | tf_op jit(solution)/shard_map/dot_general | solution.py:193
  168.2 4.6 %fusion.4 = bf16[256,1600]{0,1:T(8,128)(2,1)} fusion(f32[256,1600]{0,1:T(8,128)} %fusion.12, bf16[2,480,1600]{2,1,0:T(8,128)(2,1)S(1)} %concatenate.3, bf16[256,1600]{0,1:T(8,128)(2,1)} %collective-permute-done.15), kind=kOutput, calls=%fused_computation.11 | convolution fusion | flops 788357120 | bytes 6348800 | tf_op jit(solution)/shard_map/dot_general | solution.py:193
  172.8 13.3 %fusion.13 = f32[256,1600]{0,1:T(8,128)} fusion(bf16[1,1440,1600]{2,0,1:T(2,128)(2,1)} %get-tuple-element.8, bf16[256,1600]{0,1:T(8,128)(2,1)} %divide_convert_fusion, bf16[1,1440,1600]{2,0,1:T(2,128)(2,1)} %get-tuple-element.7), kind=kOutput, calls=%fused_computation.24 | convolution fusion | flops 2362613760 | bytes 11673600 | tf_op jit(solution)/shard_map/dot_general | solution.py:193
  186.1 6.5 %fusion.3 = f32[256,1600]{0,1:T(8,128)} fusion(f32[256,1600]{0,1:T(8,128)} %copy-done.2, f32[256,1600]{0,1:T(8,128)} %fusion.13, bf16[2,480,1600]{2,1,0:T(8,128)(2,1)} %copy-done.3, bf16[256,1600]{0,1:T(8,128)(2,1)} %divide_convert_fusion), kind=kOutput, calls=%fused_computation.9 | convolution fusion | flops 788357120 | bytes 8806400 | tf_op jit(solution)/shard_map/dot_general | solution.py:193
  192.6 0.9 collective-permute-done.16
  193.5 2.7 %fusion.45 = bf16[1,256,1600]{1,2,0:T(8,128)(2,1)} fusion(f32[256,1600]{0,1:T(8,128)} %fusion.3, bf16[256,1600]{0,1:T(8,128)(2,1)} %collective-permute-done.16, pred[256]{0:T(512)(128)(4,1)S(1)} %iota_compare_fusion.2), kind=kLoop, calls=%fused_computation.59 | loop fusion | flops 1638400 | bytes 3277056 | tf_op jit(solution)/shard_map/broadcast_in_dim | solution.py:208
  (81 shorter events, 1.1 us)
Async XLA Ops:
  6.5 57.7 %copy-start = (bf16[1024,1600]{0,1:T(8,128)(2,1)S(1)}, bf16[1024,1600]{0,1:T(8,128)(2,1)}, u32[]{:S(2)}) copy-start(bf16[1024,1600]{0,1:T(8,128)(2,1)} %param.19) | copy-start | bytes 9830404
  6.5 128.1 %all-gather.3.cloned.1.call-start = ((), (), s32[]{:S(2)}) async-start(), calls=%async_computation | async-start | bytes 10183680 | tf_op jit(solution)/shard_map/all_gather | solution.py:181
  10.8 53.4 %collective-permute-start = (bf16[2,30,1600]{2,1,0:T(8,128)(2,1)}, bf16[2,30,1600]{2,1,0:T(8,128)(2,1)}, u32[]{:S(2)}, u32[]{:S(2)}) collective-permute-start(bf16[2,30,1600]{2,1,0:T(8,128)(2,1)} %pad_maximum_fusion.1), channel_id=1, source_target_pairs={{0,4},{1,5},{2,0},{3,1},{4,8},{5,9},{6,2},{7,3},{8,12},{9,13},{10,... | collective-permute-start | bytes 576008 | tf_op jit(solution)/shard_map/ppermute | solution.py:52
  13.8 51.9 %collective-permute-start.1 = (bf16[2,30,1600]{2,1,0:T(8,128)(2,1)}, bf16[2,30,1600]{2,1,0:T(8,128)(2,1)}, u32[]{:S(2)}, u32[]{:S(2)}) collective-permute-start(bf16[2,30,1600]{2,1,0:T(8,128)(2,1)} %pad_maximum_fusion.1), channel_id=1, source_target_pairs={{0,2},{1,3},{2,6},{3,7},{4,0},{5,1},{6,10},{7,11},{8,4},{9,5},{10,... | collective-permute-start | bytes 576008 | tf_op jit(solution)/shard_map/ppermute | solution.py:55
  13.8 81.8 %collective-permute-start.7 = (bf16[2,30,1600]{2,1,0:T(8,128)(2,1)}, bf16[2,30,1600]{2,1,0:T(8,128)(2,1)}, u32[]{:S(2)}, u32[]{:S(2)}) collective-permute-start(bf16[2,30,1600]{2,1,0:T(8,128)(2,1)} %pad_maximum_fusion.1), channel_id=1, source_target_pairs={{0,1},{1,0},{2,3},{3,2},{4,5},{5,4},{6,7},{7,6},{8,9},{9,8},{10,11... | collective-permute-start | bytes 576008 | tf_op jit(solution)/shard_map/ppermute | solution.py:57
  16.1 6.3 %copy-start.21 = (s32[1,16]{1,0:T(1,128)S(1)}, s32[1,16]{1,0:T(1,128)}, u32[]{:S(2)}) copy-start(s32[1,16]{1,0:T(1,128)} %param.24) | copy-start | bytes 196
  16.1 6.3 %copy-start.22 = (s32[1,2]{1,0:T(1,128)S(1)}, s32[1,2]{1,0:T(1,128)}, u32[]{:S(2)}) copy-start(s32[1,2]{1,0:T(1,128)} %param.25) | copy-start | bytes 28
  16.1 7.1 %copy-start.8 = (bf16[1,8,1600]{2,1,0:T(8,128)(2,1)S(1)}, bf16[1,8,1600]{2,1,0:T(8,128)(2,1)}, u32[]{:S(2)}) copy-start(bf16[1,8,1600]{2,1,0:T(8,128)(2,1)} %param.17) | copy-start | bytes 76804
  16.1 7.4 %copy-start.19 = (bf16[1,8,2048]{2,1,0:T(8,128)(2,1)S(1)}, bf16[1,8,2048]{2,1,0:T(8,128)(2,1)}, u32[]{:S(2)}) copy-start(bf16[1,8,2048]{2,1,0:T(8,128)(2,1)} %param.16) | copy-start | bytes 98308
  28.1 28.8 %copy-start.23 = (s32[1,16]{1,0:T(1,128)S(1)}, s32[1,16]{1,0:T(1,128)}, u32[]{:S(2)}) copy-start(s32[1,16]{1,0:T(1,128)} %param.22) | copy-start | bytes 196
  28.1 28.8 %copy-start.24 = (s32[1,16]{1,0:T(1,128)S(1)}, s32[1,16]{1,0:T(1,128)}, u32[]{:S(2)}) copy-start(s32[1,16]{1,0:T(1,128)} %param.23) | copy-start | bytes 196
  56.8 3.2 %copy-start.4 = (bf16[1,256,1024]{1,2,0:T(8,128)(2,1)S(1)}, bf16[1,256,1024]{1,2,0:T(8,128)(2,1)}, u32[]{:S(2)}) copy-start(bf16[1,256,1024]{1,2,0:T(8,128)(2,1)} %copy.47) | copy-start | bytes 1572868
  56.8 3.3 %copy-start.5 = (bf16[256,1024]{0,1:T(8,128)(2,1)S(1)}, bf16[256,1024]{0,1:T(8,128)(2,1)}, u32[]{:S(2)}) copy-start(bf16[256,1024]{0,1:T(8,128)(2,1)} %copy.50) | copy-start | bytes 1572868
  61.3 1.0 copy-start.6
  62.4 1.1 copy-start.7
  63.5 1.1 copy-start.20
  64.2 12.7 %collective-permute-start.2 = (bf16[2,30,1600]{2,1,0:T(8,128)(2,1)}, bf16[2,30,1600]{2,1,0:T(8,128)(2,1)S(1)}, u32[]{:S(2)}, u32[]{:S(2)}) collective-permute-start(bf16[2,30,1600]{2,1,0:T(8,128)(2,1)} %collective-permute-done), channel_id=1, source_target_pairs={{0,4},{1,5},{2,0},{3,1},{4,8},{5,9},{6,2},{7,3},{8,12},{9,13},{10,... | collective-permute-start | bytes 576008 | tf_op jit(solution)/shard_map/ppermute | solution.py:52
  65.8 37.8 %copy-start.2 = (f32[256,1600]{0,1:T(8,128)}, f32[256,1600]{0,1:T(8,128)S(1)}, u32[]{:S(2)}) copy-start(f32[256,1600]{0,1:T(8,128)S(1)} %get-tuple-element.21) | copy-start | bytes 4915204
  65.8 17.2 %collective-permute-start.3 = (bf16[2,30,1600]{2,1,0:T(8,128)(2,1)}, bf16[2,30,1600]{2,1,0:T(8,128)(2,1)S(1)}, u32[]{:S(2)}, u32[]{:S(2)}) collective-permute-start(bf16[2,30,1600]{2,1,0:T(8,128)(2,1)} %collective-permute-done.1), channel_id=1, source_target_pairs={{0,2},{1,3},{2,6},{3,7},{4,0},{5,1},{6,10},{7,11},{8,4},{9,5},{10,... | collective-permute-start | bytes 576008 | tf_op jit(solution)/shard_map/ppermute | solution.py:55
  76.9 10.5 %collective-permute-start.4 = (bf16[2,30,1600]{2,1,0:T(8,128)(2,1)S(1)}, bf16[2,30,1600]{2,1,0:T(8,128)(2,1)S(1)}, u32[]{:S(2)}, u32[]{:S(2)}) collective-permute-start(bf16[2,30,1600]{2,1,0:T(8,128)(2,1)S(1)} %collective-permute-done.2), channel_id=1, source_target_pairs={{0,4},{1,5},{2,0},{3,1},{4,8},{5,9},{6,2},{7,3},{8,12},{9,13},{10,... | collective-permute-start | bytes 576008 | tf_op jit(solution)/shard_map/ppermute | solution.py:52
  77.2 18.5 %collective-permute-start.8 = (bf16[2,30,1600]{2,1,0:T(8,128)(2,1)}, bf16[2,30,1600]{2,1,0:T(8,128)(2,1)S(1)}, u32[]{:S(2)}, u32[]{:S(2)}) collective-permute-start(bf16[2,30,1600]{2,1,0:T(8,128)(2,1)} %collective-permute-done), channel_id=1, source_target_pairs={{0,1},{1,0},{2,3},{3,2},{4,5},{5,4},{6,7},{7,6},{8,9},{9,8},{10,11... | collective-permute-start | bytes 576008 | tf_op jit(solution)/shard_map/ppermute | solution.py:57
  77.3 19.0 %collective-permute-start.9 = (bf16[2,30,1600]{2,1,0:T(8,128)(2,1)}, bf16[2,30,1600]{2,1,0:T(8,128)(2,1)S(1)}, u32[]{:S(2)}, u32[]{:S(2)}) collective-permute-start(bf16[2,30,1600]{2,1,0:T(8,128)(2,1)} %collective-permute-done.1), channel_id=1, source_target_pairs={{0,1},{1,0},{2,3},{3,2},{4,5},{5,4},{6,7},{7,6},{8,9},{9,8},{10,11... | collective-permute-start | bytes 576008 | tf_op jit(solution)/shard_map/ppermute | solution.py:57
  83.0 23.9 %copy-start.9 = (bf16[2,30,1600]{2,1,0:T(8,128)(2,1)}, bf16[2,30,1600]{2,1,0:T(8,128)(2,1)S(1)}, u32[]{:S(2)}) copy-start(bf16[2,30,1600]{2,1,0:T(8,128)(2,1)S(1)} %collective-permute-done.3) | copy-start | bytes 576004
  83.0 16.6 %collective-permute-start.5 = (bf16[2,30,1600]{2,1,0:T(8,128)(2,1)S(1)}, bf16[2,30,1600]{2,1,0:T(8,128)(2,1)S(1)}, u32[]{:S(2)}, u32[]{:S(2)}) collective-permute-start(bf16[2,30,1600]{2,1,0:T(8,128)(2,1)S(1)} %collective-permute-done.3), channel_id=1, source_target_pairs={{0,2},{1,3},{2,6},{3,7},{4,0},{5,1},{6,10},{7,11},{8,4},{9,5},{10,... | collective-permute-start | bytes 576008 | tf_op jit(solution)/shard_map/ppermute | solution.py:55
  87.4 19.4 %copy-start.10 = (bf16[2,30,1600]{2,1,0:T(8,128)(2,1)}, bf16[2,30,1600]{2,1,0:T(8,128)(2,1)S(1)}, u32[]{:S(2)}) copy-start(bf16[2,30,1600]{2,1,0:T(8,128)(2,1)S(1)} %collective-permute-done.4) | copy-start | bytes 576004
  87.4 16.2 %collective-permute-start.6 = (bf16[2,30,1600]{2,1,0:T(8,128)(2,1)S(1)}, bf16[2,30,1600]{2,1,0:T(8,128)(2,1)S(1)}, u32[]{:S(2)}, u32[]{:S(2)}) collective-permute-start(bf16[2,30,1600]{2,1,0:T(8,128)(2,1)S(1)} %collective-permute-done.4), channel_id=1, source_target_pairs={{0,4},{1,5},{2,0},{3,1},{4,8},{5,9},{6,2},{7,3},{8,12},{9,13},{10,... | collective-permute-start | bytes 576008 | tf_op jit(solution)/shard_map/ppermute | solution.py:52
  95.7 9.0 %collective-permute-start.10 = (bf16[2,30,1600]{2,1,0:T(8,128)(2,1)S(1)}, bf16[2,30,1600]{2,1,0:T(8,128)(2,1)S(1)}, u32[]{:S(2)}, u32[]{:S(2)}) collective-permute-start(bf16[2,30,1600]{2,1,0:T(8,128)(2,1)S(1)} %collective-permute-done.2), channel_id=1, source_target_pairs={{0,1},{1,0},{2,3},{3,2},{4,5},{5,4},{6,7},{7,6},{8,9},{9,8},{10,11... | collective-permute-start | bytes 576008 | tf_op jit(solution)/shard_map/ppermute | solution.py:57
  95.8 11.1 %copy-start.11 = (bf16[2,30,1600]{2,1,0:T(8,128)(2,1)}, bf16[2,30,1600]{2,1,0:T(8,128)(2,1)S(1)}, u32[]{:S(2)}) copy-start(bf16[2,30,1600]{2,1,0:T(8,128)(2,1)S(1)} %collective-permute-done.8) | copy-start | bytes 576004
  95.8 11.0 %collective-permute-start.11 = (bf16[2,30,1600]{2,1,0:T(8,128)(2,1)S(1)}, bf16[2,30,1600]{2,1,0:T(8,128)(2,1)S(1)}, u32[]{:S(2)}, u32[]{:S(2)}) collective-permute-start(bf16[2,30,1600]{2,1,0:T(8,128)(2,1)S(1)} %collective-permute-done.3), channel_id=1, source_target_pairs={{0,1},{1,0},{2,3},{3,2},{4,5},{5,4},{6,7},{7,6},{8,9},{9,8},{10,11... | collective-permute-start | bytes 576008 | tf_op jit(solution)/shard_map/ppermute | solution.py:57
  96.3 10.6 %copy-start.12 = (bf16[2,30,1600]{2,1,0:T(8,128)(2,1)}, bf16[2,30,1600]{2,1,0:T(8,128)(2,1)S(1)}, u32[]{:S(2)}) copy-start(bf16[2,30,1600]{2,1,0:T(8,128)(2,1)S(1)} %collective-permute-done.9) | copy-start | bytes 576004
  96.3 10.5 %collective-permute-start.12 = (bf16[2,30,1600]{2,1,0:T(8,128)(2,1)S(1)}, bf16[2,30,1600]{2,1,0:T(8,128)(2,1)S(1)}, u32[]{:S(2)}, u32[]{:S(2)}) collective-permute-start(bf16[2,30,1600]{2,1,0:T(8,128)(2,1)S(1)} %collective-permute-done.4), channel_id=1, source_target_pairs={{0,1},{1,0},{2,3},{3,2},{4,5},{5,4},{6,7},{7,6},{8,9},{9,8},{10,11... | collective-permute-start | bytes 576008 | tf_op jit(solution)/shard_map/ppermute | solution.py:57
  99.6 7.3 %copy-start.13 = (bf16[2,30,1600]{2,1,0:T(8,128)(2,1)}, bf16[2,30,1600]{2,1,0:T(8,128)(2,1)S(1)}, u32[]{:S(2)}) copy-start(bf16[2,30,1600]{2,1,0:T(8,128)(2,1)S(1)} %collective-permute-done.5) | copy-start | bytes 576004
  99.6 7.2 %collective-permute-start.13 = (bf16[2,30,1600]{2,1,0:T(8,128)(2,1)S(1)}, bf16[2,30,1600]{2,1,0:T(8,128)(2,1)S(1)}, u32[]{:S(2)}, u32[]{:S(2)}) collective-permute-start(bf16[2,30,1600]{2,1,0:T(8,128)(2,1)S(1)} %collective-permute-done.5), channel_id=1, source_target_pairs={{0,1},{1,0},{2,3},{3,2},{4,5},{5,4},{6,7},{7,6},{8,9},{9,8},{10,11... | collective-permute-start | bytes 576008 | tf_op jit(solution)/shard_map/ppermute | solution.py:57
  103.6 3.3 %copy-start.14 = (bf16[2,30,1600]{2,1,0:T(8,128)(2,1)}, bf16[2,30,1600]{2,1,0:T(8,128)(2,1)S(1)}, u32[]{:S(2)}) copy-start(bf16[2,30,1600]{2,1,0:T(8,128)(2,1)S(1)} %collective-permute-done.6) | copy-start | bytes 576004
  103.6 4.7 %collective-permute-start.14 = (bf16[2,30,1600]{2,1,0:T(8,128)(2,1)S(1)}, bf16[2,30,1600]{2,1,0:T(8,128)(2,1)}, u32[]{:S(2)}, u32[]{:S(2)}) collective-permute-start(bf16[2,30,1600]{2,1,0:T(8,128)(2,1)S(1)} %collective-permute-done.6), channel_id=1, source_target_pairs={{0,1},{1,0},{2,3},{3,2},{4,5},{5,4},{6,7},{7,6},{8,9},{9,8},{10,11... | collective-permute-start | bytes 576008 | tf_op jit(solution)/shard_map/ppermute | solution.py:57
  104.7 2.2 %copy-start.15 = (bf16[2,30,1600]{2,1,0:T(8,128)(2,1)}, bf16[2,30,1600]{2,1,0:T(8,128)(2,1)S(1)}, u32[]{:S(2)}) copy-start(bf16[2,30,1600]{2,1,0:T(8,128)(2,1)S(1)} %collective-permute-done.10) | copy-start | bytes 576004
  104.7 50.3 %collective-permute-start.15 = (bf16[256,1600]{0,1:T(8,128)(2,1)}, bf16[256,1600]{0,1:T(8,128)(2,1)}, u32[]{:S(2)}, u32[]{:S(2)}) collective-permute-start(bf16[256,1600]{0,1:T(8,128)(2,1)} %divide_convert_fusion), channel_id=1, source_target_pairs={{0,16},{16,0},{1,17},{17,1},{2,18},{18,2},{3,19},{19,3},{4,20},{20... | collective-permute-start | bytes 2457608 | tf_op jit(solution)/shard_map/ppermute | solution.py:201
  106.8 0.7 copy-start.16
  106.8 0.8 copy-start.17
  107.6 0.7 copy-start.18
  134.6 33.6 %copy-start.3 = (bf16[2,480,1600]{2,1,0:T(8,128)(2,1)}, bf16[2,480,1600]{2,1,0:T(8,128)(2,1)S(1)}, u32[]{:S(2)}) copy-start(bf16[2,480,1600]{2,1,0:T(8,128)(2,1)S(1)} %concatenate.3) | copy-start | bytes 9216004
  172.8 20.7 %collective-permute-start.16 = (bf16[256,1600]{0,1:T(8,128)(2,1)}, bf16[256,1600]{0,1:T(8,128)(2,1)}, u32[]{:S(2)}, u32[]{:S(2)}) collective-permute-start(bf16[256,1600]{0,1:T(8,128)(2,1)} %fusion.4), channel_id=1, source_target_pairs={{0,16},{16,0},{1,17},{17,1},{2,18},{18,2},{3,19},{19,3},{4,20},{20... | collective-permute-start | bytes 2457608 | tf_op jit(solution)/shard_map/ppermute | solution.py:203
  186.1 10.1 %copy-start.1 = (bf16[1024,1600]{0,1:T(8,128)(2,1)S(1)}, bf16[1024,1600]{0,1:T(8,128)(2,1)}, u32[]{:S(2)}) copy-start(bf16[1024,1600]{0,1:T(8,128)(2,1)} %param.19) | copy-start | bytes 9830404
Sparse Core Ops, SparseCore 0:
  9.6 93.6 all-gather.2

commit v11 on v10

--- a/solution.py
+++ b/solution.py
@@ -55,7 +55,7 @@
             behind = lax.ppermute(behind, "dev", backward)
             pieces.append(behind)
     pieces = pieces + [lax.ppermute(piece, "dev", swap) for piece in pieces]
-    return jnp.concatenate(pieces, axis=1)
+    return jnp.stack(pieces, axis=1)
 
 
 def plan_ring(mesh):
@@ -172,7 +172,7 @@
     group_count = lax.axis_size("group")
     hidden_part = fc_weight.shape[1]
     both = jnp.stack([fc_weight.T, proj_weight])
-    keep = hidden_part * 3 // 4
+    keep = hidden_part * 4 // 5 // 16 * 16
     if ring_plan is None or keep == 0:
         banks = [lax.all_gather(both, "dev", axis=1)]
     else:
@@ -184,13 +184,22 @@
     def feed(rows_in):
         total = None
         for bank in banks:
-            fc_rows = bank[0].reshape(-1, both.shape[2])
-            proj_rows = bank[1].reshape(-1, both.shape[2])
-            inner = lax.dot_general(
-                rows_in, fc_rows, (((1,), (1,)), ((), ())), preferred_element_type=jnp.float32
-            )
-            activated = jax.nn.gelu(inner, approximate=True).astype(jnp.bfloat16)
-            part = jnp.dot(activated, proj_rows, preferred_element_type=jnp.float32)
+            if bank.ndim == 4 and bank is banks[0] and len(banks) > 1:
+                inner = jnp.einsum(
+                    "td,shd->tsh", rows_in, bank[0], preferred_element_type=jnp.float32
+                )
+                activated = jax.nn.gelu(inner, approximate=True).astype(jnp.bfloat16)
+                part = jnp.einsum(
+                    "tsh,shd->td", activated, bank[1], preferred_element_type=jnp.float32
+                )
+            else:
+                fc_rows = bank[0].reshape(-1, both.shape[2])
+                proj_rows = bank[1].reshape(-1, both.shape[2])
+                inner = lax.dot_general(
+                    rows_in, fc_rows, (((1,), (1,)), ((), ())), preferred_element_type=jnp.float32
+                )
+                activated = jax.nn.gelu(inner, approximate=True).astype(jnp.bfloat16)
+                part = jnp.dot(activated, proj_rows, preferred_element_type=jnp.float32)
             total = part if total is None else total + part
         return total
 

time: 205 us -> 166 us (0.81)
  local copies, waits for them, and re-layouts: 61.7 us -> 25.4 us
  matrix products: 47.3 us -> 38.3 us
  waiting for transfers between devices: 27.3 us -> 33.8 us
    concatenate x1 -> x0, local copies, waits for them, and re-layouts: 26.3 us -> none  [ring_gather(): return jnp.concatenate(pieces, axis=1)]
    slice x2 -> x0, local copies, waits for them, and re-layouts: 21.6 us -> none  [the longest x1 20.3 us: feed(): fc_rows = bank[0].reshape(-1, both.shape[2])]
    dot_general x4 -> x2, matrix products: 37.5 us -> 18.8 us  [feed(): part = jnp.dot(activated, proj_rows, preferred_element_type=jnp.float32)]
    unnamed x51 -> x41, local copies, waits for them, and re-layouts: 4 us -> 14.9 us
    dot_general x0 -> x2, matrix products: none -> 9.76 us  [feed(): jnp.einsum('tsh,shd->td', activated, bank[1], preferred_element_type=jnp....]
    ppermute x1, waiting for transfers between devices: 0.9 us -> 10 us  [per_device(): returned.append(lax.ppermute(partner_feed, 'group', back))]
    ppermute x4, starting transfers between devices: 11.4 us -> 3.48 us  [ring_gather(): ahead = lax.ppermute(ahead, 'dev', forward)]
    ppermute x3, starting transfers between devices: 1.61 us -> 9.53 us  [ring_gather(): behind = lax.ppermute(behind, 'dev', backward)]
  transfers between devices with their start and end apart: 18 -> 18, of which waited for: 6 -> 6; matrix products, arithmetic and copies ran while one was open for 47% -> 37% of each run, Pallas kernels for 0% -> 0%
where the time goes in v11:
time: 166 us; the launch traced here: 165 us
  matrix products  38.3 us (23%)
  waiting for transfers between devices  33.8 us (20%)
  local copies, waits for them, and re-layouts  25.4 us (15%)
  blocking collectives  25.3 us (15%)
  starting transfers between devices  16.7 us (10%)
  between operations  13.6 us (8%)
  other arithmetic  12 us (7%)
    all_gather x1, blocking collectives, per_device(): gathered = lax.all_gather(local_kv, 'dev', axis=0, tiled=True)  25.3 us
    dot_general x2, matrix products, feed(): part = jnp.dot(activated, proj_rows, preferred_element_type=jnp.float32)  18.8 us
    ppermute x4, waiting for transfers between devices, ring_gather(): ahead = lax.ppermute(ahead, 'dev', forward)  16 us
    unnamed x41, local copies, waits for them, and re-layouts  14.9 us
    ppermute x1, waiting for transfers between devices, per_device(): returned.append(lax.ppermute(partner_feed, 'group', back))  10 us
    dot_general x2, matrix products, feed(): jnp.einsum('tsh,shd->td', activated, bank[1], preferred_element_type=jnp....  9.76 us
    ppermute x3, starting transfers between devices, ring_gather(): behind = lax.ppermute(behind, 'dev', backward)  9.53 us
    ppermute x3, waiting for transfers between devices, ring_gather(): behind = lax.ppermute(behind, 'dev', backward)  7.7 us
  transfers between devices with their start and end apart: 18, of which 6 were waited for; matrix products, arithmetic and copies ran while one was open for 37% of the time, Pallas kernels for 0%

profile of v11, /device:TPU:0, one launch (start us, length us, event | category | flops | bytes accessed | tf_op | source)
XLA Modules:
  0.0 165.2 jit_solution(489356435802715791)
XLA Ops:
  6.5 2.1 %pad_maximum_fusion = bf16[2,96,1600]{2,1,0:T(8,128)(2,1)} fusion(bf16[1,120,1600]{2,1,0:T(8,128)(2,1)} %bitcast.226, bf16[1,120,1600]{2,1,0:T(8,128)(2,1)} %bitcast.228), kind=kLoop, calls=%fused_computation.72 | loop fusion | flops 1228800 | bytes 1382400 | tf_op jit(solution)/shard_map/stack | solution.py:174
  8.7 1.7 %bitcast_dynamic-update-slice_fusion.14 = (bf16[2,16,24,1600]{3,2,1,0:T(8,128)(2,1)}, bf16[2,24,1600]{2,1,0:T(8,128)(2,1)}) fusion(bf16[1,120,1600]{2,1,0:T(8,128)(2,1)} %bitcast.227, bf16[1,120,1600]{2,1,0:T(8,128)(2,1)} %bitcast.229), kind=kLoop, calls=%fused_computation.116 | loop fusion | flops 307199 | bytes 1087488
  10.3 3.0 %collective-permute-start = (bf16[2,24,1600]{2,1,0:T(8,128)(2,1)}, bf16[2,24,1600]{2,1,0:T(8,128)(2,1)}, u32[]{:S(2)}, u32[]{:S(2)}) collective-permute-start(bf16[2,24,1600]{2,1,0:T(8,128)(2,1)} %get-tuple-element.6), channel_id=1, source_target_pairs={{0,4},{1,5},{2,0},{3,1},{4,8},{5,9},{6,2},{7,3},{8,12},{9,13},{10,... | collective-permute-start | bytes 460808 | tf_op jit(solution)/shard_map/ppermute | solution.py:52
  13.4 2.3 %fusion.131 = (bf16[256,1024]{1,0:T(8,128)(2,1)}, bf16[256,1024]{1,0:T(8,128)(2,1)}) fusion(bf16[256,2048]{1,0:T(8,128)(2,1)} %bitcast.230), kind=kLoop, calls=%fused_computation.169 | loop fusion | bytes 2097152 | tf_op jit(solution)/shard_map/slice | solution.py:30
  15.7 2.1 %copy.64 = bf16[256,1024]{0,1:T(8,128)(2,1)} copy(bf16[256,1024]{1,0:T(8,128)(2,1)} %get-tuple-element.10) | data formatting | bytes 1048576 | tf_op jit(solution)/shard_map/slice | solution.py:31
  17.8 2.0 %copy.60 = bf16[1,256,1024]{1,2,0:T(8,128)(2,1)} copy(bf16[1,256,1024]{2,1,0:T(8,128)(2,1)} %param.14) | data formatting | bytes 1048576 | tf_op args[1]
  19.8 2.1 %copy.63 = bf16[256,1024]{0,1:T(8,128)(2,1)} copy(bf16[256,1024]{1,0:T(8,128)(2,1)} %get-tuple-element.9) | data formatting | bytes 1048576 | tf_op jit(solution)/shard_map/slice | solution.py:30
  23.1 4.5 %fusion.11 = bf16[8,2048]{1,0:T(8,128)(2,1)S(1)} fusion(bf16[1600,2048]{1,0:T(8,128)(2,1)} %param.18, bf16[1,8,2048]{2,1,0:T(8,128)(2,1)S(1)} %copy-done.7, pred[]{:T(512)} %compare_reduce_fusion, bf16[1,8,1600]{2,1,0:T(8,128)(2,1)S(1)} %copy-done.6, f32[8]{0:T(128)S(1)} %add_sqrt_fusion.1, f32[8]{0:T(128)S(1)} %broadcast_multiply_fusion.1), kind=kOutput, calls=%fused_computation.21 | convolution fusion | flops 52512768 | bytes 6644801 | tf_op jit(solution)/shard_map/dot_general | solution.py:140
  27.6 25.3 %all_gather.9 = bf16[128,2048]{1,0:T(8,128)(2,1)S(1)} all-gather(bf16[8,2048]{1,0:T(8,128)(2,1)S(1)} %fusion.11), channel_id=1, replica_groups=mesh['group'=2,'dev'=16] {'dev'}, dimensions={0}, use_global_device_ids=true | all-gather | bytes 557056 | tf_op jit(solution)/shard_map/all_gather | solution.py:146
  52.9 0.7 fusion.132
  53.7 1.8 %copy.59 = bf16[128,1024]{0,1:T(8,128)(2,1)} copy(bf16[128,1024]{1,0:T(8,128)(2,1)} %get-tuple-element.12) | data formatting | bytes 524288 | tf_op jit(solution)/shard_map/slice | solution.py:30
  55.5 0.8 copy.61
  56.4 0.7 fusion.108
  57.8 1.6 bitcast_reduce_fusion
  59.5 0.8 fusion.4
  60.8 1.0 fusion.5
  61.8 1.1 fusion.34
  64.1 1.1 fusion.133
  65.4 1.1 divide_convert_fusion
  66.6 1.5 collective-permute-start.15
  68.1 2.0 %collective-permute-start.3 = (bf16[2,24,1600]{2,1,0:T(8,128)(2,1)}, bf16[2,24,1600]{2,1,0:T(8,128)(2,1)S(1)}, u32[]{:S(2)}, u32[]{:S(2)}) collective-permute-start(bf16[2,24,1600]{2,1,0:T(8,128)(2,1)} %collective-permute-done.1), channel_id=1, source_target_pairs={{0,2},{1,3},{2,6},{3,7},{4,0},{5,1},{6,10},{7,11},{8,4},{9,5},{10,... | collective-permute-start | bytes 460808 | tf_op jit(solution)/shard_map/ppermute | solution.py:55
  70.1 1.6 bitcast_dynamic-update-slice_fusion.13
  71.7 1.6 bitcast_dynamic-update-slice_fusion.12
  73.3 5.1 %collective-permute-done.2 = bf16[2,24,1600]{2,1,0:T(8,128)(2,1)S(1)} collective-permute-done((bf16[2,24,1600]{2,1,0:T(8,128)(2,1)}, bf16[2,24,1600]{2,1,0:T(8,128)(2,1)S(1)}, u32[]{:S(2)}, u32[]{:S(2)}) %collective-permute-start.2) | collective-permute-done | bytes 153632 | tf_op jit(solution)/shard_map/ppermute | solution.py:52
  78.4 0.7 bitcast_dynamic-update-slice_fusion.11
  79.0 2.7 %collective-permute-done.3 = bf16[2,24,1600]{2,1,0:T(8,128)(2,1)S(1)} collective-permute-done((bf16[2,24,1600]{2,1,0:T(8,128)(2,1)}, bf16[2,24,1600]{2,1,0:T(8,128)(2,1)S(1)}, u32[]{:S(2)}, u32[]{:S(2)}) %collective-permute-start.3) | collective-permute-done | bytes 153632 | tf_op jit(solution)/shard_map/ppermute | solution.py:55
  81.7 0.7 bitcast_dynamic-update-slice_fusion.10
  82.4 6.0 %collective-permute-done.4 = bf16[2,24,1600]{2,1,0:T(8,128)(2,1)S(1)} collective-permute-done((bf16[2,24,1600]{2,1,0:T(8,128)(2,1)S(1)}, bf16[2,24,1600]{2,1,0:T(8,128)(2,1)S(1)}, u32[]{:S(2)}, u32[]{:S(2)}) %collective-permute-start.4) | collective-permute-done | bytes 153632 | tf_op jit(solution)/shard_map/ppermute | solution.py:52
  88.4 7.6 %collective-permute-start.5 = (bf16[2,24,1600]{2,1,0:T(8,128)(2,1)S(1)}, bf16[2,24,1600]{2,1,0:T(8,128)(2,1)S(1)}, u32[]{:S(2)}, u32[]{:S(2)}) collective-permute-start(bf16[2,24,1600]{2,1,0:T(8,128)(2,1)S(1)} %collective-permute-done.3), channel_id=1, source_target_pairs={{0,2},{1,3},{2,6},{3,7},{4,0},{5,1},{6,10},{7,11},{8,4},{9,5},{10,... | collective-permute-start | bytes 460808 | tf_op jit(solution)/shard_map/ppermute | solution.py:55
  96.0 0.7 bitcast_dynamic-update-slice_fusion.9
  96.6 5.0 %collective-permute-done.5 = bf16[2,24,1600]{2,1,0:T(8,128)(2,1)S(1)} collective-permute-done((bf16[2,24,1600]{2,1,0:T(8,128)(2,1)S(1)}, bf16[2,24,1600]{2,1,0:T(8,128)(2,1)S(1)}, u32[]{:S(2)}, u32[]{:S(2)}) %collective-permute-start.5) | collective-permute-done | bytes 153632 | tf_op jit(solution)/shard_map/ppermute | solution.py:55
  102.1 0.7 bitcast_dynamic-update-slice_fusion.8
  102.8 4.9 %collective-permute-done.6 = bf16[2,24,1600]{2,1,0:T(8,128)(2,1)S(1)} collective-permute-done((bf16[2,24,1600]{2,1,0:T(8,128)(2,1)S(1)}, bf16[2,24,1600]{2,1,0:T(8,128)(2,1)S(1)}, u32[]{:S(2)}, u32[]{:S(2)}) %collective-permute-start.6) | collective-permute-done | bytes 153632 | tf_op jit(solution)/shard_map/ppermute | solution.py:52
  107.7 0.7 bitcast_dynamic-update-slice_fusion.7
  108.9 1.6 bitcast_dynamic-update-slice_fusion.6
  110.5 0.7 bitcast_dynamic-update-slice_fusion.5
  111.7 0.7 bitcast_dynamic-update-slice_fusion.4
  112.4 0.7 bitcast_dynamic-update-slice_fusion.3
  113.1 0.7 bitcast_dynamic-update-slice_fusion.2
  113.8 0.7 bitcast_dynamic-update-slice_fusion.1
  115.2 0.7 bitcast_dynamic-update-slice_fusion.15
  115.8 4.9 %convolution_bitcast_fusion.1 = f32[256,1600]{0,1:T(8,128)} fusion(bf16[2,16,24,1600]{3,2,1,0:T(8,128)(2,1)} %bitcast_dynamic-update-slice_fusion.15, bf16[256,1600]{0,1:T(8,128)(2,1)} %divide_convert_fusion), kind=kOutput, calls=%fused_computation.15 | convolution fusion | flops 630030336 | bytes 4915200 | tf_op jit(solution)/shard_map/tsh,shd->td/dot_general | solution.py:192
  120.7 4.9 %convolution_bitcast_fusion = f32[256,1600]{0,1:T(8,128)} fusion(bf16[2,16,24,1600]{3,2,1,0:T(8,128)(2,1)} %bitcast_dynamic-update-slice_fusion.15, bf16[256,1600]{0,1:T(8,128)(2,1)} %collective-permute-done.15), kind=kOutput, calls=%fused_computation.14 | convolution fusion | flops 630030336 | bytes 4915200 | tf_op jit(solution)/shard_map/tsh,shd->td/dot_general | solution.py:192
  125.6 9.1 %fusion.10 = bf16[256,1600]{0,1:T(8,128)(2,1)} fusion(f32[256,1600]{0,1:T(8,128)} %convolution_bitcast_fusion, bf16[2,1536,1600]{2,1,0:T(8,128)(2,1)} %all-gather.3.cloned.1.call-done, bf16[256,1600]{0,1:T(8,128)(2,1)} %collective-permute-done.15), kind=kOutput, calls=%fused_computation.17 | convolution fusion | flops 2520940544 | bytes 13107200 | tf_op jit(solution)/shard_map/dot_general | solution.py:202
  134.6 1.2 collective-permute-start.16
  135.8 9.8 %fusion.9 = f32[256,1600]{0,1:T(8,128)} fusion(f32[256,1600]{0,1:T(8,128)} %copy-done.1, f32[256,1600]{0,1:T(8,128)} %convolution_bitcast_fusion.1, bf16[2,1536,1600]{2,1,0:T(8,128)(2,1)} %all-gather.3.cloned.1.call-done, bf16[256,1600]{0,1:T(8,128)(2,1)} %divide_convert_fusion), kind=kOutput, calls=%fused_computation.16 | convolution fusion | flops 2520940544 | bytes 15564800 | tf_op jit(solution)/shard_map/dot_general | solution.py:202
  145.6 10.0 %collective-permute-done.16 = bf16[256,1600]{0,1:T(8,128)(2,1)} collective-permute-done((bf16[256,1600]{0,1:T(8,128)(2,1)}, bf16[256,1600]{0,1:T(8,128)(2,1)}, u32[]{:S(2)}, u32[]{:S(2)}) %collective-permute-start.16) | collective-permute-done | bytes 819232 | tf_op jit(solution)/shard_map/ppermute | solution.py:212
  155.6 2.7 %fusion.47 = bf16[1,256,1600]{1,2,0:T(8,128)(2,1)} fusion(f32[256,1600]{0,1:T(8,128)} %fusion.9, bf16[256,1600]{0,1:T(8,128)(2,1)} %collective-permute-done.16, pred[256]{0:T(512)(128)(4,1)S(1)} %iota_compare_fusion.2), kind=kLoop, calls=%fused_computation.61 | loop fusion | flops 1638400 | bytes 3277056 | tf_op jit(solution)/shard_map/broadcast_in_dim | solution.py:217
  (69 shorter events, 6.1 us)
Async XLA Ops:
  6.5 57.0 %copy-start = (bf16[1024,1600]{0,1:T(8,128)(2,1)S(1)}, bf16[1024,1600]{0,1:T(8,128)(2,1)}, u32[]{:S(2)}) copy-start(bf16[1024,1600]{0,1:T(8,128)(2,1)} %param.19) | copy-start | bytes 9830404
  6.5 119.1 %all-gather.3.cloned.1.call-start = ((), (), s32[]{:S(2)}) async-start(), calls=%async_computation | async-start | bytes 10862592 | tf_op jit(solution)/shard_map/all_gather | solution.py:181
  10.3 57.7 %collective-permute-start = (bf16[2,24,1600]{2,1,0:T(8,128)(2,1)}, bf16[2,24,1600]{2,1,0:T(8,128)(2,1)}, u32[]{:S(2)}, u32[]{:S(2)}) collective-permute-start(bf16[2,24,1600]{2,1,0:T(8,128)(2,1)} %get-tuple-element.6), channel_id=1, source_target_pairs={{0,4},{1,5},{2,0},{3,1},{4,8},{5,9},{6,2},{7,3},{8,12},{9,13},{10,... | collective-permute-start | bytes 460808 | tf_op jit(solution)/shard_map/ppermute | solution.py:52
  13.4 54.8 %collective-permute-start.1 = (bf16[2,24,1600]{2,1,0:T(8,128)(2,1)}, bf16[2,24,1600]{2,1,0:T(8,128)(2,1)}, u32[]{:S(2)}, u32[]{:S(2)}) collective-permute-start(bf16[2,24,1600]{2,1,0:T(8,128)(2,1)} %get-tuple-element.6), channel_id=1, source_target_pairs={{0,2},{1,3},{2,6},{3,7},{4,0},{5,1},{6,10},{7,11},{8,4},{9,5},{10,... | collective-permute-start | bytes 460808 | tf_op jit(solution)/shard_map/ppermute | solution.py:55
  13.4 95.0 %collective-permute-start.7 = (bf16[2,24,1600]{2,1,0:T(8,128)(2,1)}, bf16[2,24,1600]{2,1,0:T(8,128)(2,1)}, u32[]{:S(2)}, u32[]{:S(2)}) collective-permute-start(bf16[2,24,1600]{2,1,0:T(8,128)(2,1)} %get-tuple-element.6), channel_id=1, source_target_pairs={{0,1},{1,0},{2,3},{3,2},{4,5},{5,4},{6,7},{7,6},{8,9},{9,8},{10,11... | collective-permute-start | bytes 460808 | tf_op jit(solution)/shard_map/ppermute | solution.py:57
  13.4 8.6 %copy-start.9 = (s32[1,16]{1,0:T(1,128)S(1)}, s32[1,16]{1,0:T(1,128)}, u32[]{:S(2)}) copy-start(s32[1,16]{1,0:T(1,128)} %param.24) | copy-start | bytes 196
  13.4 8.6 %copy-start.10 = (s32[1,2]{1,0:T(1,128)S(1)}, s32[1,2]{1,0:T(1,128)}, u32[]{:S(2)}) copy-start(s32[1,2]{1,0:T(1,128)} %param.25) | copy-start | bytes 28
  13.4 9.4 %copy-start.6 = (bf16[1,8,1600]{2,1,0:T(8,128)(2,1)S(1)}, bf16[1,8,1600]{2,1,0:T(8,128)(2,1)}, u32[]{:S(2)}) copy-start(bf16[1,8,1600]{2,1,0:T(8,128)(2,1)} %param.17) | copy-start | bytes 76804
  13.4 9.7 %copy-start.7 = (bf16[1,8,2048]{2,1,0:T(8,128)(2,1)S(1)}, bf16[1,8,2048]{2,1,0:T(8,128)(2,1)}, u32[]{:S(2)}) copy-start(bf16[1,8,2048]{2,1,0:T(8,128)(2,1)} %param.16) | copy-start | bytes 98308
  27.6 28.7 %copy-start.11 = (s32[1,16]{1,0:T(1,128)S(1)}, s32[1,16]{1,0:T(1,128)}, u32[]{:S(2)}) copy-start(s32[1,16]{1,0:T(1,128)} %param.22) | copy-start | bytes 196
  27.6 28.7 %copy-start.12 = (s32[1,16]{1,0:T(1,128)S(1)}, s32[1,16]{1,0:T(1,128)}, u32[]{:S(2)}) copy-start(s32[1,16]{1,0:T(1,128)} %param.23) | copy-start | bytes 196
  56.3 3.2 %copy-start.2 = (bf16[1,256,1024]{1,2,0:T(8,128)(2,1)S(1)}, bf16[1,256,1024]{1,2,0:T(8,128)(2,1)}, u32[]{:S(2)}) copy-start(bf16[1,256,1024]{1,2,0:T(8,128)(2,1)} %copy.60) | copy-start | bytes 1572868
  56.3 3.2 %copy-start.3 = (bf16[256,1024]{0,1:T(8,128)(2,1)S(1)}, bf16[256,1024]{0,1:T(8,128)(2,1)}, u32[]{:S(2)}) copy-start(bf16[256,1024]{0,1:T(8,128)(2,1)} %copy.63) | copy-start | bytes 1572868
  60.7 1.0 copy-start.4
  61.8 1.1 copy-start.5
  62.9 1.2 copy-start.8
  65.2 17.2 %copy-start.1 = (f32[256,1600]{0,1:T(8,128)}, f32[256,1600]{0,1:T(8,128)S(1)}, u32[]{:S(2)}) copy-start(f32[256,1600]{0,1:T(8,128)S(1)} %get-tuple-element.21) | copy-start | bytes 4915204
  66.6 54.1 %collective-permute-start.15 = (bf16[256,1600]{0,1:T(8,128)(2,1)}, bf16[256,1600]{0,1:T(8,128)(2,1)}, u32[]{:S(2)}, u32[]{:S(2)}) collective-permute-start(bf16[256,1600]{0,1:T(8,128)(2,1)} %divide_convert_fusion), channel_id=1, source_target_pairs={{0,16},{16,0},{1,17},{17,1},{2,18},{18,2},{3,19},{19,3},{4,20},{20... | collective-permute-start | bytes 2457608 | tf_op jit(solution)/shard_map/ppermute | solution.py:210
  68.1 10.3 %collective-permute-start.2 = (bf16[2,24,1600]{2,1,0:T(8,128)(2,1)}, bf16[2,24,1600]{2,1,0:T(8,128)(2,1)S(1)}, u32[]{:S(2)}, u32[]{:S(2)}) collective-permute-start(bf16[2,24,1600]{2,1,0:T(8,128)(2,1)} %collective-permute-done), channel_id=1, source_target_pairs={{0,4},{1,5},{2,0},{3,1},{4,8},{5,9},{6,2},{7,3},{8,12},{9,13},{10,... | collective-permute-start | bytes 460808 | tf_op jit(solution)/shard_map/ppermute | solution.py:52
  68.1 42.4 %collective-permute-start.8 = (bf16[2,24,1600]{2,1,0:T(8,128)(2,1)}, bf16[2,24,1600]{2,1,0:T(8,128)(2,1)S(1)}, u32[]{:S(2)}, u32[]{:S(2)}) collective-permute-start(bf16[2,24,1600]{2,1,0:T(8,128)(2,1)} %collective-permute-done), channel_id=1, source_target_pairs={{0,1},{1,0},{2,3},{3,2},{4,5},{5,4},{6,7},{7,6},{8,9},{9,8},{10,11... | collective-permute-start | bytes 460808 | tf_op jit(solution)/shard_map/ppermute | solution.py:57
  68.1 13.6 %collective-permute-start.3 = (bf16[2,24,1600]{2,1,0:T(8,128)(2,1)}, bf16[2,24,1600]{2,1,0:T(8,128)(2,1)S(1)}, u32[]{:S(2)}, u32[]{:S(2)}) collective-permute-start(bf16[2,24,1600]{2,1,0:T(8,128)(2,1)} %collective-permute-done.1), channel_id=1, source_target_pairs={{0,2},{1,3},{2,6},{3,7},{4,0},{5,1},{6,10},{7,11},{8,4},{9,5},{10,... | collective-permute-start | bytes 460808 | tf_op jit(solution)/shard_map/ppermute | solution.py:55
  78.4 32.9 %collective-permute-start.9 = (bf16[2,24,1600]{2,1,0:T(8,128)(2,1)}, bf16[2,24,1600]{2,1,0:T(8,128)(2,1)S(1)}, u32[]{:S(2)}, u32[]{:S(2)}) collective-permute-start(bf16[2,24,1600]{2,1,0:T(8,128)(2,1)} %collective-permute-done.1), channel_id=1, source_target_pairs={{0,1},{1,0},{2,3},{3,2},{4,5},{5,4},{6,7},{7,6},{8,9},{9,8},{10,11... | collective-permute-start | bytes 460808 | tf_op jit(solution)/shard_map/ppermute | solution.py:57
  81.7 6.7 %collective-permute-start.4 = (bf16[2,24,1600]{2,1,0:T(8,128)(2,1)S(1)}, bf16[2,24,1600]{2,1,0:T(8,128)(2,1)S(1)}, u32[]{:S(2)}, u32[]{:S(2)}) collective-permute-start(bf16[2,24,1600]{2,1,0:T(8,128)(2,1)S(1)} %collective-permute-done.2), channel_id=1, source_target_pairs={{0,4},{1,5},{2,0},{3,1},{4,8},{5,9},{6,2},{7,3},{8,12},{9,13},{10,... | collective-permute-start | bytes 460808 | tf_op jit(solution)/shard_map/ppermute | solution.py:52
  88.4 13.3 %collective-permute-start.5 = (bf16[2,24,1600]{2,1,0:T(8,128)(2,1)S(1)}, bf16[2,24,1600]{2,1,0:T(8,128)(2,1)S(1)}, u32[]{:S(2)}, u32[]{:S(2)}) collective-permute-start(bf16[2,24,1600]{2,1,0:T(8,128)(2,1)S(1)} %collective-permute-done.3), channel_id=1, source_target_pairs={{0,2},{1,3},{2,6},{3,7},{4,0},{5,1},{6,10},{7,11},{8,4},{9,5},{10,... | collective-permute-start | bytes 460808 | tf_op jit(solution)/shard_map/ppermute | solution.py:55
  101.7 6.0 %collective-permute-start.6 = (bf16[2,24,1600]{2,1,0:T(8,128)(2,1)S(1)}, bf16[2,24,1600]{2,1,0:T(8,128)(2,1)S(1)}, u32[]{:S(2)}, u32[]{:S(2)}) collective-permute-start(bf16[2,24,1600]{2,1,0:T(8,128)(2,1)S(1)} %collective-permute-done.4), channel_id=1, source_target_pairs={{0,4},{1,5},{2,0},{3,1},{4,8},{5,9},{6,2},{7,3},{8,12},{9,13},{10,... | collective-permute-start | bytes 460808 | tf_op jit(solution)/shard_map/ppermute | solution.py:52
  107.7 4.7 %collective-permute-start.10 = (bf16[2,24,1600]{2,1,0:T(8,128)(2,1)S(1)}, bf16[2,24,1600]{2,1,0:T(8,128)(2,1)S(1)}, u32[]{:S(2)}, u32[]{:S(2)}) collective-permute-start(bf16[2,24,1600]{2,1,0:T(8,128)(2,1)S(1)} %collective-permute-done.2), channel_id=1, source_target_pairs={{0,1},{1,0},{2,3},{3,2},{4,5},{5,4},{6,7},{7,6},{8,9},{9,8},{10,11... | collective-permute-start | bytes 460808 | tf_op jit(solution)/shard_map/ppermute | solution.py:57
  108.4 4.7 %collective-permute-start.11 = (bf16[2,24,1600]{2,1,0:T(8,128)(2,1)S(1)}, bf16[2,24,1600]{2,1,0:T(8,128)(2,1)S(1)}, u32[]{:S(2)}, u32[]{:S(2)}) collective-permute-start(bf16[2,24,1600]{2,1,0:T(8,128)(2,1)S(1)} %collective-permute-done.3), channel_id=1, source_target_pairs={{0,1},{1,0},{2,3},{3,2},{4,5},{5,4},{6,7},{7,6},{8,9},{9,8},{10,11... | collective-permute-start | bytes 460808 | tf_op jit(solution)/shard_map/ppermute | solution.py:57
  110.5 3.3 %collective-permute-start.12 = (bf16[2,24,1600]{2,1,0:T(8,128)(2,1)S(1)}, bf16[2,24,1600]{2,1,0:T(8,128)(2,1)S(1)}, u32[]{:S(2)}, u32[]{:S(2)}) collective-permute-start(bf16[2,24,1600]{2,1,0:T(8,128)(2,1)S(1)} %collective-permute-done.4), channel_id=1, source_target_pairs={{0,1},{1,0},{2,3},{3,2},{4,5},{5,4},{6,7},{7,6},{8,9},{9,8},{10,11... | collective-permute-start | bytes 460808 | tf_op jit(solution)/shard_map/ppermute | solution.py:57
  111.2 3.3 %collective-permute-start.13 = (bf16[2,24,1600]{2,1,0:T(8,128)(2,1)S(1)}, bf16[2,24,1600]{2,1,0:T(8,128)(2,1)S(1)}, u32[]{:S(2)}, u32[]{:S(2)}) collective-permute-start(bf16[2,24,1600]{2,1,0:T(8,128)(2,1)S(1)} %collective-permute-done.5), channel_id=1, source_target_pairs={{0,1},{1,0},{2,3},{3,2},{4,5},{5,4},{6,7},{7,6},{8,9},{9,8},{10,11... | collective-permute-start | bytes 460808 | tf_op jit(solution)/shard_map/ppermute | solution.py:57
  112.4 2.8 %collective-permute-start.14 = (bf16[2,24,1600]{2,1,0:T(8,128)(2,1)S(1)}, bf16[2,24,1600]{2,1,0:T(8,128)(2,1)S(1)}, u32[]{:S(2)}, u32[]{:S(2)}) collective-permute-start(bf16[2,24,1600]{2,1,0:T(8,128)(2,1)S(1)} %collective-permute-done.6), channel_id=1, source_target_pairs={{0,1},{1,0},{2,3},{3,2},{4,5},{5,4},{6,7},{7,6},{8,9},{9,8},{10,11... | collective-permute-start | bytes 460808 | tf_op jit(solution)/shard_map/ppermute | solution.py:57
  134.6 21.0 %collective-permute-start.16 = (bf16[256,1600]{0,1:T(8,128)(2,1)}, bf16[256,1600]{0,1:T(8,128)(2,1)}, u32[]{:S(2)}, u32[]{:S(2)}) collective-permute-start(bf16[256,1600]{0,1:T(8,128)(2,1)} %fusion.10), channel_id=1, source_target_pairs={{0,16},{16,0},{1,17},{17,1},{2,18},{18,2},{3,19},{19,3},{4,20},{20... | collective-permute-start | bytes 2457608 | tf_op jit(solution)/shard_map/ppermute | solution.py:212
Sparse Core Ops, SparseCore 0:
  9.6 94.5 all-gather.2

commit v12 on v11

--- a/solution.py
+++ b/solution.py
@@ -44,16 +44,37 @@
     return (new_top, running_total, accumulated)
 
 
-def ring_gather(shard, forward, backward, swap, steps_forward, steps_backward):
-    pieces = [shard]
-    ahead = shard
-    behind = shard
-    for step in range(steps_forward):
-        ahead = lax.ppermute(ahead, "dev", forward)
-        pieces.append(ahead)
-        if step < steps_backward:
-            behind = lax.ppermute(behind, "dev", backward)
-            pieces.append(behind)
+def ring_issue(state, plan):
+    forward, backward, full_steps, split = plan[0], plan[1], plan[3], plan[4]
+    ahead, behind, pieces, done = state
+    if done < full_steps:
+        return lax.ppermute(ahead, "dev", forward), lax.ppermute(behind, "dev", backward)
+    if done == full_steps and split:
+        return lax.ppermute(ahead, "dev", forward), None
+    return None
+
+
+def ring_land(state, plan, sent, tie):
+    ahead, behind, pieces, done = state
+    if sent is None:
+        return state, tie
+    first, second = sent
+    if second is None:
+        tie, first = lax.optimization_barrier((tie, first))
+        return (first, behind, pieces + [first], done + 1), tie
+    tie, first, second = lax.optimization_barrier((tie, first, second))
+    return (first, second, pieces + [first, second], done + 1), tie
+
+
+def ring_step(state, plan, tie):
+    return ring_land(state, plan, ring_issue(state, plan), tie)
+
+
+def ring_finish(state, plan):
+    swap = plan[2]
+    while state[3] <= plan[3]:
+        state, _ = ring_step(state, plan, jnp.zeros((), jnp.float32))
+    pieces = state[2]
     pieces = pieces + [lax.ppermute(piece, "dev", swap) for piece in pieces]
     return jnp.stack(pieces, axis=1)
 
@@ -99,8 +120,8 @@
     forward = [(2 * k + c, 2 * after[k] + c) for k in range(chip_count) for c in range(2)]
     backward = [(2 * k + c, 2 * before[k] + c) for k in range(chip_count) for c in range(2)]
     swap = [(2 * k + c, 2 * k + 1 - c) for k in range(chip_count) for c in range(2)]
-    steps_forward = chip_count // 2
-    return forward, backward, swap, steps_forward, chip_count - 1 - steps_forward
+    full_steps = (chip_count - 1) // 2
+    return forward, backward, swap, full_steps, chip_count % 2 == 0
 
 
 def per_device(
@@ -143,7 +164,17 @@
     my_stale = jnp.any(chosen_owner == my_device)
     local_kv = jnp.where(my_stale, fresh, prefix_keyval[0])
     skip_device = jnp.zeros_like(stale_device)
+    both = jnp.stack([fc_weight.T, proj_weight])
+    hidden_part = fc_weight.shape[1]
+    keep = hidden_part * 4 // 5 // 16 * 16
+    use_ring = ring_plan is not None and keep > 0
+    if use_ring:
+        ring = (both[:, keep:], both[:, keep:], [both[:, keep:]], 0)
+        ring, local_kv = ring_step(ring, ring_plan, local_kv)
+        sent = ring_issue(ring, ring_plan)
     gathered = lax.all_gather(local_kv, "dev", axis=0, tiled=True)
+    if use_ring:
+        ring, gathered = ring_land(ring, ring_plan, sent, gathered)
     prefix_count = gathered.shape[0]
     row_device = jnp.arange(prefix_count, dtype=jnp.int32) // block_rows
     skipped = jnp.any((row_device[:, None] == device_ids[None, :]) & skip_device[None, :], axis=1)
@@ -169,15 +200,14 @@
     projected = jnp.dot(attended, out_weight, preferred_element_type=jnp.float32)
     residual = suffix_x[0].astype(jnp.float32) + projected
     normed = normalize(residual).astype(jnp.bfloat16)
+    if use_ring:
+        ring, normed = ring_step(ring, ring_plan, normed)
     group_count = lax.axis_size("group")
-    hidden_part = fc_weight.shape[1]
-    both = jnp.stack([fc_weight.T, proj_weight])
-    keep = hidden_part * 4 // 5 // 16 * 16
-    if ring_plan is None or keep == 0:
+    if not use_ring:
         banks = [lax.all_gather(both, "dev", axis=1)]
     else:
         banks = [
-            ring_gather(both[:, keep:], *ring_plan),
+            ring_finish(ring, ring_plan),
             lax.all_gather(both[:, :keep], "dev", axis=1),
         ]
 

time: 166 us -> 164 us (0.988); the launches traced: 165 us -> 160 us
  starting transfers between devices: 16.7 us -> 9.48 us
  local copies, waits for them, and re-layouts: 25.4 us -> 29 us
  waiting for transfers between devices: 33.8 us -> 30.3 us
  matrix products: 38.3 us -> 40.6 us
    ppermute x15, waiting for transfers between devices: 23.7 us -> 10.2 us  [the longest x1 7.71 us: ring_issue(): return (lax.ppermute(ahead, 'dev', forward), None)]
    ppermute x1, waiting for transfers between devices: 0.01 us -> 10.2 us  [per_device(): partner_normed = lax.ppermute(normed, 'group', there)]
    ppermute x15, starting transfers between devices: 14.1 us -> 8.4 us  [the longest x3 5.04 us: ring_issue(): lax.ppermute(ahead, 'dev', forward)]
    unnamed x41 -> x55, local copies, waits for them, and re-layouts: 14.9 us -> 18.6 us
    dot_general x2, matrix products: 2.48 us -> 4.51 us  [absorb(): jnp.einsum('qhd,khd->hqk', queries, key_rows, preferred_element_type=jnp....]
  transfers between devices with their start and end apart: 18 -> 18, of which waited for: 6 -> 4; matrix products, arithmetic and copies ran while one was open for 37% -> 41% of each run, Pallas kernels for 0% -> 0%
where the time goes in v12:
time: 164 us; the launch traced here: 160 us
  matrix products  40.6 us (25%)
  waiting for transfers between devices  30.3 us (18%)
  local copies, waits for them, and re-layouts  29 us (18%)
  blocking collectives  25.4 us (15%)
  between operations  13.7 us (8%)
  other arithmetic  12 us (7%)
  starting transfers between devices  9.48 us (6%)
    all_gather x1, blocking collectives, per_device(): gathered = lax.all_gather(local_kv, 'dev', axis=0, tiled=True)  25.4 us
    dot_general x2, matrix products, feed(): part = jnp.dot(activated, proj_rows, preferred_element_type=jnp.float32)  18.9 us
    unnamed x55, local copies, waits for them, and re-layouts  18.6 us
    ppermute x1, waiting for transfers between devices, per_device(): partner_normed = lax.ppermute(normed, 'group', there)  10.2 us
    dot_general x2, matrix products, feed(): jnp.einsum('tsh,shd->td', activated, bank[1], preferred_element_type=jnp....  9.86 us
    ppermute x1, waiting for transfers between devices, per_device(): returned.append(lax.ppermute(partner_feed, 'group', back))  9.77 us
    ppermute x1, waiting for transfers between devices, ring_issue(): return (lax.ppermute(ahead, 'dev', forward), None)  7.71 us
    slice x3, local copies, waits for them, and re-layouts, absorb(): key_rows = keyval[:, :width_att].reshape(row_count, head_count, head_size)  6.14 us
  transfers between devices with their start and end apart: 18, of which 4 were waited for; matrix products, arithmetic and copies ran while one was open for 41% of the time, Pallas kernels for 0%

profile of v12, /device:TPU:0, one launch (start us, length us, event | category | flops | bytes accessed | tf_op | source)
XLA Modules:
  0.0 160.4 jit_solution(1468596113011533200)
XLA Ops:
  6.5 2.1 %pad_maximum_fusion = bf16[2,96,1600]{2,1,0:T(8,128)(2,1)} fusion(bf16[1,120,1600]{2,1,0:T(8,128)(2,1)} %bitcast.226, bf16[1,120,1600]{2,1,0:T(8,128)(2,1)} %bitcast.228), kind=kLoop, calls=%fused_computation.72 | loop fusion | flops 1228800 | bytes 1382400 | tf_op jit(solution)/shard_map/stack | solution.py:167
  8.7 1.7 %bitcast_dynamic-update-slice_fusion.14 = (bf16[2,16,24,1600]{3,2,1,0:T(8,128)(2,1)}, bf16[2,24,1600]{2,1,0:T(8,128)(2,1)}) fusion(bf16[1,120,1600]{2,1,0:T(8,128)(2,1)} %bitcast.227, bf16[1,120,1600]{2,1,0:T(8,128)(2,1)} %bitcast.229), kind=kLoop, calls=%fused_computation.116 | loop fusion | flops 307199 | bytes 1087488
  10.5 3.0 %collective-permute-start = (bf16[2,24,1600]{2,1,0:T(8,128)(2,1)}, bf16[2,24,1600]{2,1,0:T(8,128)(2,1)}, u32[]{:S(2)}, u32[]{:S(2)}) collective-permute-start(bf16[2,24,1600]{2,1,0:T(8,128)(2,1)} %get-tuple-element.26), channel_id=1, source_target_pairs={{0,4},{1,5},{2,0},{3,1},{4,8},{5,9},{6,2},{7,3},{8,12},{9,13},{10,... | collective-permute-start | bytes 460808 | tf_op jit(solution)/shard_map/ppermute | solution.py:51
  13.5 2.1 %copy.60 = bf16[1,256,1024]{1,2,0:T(8,128)(2,1)} copy(bf16[1,256,1024]{2,1,0:T(8,128)(2,1)} %param.14) | data formatting | bytes 1048576 | tf_op args[1]
  15.5 2.2 %fusion.131 = (bf16[256,1024]{1,0:T(8,128)(2,1)}, bf16[256,1024]{1,0:T(8,128)(2,1)}) fusion(bf16[256,2048]{1,0:T(8,128)(2,1)} %bitcast.230), kind=kLoop, calls=%fused_computation.169 | loop fusion | bytes 2097152 | tf_op jit(solution)/shard_map/slice | solution.py:30
  17.8 2.0 %copy.63 = bf16[256,1024]{0,1:T(8,128)(2,1)} copy(bf16[256,1024]{1,0:T(8,128)(2,1)} %get-tuple-element.29) | data formatting | bytes 1048576 | tf_op jit(solution)/shard_map/slice | solution.py:30
  19.9 0.6 fusion.108
  20.6 0.7 iota_compare_fusion.2
  21.4 0.6 compare_reduce_fusion
  22.6 4.6 %fusion.11 = bf16[8,2048]{1,0:T(8,128)(2,1)S(1)} fusion(bf16[1600,2048]{1,0:T(8,128)(2,1)} %param.18, bf16[1,8,2048]{2,1,0:T(8,128)(2,1)S(1)} %copy-done.12, pred[]{:T(512)} %compare_reduce_fusion, bf16[1,8,1600]{2,1,0:T(8,128)(2,1)S(1)} %copy-done.9, f32[8]{0:T(128)S(1)} %add_sqrt_fusion.1, f32[8]{0:T(128)S(1)} %broadcast_multiply_fusion.1), kind=kOutput, calls=%fused_computation.21 | convolution fusion | flops 52512768 | bytes 6644801 | tf_op jit(solution)/shard_map/dot_general | solution.py:161
  27.2 2.9 %fusion.4 = (f32[16,256]{1,0:T(8,128)S(1)}, f32[16,256,256]{1,2,0:T(8,128)}) fusion(pred[256,256]{0,1:T(8,128)(4,1)S(1)} %fusion.86, bf16[256,16,64]{0,2,1:T(8,128)(2,1)S(1)} %bitcast.224, bf16[256,16,64]{0,2,1:T(8,128)(2,1)S(1)} %bitcast.225), kind=kOutput, calls=%fused_computation.8 | convolution fusion | flops 137359360 | bytes 5324800 | tf_op jit(solution)/shard_map/qhd,khd->hqk/dot_general | solution.py:33
  30.1 2.0 %copy.64 = bf16[256,1024]{0,1:T(8,128)(2,1)} copy(bf16[256,1024]{1,0:T(8,128)(2,1)} %get-tuple-element.30) | data formatting | bytes 1048576 | tf_op jit(solution)/shard_map/slice | solution.py:31
  32.1 2.0 %collective-permute-start.2 = (bf16[2,24,1600]{2,1,0:T(8,128)(2,1)}, bf16[2,24,1600]{2,1,0:T(8,128)(2,1)S(1)}, u32[]{:S(2)}, u32[]{:S(2)}) collective-permute-start(bf16[2,24,1600]{2,1,0:T(8,128)(2,1)} %collective-permute-done), channel_id=1, source_target_pairs={{0,4},{1,5},{2,0},{3,1},{4,8},{5,9},{6,2},{7,3},{8,12},{9,13},{10,... | collective-permute-start | bytes 460808 | tf_op jit(solution)/shard_map/ppermute | solution.py:51
  34.7 1.6 bitcast_dynamic-update-slice_fusion.13
  36.3 1.6 bitcast_dynamic-update-slice_fusion.12
  37.9 25.4 %all_gather.9 = bf16[128,2048]{1,0:T(8,128)(2,1)S(1)} all-gather(bf16[8,2048]{1,0:T(8,128)(2,1)S(1)} %fusion.11), channel_id=1, replica_groups=mesh['group'=2,'dev'=16] {'dev'}, dimensions={0}, use_global_device_ids=true | all-gather | bytes 557056 | tf_op jit(solution)/shard_map/all_gather | solution.py:175
  63.3 0.7 copy-done.10
  64.0 0.7 fusion.132
  64.7 1.9 %copy.59 = bf16[128,1024]{0,1:T(8,128)(2,1)} copy(bf16[128,1024]{1,0:T(8,128)(2,1)} %get-tuple-element.32) | data formatting | bytes 524288 | tf_op jit(solution)/shard_map/slice | solution.py:30
  66.5 0.8 copy.61
  67.4 2.0 %collective-permute-start.5 = (bf16[2,24,1600]{2,1,0:T(8,128)(2,1)}, bf16[2,24,1600]{2,1,0:T(8,128)(2,1)S(1)}, u32[]{:S(2)}, u32[]{:S(2)}) collective-permute-start(bf16[2,24,1600]{2,1,0:T(8,128)(2,1)} %collective-permute-done.3), channel_id=1, source_target_pairs={{0,2},{1,3},{2,6},{3,7},{4,0},{5,1},{6,10},{7,11},{8,4},{9,5},{10,... | collective-permute-start | bytes 460808 | tf_op jit(solution)/shard_map/ppermute | solution.py:51
  69.4 1.6 %bitcast_reduce_fusion = (f32[16,256]{1,0:T(8,128)S(1)}, f32[16,128,256]{2,1,0:T(8,128)S(1)}) fusion(bf16[128,16,64]{0,2,1:T(8,128)(2,1)} %bitcast.231, bf16[256,16,64]{0,2,1:T(8,128)(2,1)} %bitcast.223), kind=kOutput, calls=%fused_computation.23 | convolution fusion | flops 68153344 | bytes 2899968 | tf_op jit(solution)/shard_map/qhd,khd->hqk/dot_general | solution.py:33
  71.5 1.0 fusion.5
  72.6 1.1 fusion.34
  74.8 1.1 fusion.133
  76.2 1.0 bitcast_dynamic-update-slice_fusion.11
  77.1 1.1 divide_convert_fusion
  78.2 1.6 bitcast_dynamic-update-slice_fusion.10
  79.8 2.5 %collective-permute-done.5 = bf16[2,24,1600]{2,1,0:T(8,128)(2,1)S(1)} collective-permute-done((bf16[2,24,1600]{2,1,0:T(8,128)(2,1)}, bf16[2,24,1600]{2,1,0:T(8,128)(2,1)S(1)}, u32[]{:S(2)}, u32[]{:S(2)}) %collective-permute-start.5) | collective-permute-done | bytes 153632 | tf_op jit(solution)/shard_map/ppermute | solution.py:51
  82.3 0.7 bitcast_dynamic-update-slice_fusion.9
  83.0 0.7 bitcast_dynamic-update-slice_fusion.8
  83.7 7.7 %collective-permute-done.6 = bf16[2,24,1600]{2,1,0:T(8,128)(2,1)S(1)} collective-permute-done((bf16[2,24,1600]{2,1,0:T(8,128)(2,1)S(1)}, bf16[2,24,1600]{2,1,0:T(8,128)(2,1)S(1)}, u32[]{:S(2)}, u32[]{:S(2)}) %collective-permute-start.6) | collective-permute-done | bytes 153632 | tf_op jit(solution)/shard_map/ppermute | solution.py:53
  91.4 0.7 bitcast_dynamic-update-slice_fusion.7
  92.6 1.6 %bitcast_dynamic-update-slice_fusion.6 = bf16[2,16,24,1600]{3,2,1,0:T(8,128)(2,1)} fusion(bf16[2,16,24,1600]{3,2,1,0:T(8,128)(2,1)} %bitcast_dynamic-update-slice_fusion.7, bf16[2,24,1600]{2,1,0:T(8,128)(2,1)} %collective-permute-done.7), kind=kLoop, calls=%fused_computation.108 | loop fusion | bytes 319488
  94.2 1.6 bitcast_dynamic-update-slice_fusion.5
  96.4 1.6 bitcast_dynamic-update-slice_fusion.4
  98.1 0.7 bitcast_dynamic-update-slice_fusion.3
  98.8 0.7 bitcast_dynamic-update-slice_fusion.2
  99.5 0.7 bitcast_dynamic-update-slice_fusion.1
  100.2 0.7 bitcast_dynamic-update-slice_fusion
  100.9 0.7 bitcast_dynamic-update-slice_fusion.15
  101.5 5.0 %convolution_bitcast_fusion.1 = f32[256,1600]{0,1:T(8,128)} fusion(bf16[2,16,24,1600]{3,2,1,0:T(8,128)(2,1)} %bitcast_dynamic-update-slice_fusion.15, bf16[256,1600]{0,1:T(8,128)(2,1)} %divide_convert_fusion), kind=kOutput, calls=%fused_computation.15 | convolution fusion | flops 630030336 | bytes 4915200 | tf_op jit(solution)/shard_map/tsh,shd->td/dot_general | solution.py:222
  106.5 10.2 %collective-permute-done.15 = bf16[256,1600]{0,1:T(8,128)(2,1)} collective-permute-done((bf16[256,1600]{0,1:T(8,128)(2,1)}, bf16[256,1600]{0,1:T(8,128)(2,1)}, u32[]{:S(2)}, u32[]{:S(2)}) %collective-permute-start.15) | collective-permute-done | bytes 819232 | tf_op jit(solution)/shard_map/ppermute | solution.py:240
  116.8 4.9 %convolution_bitcast_fusion = f32[256,1600]{0,1:T(8,128)} fusion(bf16[2,16,24,1600]{3,2,1,0:T(8,128)(2,1)} %bitcast_dynamic-update-slice_fusion.15, bf16[256,1600]{0,1:T(8,128)(2,1)} %collective-permute-done.15), kind=kOutput, calls=%fused_computation.14 | convolution fusion | flops 630030336 | bytes 4915200 | tf_op jit(solution)/shard_map/tsh,shd->td/dot_general | solution.py:222
  121.7 9.0 %fusion.10 = bf16[256,1600]{0,1:T(8,128)(2,1)} fusion(f32[256,1600]{0,1:T(8,128)} %convolution_bitcast_fusion, bf16[2,1536,1600]{2,1,0:T(8,128)(2,1)} %all-gather.3.cloned.1.call-done, bf16[256,1600]{0,1:T(8,128)(2,1)} %collective-permute-done.15), kind=kOutput, calls=%fused_computation.17 | convolution fusion | flops 2520940544 | bytes 13107200 | tf_op jit(solution)/shard_map/dot_general | solution.py:232
  131.2 9.8 %fusion.9 = f32[256,1600]{0,1:T(8,128)} fusion(f32[256,1600]{0,1:T(8,128)} %copy-done.2, f32[256,1600]{0,1:T(8,128)} %convolution_bitcast_fusion.1, bf16[2,1536,1600]{2,1,0:T(8,128)(2,1)} %all-gather.3.cloned.1.call-done, bf16[256,1600]{0,1:T(8,128)(2,1)} %divide_convert_fusion), kind=kOutput, calls=%fused_computation.16 | convolution fusion | flops 2520940544 | bytes 15564800 | tf_op jit(solution)/shard_map/dot_general | solution.py:232
  141.1 9.8 %collective-permute-done.16 = bf16[256,1600]{0,1:T(8,128)(2,1)} collective-permute-done((bf16[256,1600]{0,1:T(8,128)(2,1)}, bf16[256,1600]{0,1:T(8,128)(2,1)}, u32[]{:S(2)}, u32[]{:S(2)}) %collective-permute-start.16) | collective-permute-done | bytes 819232 | tf_op jit(solution)/shard_map/ppermute | solution.py:242
  150.8 2.7 %fusion.47 = bf16[1,256,1600]{1,2,0:T(8,128)(2,1)} fusion(f32[256,1600]{0,1:T(8,128)} %fusion.9, bf16[256,1600]{0,1:T(8,128)(2,1)} %collective-permute-done.16, pred[256]{0:T(512)(128)(4,1)S(1)} %copy-done.14), kind=kLoop, calls=%fused_computation.61 | loop fusion | flops 1638400 | bytes 3277056 | tf_op jit(solution)/shard_map/broadcast_in_dim | solution.py:247
  (83 shorter events, 5.1 us)
Async XLA Ops:
  6.5 67.8 %copy-start = (bf16[1024,1600]{0,1:T(8,128)(2,1)S(1)}, bf16[1024,1600]{0,1:T(8,128)(2,1)}, u32[]{:S(2)}) copy-start(bf16[1024,1600]{0,1:T(8,128)(2,1)} %param.19) | copy-start | bytes 9830404
  6.5 115.1 %all-gather.3.cloned.1.call-start = ((), (), s32[]{:S(2)}) async-start(), calls=%async_computation | async-start | bytes 10862592 | tf_op jit(solution)/shard_map/all_gather | solution.py:211
  8.7 11.2 %copy-start.16 = (s32[1,16]{1,0:T(1,128)S(1)}, s32[1,16]{1,0:T(1,128)}, u32[]{:S(2)}) copy-start(s32[1,16]{1,0:T(1,128)} %param.22) | copy-start | bytes 196
  8.7 11.2 %copy-start.17 = (s32[1,16]{1,0:T(1,128)S(1)}, s32[1,16]{1,0:T(1,128)}, u32[]{:S(2)}) copy-start(s32[1,16]{1,0:T(1,128)} %param.23) | copy-start | bytes 196
  8.7 12.5 %copy-start.18 = (s32[1,16]{1,0:T(1,128)S(1)}, s32[1,16]{1,0:T(1,128)}, u32[]{:S(2)}) copy-start(s32[1,16]{1,0:T(1,128)} %param.24) | copy-start | bytes 196
  8.7 12.5 %copy-start.19 = (s32[1,2]{1,0:T(1,128)S(1)}, s32[1,2]{1,0:T(1,128)}, u32[]{:S(2)}) copy-start(s32[1,2]{1,0:T(1,128)} %param.25) | copy-start | bytes 28
  8.7 13.4 %copy-start.9 = (bf16[1,8,1600]{2,1,0:T(8,128)(2,1)S(1)}, bf16[1,8,1600]{2,1,0:T(8,128)(2,1)}, u32[]{:S(2)}) copy-start(bf16[1,8,1600]{2,1,0:T(8,128)(2,1)} %param.17) | copy-start | bytes 76804
  8.7 13.8 %copy-start.12 = (bf16[1,8,2048]{2,1,0:T(8,128)(2,1)S(1)}, bf16[1,8,2048]{2,1,0:T(8,128)(2,1)}, u32[]{:S(2)}) copy-start(bf16[1,8,2048]{2,1,0:T(8,128)(2,1)} %param.16) | copy-start | bytes 98308
  10.5 21.7 %collective-permute-start = (bf16[2,24,1600]{2,1,0:T(8,128)(2,1)}, bf16[2,24,1600]{2,1,0:T(8,128)(2,1)}, u32[]{:S(2)}, u32[]{:S(2)}) collective-permute-start(bf16[2,24,1600]{2,1,0:T(8,128)(2,1)} %get-tuple-element.26), channel_id=1, source_target_pairs={{0,4},{1,5},{2,0},{3,1},{4,8},{5,9},{6,2},{7,3},{8,12},{9,13},{10,... | collective-permute-start | bytes 460808 | tf_op jit(solution)/shard_map/ppermute | solution.py:51
  13.5 18.6 %collective-permute-start.1 = (bf16[2,24,1600]{2,1,0:T(8,128)(2,1)}, bf16[2,24,1600]{2,1,0:T(8,128)(2,1)}, u32[]{:S(2)}, u32[]{:S(2)}) collective-permute-start(bf16[2,24,1600]{2,1,0:T(8,128)(2,1)} %get-tuple-element.26), channel_id=1, source_target_pairs={{0,2},{1,3},{2,6},{3,7},{4,0},{5,1},{6,10},{7,11},{8,4},{9,5},{10,... | collective-permute-start | bytes 460808 | tf_op jit(solution)/shard_map/ppermute | solution.py:51
  13.5 78.6 %collective-permute-start.7 = (bf16[2,24,1600]{2,1,0:T(8,128)(2,1)}, bf16[2,24,1600]{2,1,0:T(8,128)(2,1)}, u32[]{:S(2)}, u32[]{:S(2)}) collective-permute-start(bf16[2,24,1600]{2,1,0:T(8,128)(2,1)} %get-tuple-element.26), channel_id=1, source_target_pairs={{0,1},{1,0},{2,3},{3,2},{4,5},{5,4},{6,7},{7,6},{8,9},{9,8},{10,11... | collective-permute-start | bytes 460808 | tf_op jit(solution)/shard_map/ppermute | solution.py:78
  21.2 1.2 copy-start.13
  22.5 4.6 %copy-start.5 = (pred[256,256]{0,1:T(8,128)(4,1)}, pred[256,256]{0,1:T(8,128)(4,1)S(1)}, u32[]{:S(2)}) copy-start(pred[256,256]{0,1:T(8,128)(4,1)S(1)} %fusion.86) | copy-start | bytes 196612
  22.6 4.6 %copy-start.3 = (bf16[1,256,1024]{1,2,0:T(8,128)(2,1)S(1)}, bf16[1,256,1024]{1,2,0:T(8,128)(2,1)}, u32[]{:S(2)}) copy-start(bf16[1,256,1024]{1,2,0:T(8,128)(2,1)} %copy.60) | copy-start | bytes 1572868
  22.6 4.6 %copy-start.4 = (bf16[256,1024]{0,1:T(8,128)(2,1)S(1)}, bf16[256,1024]{0,1:T(8,128)(2,1)}, u32[]{:S(2)}) copy-start(bf16[256,1024]{0,1:T(8,128)(2,1)} %copy.63) | copy-start | bytes 1572868
  32.1 31.2 %collective-permute-start.2 = (bf16[2,24,1600]{2,1,0:T(8,128)(2,1)}, bf16[2,24,1600]{2,1,0:T(8,128)(2,1)S(1)}, u32[]{:S(2)}, u32[]{:S(2)}) collective-permute-start(bf16[2,24,1600]{2,1,0:T(8,128)(2,1)} %collective-permute-done), channel_id=1, source_target_pairs={{0,4},{1,5},{2,0},{3,1},{4,8},{5,9},{6,2},{7,3},{8,12},{9,13},{10,... | collective-permute-start | bytes 460808 | tf_op jit(solution)/shard_map/ppermute | solution.py:51
  34.1 60.0 %collective-permute-start.8 = (bf16[2,24,1600]{2,1,0:T(8,128)(2,1)}, bf16[2,24,1600]{2,1,0:T(8,128)(2,1)}, u32[]{:S(2)}, u32[]{:S(2)}) collective-permute-start(bf16[2,24,1600]{2,1,0:T(8,128)(2,1)} %collective-permute-done), channel_id=1, source_target_pairs={{0,1},{1,0},{2,3},{3,2},{4,5},{5,4},{6,7},{7,6},{8,9},{9,8},{10,11... | collective-permute-start | bytes 460808 | tf_op jit(solution)/shard_map/ppermute | solution.py:78
  34.4 29.5 %collective-permute-start.3 = (bf16[2,24,1600]{2,1,0:T(8,128)(2,1)}, bf16[2,24,1600]{2,1,0:T(8,128)(2,1)}, u32[]{:S(2)}, u32[]{:S(2)}) collective-permute-start(bf16[2,24,1600]{2,1,0:T(8,128)(2,1)} %collective-permute-done.1), channel_id=1, source_target_pairs={{0,2},{1,3},{2,6},{3,7},{4,0},{5,1},{6,10},{7,11},{8,4},{9,5},{10,... | collective-permute-start | bytes 460808 | tf_op jit(solution)/shard_map/ppermute | solution.py:51
  34.7 61.1 %collective-permute-start.9 = (bf16[2,24,1600]{2,1,0:T(8,128)(2,1)}, bf16[2,24,1600]{2,1,0:T(8,128)(2,1)}, u32[]{:S(2)}, u32[]{:S(2)}) collective-permute-start(bf16[2,24,1600]{2,1,0:T(8,128)(2,1)} %collective-permute-done.1), channel_id=1, source_target_pairs={{0,1},{1,0},{2,3},{3,2},{4,5},{5,4},{6,7},{7,6},{8,9},{9,8},{10,11... | collective-permute-start | bytes 460808 | tf_op jit(solution)/shard_map/ppermute | solution.py:78
  63.3 0.7 copy-start.10
  67.4 4.1 %copy-start.1 = (f32[16,256,256]{1,2,0:T(8,128)S(1)}, f32[16,256,256]{1,2,0:T(8,128)}, u32[]{:S(2)}) copy-start(f32[16,256,256]{1,2,0:T(8,128)} %get-tuple-element.39) | copy-start | bytes 12582916
  67.4 4.1 %copy-start.6 = (pred[256,256]{0,1:T(8,128)(4,1)S(1)}, pred[256,256]{0,1:T(8,128)(4,1)}, u32[]{:S(2)}) copy-start(pred[256,256]{0,1:T(8,128)(4,1)} %copy-done.5) | copy-start | bytes 196612
  67.4 12.4 %collective-permute-start.4 = (bf16[2,24,1600]{2,1,0:T(8,128)(2,1)}, bf16[2,24,1600]{2,1,0:T(8,128)(2,1)S(1)}, u32[]{:S(2)}, u32[]{:S(2)}) collective-permute-start(bf16[2,24,1600]{2,1,0:T(8,128)(2,1)} %copy-done.10), channel_id=1, source_target_pairs={{0,4},{1,5},{2,0},{3,1},{4,8},{5,9},{6,2},{7,3},{8,12},{9,13},{10,... | collective-permute-start | bytes 460808 | tf_op jit(solution)/shard_map/ppermute | solution.py:51
  67.4 14.9 %collective-permute-start.5 = (bf16[2,24,1600]{2,1,0:T(8,128)(2,1)}, bf16[2,24,1600]{2,1,0:T(8,128)(2,1)S(1)}, u32[]{:S(2)}, u32[]{:S(2)}) collective-permute-start(bf16[2,24,1600]{2,1,0:T(8,128)(2,1)} %collective-permute-done.3), channel_id=1, source_target_pairs={{0,2},{1,3},{2,6},{3,7},{4,0},{5,1},{6,10},{7,11},{8,4},{9,5},{10,... | collective-permute-start | bytes 460808 | tf_op jit(solution)/shard_map/ppermute | solution.py:51
  71.5 1.1 copy-start.7
  72.5 1.1 copy-start.8
  73.7 1.1 copy-start.15
  74.8 1.4 copy-start.11
  75.9 7.7 %copy-start.2 = (f32[256,1600]{0,1:T(8,128)}, f32[256,1600]{0,1:T(8,128)S(1)}, u32[]{:S(2)}) copy-start(f32[256,1600]{0,1:T(8,128)S(1)} %get-tuple-element.41) | copy-start | bytes 4915204
  79.8 18.2 %collective-permute-start.10 = (bf16[2,24,1600]{2,1,0:T(8,128)(2,1)S(1)}, bf16[2,24,1600]{2,1,0:T(8,128)(2,1)S(1)}, u32[]{:S(2)}, u32[]{:S(2)}) collective-permute-start(bf16[2,24,1600]{2,1,0:T(8,128)(2,1)S(1)} %copy-done.11), channel_id=1, source_target_pairs={{0,1},{1,0},{2,3},{3,2},{4,5},{5,4},{6,7},{7,6},{8,9},{9,8},{10,11... | collective-permute-start | bytes 460808 | tf_op jit(solution)/shard_map/ppermute | solution.py:78
  82.3 9.1 %collective-permute-start.6 = (bf16[2,24,1600]{2,1,0:T(8,128)(2,1)S(1)}, bf16[2,24,1600]{2,1,0:T(8,128)(2,1)S(1)}, u32[]{:S(2)}, u32[]{:S(2)}) collective-permute-start(bf16[2,24,1600]{2,1,0:T(8,128)(2,1)S(1)} %collective-permute-done.4), channel_id=1, source_target_pairs={{0,4},{1,5},{2,0},{3,1},{4,8},{5,9},{6,2},{7,3},{8,12},{9,13},{10,... | collective-permute-start | bytes 460808 | tf_op jit(solution)/shard_map/ppermute | solution.py:53
  91.4 7.4 %collective-permute-start.11 = (bf16[2,24,1600]{2,1,0:T(8,128)(2,1)}, bf16[2,24,1600]{2,1,0:T(8,128)(2,1)S(1)}, u32[]{:S(2)}, u32[]{:S(2)}) collective-permute-start(bf16[2,24,1600]{2,1,0:T(8,128)(2,1)} %collective-permute-done.3), channel_id=1, source_target_pairs={{0,1},{1,0},{2,3},{3,2},{4,5},{5,4},{6,7},{7,6},{8,9},{9,8},{10,11... | collective-permute-start | bytes 460808 | tf_op jit(solution)/shard_map/ppermute | solution.py:78
  92.1 7.4 %collective-permute-start.12 = (bf16[2,24,1600]{2,1,0:T(8,128)(2,1)S(1)}, bf16[2,24,1600]{2,1,0:T(8,128)(2,1)S(1)}, u32[]{:S(2)}, u32[]{:S(2)}) collective-permute-start(bf16[2,24,1600]{2,1,0:T(8,128)(2,1)S(1)} %collective-permute-done.4), channel_id=1, source_target_pairs={{0,1},{1,0},{2,3},{3,2},{4,5},{5,4},{6,7},{7,6},{8,9},{9,8},{10,11... | collective-permute-start | bytes 460808 | tf_op jit(solution)/shard_map/ppermute | solution.py:78
  94.2 6.0 %collective-permute-start.13 = (bf16[2,24,1600]{2,1,0:T(8,128)(2,1)S(1)}, bf16[2,24,1600]{2,1,0:T(8,128)(2,1)S(1)}, u32[]{:S(2)}, u32[]{:S(2)}) collective-permute-start(bf16[2,24,1600]{2,1,0:T(8,128)(2,1)S(1)} %collective-permute-done.5), channel_id=1, source_target_pairs={{0,1},{1,0},{2,3},{3,2},{4,5},{5,4},{6,7},{7,6},{8,9},{9,8},{10,11... | collective-permute-start | bytes 460808 | tf_op jit(solution)/shard_map/ppermute | solution.py:78
  95.8 20.9 %collective-permute-start.15 = (bf16[256,1600]{0,1:T(8,128)(2,1)}, bf16[256,1600]{0,1:T(8,128)(2,1)}, u32[]{:S(2)}, u32[]{:S(2)}) collective-permute-start(bf16[256,1600]{0,1:T(8,128)(2,1)} %divide_convert_fusion), channel_id=1, source_target_pairs={{0,16},{16,0},{1,17},{17,1},{2,18},{18,2},{3,19},{19,3},{4,20},{20... | collective-permute-start | bytes 2457608 | tf_op jit(solution)/shard_map/ppermute | solution.py:240
  98.0 2.9 %collective-permute-start.14 = (bf16[2,24,1600]{2,1,0:T(8,128)(2,1)S(1)}, bf16[2,24,1600]{2,1,0:T(8,128)(2,1)S(1)}, u32[]{:S(2)}, u32[]{:S(2)}) collective-permute-start(bf16[2,24,1600]{2,1,0:T(8,128)(2,1)S(1)} %collective-permute-done.6), channel_id=1, source_target_pairs={{0,1},{1,0},{2,3},{3,2},{4,5},{5,4},{6,7},{7,6},{8,9},{9,8},{10,11... | collective-permute-start | bytes 460808 | tf_op jit(solution)/shard_map/ppermute | solution.py:78
  130.7 20.1 %copy-start.14 = (pred[256]{0:T(512)(128)(4,1)S(1)}, pred[256]{0:T(512)(128)(4,1)}, u32[]{:S(2)}) copy-start(pred[256]{0:T(512)(128)(4,1)} %copy-done.13) | copy-start | bytes 772
  130.7 20.1 %collective-permute-start.16 = (bf16[256,1600]{0,1:T(8,128)(2,1)}, bf16[256,1600]{0,1:T(8,128)(2,1)}, u32[]{:S(2)}, u32[]{:S(2)}) collective-permute-start(bf16[256,1600]{0,1:T(8,128)(2,1)} %fusion.10), channel_id=1, source_target_pairs={{0,16},{16,0},{1,17},{17,1},{2,18},{18,2},{3,19},{19,3},{4,20},{20... | collective-permute-start | bytes 2457608 | tf_op jit(solution)/shard_map/ppermute | solution.py:242
Sparse Core Ops, SparseCore 0:
  9.6 95.9 all-gather.2

commit v13 on v12

--- a/solution.py
+++ b/solution.py
@@ -201,7 +201,7 @@
     residual = suffix_x[0].astype(jnp.float32) + projected
     normed = normalize(residual).astype(jnp.bfloat16)
     if use_ring:
-        ring, normed = ring_step(ring, ring_plan, normed)
+        ring, _ = ring_step(ring, ring_plan, normed)
     group_count = lax.axis_size("group")
     if not use_ring:
         banks = [lax.all_gather(both, "dev", axis=1)]

time: 164 us -> 160 us (0.976)
  waiting for transfers between devices: 30.3 us -> 26.6 us
    ppermute x1, waiting for transfers between devices: 10.2 us -> 6.52 us  [per_device(): partner_normed = lax.ppermute(normed, 'group', there)]
  transfers between devices with their start and end apart: 18 -> 18, of which waited for: 4 -> 4; matrix products, arithmetic and copies ran while one was open for 41% -> 42% of each run, Pallas kernels for 0% -> 0%
where the time goes in v13:
time: 160 us; the launch traced here: 157 us
  matrix products  40.6 us (25%)
  local copies, waits for them, and re-layouts  29 us (18%)
  waiting for transfers between devices  26.6 us (17%)
  blocking collectives  25.4 us (16%)
  between operations  13.7 us (9%)
  other arithmetic  12 us (8%)
  starting transfers between devices  9.5 us (6%)
    all_gather x1, blocking collectives, per_device(): gathered = lax.all_gather(local_kv, 'dev', axis=0, tiled=True)  25.4 us
    dot_general x2, matrix products, feed(): part = jnp.dot(activated, proj_rows, preferred_element_type=jnp.float32)  18.9 us
    unnamed x55, local copies, waits for them, and re-layouts  18.6 us
    dot_general x2, matrix products, feed(): jnp.einsum('tsh,shd->td', activated, bank[1], preferred_element_type=jnp....  9.86 us
    ppermute x1, waiting for transfers between devices, per_device(): returned.append(lax.ppermute(partner_feed, 'group', back))  9.8 us
    ppermute x1, waiting for transfers between devices, ring_issue(): return (lax.ppermute(ahead, 'dev', forward), None)  7.71 us
    ppermute x1, waiting for transfers between devices, per_device(): partner_normed = lax.ppermute(normed, 'group', there)  6.52 us
    slice x3, local copies, waits for them, and re-layouts, absorb(): key_rows = keyval[:, :width_att].reshape(row_count, head_count, head_size)  6.14 us
  transfers between devices with their start and end apart: 18, of which 4 were waited for; matrix products, arithmetic and copies ran while one was open for 42% of the time, Pallas kernels for 0%

profile of v13, /device:TPU:0, one launch (start us, length us, event | category | flops | bytes accessed | tf_op | source)
XLA Modules:
  0.0 156.7 jit_solution(10048853740049609240)
XLA Ops:
  6.5 2.1 %pad_maximum_fusion = bf16[2,96,1600]{2,1,0:T(8,128)(2,1)} fusion(bf16[1,120,1600]{2,1,0:T(8,128)(2,1)} %bitcast.226, bf16[1,120,1600]{2,1,0:T(8,128)(2,1)} %bitcast.228), kind=kLoop, calls=%fused_computation.72 | loop fusion | flops 1228800 | bytes 1382400 | tf_op jit(solution)/shard_map/stack | solution.py:167
  8.7 1.7 %bitcast_dynamic-update-slice_fusion.14 = (bf16[2,16,24,1600]{3,2,1,0:T(8,128)(2,1)}, bf16[2,24,1600]{2,1,0:T(8,128)(2,1)}) fusion(bf16[1,120,1600]{2,1,0:T(8,128)(2,1)} %bitcast.227, bf16[1,120,1600]{2,1,0:T(8,128)(2,1)} %bitcast.229), kind=kLoop, calls=%fused_computation.116 | loop fusion | flops 307199 | bytes 1087488
  10.5 3.0 %collective-permute-start = (bf16[2,24,1600]{2,1,0:T(8,128)(2,1)}, bf16[2,24,1600]{2,1,0:T(8,128)(2,1)}, u32[]{:S(2)}, u32[]{:S(2)}) collective-permute-start(bf16[2,24,1600]{2,1,0:T(8,128)(2,1)} %get-tuple-element.24), channel_id=1, source_target_pairs={{0,4},{1,5},{2,0},{3,1},{4,8},{5,9},{6,2},{7,3},{8,12},{9,13},{10,... | collective-permute-start | bytes 460808 | tf_op jit(solution)/shard_map/ppermute | solution.py:51
  13.5 2.1 %copy.60 = bf16[1,256,1024]{1,2,0:T(8,128)(2,1)} copy(bf16[1,256,1024]{2,1,0:T(8,128)(2,1)} %param.14) | data formatting | bytes 1048576 | tf_op args[1]
  15.5 2.2 %fusion.131 = (bf16[256,1024]{1,0:T(8,128)(2,1)}, bf16[256,1024]{1,0:T(8,128)(2,1)}) fusion(bf16[256,2048]{1,0:T(8,128)(2,1)} %bitcast.230), kind=kLoop, calls=%fused_computation.169 | loop fusion | bytes 2097152 | tf_op jit(solution)/shard_map/slice | solution.py:30
  17.8 2.0 %copy.63 = bf16[256,1024]{0,1:T(8,128)(2,1)} copy(bf16[256,1024]{1,0:T(8,128)(2,1)} %get-tuple-element.27) | data formatting | bytes 1048576 | tf_op jit(solution)/shard_map/slice | solution.py:30
  19.9 0.6 fusion.108
  20.6 0.7 iota_compare_fusion.2
  21.4 0.6 compare_reduce_fusion
  22.6 4.6 %fusion.11 = bf16[8,2048]{1,0:T(8,128)(2,1)S(1)} fusion(bf16[1600,2048]{1,0:T(8,128)(2,1)} %param.18, bf16[1,8,2048]{2,1,0:T(8,128)(2,1)S(1)} %copy-done.12, pred[]{:T(512)} %compare_reduce_fusion, bf16[1,8,1600]{2,1,0:T(8,128)(2,1)S(1)} %copy-done.9, f32[8]{0:T(128)S(1)} %add_sqrt_fusion.1, f32[8]{0:T(128)S(1)} %broadcast_multiply_fusion.1), kind=kOutput, calls=%fused_computation.21 | convolution fusion | flops 52512768 | bytes 6644801 | tf_op jit(solution)/shard_map/dot_general | solution.py:161
  27.2 2.9 %fusion.4 = (f32[16,256]{1,0:T(8,128)S(1)}, f32[16,256,256]{1,2,0:T(8,128)}) fusion(pred[256,256]{0,1:T(8,128)(4,1)S(1)} %fusion.86, bf16[256,16,64]{0,2,1:T(8,128)(2,1)S(1)} %bitcast.224, bf16[256,16,64]{0,2,1:T(8,128)(2,1)S(1)} %bitcast.225), kind=kOutput, calls=%fused_computation.8 | convolution fusion | flops 137359360 | bytes 5324800 | tf_op jit(solution)/shard_map/qhd,khd->hqk/dot_general | solution.py:33
  30.1 2.0 %copy.64 = bf16[256,1024]{0,1:T(8,128)(2,1)} copy(bf16[256,1024]{1,0:T(8,128)(2,1)} %get-tuple-element.28) | data formatting | bytes 1048576 | tf_op jit(solution)/shard_map/slice | solution.py:31
  32.1 2.0 %collective-permute-start.2 = (bf16[2,24,1600]{2,1,0:T(8,128)(2,1)}, bf16[2,24,1600]{2,1,0:T(8,128)(2,1)S(1)}, u32[]{:S(2)}, u32[]{:S(2)}) collective-permute-start(bf16[2,24,1600]{2,1,0:T(8,128)(2,1)} %collective-permute-done), channel_id=1, source_target_pairs={{0,4},{1,5},{2,0},{3,1},{4,8},{5,9},{6,2},{7,3},{8,12},{9,13},{10,... | collective-permute-start | bytes 460808 | tf_op jit(solution)/shard_map/ppermute | solution.py:51
  34.7 1.6 %bitcast_dynamic-update-slice_fusion.13 = bf16[2,16,24,1600]{3,2,1,0:T(8,128)(2,1)} fusion(bf16[2,16,24,1600]{3,2,1,0:T(8,128)(2,1)} %get-tuple-element.23, bf16[2,24,1600]{2,1,0:T(8,128)(2,1)} %collective-permute-done), kind=kLoop, calls=%fused_computation.115 | loop fusion | bytes 319488
  36.3 1.6 %bitcast_dynamic-update-slice_fusion.12 = bf16[2,16,24,1600]{3,2,1,0:T(8,128)(2,1)} fusion(bf16[2,16,24,1600]{3,2,1,0:T(8,128)(2,1)} %bitcast_dynamic-update-slice_fusion.13, bf16[2,24,1600]{2,1,0:T(8,128)(2,1)} %collective-permute-done.1), kind=kLoop, calls=%fused_computation.114 | loop fusion | bytes 319488
  37.9 25.4 %all_gather.9 = bf16[128,2048]{1,0:T(8,128)(2,1)S(1)} all-gather(bf16[8,2048]{1,0:T(8,128)(2,1)S(1)} %fusion.11), channel_id=1, replica_groups=mesh['group'=2,'dev'=16] {'dev'}, dimensions={0}, use_global_device_ids=true | all-gather | bytes 557056 | tf_op jit(solution)/shard_map/all_gather | solution.py:175
  63.3 0.7 copy-done.10
  64.0 0.7 fusion.132
  64.7 1.9 %copy.59 = bf16[128,1024]{0,1:T(8,128)(2,1)} copy(bf16[128,1024]{1,0:T(8,128)(2,1)} %get-tuple-element.30) | data formatting | bytes 524288 | tf_op jit(solution)/shard_map/slice | solution.py:30
  66.5 0.8 copy.61
  67.4 2.0 %collective-permute-start.5 = (bf16[2,24,1600]{2,1,0:T(8,128)(2,1)}, bf16[2,24,1600]{2,1,0:T(8,128)(2,1)S(1)}, u32[]{:S(2)}, u32[]{:S(2)}) collective-permute-start(bf16[2,24,1600]{2,1,0:T(8,128)(2,1)} %collective-permute-done.3), channel_id=1, source_target_pairs={{0,2},{1,3},{2,6},{3,7},{4,0},{5,1},{6,10},{7,11},{8,4},{9,5},{10,... | collective-permute-start | bytes 460808 | tf_op jit(solution)/shard_map/ppermute | solution.py:51
  69.4 1.6 %bitcast_reduce_fusion = (f32[16,256]{1,0:T(8,128)S(1)}, f32[16,128,256]{2,1,0:T(8,128)S(1)}) fusion(bf16[128,16,64]{0,2,1:T(8,128)(2,1)} %bitcast.231, bf16[256,16,64]{0,2,1:T(8,128)(2,1)} %bitcast.223), kind=kOutput, calls=%fused_computation.23 | convolution fusion | flops 68153344 | bytes 2899968 | tf_op jit(solution)/shard_map/qhd,khd->hqk/dot_general | solution.py:33
  71.5 1.0 fusion.5
  72.6 1.1 fusion.34
  74.8 1.1 fusion.133
  76.2 1.0 bitcast_dynamic-update-slice_fusion.11
  77.1 1.1 divide_convert_fusion
  78.2 1.6 %bitcast_dynamic-update-slice_fusion.10 = bf16[2,16,24,1600]{3,2,1,0:T(8,128)(2,1)} fusion(bf16[2,16,24,1600]{3,2,1,0:T(8,128)(2,1)} %bitcast_dynamic-update-slice_fusion.11, bf16[2,24,1600]{2,1,0:T(8,128)(2,1)} %collective-permute-done.3), kind=kLoop, calls=%fused_computation.112 | loop fusion | bytes 319488
  79.8 2.5 %collective-permute-done.5 = bf16[2,24,1600]{2,1,0:T(8,128)(2,1)S(1)} collective-permute-done((bf16[2,24,1600]{2,1,0:T(8,128)(2,1)}, bf16[2,24,1600]{2,1,0:T(8,128)(2,1)S(1)}, u32[]{:S(2)}, u32[]{:S(2)}) %collective-permute-start.5) | collective-permute-done | bytes 153632 | tf_op jit(solution)/shard_map/ppermute | solution.py:51
  82.3 0.7 bitcast_dynamic-update-slice_fusion.9
  83.0 0.7 bitcast_dynamic-update-slice_fusion.8
  83.7 7.7 %collective-permute-done.6 = bf16[2,24,1600]{2,1,0:T(8,128)(2,1)S(1)} collective-permute-done((bf16[2,24,1600]{2,1,0:T(8,128)(2,1)S(1)}, bf16[2,24,1600]{2,1,0:T(8,128)(2,1)S(1)}, u32[]{:S(2)}, u32[]{:S(2)}) %collective-permute-start.6) | collective-permute-done | bytes 153632 | tf_op jit(solution)/shard_map/ppermute | solution.py:53
  91.4 0.7 bitcast_dynamic-update-slice_fusion.7
  92.6 1.6 %bitcast_dynamic-update-slice_fusion.6 = bf16[2,16,24,1600]{3,2,1,0:T(8,128)(2,1)} fusion(bf16[2,16,24,1600]{3,2,1,0:T(8,128)(2,1)} %bitcast_dynamic-update-slice_fusion.7, bf16[2,24,1600]{2,1,0:T(8,128)(2,1)} %collective-permute-done.7), kind=kLoop, calls=%fused_computation.108 | loop fusion | bytes 319488
  94.5 1.6 %bitcast_dynamic-update-slice_fusion.5 = bf16[2,16,24,1600]{3,2,1,0:T(8,128)(2,1)} fusion(bf16[2,16,24,1600]{3,2,1,0:T(8,128)(2,1)} %bitcast_dynamic-update-slice_fusion.6, bf16[2,24,1600]{2,1,0:T(8,128)(2,1)} %collective-permute-done.8), kind=kLoop, calls=%fused_computation.107 | loop fusion | bytes 319488
  96.4 1.6 %bitcast_dynamic-update-slice_fusion.4 = bf16[2,16,24,1600]{3,2,1,0:T(8,128)(2,1)} fusion(bf16[2,16,24,1600]{3,2,1,0:T(8,128)(2,1)} %bitcast_dynamic-update-slice_fusion.5, bf16[2,24,1600]{2,1,0:T(8,128)(2,1)} %collective-permute-done.9), kind=kLoop, calls=%fused_computation.106 | loop fusion | bytes 319488
  98.1 0.7 bitcast_dynamic-update-slice_fusion.3
  98.8 0.7 bitcast_dynamic-update-slice_fusion.2
  99.5 0.7 bitcast_dynamic-update-slice_fusion.1
  100.2 0.7 bitcast_dynamic-update-slice_fusion
  100.9 0.7 bitcast_dynamic-update-slice_fusion.15
  101.5 5.0 %convolution_bitcast_fusion.1 = f32[256,1600]{0,1:T(8,128)} fusion(bf16[2,16,24,1600]{3,2,1,0:T(8,128)(2,1)} %bitcast_dynamic-update-slice_fusion.15, bf16[256,1600]{0,1:T(8,128)(2,1)} %divide_convert_fusion), kind=kOutput, calls=%fused_computation.15 | convolution fusion | flops 630030336 | bytes 4915200 | tf_op jit(solution)/shard_map/tsh,shd->td/dot_general | solution.py:222
  106.5 6.5 %collective-permute-done.15 = bf16[256,1600]{0,1:T(8,128)(2,1)} collective-permute-done((bf16[256,1600]{0,1:T(8,128)(2,1)}, bf16[256,1600]{0,1:T(8,128)(2,1)}, u32[]{:S(2)}, u32[]{:S(2)}) %collective-permute-start.15) | collective-permute-done | bytes 819232 | tf_op jit(solution)/shard_map/ppermute | solution.py:240
  113.0 4.9 %convolution_bitcast_fusion = f32[256,1600]{0,1:T(8,128)} fusion(bf16[2,16,24,1600]{3,2,1,0:T(8,128)(2,1)} %bitcast_dynamic-update-slice_fusion.15, bf16[256,1600]{0,1:T(8,128)(2,1)} %collective-permute-done.15), kind=kOutput, calls=%fused_computation.14 | convolution fusion | flops 630030336 | bytes 4915200 | tf_op jit(solution)/shard_map/tsh,shd->td/dot_general | solution.py:222
  117.9 9.0 %fusion.10 = bf16[256,1600]{0,1:T(8,128)(2,1)} fusion(f32[256,1600]{0,1:T(8,128)} %convolution_bitcast_fusion, bf16[2,1536,1600]{2,1,0:T(8,128)(2,1)} %all-gather.3.cloned.1.call-done, bf16[256,1600]{0,1:T(8,128)(2,1)} %collective-permute-done.15), kind=kOutput, calls=%fused_computation.17 | convolution fusion | flops 2520940544 | bytes 13107200 | tf_op jit(solution)/shard_map/dot_general | solution.py:232
  127.5 9.8 %fusion.9 = f32[256,1600]{0,1:T(8,128)} fusion(f32[256,1600]{0,1:T(8,128)} %copy-done.2, f32[256,1600]{0,1:T(8,128)} %convolution_bitcast_fusion.1, bf16[2,1536,1600]{2,1,0:T(8,128)(2,1)} %all-gather.3.cloned.1.call-done, bf16[256,1600]{0,1:T(8,128)(2,1)} %divide_convert_fusion), kind=kOutput, calls=%fused_computation.16 | convolution fusion | flops 2520940544 | bytes 15564800 | tf_op jit(solution)/shard_map/dot_general | solution.py:232
  137.4 9.8 %collective-permute-done.16 = bf16[256,1600]{0,1:T(8,128)(2,1)} collective-permute-done((bf16[256,1600]{0,1:T(8,128)(2,1)}, bf16[256,1600]{0,1:T(8,128)(2,1)}, u32[]{:S(2)}, u32[]{:S(2)}) %collective-permute-start.16) | collective-permute-done | bytes 819232 | tf_op jit(solution)/shard_map/ppermute | solution.py:242
  147.2 2.7 %fusion.47 = bf16[1,256,1600]{1,2,0:T(8,128)(2,1)} fusion(f32[256,1600]{0,1:T(8,128)} %fusion.9, bf16[256,1600]{0,1:T(8,128)(2,1)} %collective-permute-done.16, pred[256]{0:T(512)(128)(4,1)S(1)} %copy-done.14), kind=kLoop, calls=%fused_computation.61 | loop fusion | flops 1638400 | bytes 3277056 | tf_op jit(solution)/shard_map/broadcast_in_dim | solution.py:247
  (83 shorter events, 5.1 us)
Async XLA Ops:
  6.5 67.8 %copy-start = (bf16[1024,1600]{0,1:T(8,128)(2,1)S(1)}, bf16[1024,1600]{0,1:T(8,128)(2,1)}, u32[]{:S(2)}) copy-start(bf16[1024,1600]{0,1:T(8,128)(2,1)} %param.19) | copy-start | bytes 9830404
  6.5 111.4 %all-gather.3.cloned.1.call-start = ((), (), s32[]{:S(2)}) async-start(), calls=%async_computation | async-start | bytes 10862592 | tf_op jit(solution)/shard_map/all_gather | solution.py:211
  8.7 11.2 %copy-start.16 = (s32[1,16]{1,0:T(1,128)S(1)}, s32[1,16]{1,0:T(1,128)}, u32[]{:S(2)}) copy-start(s32[1,16]{1,0:T(1,128)} %param.22) | copy-start | bytes 196
  8.7 11.2 %copy-start.17 = (s32[1,16]{1,0:T(1,128)S(1)}, s32[1,16]{1,0:T(1,128)}, u32[]{:S(2)}) copy-start(s32[1,16]{1,0:T(1,128)} %param.23) | copy-start | bytes 196
  8.7 12.5 %copy-start.18 = (s32[1,16]{1,0:T(1,128)S(1)}, s32[1,16]{1,0:T(1,128)}, u32[]{:S(2)}) copy-start(s32[1,16]{1,0:T(1,128)} %param.24) | copy-start | bytes 196
  8.7 12.5 %copy-start.19 = (s32[1,2]{1,0:T(1,128)S(1)}, s32[1,2]{1,0:T(1,128)}, u32[]{:S(2)}) copy-start(s32[1,2]{1,0:T(1,128)} %param.25) | copy-start | bytes 28
  8.7 13.4 %copy-start.9 = (bf16[1,8,1600]{2,1,0:T(8,128)(2,1)S(1)}, bf16[1,8,1600]{2,1,0:T(8,128)(2,1)}, u32[]{:S(2)}) copy-start(bf16[1,8,1600]{2,1,0:T(8,128)(2,1)} %param.17) | copy-start | bytes 76804
  8.7 13.8 %copy-start.12 = (bf16[1,8,2048]{2,1,0:T(8,128)(2,1)S(1)}, bf16[1,8,2048]{2,1,0:T(8,128)(2,1)}, u32[]{:S(2)}) copy-start(bf16[1,8,2048]{2,1,0:T(8,128)(2,1)} %param.16) | copy-start | bytes 98308
  10.5 21.7 %collective-permute-start = (bf16[2,24,1600]{2,1,0:T(8,128)(2,1)}, bf16[2,24,1600]{2,1,0:T(8,128)(2,1)}, u32[]{:S(2)}, u32[]{:S(2)}) collective-permute-start(bf16[2,24,1600]{2,1,0:T(8,128)(2,1)} %get-tuple-element.24), channel_id=1, source_target_pairs={{0,4},{1,5},{2,0},{3,1},{4,8},{5,9},{6,2},{7,3},{8,12},{9,13},{10,... | collective-permute-start | bytes 460808 | tf_op jit(solution)/shard_map/ppermute | solution.py:51
  13.5 18.6 %collective-permute-start.1 = (bf16[2,24,1600]{2,1,0:T(8,128)(2,1)}, bf16[2,24,1600]{2,1,0:T(8,128)(2,1)}, u32[]{:S(2)}, u32[]{:S(2)}) collective-permute-start(bf16[2,24,1600]{2,1,0:T(8,128)(2,1)} %get-tuple-element.24), channel_id=1, source_target_pairs={{0,2},{1,3},{2,6},{3,7},{4,0},{5,1},{6,10},{7,11},{8,4},{9,5},{10,... | collective-permute-start | bytes 460808 | tf_op jit(solution)/shard_map/ppermute | solution.py:51
  13.5 78.6 %collective-permute-start.7 = (bf16[2,24,1600]{2,1,0:T(8,128)(2,1)}, bf16[2,24,1600]{2,1,0:T(8,128)(2,1)}, u32[]{:S(2)}, u32[]{:S(2)}) collective-permute-start(bf16[2,24,1600]{2,1,0:T(8,128)(2,1)} %get-tuple-element.24), channel_id=1, source_target_pairs={{0,1},{1,0},{2,3},{3,2},{4,5},{5,4},{6,7},{7,6},{8,9},{9,8},{10,11... | collective-permute-start | bytes 460808 | tf_op jit(solution)/shard_map/ppermute | solution.py:78
  21.2 1.2 copy-start.13
  22.5 4.6 %copy-start.5 = (pred[256,256]{0,1:T(8,128)(4,1)}, pred[256,256]{0,1:T(8,128)(4,1)S(1)}, u32[]{:S(2)}) copy-start(pred[256,256]{0,1:T(8,128)(4,1)S(1)} %fusion.86) | copy-start | bytes 196612
  22.6 4.6 %copy-start.3 = (bf16[1,256,1024]{1,2,0:T(8,128)(2,1)S(1)}, bf16[1,256,1024]{1,2,0:T(8,128)(2,1)}, u32[]{:S(2)}) copy-start(bf16[1,256,1024]{1,2,0:T(8,128)(2,1)} %copy.60) | copy-start | bytes 1572868
  22.6 4.6 %copy-start.4 = (bf16[256,1024]{0,1:T(8,128)(2,1)S(1)}, bf16[256,1024]{0,1:T(8,128)(2,1)}, u32[]{:S(2)}) copy-start(bf16[256,1024]{0,1:T(8,128)(2,1)} %copy.63) | copy-start | bytes 1572868
  32.1 31.2 %collective-permute-start.2 = (bf16[2,24,1600]{2,1,0:T(8,128)(2,1)}, bf16[2,24,1600]{2,1,0:T(8,128)(2,1)S(1)}, u32[]{:S(2)}, u32[]{:S(2)}) collective-permute-start(bf16[2,24,1600]{2,1,0:T(8,128)(2,1)} %collective-permute-done), channel_id=1, source_target_pairs={{0,4},{1,5},{2,0},{3,1},{4,8},{5,9},{6,2},{7,3},{8,12},{9,13},{10,... | collective-permute-start | bytes 460808 | tf_op jit(solution)/shard_map/ppermute | solution.py:51
  34.1 60.1 %collective-permute-start.8 = (bf16[2,24,1600]{2,1,0:T(8,128)(2,1)}, bf16[2,24,1600]{2,1,0:T(8,128)(2,1)}, u32[]{:S(2)}, u32[]{:S(2)}) collective-permute-start(bf16[2,24,1600]{2,1,0:T(8,128)(2,1)} %collective-permute-done), channel_id=1, source_target_pairs={{0,1},{1,0},{2,3},{3,2},{4,5},{5,4},{6,7},{7,6},{8,9},{9,8},{10,11... | collective-permute-start | bytes 460808 | tf_op jit(solution)/shard_map/ppermute | solution.py:78
  34.4 29.5 %collective-permute-start.3 = (bf16[2,24,1600]{2,1,0:T(8,128)(2,1)}, bf16[2,24,1600]{2,1,0:T(8,128)(2,1)}, u32[]{:S(2)}, u32[]{:S(2)}) collective-permute-start(bf16[2,24,1600]{2,1,0:T(8,128)(2,1)} %collective-permute-done.1), channel_id=1, source_target_pairs={{0,2},{1,3},{2,6},{3,7},{4,0},{5,1},{6,10},{7,11},{8,4},{9,5},{10,... | collective-permute-start | bytes 460808 | tf_op jit(solution)/shard_map/ppermute | solution.py:51
  34.7 61.3 %collective-permute-start.9 = (bf16[2,24,1600]{2,1,0:T(8,128)(2,1)}, bf16[2,24,1600]{2,1,0:T(8,128)(2,1)}, u32[]{:S(2)}, u32[]{:S(2)}) collective-permute-start(bf16[2,24,1600]{2,1,0:T(8,128)(2,1)} %collective-permute-done.1), channel_id=1, source_target_pairs={{0,1},{1,0},{2,3},{3,2},{4,5},{5,4},{6,7},{7,6},{8,9},{9,8},{10,11... | collective-permute-start | bytes 460808 | tf_op jit(solution)/shard_map/ppermute | solution.py:78
  63.3 0.7 copy-start.10
  67.4 4.1 %copy-start.1 = (f32[16,256,256]{1,2,0:T(8,128)S(1)}, f32[16,256,256]{1,2,0:T(8,128)}, u32[]{:S(2)}) copy-start(f32[16,256,256]{1,2,0:T(8,128)} %get-tuple-element.37) | copy-start | bytes 12582916
  67.4 4.1 %copy-start.6 = (pred[256,256]{0,1:T(8,128)(4,1)S(1)}, pred[256,256]{0,1:T(8,128)(4,1)}, u32[]{:S(2)}) copy-start(pred[256,256]{0,1:T(8,128)(4,1)} %copy-done.5) | copy-start | bytes 196612
  67.4 12.4 %collective-permute-start.4 = (bf16[2,24,1600]{2,1,0:T(8,128)(2,1)}, bf16[2,24,1600]{2,1,0:T(8,128)(2,1)S(1)}, u32[]{:S(2)}, u32[]{:S(2)}) collective-permute-start(bf16[2,24,1600]{2,1,0:T(8,128)(2,1)} %copy-done.10), channel_id=1, source_target_pairs={{0,4},{1,5},{2,0},{3,1},{4,8},{5,9},{6,2},{7,3},{8,12},{9,13},{10,... | collective-permute-start | bytes 460808 | tf_op jit(solution)/shard_map/ppermute | solution.py:51
  67.4 14.9 %collective-permute-start.5 = (bf16[2,24,1600]{2,1,0:T(8,128)(2,1)}, bf16[2,24,1600]{2,1,0:T(8,128)(2,1)S(1)}, u32[]{:S(2)}, u32[]{:S(2)}) collective-permute-start(bf16[2,24,1600]{2,1,0:T(8,128)(2,1)} %collective-permute-done.3), channel_id=1, source_target_pairs={{0,2},{1,3},{2,6},{3,7},{4,0},{5,1},{6,10},{7,11},{8,4},{9,5},{10,... | collective-permute-start | bytes 460808 | tf_op jit(solution)/shard_map/ppermute | solution.py:51
  71.5 1.1 copy-start.7
  72.5 1.1 copy-start.8
  73.7 1.1 copy-start.15
  74.8 1.4 copy-start.11
  75.9 7.7 %copy-start.2 = (f32[256,1600]{0,1:T(8,128)}, f32[256,1600]{0,1:T(8,128)S(1)}, u32[]{:S(2)}) copy-start(f32[256,1600]{0,1:T(8,128)S(1)} %get-tuple-element.39) | copy-start | bytes 4915204
  79.8 18.1 %collective-permute-start.10 = (bf16[2,24,1600]{2,1,0:T(8,128)(2,1)S(1)}, bf16[2,24,1600]{2,1,0:T(8,128)(2,1)S(1)}, u32[]{:S(2)}, u32[]{:S(2)}) collective-permute-start(bf16[2,24,1600]{2,1,0:T(8,128)(2,1)S(1)} %copy-done.11), channel_id=1, source_target_pairs={{0,1},{1,0},{2,3},{3,2},{4,5},{5,4},{6,7},{7,6},{8,9},{9,8},{10,11... | collective-permute-start | bytes 460808 | tf_op jit(solution)/shard_map/ppermute | solution.py:78
  82.3 9.1 %collective-permute-start.6 = (bf16[2,24,1600]{2,1,0:T(8,128)(2,1)S(1)}, bf16[2,24,1600]{2,1,0:T(8,128)(2,1)S(1)}, u32[]{:S(2)}, u32[]{:S(2)}) collective-permute-start(bf16[2,24,1600]{2,1,0:T(8,128)(2,1)S(1)} %collective-permute-done.4), channel_id=1, source_target_pairs={{0,4},{1,5},{2,0},{3,1},{4,8},{5,9},{6,2},{7,3},{8,12},{9,13},{10,... | collective-permute-start | bytes 460808 | tf_op jit(solution)/shard_map/ppermute | solution.py:53
  91.4 7.4 %collective-permute-start.11 = (bf16[2,24,1600]{2,1,0:T(8,128)(2,1)}, bf16[2,24,1600]{2,1,0:T(8,128)(2,1)S(1)}, u32[]{:S(2)}, u32[]{:S(2)}) collective-permute-start(bf16[2,24,1600]{2,1,0:T(8,128)(2,1)} %collective-permute-done.3), channel_id=1, source_target_pairs={{0,1},{1,0},{2,3},{3,2},{4,5},{5,4},{6,7},{7,6},{8,9},{9,8},{10,11... | collective-permute-start | bytes 460808 | tf_op jit(solution)/shard_map/ppermute | solution.py:78
  92.1 21.0 %collective-permute-start.15 = (bf16[256,1600]{0,1:T(8,128)(2,1)}, bf16[256,1600]{0,1:T(8,128)(2,1)}, u32[]{:S(2)}, u32[]{:S(2)}) collective-permute-start(bf16[256,1600]{0,1:T(8,128)(2,1)} %divide_convert_fusion), channel_id=1, source_target_pairs={{0,16},{16,0},{1,17},{17,1},{2,18},{18,2},{3,19},{19,3},{4,20},{20... | collective-permute-start | bytes 2457608 | tf_op jit(solution)/shard_map/ppermute | solution.py:240
  94.2 5.3 %collective-permute-start.12 = (bf16[2,24,1600]{2,1,0:T(8,128)(2,1)S(1)}, bf16[2,24,1600]{2,1,0:T(8,128)(2,1)S(1)}, u32[]{:S(2)}, u32[]{:S(2)}) collective-permute-start(bf16[2,24,1600]{2,1,0:T(8,128)(2,1)S(1)} %collective-permute-done.4), channel_id=1, source_target_pairs={{0,1},{1,0},{2,3},{3,2},{4,5},{5,4},{6,7},{7,6},{8,9},{9,8},{10,11... | collective-permute-start | bytes 460808 | tf_op jit(solution)/shard_map/ppermute | solution.py:78
  96.0 4.1 %collective-permute-start.13 = (bf16[2,24,1600]{2,1,0:T(8,128)(2,1)S(1)}, bf16[2,24,1600]{2,1,0:T(8,128)(2,1)S(1)}, u32[]{:S(2)}, u32[]{:S(2)}) collective-permute-start(bf16[2,24,1600]{2,1,0:T(8,128)(2,1)S(1)} %collective-permute-done.5), channel_id=1, source_target_pairs={{0,1},{1,0},{2,3},{3,2},{4,5},{5,4},{6,7},{7,6},{8,9},{9,8},{10,11... | collective-permute-start | bytes 460808 | tf_op jit(solution)/shard_map/ppermute | solution.py:78
  97.9 2.9 %collective-permute-start.14 = (bf16[2,24,1600]{2,1,0:T(8,128)(2,1)S(1)}, bf16[2,24,1600]{2,1,0:T(8,128)(2,1)S(1)}, u32[]{:S(2)}, u32[]{:S(2)}) collective-permute-start(bf16[2,24,1600]{2,1,0:T(8,128)(2,1)S(1)} %collective-permute-done.6), channel_id=1, source_target_pairs={{0,1},{1,0},{2,3},{3,2},{4,5},{5,4},{6,7},{7,6},{8,9},{9,8},{10,11... | collective-permute-start | bytes 460808 | tf_op jit(solution)/shard_map/ppermute | solution.py:78
  127.0 20.2 %copy-start.14 = (pred[256]{0:T(512)(128)(4,1)S(1)}, pred[256]{0:T(512)(128)(4,1)}, u32[]{:S(2)}) copy-start(pred[256]{0:T(512)(128)(4,1)} %copy-done.13) | copy-start | bytes 772
  127.0 20.2 %collective-permute-start.16 = (bf16[256,1600]{0,1:T(8,128)(2,1)}, bf16[256,1600]{0,1:T(8,128)(2,1)}, u32[]{:S(2)}, u32[]{:S(2)}) collective-permute-start(bf16[256,1600]{0,1:T(8,128)(2,1)} %fusion.10), channel_id=1, source_target_pairs={{0,16},{16,0},{1,17},{17,1},{2,18},{18,2},{3,19},{19,3},{4,20},{20... | collective-permute-start | bytes 2457608 | tf_op jit(solution)/shard_map/ppermute | solution.py:242
Sparse Core Ops, SparseCore 0:
  9.6 95.9 all-gather.2

commit v14 on v13

--- a/solution.py
+++ b/solution.py
@@ -74,9 +74,8 @@
     swap = plan[2]
     while state[3] <= plan[3]:
         state, _ = ring_step(state, plan, jnp.zeros((), jnp.float32))
-    pieces = state[2]
-    pieces = pieces + [lax.ppermute(piece, "dev", swap) for piece in pieces]
-    return jnp.stack(pieces, axis=1)
+    mine = jnp.stack(state[2], axis=1)
+    return jnp.concatenate([mine, lax.ppermute(mine, "dev", swap)], axis=1)
 
 
 def plan_ring(mesh):
@@ -200,8 +199,6 @@
     projected = jnp.dot(attended, out_weight, preferred_element_type=jnp.float32)
     residual = suffix_x[0].astype(jnp.float32) + projected
     normed = normalize(residual).astype(jnp.bfloat16)
-    if use_ring:
-        ring, _ = ring_step(ring, ring_plan, normed)
     group_count = lax.axis_size("group")
     if not use_ring:
         banks = [lax.all_gather(both, "dev", axis=1)]

time: 160 us -> 160 us (level)
  the two profiles are of different devices: /device:TPU:0 before, /device:TPU:4 now
where the time goes in v14:
time: 160 us; the launch traced here: 159 us
  matrix products  41 us (26%)
  waiting for transfers between devices  35.2 us (22%)
  local copies, waits for them, and re-layouts  26.3 us (16%)
  blocking collectives  22.6 us (14%)
  between operations  13.6 us (8%)
  other arithmetic  10.9 us (7%)
  starting transfers between devices  9.41 us (6%)
    all_gather x1, blocking collectives, per_device(): gathered = lax.all_gather(local_kv, 'dev', axis=0, tiled=True)  22.6 us
    dot_general x2, matrix products, feed(): part = jnp.dot(activated, proj_rows, preferred_element_type=jnp.float32)  17.9 us
    ppermute x1, waiting for transfers between devices, per_device(): partner_normed = lax.ppermute(normed, 'group', there)  16.3 us
    unnamed x48, local copies, waits for them, and re-layouts  14.7 us
    ppermute x1, waiting for transfers between devices, ring_issue(): return (lax.ppermute(ahead, 'dev', forward), None)  11.4 us
    dot_general x2, matrix products, feed(): jnp.einsum('tsh,shd->td', activated, bank[1], preferred_element_type=jnp....  11.1 us
    slice x3, local copies, waits for them, and re-layouts, absorb(): key_rows = keyval[:, :width_att].reshape(row_count, head_count, head_size)  6.11 us
    ppermute x1, waiting for transfers between devices, per_device(): returned.append(lax.ppermute(partner_feed, 'group', back))  5.02 us
  transfers between devices with their start and end apart: 11, of which 4 were waited for; matrix products, arithmetic and copies ran while one was open for 36% of the time, Pallas kernels for 0%

profile of v14, /device:TPU:4, one launch (start us, length us, event | category | flops | bytes accessed | tf_op | source)
XLA Modules:
  0.0 159.1 jit_solution(3146258968789961114)
XLA Ops:
  6.5 2.1 %pad_maximum_fusion = bf16[2,96,1600]{2,1,0:T(8,128)(2,1)} fusion(bf16[1,120,1600]{2,1,0:T(8,128)(2,1)} %bitcast.209, bf16[1,120,1600]{2,1,0:T(8,128)(2,1)} %bitcast.211), kind=kLoop, calls=%fused_computation.64 | loop fusion | flops 1228800 | bytes 1382400 | tf_op jit(solution)/shard_map/stack | solution.py:166
  8.7 1.6 %bitcast_dynamic-update-slice_fusion.12 = (bf16[2,8,24,1600]{3,2,1,0:T(8,128)(2,1)}, bf16[2,24,1600]{2,1,0:T(8,128)(2,1)S(1)}) fusion(bf16[1,120,1600]{2,1,0:T(8,128)(2,1)} %bitcast.210, bf16[1,120,1600]{2,1,0:T(8,128)(2,1)} %bitcast.212), kind=kLoop, calls=%fused_computation.106 | loop fusion | flops 307199 | bytes 1081344
  10.3 2.0 %collective-permute-start.1 = (bf16[2,24,1600]{2,1,0:T(8,128)(2,1)S(1)}, bf16[2,24,1600]{2,1,0:T(8,128)(2,1)}, u32[]{:S(2)}, u32[]{:S(2)}) collective-permute-start(bf16[2,24,1600]{2,1,0:T(8,128)(2,1)S(1)} %get-tuple-element.24), channel_id=1, source_target_pairs={{0,2},{1,3},{2,6},{3,7},{4,0},{5,1},{6,10},{7,11},{8,4},{9,5},{10,... | collective-permute-start | bytes 460808 | tf_op jit(solution)/shard_map/ppermute | solution.py:51
  12.3 2.1 %copy.58 = bf16[1,256,1024]{1,2,0:T(8,128)(2,1)} copy(bf16[1,256,1024]{2,1,0:T(8,128)(2,1)} %param.14) | data formatting | bytes 1048576 | tf_op args[1]
  14.4 2.2 %fusion.123 = (bf16[256,1024]{1,0:T(8,128)(2,1)}, bf16[256,1024]{1,0:T(8,128)(2,1)}) fusion(bf16[256,2048]{1,0:T(8,128)(2,1)} %bitcast.213), kind=kLoop, calls=%fused_computation.162 | loop fusion | bytes 2097152 | tf_op jit(solution)/shard_map/slice | solution.py:30
  16.7 2.1 %copy.61 = bf16[256,1024]{0,1:T(8,128)(2,1)} copy(bf16[256,1024]{1,0:T(8,128)(2,1)} %get-tuple-element.27) | data formatting | bytes 1048576 | tf_op jit(solution)/shard_map/slice | solution.py:30
  18.8 0.6 fusion.100
  19.5 0.7 iota_compare_fusion.2
  20.4 0.6 compare_reduce_fusion
  21.5 4.6 %fusion.11 = bf16[8,2048]{1,0:T(8,128)(2,1)S(1)} fusion(bf16[1600,2048]{1,0:T(8,128)(2,1)} %param.18, bf16[1,8,2048]{2,1,0:T(8,128)(2,1)S(1)} %copy-done.11, pred[]{:T(512)} %compare_reduce_fusion, bf16[1,8,1600]{2,1,0:T(8,128)(2,1)S(1)} %copy-done.10, f32[8]{0:T(128)S(1)} %add_sqrt_fusion.1, f32[8]{0:T(128)S(1)} %broadcast_multiply_fusion.1), kind=kOutput, calls=%fused_computation.21 | convolution fusion | flops 52512768 | bytes 6644801 | tf_op jit(solution)/shard_map/dot_general | solution.py:160
  26.1 0.7 bitcast_dynamic-update-slice_fusion.13
  26.8 2.9 %fusion.4 = (f32[16,256]{1,0:T(8,128)S(1)}, f32[16,256,256]{1,2,0:T(8,128)}) fusion(pred[256,256]{0,1:T(8,128)(4,1)S(1)} %fusion.78, bf16[256,16,64]{0,2,1:T(8,128)(2,1)S(1)} %bitcast.207, bf16[256,16,64]{0,2,1:T(8,128)(2,1)S(1)} %bitcast.208), kind=kOutput, calls=%fused_computation.8 | convolution fusion | flops 137359360 | bytes 5324800 | tf_op jit(solution)/shard_map/qhd,khd->hqk/dot_general | solution.py:33
  29.7 2.0 %copy.62 = bf16[256,1024]{0,1:T(8,128)(2,1)} copy(bf16[256,1024]{1,0:T(8,128)(2,1)} %get-tuple-element.28) | data formatting | bytes 1048576 | tf_op jit(solution)/shard_map/slice | solution.py:31
  31.8 2.0 %collective-permute-start.3 = (bf16[2,24,1600]{2,1,0:T(8,128)(2,1)}, bf16[2,24,1600]{2,1,0:T(8,128)(2,1)}, u32[]{:S(2)}, u32[]{:S(2)}) collective-permute-start(bf16[2,24,1600]{2,1,0:T(8,128)(2,1)} %collective-permute-done.1), channel_id=1, source_target_pairs={{0,2},{1,3},{2,6},{3,7},{4,0},{5,1},{6,10},{7,11},{8,4},{9,5},{10,... | collective-permute-start | bytes 460808 | tf_op jit(solution)/shard_map/ppermute | solution.py:51
  33.7 1.7 %bitcast_dynamic-update-slice_fusion.10 = (bf16[2,8,24,1600]{3,2,1,0:T(8,128)(2,1)}, bf16[2,16,24,1600]{3,2,1,0:T(8,128)(2,1)}) fusion(bf16[2,8,24,1600]{3,2,1,0:T(8,128)(2,1)} %get-tuple-element.23, bf16[2,24,1600]{2,1,0:T(8,128)(2,1)} %collective-permute-done, bf16[2,16,24,1600]{3,2,1,0:T(8,128)(2,1)} %bitcast_dynamic-update-slice_fusion.13), kind=kLoop, calls=%fused_computation.104 | loop fusion | bytes 479232
  35.4 1.7 %bitcast_dynamic-update-slice_fusion.8 = (bf16[2,8,24,1600]{3,2,1,0:T(8,128)(2,1)}, bf16[2,16,24,1600]{3,2,1,0:T(8,128)(2,1)}) fusion(bf16[2,8,24,1600]{3,2,1,0:T(8,128)(2,1)} %get-tuple-element.43, bf16[2,24,1600]{2,1,0:T(8,128)(2,1)} %collective-permute-done.1, bf16[2,16,24,1600]{3,2,1,0:T(8,128)(2,1)} %get-tuple-element.44), kind=kLoop, calls=%fused_computation.102 | loop fusion | bytes 479232
  37.1 22.6 %all_gather.9 = bf16[128,2048]{1,0:T(8,128)(2,1)S(1)} all-gather(bf16[8,2048]{1,0:T(8,128)(2,1)S(1)} %fusion.11), channel_id=1, replica_groups=mesh['group'=2,'dev'=16] {'dev'}, dimensions={0}, use_global_device_ids=true | all-gather | bytes 557056 | tf_op jit(solution)/shard_map/all_gather | solution.py:174
  59.7 2.7 %collective-permute-start.4 = (bf16[2,24,1600]{2,1,0:T(8,128)(2,1)}, bf16[2,24,1600]{2,1,0:T(8,128)(2,1)}, u32[]{:S(2)}, u32[]{:S(2)}) collective-permute-start(bf16[2,24,1600]{2,1,0:T(8,128)(2,1)} %collective-permute-done.2), channel_id=1, source_target_pairs={{0,4},{1,5},{2,0},{3,1},{4,8},{5,9},{6,2},{7,3},{8,12},{9,13},{10,... | collective-permute-start | bytes 460808 | tf_op jit(solution)/shard_map/ppermute | solution.py:51
  62.5 0.7 fusion.124
  63.2 1.8 %copy.57 = bf16[128,1024]{0,1:T(8,128)(2,1)} copy(bf16[128,1024]{1,0:T(8,128)(2,1)} %get-tuple-element.30) | data formatting | bytes 524288 | tf_op jit(solution)/shard_map/slice | solution.py:30
  65.0 0.8 copy.59
  65.9 1.8 %bitcast_reduce_fusion = (f32[16,256]{1,0:T(8,128)S(1)}, f32[16,128,256]{2,1,0:T(8,128)S(1)}) fusion(bf16[128,16,64]{0,2,1:T(8,128)(2,1)} %bitcast.214, bf16[256,16,64]{0,2,1:T(8,128)(2,1)} %bitcast.206), kind=kOutput, calls=%fused_computation.23 | convolution fusion | flops 68153344 | bytes 2899968 | tf_op jit(solution)/shard_map/qhd,khd->hqk/dot_general | solution.py:33
  67.7 0.4 fusion.16
  68.1 0.3 copy-done.1
  68.3 1.0 fusion.5
  69.4 1.1 fusion.34
  70.5 0.6 fusion.41
  71.1 0.5 copy-done.15
  71.6 1.1 fusion.125
  72.9 1.8 %bitcast_dynamic-update-slice_fusion.6 = (bf16[2,8,24,1600]{3,2,1,0:T(8,128)(2,1)S(1)}, bf16[2,16,24,1600]{3,2,1,0:T(8,128)(2,1)}) fusion(bf16[2,8,24,1600]{3,2,1,0:T(8,128)(2,1)S(1)} %copy-done.12, bf16[2,24,1600]{2,1,0:T(8,128)(2,1)} %collective-permute-done.2, bf16[2,16,24,1600]{3,2,1,0:T(8,128)(2,1)} %get-tuple-element.42), kind=kLoop, calls=%fused_computation.100 | loop fusion | bytes 479232
  74.8 1.6 %bitcast_dynamic-update-slice_fusion.4 = (bf16[2,8,24,1600]{3,2,1,0:T(8,128)(2,1)S(1)}, bf16[2,16,24,1600]{3,2,1,0:T(8,128)(2,1)}) fusion(bf16[2,8,24,1600]{3,2,1,0:T(8,128)(2,1)S(1)} %get-tuple-element.39, bf16[2,24,1600]{2,1,0:T(8,128)(2,1)} %collective-permute-done.3, bf16[2,16,24,1600]{3,2,1,0:T(8,128)(2,1)} %get-tuple-element.40), kind=kLoop, calls=%fused_computation.98 | loop fusion | bytes 479232
  76.3 0.2 multiply_reduce_fusion
  76.6 2.3 %collective-permute-start.6 = (bf16[2,24,1600]{2,1,0:T(8,128)(2,1)}, bf16[2,24,1600]{2,1,0:T(8,128)(2,1)S(1)}, u32[]{:S(2)}, u32[]{:S(2)}) collective-permute-start(bf16[2,24,1600]{2,1,0:T(8,128)(2,1)} %collective-permute-done.4), channel_id=1, source_target_pairs={{0,4},{1,5},{2,0},{3,1},{4,8},{5,9},{6,2},{7,3},{8,12},{9,13},{10,... | collective-permute-start | bytes 460808 | tf_op jit(solution)/shard_map/ppermute | solution.py:53
  78.9 1.6 %bitcast_dynamic-update-slice_fusion.2 = (bf16[2,8,24,1600]{3,2,1,0:T(8,128)(2,1)S(1)}, bf16[2,16,24,1600]{3,2,1,0:T(8,128)(2,1)}) fusion(bf16[2,8,24,1600]{3,2,1,0:T(8,128)(2,1)S(1)} %get-tuple-element.37, bf16[2,24,1600]{2,1,0:T(8,128)(2,1)} %collective-permute-done.4, bf16[2,16,24,1600]{3,2,1,0:T(8,128)(2,1)} %get-tuple-element.38), kind=kLoop, calls=%fused_computation.96 | loop fusion | bytes 479232
  80.5 1.6 %bitcast_dynamic-update-slice_fusion = (bf16[2,8,24,1600]{3,2,1,0:T(8,128)(2,1)S(1)}, bf16[2,16,24,1600]{3,2,1,0:T(8,128)(2,1)}) fusion(bf16[2,8,24,1600]{3,2,1,0:T(8,128)(2,1)S(1)} %get-tuple-element.35, bf16[2,24,1600]{2,1,0:T(8,128)(2,1)} %collective-permute-done.5, bf16[2,16,24,1600]{3,2,1,0:T(8,128)(2,1)} %get-tuple-element.36), kind=kLoop, calls=%fused_computation.94 | loop fusion | bytes 479232
  82.1 11.4 %collective-permute-done.6 = bf16[2,24,1600]{2,1,0:T(8,128)(2,1)S(1)} collective-permute-done((bf16[2,24,1600]{2,1,0:T(8,128)(2,1)}, bf16[2,24,1600]{2,1,0:T(8,128)(2,1)S(1)}, u32[]{:S(2)}, u32[]{:S(2)}) %collective-permute-start.6) | collective-permute-done | bytes 153632 | tf_op jit(solution)/shard_map/ppermute | solution.py:53
  93.5 0.7 bitcast_dynamic-update-slice_fusion.15
  94.5 0.8 copy-done.4
  95.3 2.5 %collective-permute-done.7 = bf16[2,8,24,1600]{3,2,1,0:T(8,128)(2,1)S(1)} collective-permute-done((bf16[2,8,24,1600]{3,2,1,0:T(8,128)(2,1)S(1)}, bf16[2,8,24,1600]{3,2,1,0:T(8,128)(2,1)S(1)}, u32[]{:S(2)}, u32[]{:S(2)}) %collective-permute-start.7) | collective-permute-done | bytes 1228832 | tf_op jit(solution)/shard_map/ppermute | solution.py:78
  97.8 1.1 constant_dynamic-update-slice_fusion
  98.9 16.3 %collective-permute-done.8 = bf16[256,1600]{0,1:T(8,128)(2,1)} collective-permute-done((bf16[256,1600]{0,1:T(8,128)(2,1)S(1)}, bf16[256,1600]{0,1:T(8,128)(2,1)}, u32[]{:S(2)}, u32[]{:S(2)}) %collective-permute-start.8) | collective-permute-done | bytes 819232 | tf_op jit(solution)/shard_map/ppermute | solution.py:237
  115.2 8.9 %fusion.2 = f32[256,1600]{0,1:T(8,128)} fusion(bf16[2,1536,1600]{2,1,0:T(8,128)(2,1)} %all-gather.3.cloned.1.call-done, bf16[256,1600]{0,1:T(8,128)(2,1)} %collective-permute-done.8), kind=kOutput, calls=%fused_computation.4 | convolution fusion | flops 2520121344 | bytes 12288000 | tf_op jit(solution)/shard_map/dot_general | solution.py:229
  124.2 5.1 %fusion.10 = bf16[256,1600]{0,1:T(8,128)(2,1)} fusion(f32[256,1600]{0,1:T(8,128)} %fusion.2, bf16[2,16,24,1600]{3,2,1,0:T(8,128)(2,1)} %constant_dynamic-update-slice_fusion, bf16[256,1600]{0,1:T(8,128)(2,1)} %collective-permute-done.8), kind=kOutput, calls=%fused_computation.17 | convolution fusion | flops 630849536 | bytes 5734400 | tf_op jit(solution)/shard_map/tsh,shd->td/dot_general | solution.py:219
  129.3 0.3 collective-permute-start.9
  129.6 8.9 %fusion.3 = f32[256,1600]{0,1:T(8,128)} fusion(bf16[2,1536,1600]{2,1,0:T(8,128)(2,1)} %all-gather.3.cloned.1.call-done, bf16[256,1600]{0,1:T(8,128)(2,1)} %copy-done.4), kind=kOutput, calls=%fused_computation.5 | convolution fusion | flops 2520121344 | bytes 12288000 | tf_op jit(solution)/shard_map/dot_general | solution.py:229
  138.5 6.0 %fusion.8 = f32[256,1600]{0,1:T(8,128)} fusion(f32[256,1600]{0,1:T(8,128)} %copy-done.2, f32[256,1600]{0,1:T(8,128)} %fusion.3, bf16[2,16,24,1600]{3,2,1,0:T(8,128)(2,1)} %constant_dynamic-update-slice_fusion, bf16[256,1600]{0,1:T(8,128)(2,1)} %copy-done.4), kind=kOutput, calls=%fused_computation.15 | convolution fusion | flops 630849536 | bytes 8192000 | tf_op jit(solution)/shard_map/tsh,shd->td/dot_general | solution.py:219
  144.5 5.0 %collective-permute-done.9 = bf16[256,1600]{0,1:T(8,128)(2,1)} collective-permute-done((bf16[256,1600]{0,1:T(8,128)(2,1)}, bf16[256,1600]{0,1:T(8,128)(2,1)}, u32[]{:S(2)}, u32[]{:S(2)}) %collective-permute-start.9) | collective-permute-done | bytes 819232 | tf_op jit(solution)/shard_map/ppermute | solution.py:239
  149.5 2.7 %fusion.47 = bf16[1,256,1600]{1,2,0:T(8,128)(2,1)} fusion(f32[256,1600]{0,1:T(8,128)} %fusion.8, bf16[256,1600]{0,1:T(8,128)(2,1)} %collective-permute-done.9, pred[256]{0:T(512)(128)(4,1)S(1)} %copy-done.14), kind=kLoop, calls=%fused_computation.61 | loop fusion | flops 1638400 | bytes 3277056 | tf_op jit(solution)/shard_map/broadcast_in_dim | solution.py:244
  (63 shorter events, 1.4 us)
Async XLA Ops:
  6.5 64.6 %copy-start = (bf16[1024,1600]{0,1:T(8,128)(2,1)S(1)}, bf16[1024,1600]{0,1:T(8,128)(2,1)}, u32[]{:S(2)}) copy-start(bf16[1024,1600]{0,1:T(8,128)(2,1)} %param.19) | copy-start | bytes 9830404
  6.5 108.7 %all-gather.3.cloned.1.call-start = ((), (), s32[]{:S(2)}) async-start(), calls=%async_computation | async-start | bytes 10862592 | tf_op jit(solution)/shard_map/all_gather | solution.py:208
  10.3 21.4 %collective-permute-start = (bf16[2,24,1600]{2,1,0:T(8,128)(2,1)S(1)}, bf16[2,24,1600]{2,1,0:T(8,128)(2,1)}, u32[]{:S(2)}, u32[]{:S(2)}) collective-permute-start(bf16[2,24,1600]{2,1,0:T(8,128)(2,1)S(1)} %get-tuple-element.24), channel_id=1, source_target_pairs={{0,4},{1,5},{2,0},{3,1},{4,8},{5,9},{6,2},{7,3},{8,12},{9,13},{10,... | collective-permute-start | bytes 460808 | tf_op jit(solution)/shard_map/ppermute | solution.py:51
  10.3 21.4 %collective-permute-start.1 = (bf16[2,24,1600]{2,1,0:T(8,128)(2,1)S(1)}, bf16[2,24,1600]{2,1,0:T(8,128)(2,1)}, u32[]{:S(2)}, u32[]{:S(2)}) collective-permute-start(bf16[2,24,1600]{2,1,0:T(8,128)(2,1)S(1)} %get-tuple-element.24), channel_id=1, source_target_pairs={{0,2},{1,3},{2,6},{3,7},{4,0},{5,1},{6,10},{7,11},{8,4},{9,5},{10,... | collective-permute-start | bytes 460808 | tf_op jit(solution)/shard_map/ppermute | solution.py:51
  12.3 6.5 %copy-start.16 = (s32[1,16]{1,0:T(1,128)S(1)}, s32[1,16]{1,0:T(1,128)}, u32[]{:S(2)}) copy-start(s32[1,16]{1,0:T(1,128)} %param.22) | copy-start | bytes 196
  12.3 6.5 %copy-start.17 = (s32[1,16]{1,0:T(1,128)S(1)}, s32[1,16]{1,0:T(1,128)}, u32[]{:S(2)}) copy-start(s32[1,16]{1,0:T(1,128)} %param.23) | copy-start | bytes 196
  12.3 7.8 %copy-start.18 = (s32[1,16]{1,0:T(1,128)S(1)}, s32[1,16]{1,0:T(1,128)}, u32[]{:S(2)}) copy-start(s32[1,16]{1,0:T(1,128)} %param.24) | copy-start | bytes 196
  12.3 7.8 %copy-start.19 = (s32[1,2]{1,0:T(1,128)S(1)}, s32[1,2]{1,0:T(1,128)}, u32[]{:S(2)}) copy-start(s32[1,2]{1,0:T(1,128)} %param.25) | copy-start | bytes 28
  12.3 8.7 %copy-start.10 = (bf16[1,8,1600]{2,1,0:T(8,128)(2,1)S(1)}, bf16[1,8,1600]{2,1,0:T(8,128)(2,1)}, u32[]{:S(2)}) copy-start(bf16[1,8,1600]{2,1,0:T(8,128)(2,1)} %param.17) | copy-start | bytes 76804
  12.3 9.1 %copy-start.11 = (bf16[1,8,2048]{2,1,0:T(8,128)(2,1)S(1)}, bf16[1,8,2048]{2,1,0:T(8,128)(2,1)}, u32[]{:S(2)}) copy-start(bf16[1,8,2048]{2,1,0:T(8,128)(2,1)} %param.16) | copy-start | bytes 98308
  20.1 1.2 copy-start.13
  21.5 5.3 %copy-start.6 = (pred[256,256]{0,1:T(8,128)(4,1)}, pred[256,256]{0,1:T(8,128)(4,1)S(1)}, u32[]{:S(2)}) copy-start(pred[256,256]{0,1:T(8,128)(4,1)S(1)} %fusion.78) | copy-start | bytes 196612
  21.5 5.3 %copy-start.3 = (bf16[1,256,1024]{1,2,0:T(8,128)(2,1)S(1)}, bf16[1,256,1024]{1,2,0:T(8,128)(2,1)}, u32[]{:S(2)}) copy-start(bf16[1,256,1024]{1,2,0:T(8,128)(2,1)} %copy.58) | copy-start | bytes 1572868
  21.5 5.3 %copy-start.5 = (bf16[256,1024]{0,1:T(8,128)(2,1)S(1)}, bf16[256,1024]{0,1:T(8,128)(2,1)}, u32[]{:S(2)}) copy-start(bf16[256,1024]{0,1:T(8,128)(2,1)} %copy.61) | copy-start | bytes 1572868
  31.7 28.0 %collective-permute-start.2 = (bf16[2,24,1600]{2,1,0:T(8,128)(2,1)}, bf16[2,24,1600]{2,1,0:T(8,128)(2,1)}, u32[]{:S(2)}, u32[]{:S(2)}) collective-permute-start(bf16[2,24,1600]{2,1,0:T(8,128)(2,1)} %collective-permute-done), channel_id=1, source_target_pairs={{0,4},{1,5},{2,0},{3,1},{4,8},{5,9},{6,2},{7,3},{8,12},{9,13},{10,... | collective-permute-start | bytes 460808 | tf_op jit(solution)/shard_map/ppermute | solution.py:51
  31.8 28.0 %collective-permute-start.3 = (bf16[2,24,1600]{2,1,0:T(8,128)(2,1)}, bf16[2,24,1600]{2,1,0:T(8,128)(2,1)}, u32[]{:S(2)}, u32[]{:S(2)}) collective-permute-start(bf16[2,24,1600]{2,1,0:T(8,128)(2,1)} %collective-permute-done.1), channel_id=1, source_target_pairs={{0,2},{1,3},{2,6},{3,7},{4,0},{5,1},{6,10},{7,11},{8,4},{9,5},{10,... | collective-permute-start | bytes 460808 | tf_op jit(solution)/shard_map/ppermute | solution.py:51
  59.7 16.9 %collective-permute-start.4 = (bf16[2,24,1600]{2,1,0:T(8,128)(2,1)}, bf16[2,24,1600]{2,1,0:T(8,128)(2,1)}, u32[]{:S(2)}, u32[]{:S(2)}) collective-permute-start(bf16[2,24,1600]{2,1,0:T(8,128)(2,1)} %collective-permute-done.2), channel_id=1, source_target_pairs={{0,4},{1,5},{2,0},{3,1},{4,8},{5,9},{6,2},{7,3},{8,12},{9,13},{10,... | collective-permute-start | bytes 460808 | tf_op jit(solution)/shard_map/ppermute | solution.py:51
  62.5 14.1 %collective-permute-start.5 = (bf16[2,24,1600]{2,1,0:T(8,128)(2,1)}, bf16[2,24,1600]{2,1,0:T(8,128)(2,1)}, u32[]{:S(2)}, u32[]{:S(2)}) collective-permute-start(bf16[2,24,1600]{2,1,0:T(8,128)(2,1)} %collective-permute-done.3), channel_id=1, source_target_pairs={{0,2},{1,3},{2,6},{3,7},{4,0},{5,1},{6,10},{7,11},{8,4},{9,5},{10,... | collective-permute-start | bytes 460808 | tf_op jit(solution)/shard_map/ppermute | solution.py:51
  65.9 2.4 %copy-start.1 = (f32[16,256,256]{1,2,0:T(8,128)S(1)}, f32[16,256,256]{1,2,0:T(8,128)}, u32[]{:S(2)}) copy-start(f32[16,256,256]{1,2,0:T(8,128)} %get-tuple-element.51) | copy-start | bytes 12582916
  65.9 2.4 %copy-start.7 = (pred[256,256]{0,1:T(8,128)(4,1)S(1)}, pred[256,256]{0,1:T(8,128)(4,1)}, u32[]{:S(2)}) copy-start(pred[256,256]{0,1:T(8,128)(4,1)} %copy-done.6) | copy-start | bytes 196612
  68.3 1.0 copy-start.8
  69.3 1.1 copy-start.9
  70.5 1.1 copy-start.15
  71.6 1.3 copy-start.12
  72.7 21.7 %copy-start.2 = (f32[256,1600]{0,1:T(8,128)}, f32[256,1600]{0,1:T(8,128)S(1)}, u32[]{:S(2)}) copy-start(f32[256,1600]{0,1:T(8,128)S(1)} %get-tuple-element.53) | copy-start | bytes 4915204
  76.6 16.9 %collective-permute-start.6 = (bf16[2,24,1600]{2,1,0:T(8,128)(2,1)}, bf16[2,24,1600]{2,1,0:T(8,128)(2,1)S(1)}, u32[]{:S(2)}, u32[]{:S(2)}) collective-permute-start(bf16[2,24,1600]{2,1,0:T(8,128)(2,1)} %collective-permute-done.4), channel_id=1, source_target_pairs={{0,4},{1,5},{2,0},{3,1},{4,8},{5,9},{6,2},{7,3},{8,12},{9,13},{10,... | collective-permute-start | bytes 460808 | tf_op jit(solution)/shard_map/ppermute | solution.py:53
  94.2 3.6 %collective-permute-start.7 = (bf16[2,8,24,1600]{3,2,1,0:T(8,128)(2,1)S(1)}, bf16[2,8,24,1600]{3,2,1,0:T(8,128)(2,1)S(1)}, u32[]{:S(2)}, u32[]{:S(2)}) collective-permute-start(bf16[2,8,24,1600]{3,2,1,0:T(8,128)(2,1)S(1)} %get-tuple-element.31), channel_id=1, source_target_pairs={{0,1},{1,0},{2,3},{3,2},{4,5},{5,4},{6,7},{7,6},{8,9},{9,8},{10,11... | collective-permute-start | bytes 3686408 | tf_op jit(solution)/shard_map/ppermute | solution.py:78
  94.4 0.9 copy-start.4
  94.4 20.8 %collective-permute-start.8 = (bf16[256,1600]{0,1:T(8,128)(2,1)S(1)}, bf16[256,1600]{0,1:T(8,128)(2,1)}, u32[]{:S(2)}, u32[]{:S(2)}) collective-permute-start(bf16[256,1600]{0,1:T(8,128)(2,1)S(1)} %divide_convert_fusion), channel_id=1, source_target_pairs={{0,16},{16,0},{1,17},{17,1},{2,18},{18,2},{3,19},{19,3},{4,20},{20... | collective-permute-start | bytes 2457608 | tf_op jit(solution)/shard_map/ppermute | solution.py:237
  129.3 20.2 %collective-permute-start.9 = (bf16[256,1600]{0,1:T(8,128)(2,1)}, bf16[256,1600]{0,1:T(8,128)(2,1)}, u32[]{:S(2)}, u32[]{:S(2)}) collective-permute-start(bf16[256,1600]{0,1:T(8,128)(2,1)} %fusion.10), channel_id=1, source_target_pairs={{0,16},{16,0},{1,17},{17,1},{2,18},{18,2},{3,19},{19,3},{4,20},{20... | collective-permute-start | bytes 2457608 | tf_op jit(solution)/shard_map/ppermute | solution.py:239
  138.5 11.0 %copy-start.14 = (pred[256]{0:T(512)(128)(4,1)S(1)}, pred[256]{0:T(512)(128)(4,1)}, u32[]{:S(2)}) copy-start(pred[256]{0:T(512)(128)(4,1)} %copy-done.13) | copy-start | bytes 772
Sparse Core Ops, SparseCore 0:
  9.6 95.9 all-gather.2

commit v15 on v11

--- a/solution.py
+++ b/solution.py
@@ -172,7 +172,7 @@
     group_count = lax.axis_size("group")
     hidden_part = fc_weight.shape[1]
     both = jnp.stack([fc_weight.T, proj_weight])
-    keep = hidden_part * 4 // 5 // 16 * 16
+    keep = (hidden_part - 8) // 16 * 16
     if ring_plan is None or keep == 0:
         banks = [lax.all_gather(both, "dev", axis=1)]
     else:

time: 166 us -> 154 us (0.928)
  starting transfers between devices: 16.7 us -> 6.27 us
  waiting for transfers between devices: 33.8 us -> 26.6 us
  local copies, waits for them, and re-layouts: 25.4 us -> 30 us
  blocking collectives: 25.3 us -> 27 us
    another operation x1 -> x17, local copies, waits for them, and re-layouts: 0.68 us -> 17.5 us  [ring_gather(): return jnp.stack(pieces, axis=1)]
    unnamed x41 -> x31, local copies, waits for them, and re-layouts: 14.9 us -> 2.66 us
    ppermute x3, starting transfers between devices: 9.53 us -> 2.02 us  [ring_gather(): behind = lax.ppermute(behind, 'dev', backward)]
    ppermute x4, waiting for transfers between devices: 16 us -> 9.85 us  [ring_gather(): ahead = lax.ppermute(ahead, 'dev', forward)]
    ppermute x4, starting transfers between devices: 3.48 us -> 0.54 us  [ring_gather(): ahead = lax.ppermute(ahead, 'dev', forward)]
    dot_general x2, matrix products: 9.76 us -> 7.03 us  [feed(): jnp.einsum('tsh,shd->td', activated, bank[1], preferred_element_type=jnp....]
    dot_general x2, matrix products: 18.8 us -> 20.9 us  [feed(): part = jnp.dot(activated, proj_rows, preferred_element_type=jnp.float32)]
    all_gather x1, blocking collectives: 25.3 us -> 27 us  [per_device(): gathered = lax.all_gather(local_kv, 'dev', axis=0, tiled=True)]
  transfers between devices with their start and end apart: 18 -> 18, of which waited for: 6 -> 8; matrix products, arithmetic and copies ran while one was open for 37% -> 42% of each run, Pallas kernels for 0% -> 0%
where the time goes in v15:
time: 154 us; the launch traced here: 152 us
  matrix products  38.4 us (25%)
  local copies, waits for them, and re-layouts  30 us (19%)
  blocking collectives  27 us (18%)
  waiting for transfers between devices  26.6 us (17%)
  between operations  13.7 us (9%)
  other arithmetic  10.4 us (7%)
  starting transfers between devices  6.27 us (4%)
    all_gather x1, blocking collectives, per_device(): gathered = lax.all_gather(local_kv, 'dev', axis=0, tiled=True)  27 us
    dot_general x2, matrix products, feed(): part = jnp.dot(activated, proj_rows, preferred_element_type=jnp.float32)  20.9 us
    another operation x17, local copies, waits for them, and re-layouts, ring_gather(): return jnp.stack(pieces, axis=1)  17.5 us
    ppermute x4, waiting for transfers between devices, ring_gather(): ahead = lax.ppermute(ahead, 'dev', forward)  9.85 us
    ppermute x1, waiting for transfers between devices, per_device(): returned.append(lax.ppermute(partner_feed, 'group', back))  8.58 us
    ppermute x3, waiting for transfers between devices, ring_gather(): behind = lax.ppermute(behind, 'dev', backward)  8.14 us
    dot_general x2, matrix products, feed(): jnp.einsum('tsh,shd->td', activated, bank[1], preferred_element_type=jnp....  7.03 us
    slice x3, local copies, waits for them, and re-layouts, absorb(): key_rows = keyval[:, :width_att].reshape(row_count, head_count, head_size)  6.17 us
  transfers between devices with their start and end apart: 18, of which 8 were waited for; matrix products, arithmetic and copies ran while one was open for 42% of the time, Pallas kernels for 0%

profile of v15, /device:TPU:0, one launch (start us, length us, event | category | flops | bytes accessed | tf_op | source)
XLA Modules:
  0.0 152.4 jit_solution(3860531920203111276)
XLA Ops:
  6.5 2.2 %pad_maximum_fusion = bf16[2,112,1600]{2,1,0:T(8,128)(2,1)} fusion(bf16[1,120,1600]{2,1,0:T(8,128)(2,1)} %bitcast.180, bf16[1,120,1600]{2,1,0:T(8,128)(2,1)} %bitcast.183), kind=kLoop, calls=%fused_computation.70 | loop fusion | flops 1433600 | bytes 1484800 | tf_op jit(solution)/shard_map/stack | solution.py:174
  8.7 2.3 %fusion.131 = (bf16[256,1024]{1,0:T(8,128)(2,1)}, bf16[256,1024]{1,0:T(8,128)(2,1)}) fusion(bf16[256,2048]{1,0:T(8,128)(2,1)} %bitcast.187), kind=kLoop, calls=%fused_computation.153 | loop fusion | bytes 2097152 | tf_op jit(solution)/shard_map/slice | solution.py:30
  11.0 2.1 %copy.395 = bf16[256,1024]{0,1:T(8,128)(2,1)} copy(bf16[256,1024]{1,0:T(8,128)(2,1)} %get-tuple-element.8) | data formatting | bytes 1048576 | tf_op jit(solution)/shard_map/slice | solution.py:31
  13.1 2.1 %copy.391 = bf16[1,256,1024]{1,2,0:T(8,128)(2,1)} copy(bf16[1,256,1024]{2,1,0:T(8,128)(2,1)} %param.14) | data formatting | bytes 1048576 | tf_op args[1]
  15.2 2.1 %copy.394 = bf16[256,1024]{0,1:T(8,128)(2,1)} copy(bf16[256,1024]{1,0:T(8,128)(2,1)} %get-tuple-element.7) | data formatting | bytes 1048576 | tf_op jit(solution)/shard_map/slice | solution.py:30
  18.5 5.1 %fusion.11 = bf16[8,2048]{1,0:T(8,128)(2,1)S(1)} fusion(bf16[1600,2048]{1,0:T(8,128)(2,1)} %param.18, bf16[1,8,2048]{2,1,0:T(8,128)(2,1)S(1)} %copy-done.9, pred[]{:T(512)} %compare_reduce_fusion, bf16[1,8,1600]{2,1,0:T(8,128)(2,1)S(1)} %copy-done.8, f32[8]{0:T(128)S(1)} %add_sqrt_fusion.1, f32[8]{0:T(128)S(1)} %broadcast_multiply_fusion.1), kind=kOutput, calls=%fused_computation.21 | convolution fusion | flops 52512768 | bytes 6644801 | tf_op jit(solution)/shard_map/dot_general | solution.py:140
  23.6 27.0 %all_gather.9 = bf16[128,2048]{1,0:T(8,128)(2,1)S(1)} all-gather(bf16[8,2048]{1,0:T(8,128)(2,1)S(1)} %fusion.11), channel_id=1, replica_groups=mesh['group'=2,'dev'=16] {'dev'}, dimensions={0}, use_global_device_ids=true | all-gather | bytes 557056 | tf_op jit(solution)/shard_map/all_gather | solution.py:146
  50.6 0.7 fusion.132
  51.4 1.8 %copy.390 = bf16[128,1024]{0,1:T(8,128)(2,1)} copy(bf16[128,1024]{1,0:T(8,128)(2,1)} %get-tuple-element.10) | data formatting | bytes 524288 | tf_op jit(solution)/shard_map/slice | solution.py:30
  53.1 0.8 copy.392
  54.1 0.7 fusion.108
  55.6 1.9 %bitcast_reduce_fusion = (f32[16,256]{1,0:T(8,128)S(1)}, f32[16,128,256]{2,1,0:T(8,128)S(1)}) fusion(bf16[128,16,64]{0,2,1:T(8,128)(2,1)} %bitcast.188, bf16[256,16,64]{0,2,1:T(8,128)(2,1)} %bitcast.178), kind=kOutput, calls=%fused_computation.23 | convolution fusion | flops 68153344 | bytes 2899968 | tf_op jit(solution)/shard_map/qhd,khd->hqk/dot_general | solution.py:33
  57.5 0.8 fusion.4
  58.7 1.0 fusion.5
  59.8 1.1 fusion.34
  62.1 1.1 fusion.133
  63.5 1.1 divide_convert_fusion
  64.5 1.6 %collective-permute-start.15 = (bf16[256,1600]{0,1:T(8,128)(2,1)}, bf16[256,1600]{0,1:T(8,128)(2,1)}, u32[]{:S(2)}, u32[]{:S(2)}) collective-permute-start(bf16[256,1600]{0,1:T(8,128)(2,1)} %divide_convert_fusion), channel_id=1, source_target_pairs={{0,16},{16,0},{1,17},{17,1},{2,18},{18,2},{3,19},{19,3},{4,20},{20... | collective-permute-start | bytes 2457608 | tf_op jit(solution)/shard_map/ppermute | solution.py:210
  66.2 2.0 %collective-permute-start.1 = (bf16[2,8,1600]{2,1,0:T(8,128)(2,1)S(1)}, bf16[2,8,1600]{2,1,0:T(8,128)(2,1)S(1)}, u32[]{:S(2)}, u32[]{:S(2)}) collective-permute-start(bf16[2,8,1600]{2,1,0:T(8,128)(2,1)S(1)} %pad_maximum_fusion.1), channel_id=1, source_target_pairs={{0,2},{1,3},{2,6},{3,7},{4,0},{5,1},{6,10},{7,11},{8,4},{9,5},{10,... | collective-permute-start | bytes 153608 | tf_op jit(solution)/shard_map/ppermute | solution.py:55
  68.2 3.5 %collective-permute-done = bf16[2,8,1600]{2,1,0:T(8,128)(2,1)S(1)} collective-permute-done((bf16[2,8,1600]{2,1,0:T(8,128)(2,1)S(1)}, bf16[2,8,1600]{2,1,0:T(8,128)(2,1)S(1)}, u32[]{:S(2)}, u32[]{:S(2)}) %collective-permute-start) | collective-permute-done | bytes 51232 | tf_op jit(solution)/shard_map/ppermute | solution.py:52
  71.8 1.9 %collective-permute-done.1 = bf16[2,8,1600]{2,1,0:T(8,128)(2,1)S(1)} collective-permute-done((bf16[2,8,1600]{2,1,0:T(8,128)(2,1)S(1)}, bf16[2,8,1600]{2,1,0:T(8,128)(2,1)S(1)}, u32[]{:S(2)}, u32[]{:S(2)}) %collective-permute-start.1) | collective-permute-done | bytes 51232 | tf_op jit(solution)/shard_map/ppermute | solution.py:55
  73.9 3.0 %collective-permute-done.2 = bf16[2,8,1600]{2,1,0:T(8,128)(2,1)S(1)} collective-permute-done((bf16[2,8,1600]{2,1,0:T(8,128)(2,1)S(1)}, bf16[2,8,1600]{2,1,0:T(8,128)(2,1)S(1)}, u32[]{:S(2)}, u32[]{:S(2)}) %collective-permute-start.2) | collective-permute-done | bytes 51232 | tf_op jit(solution)/shard_map/ppermute | solution.py:52
  77.1 2.8 %collective-permute-done.3 = bf16[2,8,1600]{2,1,0:T(8,128)(2,1)S(1)} collective-permute-done((bf16[2,8,1600]{2,1,0:T(8,128)(2,1)S(1)}, bf16[2,8,1600]{2,1,0:T(8,128)(2,1)S(1)}, u32[]{:S(2)}, u32[]{:S(2)}) %collective-permute-start.3) | collective-permute-done | bytes 51232 | tf_op jit(solution)/shard_map/ppermute | solution.py:55
  80.0 2.2 %collective-permute-done.4 = bf16[2,8,1600]{2,1,0:T(8,128)(2,1)S(1)} collective-permute-done((bf16[2,8,1600]{2,1,0:T(8,128)(2,1)S(1)}, bf16[2,8,1600]{2,1,0:T(8,128)(2,1)S(1)}, u32[]{:S(2)}, u32[]{:S(2)}) %collective-permute-start.4) | collective-permute-done | bytes 51232 | tf_op jit(solution)/shard_map/ppermute | solution.py:52
  82.4 3.4 %collective-permute-done.5 = bf16[2,8,1600]{2,1,0:T(8,128)(2,1)S(1)} collective-permute-done((bf16[2,8,1600]{2,1,0:T(8,128)(2,1)S(1)}, bf16[2,8,1600]{2,1,0:T(8,128)(2,1)S(1)}, u32[]{:S(2)}, u32[]{:S(2)}) %collective-permute-start.5) | collective-permute-done | bytes 51232 | tf_op jit(solution)/shard_map/ppermute | solution.py:55
  86.3 1.1 collective-permute-done.6
  87.6 0.7 copy.399
  88.3 0.7 copy.405
  89.1 0.7 copy.400
  89.8 0.7 copy.401
  90.5 0.7 copy.406
  91.2 0.7 copy.407
  92.0 0.7 copy.402
  92.7 0.7 copy.403
  93.4 0.7 copy.408
  94.1 0.7 copy.409
  94.9 0.7 copy.404
  95.6 0.7 copy.410
  96.3 0.7 copy.411
  97.0 0.7 copy.412
  97.7 7.2 %stack.79 = bf16[2,16,8,1600]{3,1,2,0:T(8,128)(2,1)} concatenate(bf16[2,1,8,1600]{3,1,2,0:T(2,128)(2,1)S(1)} %copy.397, bf16[2,1,8,1600]{3,1,2,0:T(2,128)(2,1)S(1)} %copy.398, bf16[2,1,8,1600]{3,1,2,0:T(2,128)(2,1)} %copy.399, bf16[2,1,8,1600]{3,1,2,0:T(2,128)(2,1)} %copy.400, bf16[2,1,8,1600]{3,1,2,0:T(2,128)(2,1)} %copy.401, bf16[2,1,8,1600]{3,1,2,0:T(2,128)(2,1)} %copy.402, ...), dimensions={1} | concatenate | bytes 1638400 | tf_op jit(solution)/shard_map/stack | solution.py:58
  104.9 3.4 %convolution_bitcast_fusion.1 = f32[256,1600]{0,1:T(8,128)} fusion(bf16[2,16,8,1600]{3,1,2,0:T(8,128)(2,1)} %stack.79, bf16[256,1600]{0,1:T(8,128)(2,1)} %divide_convert_fusion), kind=kOutput, calls=%fused_computation.17 | convolution fusion | flops 210010112 | bytes 3276800 | tf_op jit(solution)/shard_map/tsh,shd->td/dot_general | solution.py:192
  108.4 3.6 %convolution_bitcast_fusion = f32[256,1600]{0,1:T(8,128)} fusion(bf16[2,16,8,1600]{3,1,2,0:T(8,128)(2,1)} %stack.79, bf16[256,1600]{0,1:T(8,128)(2,1)} %collective-permute-done.15), kind=kOutput, calls=%fused_computation.16 | convolution fusion | flops 210010112 | bytes 3276800 | tf_op jit(solution)/shard_map/tsh,shd->td/dot_general | solution.py:192
  112.0 10.1 %fusion.10 = bf16[256,1600]{0,1:T(8,128)(2,1)} fusion(f32[256,1600]{0,1:T(8,128)} %convolution_bitcast_fusion, bf16[2,1792,1600]{2,1,0:T(8,128)(2,1)} %all-gather.3.cloned.1.call-done, bf16[256,1600]{0,1:T(8,128)(2,1)} %collective-permute-done.15), kind=kOutput, calls=%fused_computation.19 | convolution fusion | flops 2940960768 | bytes 14745600 | tf_op jit(solution)/shard_map/dot_general | solution.py:202
  122.0 1.4 collective-permute-start.16
  123.4 10.8 %fusion.9 = f32[256,1600]{0,1:T(8,128)} fusion(f32[256,1600]{0,1:T(8,128)} %copy-done.1, f32[256,1600]{0,1:T(8,128)} %convolution_bitcast_fusion.1, bf16[2,1792,1600]{2,1,0:T(8,128)(2,1)} %all-gather.3.cloned.1.call-done, bf16[256,1600]{0,1:T(8,128)(2,1)} %divide_convert_fusion), kind=kOutput, calls=%fused_computation.18 | convolution fusion | flops 2940960768 | bytes 17203200 | tf_op jit(solution)/shard_map/dot_general | solution.py:202
  134.2 8.6 %collective-permute-done.16 = bf16[256,1600]{0,1:T(8,128)(2,1)} collective-permute-done((bf16[256,1600]{0,1:T(8,128)(2,1)}, bf16[256,1600]{0,1:T(8,128)(2,1)}, u32[]{:S(2)}, u32[]{:S(2)}) %collective-permute-start.16) | collective-permute-done | bytes 819232 | tf_op jit(solution)/shard_map/ppermute | solution.py:212
  142.8 2.7 %fusion.53 = bf16[1,256,1600]{1,2,0:T(8,128)(2,1)} fusion(f32[256,1600]{0,1:T(8,128)} %fusion.9, bf16[256,1600]{0,1:T(8,128)(2,1)} %collective-permute-done.16, pred[256]{0:T(512)(128)(4,1)S(1)} %iota_compare_fusion.2), kind=kLoop, calls=%fused_computation.65 | loop fusion | flops 1638400 | bytes 3277056 | tf_op jit(solution)/shard_map/broadcast_in_dim | solution.py:217
  (76 shorter events, 5.4 us)
Async XLA Ops:
  6.5 55.0 %copy-start = (bf16[1024,1600]{0,1:T(8,128)(2,1)S(1)}, bf16[1024,1600]{0,1:T(8,128)(2,1)}, u32[]{:S(2)}) copy-start(bf16[1024,1600]{0,1:T(8,128)(2,1)} %param.19) | copy-start | bytes 9830404
  6.5 105.4 %all-gather.3.cloned.1.call-start = ((), (), s32[]{:S(2)}) async-start(), calls=%async_computation | async-start | bytes 12673024 | tf_op jit(solution)/shard_map/all_gather | solution.py:181
  11.0 6.3 %copy-start.11 = (s32[1,16]{1,0:T(1,128)S(1)}, s32[1,16]{1,0:T(1,128)}, u32[]{:S(2)}) copy-start(s32[1,16]{1,0:T(1,128)} %param.24) | copy-start | bytes 196
  11.0 6.3 %copy-start.12 = (s32[1,2]{1,0:T(1,128)S(1)}, s32[1,2]{1,0:T(1,128)}, u32[]{:S(2)}) copy-start(s32[1,2]{1,0:T(1,128)} %param.25) | copy-start | bytes 28
  11.0 7.1 %copy-start.8 = (bf16[1,8,1600]{2,1,0:T(8,128)(2,1)S(1)}, bf16[1,8,1600]{2,1,0:T(8,128)(2,1)}, u32[]{:S(2)}) copy-start(bf16[1,8,1600]{2,1,0:T(8,128)(2,1)} %param.17) | copy-start | bytes 76804
  11.0 7.5 %copy-start.9 = (bf16[1,8,2048]{2,1,0:T(8,128)(2,1)S(1)}, bf16[1,8,2048]{2,1,0:T(8,128)(2,1)}, u32[]{:S(2)}) copy-start(bf16[1,8,2048]{2,1,0:T(8,128)(2,1)} %param.16) | copy-start | bytes 98308
  23.6 30.4 %copy-start.13 = (s32[1,16]{1,0:T(1,128)S(1)}, s32[1,16]{1,0:T(1,128)}, u32[]{:S(2)}) copy-start(s32[1,16]{1,0:T(1,128)} %param.22) | copy-start | bytes 196
  23.6 30.4 %copy-start.14 = (s32[1,16]{1,0:T(1,128)S(1)}, s32[1,16]{1,0:T(1,128)}, u32[]{:S(2)}) copy-start(s32[1,16]{1,0:T(1,128)} %param.23) | copy-start | bytes 196
  54.0 3.5 %copy-start.2 = (bf16[1,256,1024]{1,2,0:T(8,128)(2,1)S(1)}, bf16[1,256,1024]{1,2,0:T(8,128)(2,1)}, u32[]{:S(2)}) copy-start(bf16[1,256,1024]{1,2,0:T(8,128)(2,1)} %copy.391) | copy-start | bytes 1572868
  54.0 3.5 %copy-start.5 = (bf16[256,1024]{0,1:T(8,128)(2,1)S(1)}, bf16[256,1024]{0,1:T(8,128)(2,1)}, u32[]{:S(2)}) copy-start(bf16[256,1024]{0,1:T(8,128)(2,1)} %copy.394) | copy-start | bytes 1572868
  58.7 1.0 copy-start.6
  59.8 1.1 copy-start.7
  60.9 1.1 copy-start.10
  63.1 2.9 %copy-start.1 = (f32[256,1600]{0,1:T(8,128)}, f32[256,1600]{0,1:T(8,128)S(1)}, u32[]{:S(2)}) copy-start(f32[256,1600]{0,1:T(8,128)S(1)} %get-tuple-element.19) | copy-start | bytes 4915204
  63.2 2.9 %copy-start.3 = (bf16[120,1600]{1,0:T(8,128)(2,1)S(1)}, bf16[120,1600]{1,0:T(8,128)(2,1)}, u32[]{:S(2)}) copy-start(bf16[120,1600]{1,0:T(8,128)(2,1)} %param.21) | copy-start | bytes 1152004
  63.2 2.9 %copy-start.4 = (bf16[1600,120]{0,1:T(8,128)(2,1)S(1)}, bf16[1600,120]{0,1:T(8,128)(2,1)}, u32[]{:S(2)}) copy-start(bf16[1600,120]{0,1:T(8,128)(2,1)} %param.20) | copy-start | bytes 1152004
  64.5 43.9 %collective-permute-start.15 = (bf16[256,1600]{0,1:T(8,128)(2,1)}, bf16[256,1600]{0,1:T(8,128)(2,1)}, u32[]{:S(2)}, u32[]{:S(2)}) collective-permute-start(bf16[256,1600]{0,1:T(8,128)(2,1)} %divide_convert_fusion), channel_id=1, source_target_pairs={{0,16},{16,0},{1,17},{17,1},{2,18},{18,2},{3,19},{19,3},{4,20},{20... | collective-permute-start | bytes 2457608 | tf_op jit(solution)/shard_map/ppermute | solution.py:210
  66.1 5.6 %collective-permute-start = (bf16[2,8,1600]{2,1,0:T(8,128)(2,1)S(1)}, bf16[2,8,1600]{2,1,0:T(8,128)(2,1)S(1)}, u32[]{:S(2)}, u32[]{:S(2)}) collective-permute-start(bf16[2,8,1600]{2,1,0:T(8,128)(2,1)S(1)} %pad_maximum_fusion.1), channel_id=1, source_target_pairs={{0,4},{1,5},{2,0},{3,1},{4,8},{5,9},{6,2},{7,3},{8,12},{9,13},{10,... | collective-permute-start | bytes 153608 | tf_op jit(solution)/shard_map/ppermute | solution.py:52
  66.2 7.5 %collective-permute-start.1 = (bf16[2,8,1600]{2,1,0:T(8,128)(2,1)S(1)}, bf16[2,8,1600]{2,1,0:T(8,128)(2,1)S(1)}, u32[]{:S(2)}, u32[]{:S(2)}) collective-permute-start(bf16[2,8,1600]{2,1,0:T(8,128)(2,1)S(1)} %pad_maximum_fusion.1), channel_id=1, source_target_pairs={{0,2},{1,3},{2,6},{3,7},{4,0},{5,1},{6,10},{7,11},{8,4},{9,5},{10,... | collective-permute-start | bytes 153608 | tf_op jit(solution)/shard_map/ppermute | solution.py:55
  71.7 5.3 %collective-permute-start.2 = (bf16[2,8,1600]{2,1,0:T(8,128)(2,1)S(1)}, bf16[2,8,1600]{2,1,0:T(8,128)(2,1)S(1)}, u32[]{:S(2)}, u32[]{:S(2)}) collective-permute-start(bf16[2,8,1600]{2,1,0:T(8,128)(2,1)S(1)} %collective-permute-done), channel_id=1, source_target_pairs={{0,4},{1,5},{2,0},{3,1},{4,8},{5,9},{6,2},{7,3},{8,12},{9,13},{10,... | collective-permute-start | bytes 153608 | tf_op jit(solution)/shard_map/ppermute | solution.py:52
  71.8 5.4 %collective-permute-start.7 = (bf16[2,8,1600]{2,1,0:T(8,128)(2,1)S(1)}, bf16[2,8,1600]{2,1,0:T(8,128)(2,1)S(1)}, u32[]{:S(2)}, u32[]{:S(2)}) collective-permute-start(bf16[2,8,1600]{2,1,0:T(8,128)(2,1)S(1)} %pad_maximum_fusion.1), channel_id=1, source_target_pairs={{0,1},{1,0},{2,3},{3,2},{4,5},{5,4},{6,7},{7,6},{8,9},{9,8},{10,11... | collective-permute-start | bytes 153608 | tf_op jit(solution)/shard_map/ppermute | solution.py:57
  73.7 6.2 %collective-permute-start.3 = (bf16[2,8,1600]{2,1,0:T(8,128)(2,1)S(1)}, bf16[2,8,1600]{2,1,0:T(8,128)(2,1)S(1)}, u32[]{:S(2)}, u32[]{:S(2)}) collective-permute-start(bf16[2,8,1600]{2,1,0:T(8,128)(2,1)S(1)} %collective-permute-done.1), channel_id=1, source_target_pairs={{0,2},{1,3},{2,6},{3,7},{4,0},{5,1},{6,10},{7,11},{8,4},{9,5},{10,... | collective-permute-start | bytes 153608 | tf_op jit(solution)/shard_map/ppermute | solution.py:55
  73.7 6.2 %collective-permute-start.8 = (bf16[2,8,1600]{2,1,0:T(8,128)(2,1)S(1)}, bf16[2,8,1600]{2,1,0:T(8,128)(2,1)S(1)}, u32[]{:S(2)}, u32[]{:S(2)}) collective-permute-start(bf16[2,8,1600]{2,1,0:T(8,128)(2,1)S(1)} %collective-permute-done), channel_id=1, source_target_pairs={{0,1},{1,0},{2,3},{3,2},{4,5},{5,4},{6,7},{7,6},{8,9},{9,8},{10,11... | collective-permute-start | bytes 153608 | tf_op jit(solution)/shard_map/ppermute | solution.py:57
  76.9 5.2 %collective-permute-start.4 = (bf16[2,8,1600]{2,1,0:T(8,128)(2,1)S(1)}, bf16[2,8,1600]{2,1,0:T(8,128)(2,1)S(1)}, u32[]{:S(2)}, u32[]{:S(2)}) collective-permute-start(bf16[2,8,1600]{2,1,0:T(8,128)(2,1)S(1)} %collective-permute-done.2), channel_id=1, source_target_pairs={{0,4},{1,5},{2,0},{3,1},{4,8},{5,9},{6,2},{7,3},{8,12},{9,13},{10,... | collective-permute-start | bytes 153608 | tf_op jit(solution)/shard_map/ppermute | solution.py:52
  77.1 5.2 %collective-permute-start.9 = (bf16[2,8,1600]{2,1,0:T(8,128)(2,1)S(1)}, bf16[2,8,1600]{2,1,0:T(8,128)(2,1)S(1)}, u32[]{:S(2)}, u32[]{:S(2)}) collective-permute-start(bf16[2,8,1600]{2,1,0:T(8,128)(2,1)S(1)} %collective-permute-done.1), channel_id=1, source_target_pairs={{0,1},{1,0},{2,3},{3,2},{4,5},{5,4},{6,7},{7,6},{8,9},{9,8},{10,11... | collective-permute-start | bytes 153608 | tf_op jit(solution)/shard_map/ppermute | solution.py:57
  79.9 5.8 %collective-permute-start.5 = (bf16[2,8,1600]{2,1,0:T(8,128)(2,1)S(1)}, bf16[2,8,1600]{2,1,0:T(8,128)(2,1)S(1)}, u32[]{:S(2)}, u32[]{:S(2)}) collective-permute-start(bf16[2,8,1600]{2,1,0:T(8,128)(2,1)S(1)} %collective-permute-done.3), channel_id=1, source_target_pairs={{0,2},{1,3},{2,6},{3,7},{4,0},{5,1},{6,10},{7,11},{8,4},{9,5},{10,... | collective-permute-start | bytes 153608 | tf_op jit(solution)/shard_map/ppermute | solution.py:55
  79.9 5.8 %collective-permute-start.10 = (bf16[2,8,1600]{2,1,0:T(8,128)(2,1)S(1)}, bf16[2,8,1600]{2,1,0:T(8,128)(2,1)S(1)}, u32[]{:S(2)}, u32[]{:S(2)}) collective-permute-start(bf16[2,8,1600]{2,1,0:T(8,128)(2,1)S(1)} %collective-permute-done.2), channel_id=1, source_target_pairs={{0,1},{1,0},{2,3},{3,2},{4,5},{5,4},{6,7},{7,6},{8,9},{9,8},{10,11... | collective-permute-start | bytes 153608 | tf_op jit(solution)/shard_map/ppermute | solution.py:57
  82.2 5.2 %collective-permute-start.6 = (bf16[2,8,1600]{2,1,0:T(8,128)(2,1)S(1)}, bf16[2,8,1600]{2,1,0:T(8,128)(2,1)S(1)}, u32[]{:S(2)}, u32[]{:S(2)}) collective-permute-start(bf16[2,8,1600]{2,1,0:T(8,128)(2,1)S(1)} %collective-permute-done.4), channel_id=1, source_target_pairs={{0,4},{1,5},{2,0},{3,1},{4,8},{5,9},{6,2},{7,3},{8,12},{9,13},{10,... | collective-permute-start | bytes 153608 | tf_op jit(solution)/shard_map/ppermute | solution.py:52
  82.4 11.8 %collective-permute-start.11 = (bf16[2,8,1600]{2,1,0:T(8,128)(2,1)S(1)}, bf16[2,8,1600]{2,1,0:T(8,128)(2,1)S(1)}, u32[]{:S(2)}, u32[]{:S(2)}) collective-permute-start(bf16[2,8,1600]{2,1,0:T(8,128)(2,1)S(1)} %collective-permute-done.3), channel_id=1, source_target_pairs={{0,1},{1,0},{2,3},{3,2},{4,5},{5,4},{6,7},{7,6},{8,9},{9,8},{10,11... | collective-permute-start | bytes 153608 | tf_op jit(solution)/shard_map/ppermute | solution.py:57
  85.8 9.8 %collective-permute-start.12 = (bf16[2,8,1600]{2,1,0:T(8,128)(2,1)S(1)}, bf16[2,8,1600]{2,1,0:T(8,128)(2,1)S(1)}, u32[]{:S(2)}, u32[]{:S(2)}) collective-permute-start(bf16[2,8,1600]{2,1,0:T(8,128)(2,1)S(1)} %collective-permute-done.4), channel_id=1, source_target_pairs={{0,1},{1,0},{2,3},{3,2},{4,5},{5,4},{6,7},{7,6},{8,9},{9,8},{10,11... | collective-permute-start | bytes 153608 | tf_op jit(solution)/shard_map/ppermute | solution.py:57
  85.8 10.5 %collective-permute-start.13 = (bf16[2,8,1600]{2,1,0:T(8,128)(2,1)S(1)}, bf16[2,8,1600]{2,1,0:T(8,128)(2,1)S(1)}, u32[]{:S(2)}, u32[]{:S(2)}) collective-permute-start(bf16[2,8,1600]{2,1,0:T(8,128)(2,1)S(1)} %collective-permute-done.5), channel_id=1, source_target_pairs={{0,1},{1,0},{2,3},{3,2},{4,5},{5,4},{6,7},{7,6},{8,9},{9,8},{10,11... | collective-permute-start | bytes 153608 | tf_op jit(solution)/shard_map/ppermute | solution.py:57
  87.4 9.6 %collective-permute-start.14 = (bf16[2,8,1600]{2,1,0:T(8,128)(2,1)S(1)}, bf16[2,8,1600]{2,1,0:T(8,128)(2,1)S(1)}, u32[]{:S(2)}, u32[]{:S(2)}) collective-permute-start(bf16[2,8,1600]{2,1,0:T(8,128)(2,1)S(1)} %collective-permute-done.6), channel_id=1, source_target_pairs={{0,1},{1,0},{2,3},{3,2},{4,5},{5,4},{6,7},{7,6},{8,9},{9,8},{10,11... | collective-permute-start | bytes 153608 | tf_op jit(solution)/shard_map/ppermute | solution.py:57
  122.0 20.8 %collective-permute-start.16 = (bf16[256,1600]{0,1:T(8,128)(2,1)}, bf16[256,1600]{0,1:T(8,128)(2,1)}, u32[]{:S(2)}, u32[]{:S(2)}) collective-permute-start(bf16[256,1600]{0,1:T(8,128)(2,1)} %fusion.10), channel_id=1, source_target_pairs={{0,16},{16,0},{1,17},{17,1},{2,18},{18,2},{3,19},{19,3},{4,20},{20... | collective-permute-start | bytes 2457608 | tf_op jit(solution)/shard_map/ppermute | solution.py:212
Sparse Core Ops, SparseCore 0:
  9.5 102.3 all-gather.2
